TPU v7x, 512 devices: a whole 4x8x8 slice. The times are simulated.
512 devices in a mesh: teach: 64 (over z, y), seq: 8 (over x, core).
Axes of the slice: x: 4, y: 8, z: 8, core: 2. Of those that a mesh axis runs over, the one named last changes fastest.
Arguments:
- teacher_in: bfloat16 [2048, 4, 5120], P('teach', None, 'seq'), may hold values from -6 to 6
- teacher_proj: bfloat16 [64, 5120, 512], P('teach', 'seq'), may hold values from -0.078125 to 0.078125
- family: int32 [2048, 4, 1], replicated, may hold values from 0 to 7; in each aligned block of 128 rows (0 to 127, 128 to 255, ..., all dimensions but the last counted through in order) at most 32 rows name the same one
- x_in: bfloat16 [2048, 4, 64, 64], P('seq', None, 'teach'), may hold values from -6 to 6
- b_in: bfloat16 [2048, 4, 64, 128], P('seq', None, 'teach'), may hold values from -1.796875 to 1.796875
- c_in: bfloat16 [2048, 4, 64, 128], P('seq', None, 'teach'), may hold values from -1.796875 to 1.796875
- step_size: float32 [2048, 4, 64], P('seq', None, 'teach'), may hold values from 0.02 to 0.1
- doc_start: int32 [2048, 4], P('seq'), may hold values from 0 to 1, as said below
- a_rate: float32 [64], P('teach'), may hold values from 0.001953125 to 1
- skip_gain: float32 [64], P('teach'), may hold values from 0.5 to 1.5
Outputs:
- grad_x: bfloat16 [2048, 4, 64, 64], P('seq', None, 'teach')
- grad_b: bfloat16 [2048, 4, 64, 128], P('seq', None, 'teach')
- grad_c: bfloat16 [2048, 4, 64, 128], P('seq', None, 'teach')
Inputs may be any that keep to these rules, and one draw needn't show every extreme that they name: In each source block of 128 rows no family appears more than 32 times, and in some source block some family appears exactly 32 times. `doc_start`: in each sequence exactly two ones: at position 0 and at one position from 512 up to 1536.
All inputs are finite; a program needn't handle non-finite values.
Results may differ from a plain program's by a relative error of at most 0.011.
Values may be sent and summed in bfloat16 or wider, within the bound.
No kernel may reach another device: no remote copies, remote signals or barrier semaphores. Data moves between devices by JAX's collectives and lax.ppermute only.
A program may use at most 64 MiB of HBM per device.

v0:
```python
import jax
import jax.numpy as jnp
from jax import lax
from jax.sharding import PartitionSpec as P

TD = 5120
P_SIZE = 64
FAM = 8
HEADS_DEV = 1
CAP = 32


EPS = 1e-06
HIGH = lax.Precision.HIGHEST
QUADRATIC = lax.Precision.HIGH


def prefix(value, axis, join, neutral, backward):
    count = lax.axis_size(axis)
    place = lax.axis_index(axis)
    ahead = count - 1 - place if backward else place
    gathered = jax.tree.map(
        lambda a, kind: lax.all_gather(a.astype(kind), axis), value, (jnp.bfloat16, jnp.bfloat16)
    )
    state = jax.tree.map(lambda a, e: jnp.zeros_like(a) + jnp.asarray(e, a.dtype), value, neutral)

    def one(hop, state):
        source = count - 1 - hop if backward else hop
        return join(
            state,
            jax.tree.map(
                lambda a, own: lax.dynamic_index_in_dim(a, source, 0, False).astype(own.dtype),
                gathered,
                value,
            ),
        )

    return lax.fori_loop(0, ahead, one, state)


def family_slots(fam_block):
    onehot = (fam_block[..., None] == jnp.arange(FAM, dtype=jnp.int32)[None, None, :]).astype(
        jnp.int32
    )
    before = jnp.cumsum(onehot, axis=1) - onehot
    return jnp.sum(before * onehot, axis=2)


def decay_matrix(log_sums, counts):
    places = jnp.arange(log_sums.shape[0])
    lower = places[:, None] >= places[None, :]
    same_doc = counts.T[:, :, None] == counts.T[:, None, :]
    keep_mask = (lower[None] & same_doc)[:, None]
    sums = log_sums.transpose(1, 2, 0)
    gaps = sums[:, :, :, None] - sums[:, :, None, :]
    return jnp.where(keep_mask, jnp.exp(jnp.where(keep_mask, gaps, 0.0)), 0.0)


def chain_combine(earlier, later):
    return (earlier[0] * later[0], later[0][:, :, None, None] * earlier[1] + later[1])


def per_device(
    teacher_in, teacher_proj, family, x_in, b_in, c_in, step_size, doc_start, a_rate, skip_gain
):
    teach_n = lax.axis_size("teach")
    seq_n = lax.axis_size("seq")
    owners = teach_n // FAM
    col_share = P_SIZE // (owners * seq_n)
    heads_all = HEADS_DEV * teach_n
    groups = teach_n // seq_n
    block_pos = teacher_in.shape[0]
    batch_n = teacher_in.shape[1]
    feat_width = teacher_in.shape[2]
    block_rows = block_pos * batch_n
    fam_all = family.reshape(family.shape[0] * family.shape[1])
    own_rows = teacher_in.reshape(block_rows, feat_width)
    own_fam = lax.dynamic_slice_in_dim(fam_all, lax.axis_index("teach") * block_rows, block_rows)
    slot_ids = family_slots(own_fam.reshape(1, block_rows))[0]
    dest_cols = own_fam * CAP + slot_ids
    select = (dest_cols[:, None] == jnp.arange(FAM * CAP, dtype=jnp.int32)[None, :]).astype(
        jnp.bfloat16
    )
    packed = jnp.dot(select.T, own_rows, preferred_element_type=jnp.float32).astype(jnp.bfloat16)
    outgoing = jnp.broadcast_to(
        packed.reshape(1, FAM, CAP, feat_width), (owners, FAM, CAP, feat_width)
    )
    outgoing = outgoing.reshape(teach_n, CAP, feat_width)
    weights = teacher_proj[0]
    received = lax.all_to_all(outgoing, "teach", split_axis=0, concat_axis=0, tiled=True)
    partial_value = jnp.einsum("tkf,fc->tkc", received, weights, preferred_element_type=jnp.float32)
    sq_sums = jnp.sum(jnp.square(received.astype(jnp.float32)), axis=2)
    partial_value, sq_sums = (partial_value, sq_sums)
    totals = lax.psum(sq_sums, "seq")
    row_scale = lax.rsqrt(totals / TD + EPS)
    scaled = (partial_value * row_scale[:, :, None]).reshape(
        teach_n, CAP, heads_all, seq_n, col_share
    )
    summed = lax.psum_scatter(scaled, "seq", scatter_dimension=3, tiled=True).astype(jnp.bfloat16)
    arrived = lax.all_to_all(
        lax.all_to_all(summed[None], "teach", split_axis=3, concat_axis=0, tiled=True),
        "seq",
        split_axis=1,
        concat_axis=4,
        tiled=True,
    )
    shard_rows = groups * block_rows
    shard_fam = lax.dynamic_slice_in_dim(
        fam_all, lax.axis_index("seq") * shard_rows, shard_rows
    ).reshape(groups, block_rows)
    shard_slots = family_slots(shard_fam)
    sources = jnp.arange(groups, dtype=jnp.int32)[:, None]
    row_index = ((shard_fam * groups + sources) * CAP + shard_slots).reshape(shard_rows)
    slot_table = arrived.reshape(owners, FAM, groups, CAP, HEADS_DEV, seq_n * col_share)
    slot_table = slot_table.transpose(1, 2, 3, 0, 4, 5).reshape(
        FAM * groups * CAP, owners, HEADS_DEV, seq_n * col_share
    )
    picked = jnp.take(slot_table, row_index, axis=0)
    target = picked.transpose(0, 2, 1, 3).reshape(groups * block_pos, batch_n, HEADS_DEV, P_SIZE)
    x_full = x_in.astype(jnp.float32)
    b_full = b_in.astype(jnp.float32)
    c_full = c_in.astype(jnp.float32)
    log_sums = jnp.cumsum(-step_size * a_rate[None, None, :], axis=0)
    counts = jnp.cumsum(doc_start, axis=0)
    same_end = (counts == counts[-1][None, :]).astype(jnp.float32)
    to_end = jnp.exp(log_sums[-1][None] - log_sums) * same_end[:, :, None]
    from_start = jnp.exp(log_sums) * (counts == 0).astype(jnp.float32)[:, :, None]
    through = jnp.exp(log_sums[-1]) * (counts[-1] == 0).astype(jnp.float32)[:, None]
    inputs = step_size[..., None] * x_full
    local_state = jnp.einsum("jbh,jbhp,jbhn->bhpn", to_end, inputs, b_full, precision=HIGH)
    start_ones = jnp.ones_like(through)
    _, state_in = prefix(
        (through, local_state),
        "seq",
        chain_combine,
        (start_ones, jnp.zeros_like(local_state)),
        False,
    )
    decay_mat = decay_matrix(log_sums, counts)
    scores = jnp.einsum("ibhn,jbhn->bhij", c_in, b_in, preferred_element_type=jnp.float32)
    mixing = decay_mat * scores
    output = jnp.einsum("bhij,jbhp->ibhp", mixing, inputs, precision=QUADRATIC)
    output = output + from_start[..., None] * jnp.einsum(
        "ibhn,bhpn->ibhp", c_full, state_in, precision=HIGH
    )
    output = output + skip_gain[None, None, :, None] * x_full
    residual = output - target.astype(jnp.float32)
    local_adjoint = jnp.einsum("ibh,ibhn,ibhp->bhnp", from_start, c_full, residual, precision=HIGH)
    _, adjoint_in = prefix(
        (through, local_adjoint),
        "seq",
        chain_combine,
        (start_ones, jnp.zeros_like(local_adjoint)),
        True,
    )
    grad_u = jnp.einsum("bhij,ibhp->jbhp", mixing, residual, precision=QUADRATIC)
    grad_u = grad_u + to_end[..., None] * jnp.einsum(
        "jbhn,bhnp->jbhp", b_full, adjoint_in, precision=HIGH
    )
    grad_x = step_size[..., None] * grad_u + skip_gain[None, None, :, None] * residual
    pair = decay_mat * jnp.einsum("ibhp,jbhp->bhij", residual, inputs, precision=QUADRATIC)
    grad_b = jnp.einsum("bhij,ibhn->jbhn", pair, c_full, precision=QUADRATIC)
    grad_b = grad_b + to_end[..., None] * jnp.einsum(
        "jbhp,bhnp->jbhn", inputs, adjoint_in, precision=HIGH
    )
    grad_c = jnp.einsum("bhij,jbhn->ibhn", pair, b_full, precision=QUADRATIC)
    grad_c = grad_c + from_start[..., None] * jnp.einsum(
        "ibhp,bhpn->ibhn", residual, state_in, precision=HIGH
    )
    return (grad_x.astype(jnp.bfloat16), grad_b.astype(jnp.bfloat16), grad_c.astype(jnp.bfloat16))


def solution(mesh):
    placed = (
        P("teach", None, "seq"),
        P("teach", "seq", None),
        P(),
        P("seq", None, "teach", None),
        P("seq", None, "teach", None),
        P("seq", None, "teach", None),
        P("seq", None, "teach"),
        P("seq", None),
        P("teach"),
        P("teach"),
    )
    return jax.shard_map(
        per_device,
        mesh=mesh,
        in_specs=placed,
        out_specs=(
            P("seq", None, "teach", None),
            P("seq", None, "teach", None),
            P("seq", None, "teach", None),
        ),
        check_vma=False,
    )
```

profile of v0, /device:TPU:1, one launch (start us, length us, event | category | flops | bytes accessed | tf_op | source)
XLA Modules:
  0.0 285.0 jit_solution(6432824276978671787)
XLA Ops:
  7.2 1.2 copy.290
  8.4 0.6 reshape.413
  9.7 1.0 reshape.414
  10.6 0.4 convolution_convert_fusion
  11.0 0.3 broadcast_in_dim.78
  11.3 79.0 %all_to_all.38 = bf16[64,32,640]{2,1,0:T(8,128)(2,1)S(1)} all-to-all(bf16[64,32,640]{2,1,0:T(8,128)(2,1)S(1)} %bitcast.257), channel_id=1, replica_groups=mesh['teach'=64,'seq'=8] {'teach'}, dimensions={0} | all-to-all | bytes 5242880 | tf_op jit(solution)/shard_map/all_to_all | solution.py:90
  90.3 0.6 multiply_reduce_fusion
  90.8 23.5 %psum.7 = f32[64,32]{1,0:T(8,128)S(1)} all-reduce(f32[64,32]{1,0:T(8,128)S(1)} %multiply_reduce_fusion), channel_id=1, replica_groups=mesh['teach'=64,'seq'=8] {'seq'}, use_global_device_ids=true, to_apply=%region_11.12 | all-reduce | flops 2048 | bytes 16384 | tf_op jit(solution)/shard_map/psum | solution.py:94
  114.3 3.7 %convolution_multiply_fusion = f32[64,32,512]{2,1,0:T(8,128)} fusion(bf16[64,32,640]{2,1,0:T(8,128)(2,1)S(1)} %all_to_all.38, f32[64,32]{1,0:T(8,128)S(1)} %add_rsqrt_fusion, bf16[1,640,512]{2,1,0:T(8,128)(2,1)S(1)} %copy-done), kind=kOutput, calls=%fused_computation.7 | convolution fusion | flops 1343225856 | bytes 7479296 | tf_op jit(solution)/shard_map/tkf,fc->tkc/dot_general | solution.py:91
  118.1 6.9 %copy.294 = f32[64,32,512]{0,2,1:T(8,128)} copy(f32[64,32,512]{2,1,0:T(8,128)} %convolution_multiply_fusion) | data formatting | bytes 8388608 | tf_op jit(solution)/shard_map/mul | solution.py:96
  125.0 8.3 %copy.295 = f32[64,32,64,8,1]{2,1,4,0,3:T(8,128)} copy(f32[64,32,64,8,1]{0,3,2,1,4:T(8,128)} %bitcast.256) | data formatting | bytes 8388608 | tf_op jit(solution)/shard_map/reshape | solution.py:96
  134.1 1.2 reduce-window.16
  135.5 1.2 reduce-window.14
  137.2 0.2 slice_reduce_fusion
  137.4 0.3 copy.283
  137.8 0.2 compare_reduce_fusion
  138.0 1.0 exponential_select_fusion.2
  139.1 11.3 %all_gather.18 = bf16[8,4,1]{1,2,0:T(2,128)(2,1)S(1)} all-gather(bf16[1,4,1]{1,2,0:T(2,128)(2,1)S(1)} %get-tuple-element.260), channel_id=1, replica_groups=mesh['teach'=64,'seq'=8] {'seq'}, dimensions={0}, use_global_device_ids=true | all-gather | bytes 72 | tf_op jit(solution)/shard_map/all_gather | solution.py:23
  150.5 2.5 select_reduce_fusion
  153.1 0.3 copy.285
  153.4 0.3 exponential_select_fusion.1
  153.8 0.3 convolution_convert_fusion.2
  154.0 13.8 %all-gather = bf16[32,64,128]{2,1,0:T(8,128)(2,1)S(1)} all-gather(bf16[4,64,128]{2,1,0:T(8,128)(2,1)S(1)} %convolution_convert_fusion.2), channel_id=2, replica_groups=mesh['teach'=64,'seq'=8] {'seq'}, dimensions={0}, use_global_device_ids=true | all-gather | bytes 589824 | tf_op jit(solution)/shard_map/all_gather | solution.py:23
  167.9 0.3 while.26
  168.2 22.4 %reduce-scatter.2.cloned.1.call-done = f32[64,32,64,1,1]{2,1,4,0,3:T(8,128)} async-done(((f32[64,32,64,8,1]{2,1,4,0,3:T(8,128)}), f32[64,32,64,1,1]{2,1,4,0,3:T(8,128)}) %reduce-scatter.2.cloned.1.call-update) | async-done | bytes 524304 | tf_op jit(solution)/shard_map/reduce_scatter | solution.py:99
  190.6 1.3 fusion.22
  192.0 1.1 copy.297
  193.0 1.0 reshape.443
  194.1 13.0 %all-to-all-start.1 = ((bf16[64,2,1024]{2,1,0:T(2,128)(2,1)}), bf16[64,2,1024]{2,1,0:T(2,128)(2,1)S(1)}, u32[]{:S(2)}, u32[]{:S(2)}) async-start(bf16[64,2,1024]{2,1,0:T(2,128)(2,1)} %reshape.443), calls=%async_computation.2 | async-start | bytes 524288 | tf_op jit(solution)/shard_map/all_to_all | solution.py:101
  207.2 0.5 convolution_multiply_fusion.2
  207.7 11.8 %all-to-all-done.1 = bf16[64,2,1024]{2,1,0:T(2,128)(2,1)S(1)} async-done(((bf16[64,2,1024]{2,1,0:T(2,128)(2,1)}), bf16[64,2,1024]{2,1,0:T(2,128)(2,1)S(1)}, u32[]{:S(2)}, u32[]{:S(2)}) %all-to-all-start.1) | async-done | bytes 262176 | tf_op jit(solution)/shard_map/all_to_all | solution.py:101
  219.5 0.3 reshape.444
  219.9 1.1 copy.298
  221.0 1.1 reshape.445
  222.1 6.8 %all-to-all-start.2 = ((bf16[8,2,8192]{2,1,0:T(2,128)(2,1)}), bf16[8,2,8192]{2,1,0:T(2,128)(2,1)S(1)}, u32[]{:S(2)}, u32[]{:S(2)}) async-start(bf16[8,2,8192]{2,1,0:T(2,128)(2,1)} %reshape.445), calls=%async_computation.3 | async-start | bytes 524288 | tf_op jit(solution)/shard_map/all_to_all | solution.py:100
  228.9 1.3 convolution_bitcast_fusion.7
  230.4 0.7 copy.293
  231.1 1.0 copy.284
  232.7 0.7 broadcast_clamp_fusion
  233.4 2.0 all-to-all-done.2
  235.4 0.3 reshape.446
  235.8 1.6 copy.299
  237.4 3.6 %copy.325 = bf16[8,8,32,8,1,8]{5,3,2,1,0,4:T(8,128)(2,1)} copy(bf16[8,8,32,8,1,8]{2,5,1,0,3,4:T(8,128)(2,1)S(1)} %bitcast.259) | data formatting | bytes 524288 | tf_op jit(solution)/shard_map/reshape | solution.py:115
  241.0 5.5 %gather_fusion = bf16[1024,8,8]{2,1,0:T(8,128)(2,1)S(1)} fusion(bf16[2048,8,8]{2,1,0:T(8,128)(2,1)} %bitcast.258, s32[1024]{0:T(1024)S(1)} %broadcast_clamp_fusion), kind=kCustom, calls=%fused_computation | custom fusion | bytes 266240 | tf_op jit(solution)/shard_map/jit(_take)/gather | solution.py:118
  246.6 1.4 gather.7
  248.2 1.4 fusion.11
  249.6 1.8 convolution_multiply_fusion.1
  251.5 0.5 convolution_bitcast_fusion.1
  251.9 0.8 convolution_bitcast_fusion.3
  252.7 0.3 fusion.16
  253.0 0.4 convolution_bitcast_fusion.6
  253.4 1.1 fusion.4
  254.6 0.9 copy.319
  255.5 14.0 %all-gather.1 = bf16[32,128,64]{1,2,0:T(8,128)(2,1)S(1)} all-gather(bf16[4,128,64]{1,2,0:T(8,128)(2,1)S(1)} %fusion.16), channel_id=3, replica_groups=mesh['teach'=64,'seq'=8] {'seq'}, dimensions={0}, use_global_device_ids=true | all-gather | bytes 589824 | tf_op jit(solution)/shard_map/all_gather | solution.py:23
  269.5 5.5 %while.27 = (s32[]{:T(128)}, f32[4,1,128,64]{3,2,1,0:T(8,128)S(1)}, s32[]{:T(128)}, bf16[8,4,1]{1,2,0:T(2,128)(2,1)}, bf16[8,4,1,128,64]{3,4,1,0,2:T(8,128)(2,1)...) while((s32[]{:T(128)}, f32[4,1,128,64]{3,2,1,0:T(8,128)S(1)}, s32[]{:T(128)}, ...), condition=%wide.region_14.15_spmd, body=%wide.region_13.14_spmd.sunk | while | flops 98314 | bytes 590011 | solution.py:38
  269.6 0.6 bitcast_convert_fusion.6
  270.6 0.6 bitcast_convert_fusion.6
  271.5 0.6 bitcast_convert_fusion.6
  272.3 0.7 bitcast_convert_fusion.6
  273.3 0.6 bitcast_convert_fusion.6
  274.2 0.7 bitcast_convert_fusion.6
  275.0 1.1 fusion.5
  276.1 0.9 copy.318
  277.0 1.1 fusion.15
  (89 shorter events, 3.9 us)
Async XLA Ops:
  7.2 107.2 %copy-start = (bf16[1,640,512]{2,1,0:T(8,128)(2,1)S(1)}, bf16[1,640,512]{2,1,0:T(8,128)(2,1)}, u32[]{:S(2)}) copy-start(bf16[1,640,512]{2,1,0:T(8,128)(2,1)} %param.15) | copy-start | bytes 1966084
  7.2 183.5 %reduce-scatter.2.cloned.1.call-start = ((), (), s32[]{:S(2)}) async-start(), calls=%async_computation.4 | async-start | bytes 9437184 | tf_op jit(solution)/shard_map/reduce_scatter | solution.py:99
  9.1 144.7 %copy-start.8 = (s32[8192]{0:T(1024)}, s32[8192]{0:T(1024)S(1)}, u32[]{:S(2)}) copy-start(s32[8192]{0:T(1024)S(1)} %reshape.413) | copy-start | bytes 98308
  133.3 0.8 copy-start.11
  133.3 2.2 copy-start.14
  133.3 20.4 %copy-start.4 = (bf16[256,4,1,64]{0,3,2,1:T(8,128)(2,1)S(1)}, bf16[256,4,1,64]{0,3,2,1:T(8,128)(2,1)}, u32[]{:S(2)}) copy-start(bf16[256,4,1,64]{0,3,2,1:T(8,128)(2,1)} %param.17) | copy-start | bytes 393220
  133.3 20.5 %copy-start.5 = (bf16[256,4,1,128]{3,1,2,0:T(4,128)(2,1)S(1)}, bf16[256,4,1,128]{3,1,2,0:T(4,128)(2,1)}, u32[]{:S(2)}) copy-start(bf16[256,4,1,128]{3,1,2,0:T(4,128)(2,1)} %param.18) | copy-start | bytes 786436
  137.2 70.0 %copy-start.9 = (s32[1,4,2,128]{3,1,2,0:T(4,128)}, s32[1,4,2,128]{3,1,2,0:T(4,128)S(1)}, u32[]{:S(2)}) copy-start(s32[1,4,2,128]{3,1,2,0:T(4,128)S(1)} %copy.357) | copy-start | bytes 12292
  139.0 68.2 %copy-start.3 = (bf16[256,4,1,128]{3,1,2,0:T(4,128)(2,1)S(1)}, bf16[256,4,1,128]{3,1,2,0:T(4,128)(2,1)}, u32[]{:S(2)}) copy-start(bf16[256,4,1,128]{3,1,2,0:T(4,128)(2,1)} %param.19) | copy-start | bytes 786436
  168.2 51.3 %copy-start.13 = (bf16[8,4,1]{1,2,0:T(2,128)(2,1)}, bf16[8,4,1]{1,2,0:T(2,128)(2,1)S(1)}, u32[]{:S(2)}) copy-start(bf16[8,4,1]{1,2,0:T(2,128)(2,1)S(1)} %get-tuple-element.386) | copy-start | bytes 196
  194.1 25.5 %all-to-all-start.1 = ((bf16[64,2,1024]{2,1,0:T(2,128)(2,1)}), bf16[64,2,1024]{2,1,0:T(2,128)(2,1)S(1)}, u32[]{:S(2)}, u32[]{:S(2)}) async-start(bf16[64,2,1024]{2,1,0:T(2,128)(2,1)} %reshape.443), calls=%async_computation.2 | async-start | bytes 524288 | tf_op jit(solution)/shard_map/all_to_all | solution.py:101
  207.1 0.6 copy-start.7
  207.2 12.3 %copy-start.12 = (f32[4,256]{1,0:T(4,128)}, f32[4,256]{1,0:T(4,128)S(1)}, u32[]{:S(2)}) copy-start(f32[4,256]{1,0:T(4,128)S(1)} %bitcast_add_fusion) | copy-start | bytes 12292
  207.7 28.1 %copy-start.1 = (f32[4,256,256]{2,1,0:T(8,128)}, f32[4,256,256]{2,1,0:T(8,128)S(1)}, u32[]{:S(2)}) copy-start(f32[4,256,256]{2,1,0:T(8,128)S(1)} %convolution_multiply_fusion.2) | copy-start | bytes 3145732
  222.1 13.3 %all-to-all-start.2 = ((bf16[8,2,8192]{2,1,0:T(2,128)(2,1)}), bf16[8,2,8192]{2,1,0:T(2,128)(2,1)S(1)}, u32[]{:S(2)}, u32[]{:S(2)}) async-start(bf16[8,2,8192]{2,1,0:T(2,128)(2,1)} %reshape.445), calls=%async_computation.3 | async-start | bytes 524288 | tf_op jit(solution)/shard_map/all_to_all | solution.py:100
  241.0 8.6 %copy-start.10 = (s32[1,4,2,128]{3,1,2,0:T(4,128)S(1)}, s32[1,4,2,128]{3,1,2,0:T(4,128)}, u32[]{:S(2)}) copy-start(s32[1,4,2,128]{3,1,2,0:T(4,128)} %copy-done.9) | copy-start | bytes 12292
  248.0 3.5 %copy-start.6 = (bf16[256,4,1,128]{3,1,2,0:T(4,128)(2,1)S(1)}, bf16[256,4,1,128]{3,1,2,0:T(4,128)(2,1)}, u32[]{:S(2)}) copy-start(bf16[256,4,1,128]{3,1,2,0:T(4,128)(2,1)} %param.18) | copy-start | bytes 786436
  248.0 5.0 %copy-start.2 = (f32[4,256,256]{2,1,0:T(8,128)S(1)}, f32[4,256,256]{2,1,0:T(8,128)}, u32[]{:S(2)}) copy-start(f32[4,256,256]{2,1,0:T(8,128)} %copy-done.1) | copy-start | bytes 3145732
Sparse Core Ops, SparseCore 0:
  133.4 57.1 reduce-scatter.1
where the time goes:
time: 286 us; the launch traced here: 285 us
  blocking collectives  142 us (50%)
  local copies, waits for them, and re-layouts  41.9 us (15%)
  waiting for transfers between devices  36.2 us (13%)
  starting transfers between devices  19.9 us (7%)
  between operations  15.9 us (6%)
  matrix products  14.7 us (5%)
  other arithmetic  14.3 us (5%)
    all_to_all x1, blocking collectives, per_device(): lax.all_to_all(outgoing, 'teach', split_axis=0, concat_axis=0, tiled=True)  79 us
    all_gather x3, blocking collectives, prefix(): lax.all_gather(a.astype(kind), axis)  39.1 us
    psum x1, blocking collectives, per_device(): totals = lax.psum(sq_sums, 'seq')  23.5 us
    reduce_scatter x1, waiting for transfers between devices, per_device(): lax.psum_scatter(scaled, 'seq', scatter_dimension=3, tiled=True)  22.4 us
    all_to_all x1, starting transfers between devices, per_device(): lax.all_to_all(summed[None], 'teach', split_axis=3, concat_axis=0, tiled=...  13 us
    all_to_all x1, waiting for transfers between devices, per_device(): lax.all_to_all(summed[None], 'teach', split_axis=3, concat_axis=0, tiled=...  11.8 us
    reshape x1, local copies, waits for them, and re-layouts, per_device(): (partial_value * row_scale[:, :, None]).reshape(teach_n, CAP, heads_all,...  8.29 us
    gather x3, local copies, waits for them, and re-layouts, per_device(): picked = jnp.take(slot_table, row_index, axis=0)  7.09 us
  transfers between devices with their start and end apart: 3, of which 3 were waited for; matrix products, arithmetic and copies ran while one was open for 5% of the time, Pallas kernels for 0%

commit v1 on v0

v1 whole, which is shorter than its diff:
```python
import jax
import jax.numpy as jnp
from jax import lax
from jax.sharding import Mesh
from jax.sharding import PartitionSpec as P

TD = 5120
P_SIZE = 64
FAM = 8
CAP = 32


EPS = 1e-06
HIGH = lax.Precision.HIGHEST
QUADRATIC = lax.Precision.HIGH
TEACH = ("tz", "ty")


def family_slots(fam_block):
    onehot = (fam_block[..., None] == jnp.arange(FAM, dtype=jnp.int32)[None, None, :]).astype(
        jnp.int32
    )
    before = jnp.cumsum(onehot, axis=1) - onehot
    return jnp.sum(before * onehot, axis=2)


def decay_matrix(log_sums, counts):
    places = jnp.arange(log_sums.shape[0])
    lower = places[:, None] >= places[None, :]
    same_doc = counts.T[:, :, None] == counts.T[:, None, :]
    keep_mask = (lower[None] & same_doc)[:, None]
    sums = log_sums.transpose(1, 2, 0)
    gaps = sums[:, :, :, None] - sums[:, :, None, :]
    return jnp.where(keep_mask, jnp.exp(jnp.where(keep_mask, gaps, 0.0)), 0.0)


def chain_weights(through_all, place, backward):
    count = through_all.shape[0]
    blocks = jnp.arange(count)
    s2 = blocks[:, None]
    s3 = blocks[None, :]
    if backward:
        used = (s3 > place) & (s3 < s2)
        live = blocks > place
    else:
        used = (s3 > s2) & (s3 < place)
        live = blocks < place
    factors = jnp.where(used[:, :, None, None], through_all[None], 1.0)
    weights = jnp.prod(factors, axis=1)
    return jnp.where(live[:, None, None], weights, 0.0)


def carried(local, through, axis, backward):
    place = lax.axis_index(axis)
    through_all = lax.all_gather(through, axis)
    local_all = lax.all_gather(local, axis)
    weights = chain_weights(through_all, place, backward)
    return jnp.sum(weights[:, :, :, None, None] * local_all, axis=0)


def per_device(
    teacher_in, teacher_proj, family, x_in, b_in, c_in, step_size, doc_start, a_rate, skip_gain
):
    n_z = lax.axis_size("tz")
    n_y = lax.axis_size("ty")
    seq_n = lax.axis_size("seq")
    teach_n = n_z * n_y
    heads_all = teach_n * x_in.shape[2]
    block_pos = teacher_in.shape[0]
    batch_n = teacher_in.shape[1]
    feat_width = teacher_in.shape[2]
    block_rows = block_pos * batch_n
    source = lax.axis_index("tz") * n_y + lax.axis_index("ty")
    fam_all = family.reshape(family.shape[0] * family.shape[1])

    own_rows = teacher_in.reshape(block_rows, feat_width)
    own_fam = lax.dynamic_slice_in_dim(fam_all, source * block_rows, block_rows)
    slot_ids = family_slots(own_fam.reshape(1, block_rows))[0]
    dest_cols = own_fam * CAP + slot_ids
    select = (dest_cols[:, None] == jnp.arange(FAM * CAP, dtype=jnp.int32)[None, :]).astype(
        jnp.bfloat16
    )
    packed = jnp.dot(select.T, own_rows, preferred_element_type=jnp.float32).astype(jnp.bfloat16)
    packed = packed.reshape(FAM, CAP, feat_width)
    by_family = lax.all_to_all(packed, "ty", split_axis=0, concat_axis=0, tiled=True)
    received = lax.all_gather(by_family, "tz")
    slots_all = n_z * n_y * CAP
    received = received.reshape(slots_all, feat_width)
    weights = teacher_proj[0]
    partial_value = jnp.dot(received, weights, preferred_element_type=jnp.float32)
    sq_sums = jnp.sum(jnp.square(received.astype(jnp.float32)), axis=1)
    partial_value = partial_value.reshape(n_z, n_y * CAP, heads_all, -1)
    sq_sums = sq_sums.reshape(n_z, n_y * CAP)
    summed = lax.psum_scatter(partial_value, "seq", scatter_dimension=0, tiled=True)[0]
    totals = lax.psum_scatter(sq_sums, "seq", scatter_dimension=0, tiled=True)[0]
    row_scale = lax.rsqrt(totals / TD + EPS)
    scaled = (summed * row_scale[:, None, None]).astype(jnp.bfloat16)
    cols = scaled.shape[-1]
    outgoing = scaled.transpose(1, 0, 2)
    arrived = lax.all_to_all(outgoing, TEACH, split_axis=0, concat_axis=0, tiled=True)
    arrived = arrived.reshape(n_z, n_y, n_y * CAP, cols)
    table = arrived.transpose(1, 2, 0, 3).reshape(n_y * n_y * CAP, n_z * cols)

    shard_rows = n_y * block_rows
    shard_fam = lax.dynamic_slice_in_dim(
        fam_all, lax.axis_index("seq") * shard_rows, shard_rows
    ).reshape(n_y, block_rows)
    shard_slots = family_slots(shard_fam)
    sources = jnp.arange(n_y, dtype=jnp.int32)[:, None]
    row_index = ((shard_fam * n_y + sources) * CAP + shard_slots).reshape(shard_rows)
    picked = jnp.take(table, row_index, axis=0)
    target = picked.reshape(n_y * block_pos, batch_n, 1, P_SIZE)

    x_full = x_in.astype(jnp.float32)
    b_full = b_in.astype(jnp.float32)
    c_full = c_in.astype(jnp.float32)
    log_sums = jnp.cumsum(-step_size * a_rate[None, None, :], axis=0)
    counts = jnp.cumsum(doc_start, axis=0)
    same_end = (counts == counts[-1][None, :]).astype(jnp.float32)
    to_end = jnp.exp(log_sums[-1][None] - log_sums) * same_end[:, :, None]
    from_start = jnp.exp(log_sums) * (counts == 0).astype(jnp.float32)[:, :, None]
    through = jnp.exp(log_sums[-1]) * (counts[-1] == 0).astype(jnp.float32)[:, None]
    inputs = step_size[..., None] * x_full
    local_state = jnp.einsum("jbh,jbhp,jbhn->bhpn", to_end, inputs, b_full, precision=HIGH)
    state_in = carried(local_state, through, "seq", False)
    decay_mat = decay_matrix(log_sums, counts)
    scores = jnp.einsum("ibhn,jbhn->bhij", c_in, b_in, preferred_element_type=jnp.float32)
    mixing = decay_mat * scores
    output = jnp.einsum("bhij,jbhp->ibhp", mixing, inputs, precision=QUADRATIC)
    output = output + from_start[..., None] * jnp.einsum(
        "ibhn,bhpn->ibhp", c_full, state_in, precision=HIGH
    )
    output = output + skip_gain[None, None, :, None] * x_full
    residual = output - target.astype(jnp.float32)
    local_adjoint = jnp.einsum("ibh,ibhn,ibhp->bhnp", from_start, c_full, residual, precision=HIGH)
    adjoint_in = carried(local_adjoint, through, "seq", True)
    grad_u = jnp.einsum("bhij,ibhp->jbhp", mixing, residual, precision=QUADRATIC)
    grad_u = grad_u + to_end[..., None] * jnp.einsum(
        "jbhn,bhnp->jbhp", b_full, adjoint_in, precision=HIGH
    )
    grad_x = step_size[..., None] * grad_u + skip_gain[None, None, :, None] * residual
    pair = decay_mat * jnp.einsum("ibhp,jbhp->bhij", residual, inputs, precision=QUADRATIC)
    grad_b = jnp.einsum("bhij,ibhn->jbhn", pair, c_full, precision=QUADRATIC)
    grad_b = grad_b + to_end[..., None] * jnp.einsum(
        "jbhp,bhnp->jbhn", inputs, adjoint_in, precision=HIGH
    )
    grad_c = jnp.einsum("bhij,jbhn->ibhn", pair, b_full, precision=QUADRATIC)
    grad_c = grad_c + from_start[..., None] * jnp.einsum(
        "ibhp,bhpn->ibhn", residual, state_in, precision=HIGH
    )
    return (grad_x.astype(jnp.bfloat16), grad_b.astype(jnp.bfloat16), grad_c.astype(jnp.bfloat16))


def solution(mesh):
    teach_n, seq_n = mesh.devices.shape
    n_y = FAM
    n_z = teach_n // n_y
    assert n_z == seq_n
    split = Mesh(mesh.devices.reshape(n_z, n_y, seq_n), ("tz", "ty", "seq"))
    placed = (
        P(TEACH, None, "seq"),
        P(TEACH, "seq", None),
        P(),
        P("seq", None, TEACH, None),
        P("seq", None, TEACH, None),
        P("seq", None, TEACH, None),
        P("seq", None, TEACH),
        P("seq", None),
        P(TEACH),
        P(TEACH),
    )
    return jax.shard_map(
        per_device,
        mesh=split,
        in_specs=placed,
        out_specs=(
            P("seq", None, TEACH, None),
            P("seq", None, TEACH, None),
            P("seq", None, TEACH, None),
        ),
        check_vma=False,
    )
```

time: 286 us -> 202 us (0.71)
  blocking collectives: 142 us -> 44.4 us
  waiting for transfers between devices: 36.2 us -> 88.4 us
  local copies, waits for them, and re-layouts: 41.9 us -> 12.6 us
  starting transfers between devices: 19.9 us -> 12.5 us
    all_gather x0 -> x3, waiting for transfers between devices: none -> 86.4 us  [the longest x1 44.5 us: per_device(): received = lax.all_gather(by_family, 'tz')]
    all_to_all x1, blocking collectives: 79 us -> 18.1 us  [per_device(): lax.all_to_all(packed, 'ty', split_axis=0, concat_axis=0, tiled=True)]
    all_gather x3 -> x1, blocking collectives: 39.1 us -> 14.2 us  [carried(): through_all = lax.all_gather(through, axis)]
    psum x1 -> x0, blocking collectives: 23.5 us -> none  [per_device(): totals = lax.psum(sq_sums, 'seq')]
    reduce_scatter x1, waiting for transfers between devices: 22.4 us -> 1.91 us  [per_device(): lax.psum_scatter(partial_value, 'seq', scatter_dimension=0, tiled=True)[0]]
    all_to_all x2 -> x1, waiting for transfers between devices: 13.8 us -> 0.01 us  [per_device(): lax.all_to_all(outgoing, TEACH, split_axis=0, concat_axis=0, tiled=True)]
    unnamed x0 -> x1, blocking collectives: none -> 12.1 us
    reshape x3 -> x4, local copies, waits for them, and re-layouts: 12 us -> 0.41 us  [the longest x1 0.27 us: per_device(): table = arrived.transpose(1, 2, 0, 3).reshape(n_y * n_y * CAP, n_z * cols)]
  transfers between devices with their start and end apart: 3 -> 5, of which waited for: 3 -> 4; matrix products, arithmetic and copies ran while one was open for 5% -> 11% of each run, Pallas kernels for 0% -> 0%
where the time goes in v1:
time: 202 us
  waiting for transfers between devices  88.4 us (44%)
  blocking collectives  44.4 us (22%)
  between operations  15.5 us (8%)
  matrix products  15.1 us (7%)
  other arithmetic  13.1 us (6%)
  local copies, waits for them, and re-layouts  12.6 us (6%)
  starting transfers between devices  12.5 us (6%)
    all_gather x1, waiting for transfers between devices, per_device(): received = lax.all_gather(by_family, 'tz')  44.5 us
    all_gather x2, waiting for transfers between devices, carried(): local_all = lax.all_gather(local, axis)  41.9 us
    all_to_all x1, blocking collectives, per_device(): lax.all_to_all(packed, 'ty', split_axis=0, concat_axis=0, tiled=True)  18.1 us
    all_gather x1, blocking collectives, carried(): through_all = lax.all_gather(through, axis)  14.2 us
    all_to_all x1, starting transfers between devices, per_device(): lax.all_to_all(outgoing, TEACH, split_axis=0, concat_axis=0, tiled=True)  12.2 us
    unnamed x1, blocking collectives  12.1 us
    dot_general x1, matrix products, per_device(): jnp.dot(received, weights, preferred_element_type=jnp.float32)  5.49 us
    unnamed x20, local copies, waits for them, and re-layouts  4.73 us
  transfers between devices with their start and end apart: 5, of which 4 were waited for; matrix products, arithmetic and copies ran while one was open for 11% of the time, Pallas kernels for 0%

profile of v1, /device:TPU:1, one launch (start us, length us, event | category | flops | bytes accessed | tf_op | source)
XLA Modules:
  0.0 201.7 jit_solution(13158108024508428186)
XLA Ops:
  7.2 1.2 copy.181
  8.4 0.6 reshape.514
  9.1 0.1 dynamic_slice.7
  9.2 0.1 fusion.55
  9.3 0.2 reduce_window_sum.81
  9.4 0.2 select_reduce_fusion.1
  9.6 0.1 multiply_add_fusion
  9.7 1.0 reshape.515
  10.7 0.4 convolution_convert_fusion
  11.0 18.1 %all_to_all.10 = bf16[8,32,640]{2,1,0:T(8,128)(2,1)} all-to-all(bf16[8,32,640]{2,1,0:T(8,128)(2,1)S(1)} %bitcast.239), channel_id=1, replica_groups=mesh['tz'=8,'ty'=8,'seq'=8] {'ty'}, dimensions={0} | all-to-all | bytes 655360 | tf_op jit(solution)/shard_map/all_to_all | solution.py:85
  29.2 0.3 copy.185
  29.5 44.5 %all-gather.9.cloned.1.call-done = bf16[64,32,640]{2,1,0:T(8,128)(2,1)} async-done(((bf16[8,32,640]{2,1,0:T(8,128)(2,1)}), bf16[64,32,640]{2,1,0:T(8,128)(2,1)}) %all-gather.9.cloned.1.call-update) | async-done | bytes 2621456 | tf_op jit(solution)/shard_map/all_gather | solution.py:86
  74.0 5.5 %fusion.20 = f32[8,256,64,8]{1,2,3,0:T(8,128)} fusion(bf16[8,256,640,1]{2,1,3,0:T(8,128)(2,1)} %bitcast.234, bf16[64,8,640]{2,1,0:T(8,128)(2,1)S(1)} %bitcast.246), kind=kOutput, calls=%fused_computation.37 | convolution fusion | flops 1342177280 | bytes 7471104 | tf_op jit(solution)/shard_map/dot_general | solution.py:90
  80.3 1.2 reduce-window.16
  81.6 0.1 slice.29
  81.7 1.2 reduce-window.14
  82.9 0.1 slice.28
  83.0 0.1 copy.169
  83.1 0.1 copy.170
  83.2 0.1 copy.171
  83.4 0.1 copy.172
  83.6 0.2 slice_reduce_fusion.1
  83.8 0.2 exponential_select_fusion.1
  84.0 0.1 copy_bitcast_fusion.2
  84.1 0.9 fusion.29
  85.1 0.1 copy.182
  85.2 2.5 %select_reduce_fusion = s32[8,128]{0,1:T(8,128)S(1)} fusion(s32[8,128]{0,1:T(8,128)S(1)} %copy.182), kind=kOutput, calls=%fused_computation.42 | output fusion | flops 1096704 | bytes 8192 | tf_op jit(solution)/shard_map/jit(cumsum)/reduce_window_sum | solution.py:23
  87.8 0.1 copy.176
  87.9 14.2 %all_gather.24 = f32[8,4,1]{1,2,0:T(1,128)S(1)} all-gather(f32[1,4,1]{1,2,0:T(1,128)S(1)} %copy.176), channel_id=1, replica_groups=mesh['tz'=8,'ty'=8,'seq'=8] {'seq'}, dimensions={0}, use_global_device_ids=true | all-gather | bytes 144 | tf_op jit(solution)/shard_map/all_gather | solution.py:55
  102.1 0.1 copy.177
  102.2 0.2 select_reduce_fusion.2
  102.4 0.1 copy.178
  102.5 0.2 broadcast_in_dim.121
  102.7 0.1 copy.184
  103.4 1.3 dynamic-slice
  104.8 0.5 convolution_multiply_fusion.1
  105.3 2.4 %multiply_reduce_fusion = f32[64,32]{1,0:T(8,128)S(1)} fusion(bf16[64,32,640]{2,1,0:T(8,128)(2,1)} %all-gather.9.cloned.1.call-done), kind=kLoop, calls=%fused_computation.1 | loop fusion | flops 3930112 | bytes 2629632 | tf_op jit(solution)/shard_map/reduce_sum | solution.py:91
  107.8 12.1 %all-reduce = f32[8,256]{1,0:T(8,128)S(1)} all-reduce(f32[8,256]{1,0:T(8,128)S(1)} %reshape.517), channel_id=6, replica_groups=mesh['tz'=8,'ty'=8,'seq'=8] {'seq'}, use_global_device_ids=true, to_apply=%region_12.13.clone | all-reduce | flops 2048 | bytes 16384
  119.9 0.7 fusion.60
  120.6 1.9 reduce-scatter.2.cloned.1.call-done
  122.5 1.1 fusion.31
  123.6 0.9 copy.187
  124.4 12.2 %all-to-all-start.1 = ((bf16[64,256,8]{1,2,0:T(8,128)(2,1)}), bf16[64,256,8]{1,2,0:T(8,128)(2,1)S(1)}, u32[]{:S(2)}, u32[]{:S(2)}) async-start(bf16[64,256,8]{1,2,0:T(8,128)(2,1)} %copy.187), calls=%async_computation.2 | async-start | bytes 524288 | tf_op jit(solution)/shard_map/all_to_all | solution.py:100
  136.6 0.2 all-gather.11.cloned.1.call-start
  136.8 0.6 convolution_bitcast_fusion.7
  137.5 17.8 %all-gather.7.cloned.1.call-done = f32[32,64,128]{2,1,0:T(8,128)} async-done(((f32[4,64,128]{2,1,0:T(8,128)}), f32[32,64,128]{2,1,0:T(8,128)}) %all-gather.7.cloned.1.call-update) | async-done | bytes 1048592 | tf_op jit(solution)/shard_map/all_gather | solution.py:56
  155.2 1.4 multiply_reduce_fusion.2
  156.7 0.3 copy.189
  157.0 3.2 %gather_fusion = bf16[1024,64]{1,0:T(8,128)(2,1)S(1)} fusion(bf16[2048,64]{1,0:T(8,128)(2,1)S(1)} %copy.189, s32[1024]{0:T(1024)S(1)} %broadcast_clamp_fusion), kind=kCustom, calls=%fused_computation | custom fusion | bytes 266240 | tf_op jit(solution)/shard_map/jit(_take)/gather | solution.py:111
  160.2 0.2 copy.190
  160.4 0.4 fusion.13
  160.8 0.9 convolution_bitcast_fusion.8
  161.7 0.1 copy.191
  161.8 1.0 convolution_multiply_fusion
  162.8 0.4 convolution_bitcast_fusion.1
  163.3 1.1 fusion.4
  164.4 0.9 copy.201
  165.3 0.4 convolution_bitcast_fusion.6
  165.7 0.8 convolution_bitcast_fusion.3
  166.5 24.2 %all-gather.11.cloned.1.call-done = f32[32,128,64]{1,2,0:T(8,128)} async-done(((f32[4,128,64]{1,2,0:T(8,128)}), f32[32,128,64]{1,2,0:T(8,128)}) %all-gather.11.cloned.1.call-update) | async-done | bytes 1048592 | tf_op jit(solution)/shard_map/all_gather | solution.py:56
  190.7 1.4 multiply_reduce_fusion.1
  192.0 1.1 fusion.5
  193.2 0.9 copy.200
  194.1 1.1 fusion.15
  (47 shorter events, 0.9 us)
Async XLA Ops:
  7.2 76.9 %copy-start = (bf16[256,4,1,128]{3,1,2,0:T(4,128)(2,1)S(1)}, bf16[256,4,1,128]{3,1,2,0:T(4,128)(2,1)}, u32[]{:S(2)}) copy-start(bf16[256,4,1,128]{3,1,2,0:T(4,128)(2,1)} %param.14) | copy-start | bytes 786436
  7.2 22.0 %copy-start.3 = (bf16[1,640,512]{2,1,0:T(8,128)(2,1)S(1)}, bf16[1,640,512]{2,1,0:T(8,128)(2,1)}, u32[]{:S(2)}) copy-start(bf16[1,640,512]{2,1,0:T(8,128)(2,1)} %param.11) | copy-start | bytes 1966084
  7.2 66.8 %all-gather.9.cloned.1.call-start = ((), (), s32[]{:S(2)}) async-start(), calls=%async_computation.5 | async-start | bytes 2949120 | tf_op jit(solution)/shard_map/all_gather | solution.py:86
  29.2 93.3 %reduce-scatter.2.cloned.1.call-start = ((), (), s32[]{:S(2)}) async-start(), calls=%async_computation.3 | async-start | bytes 4718592 | tf_op jit(solution)/shard_map/reduce_scatter | solution.py:94
  79.5 0.8 copy-start.4
  79.5 2.2 %copy-start.5 = (s32[256,4]{0,1:T(4,128)S(1)}, s32[256,4]{0,1:T(4,128)}, u32[]{:S(2)}) copy-start(s32[256,4]{0,1:T(4,128)} %param.17) | copy-start | bytes 12292
  79.5 4.6 %copy-start.2 = (bf16[256,4,1,64]{0,3,2,1:T(8,128)(2,1)S(1)}, bf16[256,4,1,64]{0,3,2,1:T(8,128)(2,1)}, u32[]{:S(2)}) copy-start(bf16[256,4,1,64]{0,3,2,1:T(8,128)(2,1)} %param.13) | copy-start | bytes 393220
  79.5 25.3 %copy-start.1 = (bf16[256,4,1,128]{3,1,2,0:T(4,128)(2,1)S(1)}, bf16[256,4,1,128]{3,1,2,0:T(4,128)(2,1)}, u32[]{:S(2)}) copy-start(bf16[256,4,1,128]{3,1,2,0:T(4,128)(2,1)} %param.15) | copy-start | bytes 786436
  79.5 75.7 %all-gather.7.cloned.1.call-start = ((), (), s32[]{:S(2)}) async-start(), calls=%async_computation.4 | async-start | bytes 1179648 | tf_op jit(solution)/shard_map/all_gather | solution.py:56
  124.4 32.2 %all-to-all-start.1 = ((bf16[64,256,8]{1,2,0:T(8,128)(2,1)}), bf16[64,256,8]{1,2,0:T(8,128)(2,1)S(1)}, u32[]{:S(2)}, u32[]{:S(2)}) async-start(bf16[64,256,8]{1,2,0:T(8,128)(2,1)} %copy.187), calls=%async_computation.2 | async-start | bytes 524288 | tf_op jit(solution)/shard_map/all_to_all | solution.py:100
  136.6 54.1 %all-gather.11.cloned.1.call-start = ((), (), s32[]{:S(2)}) async-start(), calls=%async_computation.6 | async-start | bytes 1179648 | tf_op jit(solution)/shard_map/all_gather | solution.py:56
Sparse Core Ops, SparseCore 0:
  29.3 44.6 all-gather.8
  79.6 42.7 reduce-scatter.1
  125.2 29.9 all-gather.6
  161.8 28.7 all-gather.10

commit v2 on v1

--- a/solution.py
+++ b/solution.py
@@ -34,28 +34,19 @@
     return jnp.where(keep_mask, jnp.exp(jnp.where(keep_mask, gaps, 0.0)), 0.0)
 
 
-def chain_weights(through_all, place, backward):
-    count = through_all.shape[0]
-    blocks = jnp.arange(count)
-    s2 = blocks[:, None]
-    s3 = blocks[None, :]
-    if backward:
-        used = (s3 > place) & (s3 < s2)
-        live = blocks > place
-    else:
-        used = (s3 > s2) & (s3 < place)
-        live = blocks < place
-    factors = jnp.where(used[:, :, None, None], through_all[None], 1.0)
-    weights = jnp.prod(factors, axis=1)
-    return jnp.where(live[:, None, None], weights, 0.0)
-
-
 def carried(local, through, axis, backward):
-    place = lax.axis_index(axis)
-    through_all = lax.all_gather(through, axis)
-    local_all = lax.all_gather(local, axis)
-    weights = chain_weights(through_all, place, backward)
-    return jnp.sum(weights[:, :, :, None, None] * local_all, axis=0)
+    count = lax.axis_size(axis)
+    total = jnp.zeros_like(local)
+    weight = jnp.ones_like(through)
+    for hop in range(1, count):
+        if backward:
+            pairs = [(src, src - hop) for src in range(hop, count)]
+        else:
+            pairs = [(src, src + hop) for src in range(count - hop)]
+        got_local, got_through = lax.ppermute((local, through), axis, pairs)
+        total = total + weight[:, :, None, None] * got_local
+        weight = weight * got_through
+    return total
 
 
 def per_device(
@@ -91,7 +82,9 @@
     sq_sums = jnp.sum(jnp.square(received.astype(jnp.float32)), axis=1)
     partial_value = partial_value.reshape(n_z, n_y * CAP, heads_all, -1)
     sq_sums = sq_sums.reshape(n_z, n_y * CAP)
-    summed = lax.psum_scatter(partial_value, "seq", scatter_dimension=0, tiled=True)[0]
+    summed = lax.psum_scatter(
+        partial_value.astype(jnp.bfloat16), "seq", scatter_dimension=0, tiled=True
+    )[0].astype(jnp.float32)
     totals = lax.psum_scatter(sq_sums, "seq", scatter_dimension=0, tiled=True)[0]
     row_scale = lax.rsqrt(totals / TD + EPS)
     scaled = (summed * row_scale[:, None, None]).astype(jnp.bfloat16)

time: 202 us -> 220 us (1.089)
  starting transfers between devices: 12.5 us -> 57 us
  blocking collectives: 44.4 us -> 31.2 us
  waiting for transfers between devices: 88.4 us -> 78.6 us
  other arithmetic: 13.1 us -> 10.2 us
    ppermute x0 -> x26, starting transfers between devices: none -> 47.1 us  [carried(): got_local, got_through = lax.ppermute((local, through), axis, pairs)]
    all_gather x2 -> x0, waiting for transfers between devices: 41.9 us -> none  [carried(): local_all = lax.all_gather(local, axis)]
    ppermute x0 -> x26, waiting for transfers between devices: none -> 37.7 us  [carried(): got_local, got_through = lax.ppermute((local, through), axis, pairs)]
    all_gather x1 -> x0, blocking collectives: 14.2 us -> none  [carried(): through_all = lax.all_gather(through, axis)]
    all_gather x1, waiting for transfers between devices: 44.5 us -> 40.8 us  [per_device(): received = lax.all_gather(by_family, 'tz')]
    reduce_sum x2 -> x0, other arithmetic: 2.74 us -> none  [carried(): return jnp.sum(weights[:, :, :, None, None] * local_all, axis=0)]
    all_to_all x1, starting transfers between devices: 12.2 us -> 9.9 us  [per_device(): lax.all_to_all(outgoing, TEACH, split_axis=0, concat_axis=0, tiled=True)]
    unnamed x20 -> x21, local copies, waits for them, and re-layouts: 4.73 us -> 4.74 us
  transfers between devices with their start and end apart: 5 -> 29, of which waited for: 4 -> 12; matrix products, arithmetic and copies ran while one was open for 11% -> 9% of each run, Pallas kernels for 0% -> 0%
where the time goes in v2:
time: 220 us; the launch traced here: 219 us
  waiting for transfers between devices  78.6 us (36%)
  starting transfers between devices  57 us (26%)
  blocking collectives  31.2 us (14%)
  between operations  16.1 us (7%)
  matrix products  13.2 us (6%)
  local copies, waits for them, and re-layouts  12.5 us (6%)
  other arithmetic  10.2 us (5%)
    ppermute x26, starting transfers between devices, carried(): got_local, got_through = lax.ppermute((local, through), axis, pairs)  47.1 us
    all_gather x1, waiting for transfers between devices, per_device(): received = lax.all_gather(by_family, 'tz')  40.8 us
    ppermute x26, waiting for transfers between devices, carried(): got_local, got_through = lax.ppermute((local, through), axis, pairs)  37.7 us
    all_to_all x1, blocking collectives, per_device(): lax.all_to_all(packed, 'ty', split_axis=0, concat_axis=0, tiled=True)  18.1 us
    unnamed x1, blocking collectives  13.1 us
    all_to_all x1, starting transfers between devices, per_device(): lax.all_to_all(outgoing, TEACH, split_axis=0, concat_axis=0, tiled=True)  9.9 us
    dot_general x1, matrix products, per_device(): jnp.dot(received, weights, preferred_element_type=jnp.float32)  4.89 us
    unnamed x21, local copies, waits for them, and re-layouts  4.74 us
  transfers between devices with their start and end apart: 29, of which 12 were waited for; matrix products, arithmetic and copies ran while one was open for 9% of the time, Pallas kernels for 0%

profile of v2, /device:TPU:1, one launch (start us, length us, event | category | flops | bytes accessed | tf_op | source)
XLA Modules:
  0.0 218.9 jit_solution(7762599797901052716)
XLA Ops:
  7.3 1.2 copy.134
  8.5 0.6 reshape.416
  9.7 1.0 reshape.417
  11.1 18.1 %all_to_all.10 = bf16[8,32,640]{2,1,0:T(8,128)(2,1)} all-to-all(bf16[8,32,640]{2,1,0:T(8,128)(2,1)S(1)} %bitcast.266), channel_id=1, replica_groups=mesh['tz'=8,'ty'=8,'seq'=8] {'ty'}, dimensions={0} | all-to-all | bytes 655360 | tf_op jit(solution)/shard_map/all_to_all | solution.py:76
  29.9 1.2 reduce-window.16
  31.2 1.2 reduce-window.14
  33.2 40.8 %all-gather.3.cloned.1.call-done = bf16[64,32,640]{2,1,0:T(8,128)(2,1)} async-done(((bf16[8,32,640]{2,1,0:T(8,128)(2,1)}), bf16[64,32,640]{2,1,0:T(8,128)(2,1)}) %all-gather.3.cloned.1.call-update) | async-done | bytes 2621456 | tf_op jit(solution)/shard_map/all_gather | solution.py:77
  74.0 4.9 %convolution_convert_fusion = bf16[8,256,64,8]{1,2,3,0:T(8,128)(2,1)} fusion(bf16[8,256,640,1]{2,1,3,0:T(8,128)(2,1)} %bitcast.261, bf16[64,8,640]{2,1,0:T(8,128)(2,1)S(1)} %bitcast.271), kind=kOutput, calls=%fused_computation.2 | convolution fusion | flops 1343225856 | bytes 5373952 | tf_op jit(solution)/shard_map/dot_general | solution.py:81
  79.6 6.8 %collective-permute-start.1 = (f32[4,1]{0,1:T(1,128)S(1)}, f32[4,1]{0,1:T(1,128)S(1)}, u32[]{:S(2)}, u32[]{:S(2)}) collective-permute-start(f32[4,1]{0,1:T(1,128)S(1)} %bitcast_select_fusion), channel_id=1, source_target_pairs={{0,1},{1,2},{2,3},{3,4},{4,5},{5,6},{6,7},{8,9},{9,10},{10,11},{11... | collective-permute-start | bytes 56 | tf_op jit(solution)/shard_map/ppermute | solution.py:46
  86.4 3.1 %collective-permute-start.9 = (f32[4,1]{0,1:T(1,128)S(1)}, f32[4,1]{0,1:T(1,128)S(1)}, u32[]{:S(2)}, u32[]{:S(2)}) collective-permute-start(f32[4,1]{0,1:T(1,128)S(1)} %bitcast_select_fusion), channel_id=1, source_target_pairs={{0,5},{1,6},{2,7},{8,13},{9,14},{10,15},{16,21},{17,22},{18,23},{2... | collective-permute-start | bytes 56 | tf_op jit(solution)/shard_map/ppermute | solution.py:46
  89.6 1.3 collective-permute-start.3
  90.9 3.4 %collective-permute-start.5 = (f32[4,1]{0,1:T(1,128)S(1)}, f32[4,1]{0,1:T(1,128)S(1)}, u32[]{:S(2)}, u32[]{:S(2)}) collective-permute-start(f32[4,1]{0,1:T(1,128)S(1)} %bitcast_select_fusion), channel_id=1, source_target_pairs={{0,3},{1,4},{2,5},{3,6},{4,7},{8,11},{9,12},{10,13},{11,14},{12,15... | collective-permute-start | bytes 56 | tf_op jit(solution)/shard_map/ppermute | solution.py:46
  94.2 1.3 collective-permute-start.7
  95.7 2.5 %select_reduce_fusion = s32[8,128]{0,1:T(8,128)S(1)} fusion(s32[8,128]{0,1:T(8,128)S(1)} %copy.135), kind=kOutput, calls=%fused_computation.41 | output fusion | flops 1096704 | bytes 8192 | tf_op jit(solution)/shard_map/jit(cumsum)/reduce_window_sum | solution.py:23
  99.2 1.3 dynamic-slice
  101.2 0.5 convolution_multiply_fusion.1
  101.7 0.6 convolution_bitcast_fusion.7
  102.3 1.3 collective-permute-start.11
  103.6 1.9 collective-permute-start
  105.6 1.3 collective-permute-start.10
  106.9 0.7 collective-permute-start.12
  107.6 3.0 %collective-permute-start.14 = (f32[4,1]{0,1:T(1,128)S(1)}, f32[4,1]{0,1:T(1,128)S(1)}, u32[]{:S(2)}, u32[]{:S(2)}) collective-permute-start(f32[4,1]{0,1:T(1,128)S(1)} %bitcast_select_fusion), channel_id=1, source_target_pairs={{1,0},{2,1},{3,2},{4,3},{5,4},{6,5},{7,6},{9,8},{10,9},{11,10},{12... | collective-permute-start | bytes 56 | tf_op jit(solution)/shard_map/ppermute | solution.py:46
  110.6 2.0 collective-permute-done.14
  112.7 1.3 collective-permute-start.22
  113.9 5.2 %collective-permute-done.22 = f32[4,1]{0,1:T(1,128)S(1)} collective-permute-done((f32[4,1]{0,1:T(1,128)S(1)}, f32[4,1]{0,1:T(1,128)S(1)}, u32[]{:S(2)}, u32[]{:S(2)}) %collective-permute-start.22) | collective-permute-done | bytes 48 | tf_op jit(solution)/shard_map/ppermute | solution.py:46
  119.1 1.3 collective-permute-start.16
  120.4 3.0 %collective-permute-done.16 = f32[4,1]{0,1:T(1,128)S(1)} collective-permute-done((f32[4,1]{0,1:T(1,128)S(1)}, f32[4,1]{0,1:T(1,128)S(1)}, u32[]{:S(2)}, u32[]{:S(2)}) %collective-permute-start.16) | collective-permute-done | bytes 48 | tf_op jit(solution)/shard_map/ppermute | solution.py:46
  123.4 1.3 collective-permute-start.18
  124.7 5.1 %collective-permute-done.18 = f32[4,1]{0,1:T(1,128)S(1)} collective-permute-done((f32[4,1]{0,1:T(1,128)S(1)}, f32[4,1]{0,1:T(1,128)S(1)}, u32[]{:S(2)}, u32[]{:S(2)}) %collective-permute-start.18) | collective-permute-done | bytes 48 | tf_op jit(solution)/shard_map/ppermute | solution.py:46
  129.8 1.3 collective-permute-start.20
  131.1 4.5 %collective-permute-done.20 = f32[4,1]{0,1:T(1,128)S(1)} collective-permute-done((f32[4,1]{0,1:T(1,128)S(1)}, f32[4,1]{0,1:T(1,128)S(1)}, u32[]{:S(2)}, u32[]{:S(2)}) %collective-permute-start.20) | collective-permute-done | bytes 48 | tf_op jit(solution)/shard_map/ppermute | solution.py:46
  135.6 1.7 collective-permute-start.2
  137.3 2.3 %multiply_reduce_fusion = f32[64,32]{1,0:T(8,128)S(1)} fusion(bf16[64,32,640]{2,1,0:T(8,128)(2,1)} %all-gather.3.cloned.1.call-done), kind=kLoop, calls=%fused_computation.1 | loop fusion | flops 3930112 | bytes 2629632 | tf_op jit(solution)/shard_map/reduce_sum | solution.py:82
  139.7 13.1 %all-reduce = f32[8,256]{1,0:T(8,128)S(1)} all-reduce(f32[8,256]{1,0:T(8,128)S(1)} %reshape.419), channel_id=4, replica_groups=mesh['tz'=8,'ty'=8,'seq'=8] {'seq'}, use_global_device_ids=true, to_apply=%region_10.11.clone | all-reduce | flops 2048 | bytes 16384
  152.8 0.7 fusion.60
  153.5 1.0 fusion.29
  154.5 0.9 copy.140
  155.4 9.9 %all-to-all-start.1 = ((bf16[64,256,8]{1,2,0:T(8,128)(2,1)}), bf16[64,256,8]{1,2,0:T(8,128)(2,1)S(1)}, u32[]{:S(2)}, u32[]{:S(2)}) async-start(bf16[64,256,8]{1,2,0:T(8,128)(2,1)} %copy.140), calls=%async_computation.2 | async-start | bytes 524288 | tf_op jit(solution)/shard_map/all_to_all | solution.py:93
  165.3 1.3 collective-permute-start.24
  166.6 4.5 %collective-permute-done.24 = f32[4,1]{0,1:T(1,128)S(1)} collective-permute-done((f32[4,1]{0,1:T(1,128)S(1)}, f32[4,1]{0,1:T(1,128)S(1)}, u32[]{:S(2)}, u32[]{:S(2)}) %collective-permute-start.24) | collective-permute-done | bytes 48 | tf_op jit(solution)/shard_map/ppermute | solution.py:46
  171.1 1.3 collective-permute-start.4
  172.4 1.3 collective-permute-start.6
  173.7 3.3 %collective-permute-start.8 = (f32[4,1,64,128]{3,2,0,1:T(8,128)S(1)}, f32[4,1,64,128]{3,2,0,1:T(8,128)S(1)}, u32[]{:S(2)}, u32[]{:S(2)}) collective-permute-start(f32[4,1,64,128]{3,2,0,1:T(8,128)S(1)} %convolution_bitcast_fusion.9), channel_id=1, source_target_pairs={{0,5},{1,6},{2,7},{8,13},{9,14},{10,15},{16,21},{17,22},{18,23},{2... | collective-permute-start | bytes 393224 | tf_op jit(solution)/shard_map/ppermute | solution.py:46
  177.1 4.9 %collective-permute-done.8 = f32[4,1,64,128]{3,2,0,1:T(8,128)S(1)} collective-permute-done((f32[4,1,64,128]{3,2,0,1:T(8,128)S(1)}, f32[4,1,64,128]{3,2,0,1:T(8,128)S(1)}, u32[]{:S(2)}, u32[]{:S(2)}) %collective-permute-start.8) | collective-permute-done | bytes 131104 | tf_op jit(solution)/shard_map/ppermute | solution.py:46
  182.5 3.2 %gather_fusion = bf16[1024,64]{1,0:T(8,128)(2,1)S(1)} fusion(bf16[2048,64]{1,0:T(8,128)(2,1)S(1)} %copy.142, s32[1024]{0:T(1024)S(1)} %broadcast_clamp_fusion), kind=kCustom, calls=%fused_computation | custom fusion | bytes 266240 | tf_op jit(solution)/shard_map/jit(_take)/gather | solution.py:104
  186.3 1.0 convolution_multiply_fusion
  187.6 1.9 collective-permute-start.13
  189.5 1.3 collective-permute-start.15
  190.8 1.3 collective-permute-start.17
  192.1 1.3 collective-permute-start.19
  193.4 1.3 collective-permute-start.21
  194.7 0.4 convolution_bitcast_fusion.1
  195.2 1.1 fusion.4
  196.3 0.9 copy.153
  197.2 0.8 convolution_bitcast_fusion.3
  198.0 1.3 collective-permute-start.23
  199.3 0.7 collective-permute-start.25
  200.0 0.4 convolution_bitcast_fusion.6
  200.5 1.8 collective-permute-done.19
  202.2 3.2 %collective-permute-done.21 = f32[4,1,128,64]{2,3,0,1:T(8,128)S(1)} collective-permute-done((f32[4,1,128,64]{2,3,0,1:T(8,128)S(1)}, f32[4,1,128,64]{2,3,0,1:T(8,128)S(1)}, u32[]{:S(2)}, u32[]{:S(2)}) %collective-permute-start.21) | collective-permute-done | bytes 131104 | tf_op jit(solution)/shard_map/ppermute | solution.py:46
  205.4 3.4 %collective-permute-done.23 = f32[4,1,128,64]{2,3,0,1:T(8,128)S(1)} collective-permute-done((f32[4,1,128,64]{2,3,0,1:T(8,128)S(1)}, f32[4,1,128,64]{2,3,0,1:T(8,128)S(1)}, u32[]{:S(2)}, u32[]{:S(2)}) %collective-permute-start.23) | collective-permute-done | bytes 131104 | tf_op jit(solution)/shard_map/ppermute | solution.py:46
  209.0 1.1 fusion.5
  210.1 0.9 copy.152
  211.0 1.1 fusion.15
  (89 shorter events, 5.4 us)
Async XLA Ops:
  7.2 93.6 %copy-start = (bf16[256,4,1,128]{3,1,2,0:T(4,128)(2,1)S(1)}, bf16[256,4,1,128]{3,1,2,0:T(4,128)(2,1)}, u32[]{:S(2)}) copy-start(bf16[256,4,1,128]{3,1,2,0:T(4,128)(2,1)} %param.14) | copy-start | bytes 786436
  7.2 22.7 %copy-start.4 = (f32[256,4,1]{0,2,1:T(1,128)S(1)}, f32[256,4,1]{0,2,1:T(1,128)}, u32[]{:S(2)}) copy-start(f32[256,4,1]{0,2,1:T(1,128)} %param.16) | copy-start | bytes 12292
  7.2 24.0 %copy-start.5 = (s32[256,4]{0,1:T(4,128)S(1)}, s32[256,4]{0,1:T(4,128)}, u32[]{:S(2)}) copy-start(s32[256,4]{0,1:T(4,128)} %param.17) | copy-start | bytes 12292
  7.2 25.7 %copy-start.3 = (bf16[1,640,512]{2,1,0:T(8,128)(2,1)S(1)}, bf16[1,640,512]{2,1,0:T(8,128)(2,1)}, u32[]{:S(2)}) copy-start(bf16[1,640,512]{2,1,0:T(8,128)(2,1)} %param.11) | copy-start | bytes 1966084
  7.2 66.8 %all-gather.3.cloned.1.call-start = ((), (), s32[]{:S(2)}) async-start(), calls=%async_computation.4 | async-start | bytes 2949120 | tf_op jit(solution)/shard_map/all_gather | solution.py:77
  29.2 124.3 %reduce-scatter.2.cloned.1.call-start = ((), (), s32[]{:S(2)}) async-start(), calls=%async_computation.3 | async-start | bytes 2359296 | tf_op jit(solution)/shard_map/reduce_scatter | solution.py:85
  78.9 21.9 %copy-start.2 = (bf16[256,4,1,64]{0,3,2,1:T(8,128)(2,1)S(1)}, bf16[256,4,1,64]{0,3,2,1:T(8,128)(2,1)}, u32[]{:S(2)}) copy-start(bf16[256,4,1,64]{0,3,2,1:T(8,128)(2,1)} %param.13) | copy-start | bytes 393220
  78.9 22.2 %copy-start.1 = (bf16[256,4,1,128]{3,1,2,0:T(4,128)(2,1)S(1)}, bf16[256,4,1,128]{3,1,2,0:T(4,128)(2,1)}, u32[]{:S(2)}) copy-start(bf16[256,4,1,128]{3,1,2,0:T(4,128)(2,1)} %param.15) | copy-start | bytes 786436
  79.6 22.7 %collective-permute-start.1 = (f32[4,1]{0,1:T(1,128)S(1)}, f32[4,1]{0,1:T(1,128)S(1)}, u32[]{:S(2)}, u32[]{:S(2)}) collective-permute-start(f32[4,1]{0,1:T(1,128)S(1)} %bitcast_select_fusion), channel_id=1, source_target_pairs={{0,1},{1,2},{2,3},{3,4},{4,5},{5,6},{6,7},{8,9},{9,10},{10,11},{11... | collective-permute-start | bytes 56 | tf_op jit(solution)/shard_map/ppermute | solution.py:46
  86.4 17.2 %collective-permute-start.9 = (f32[4,1]{0,1:T(1,128)S(1)}, f32[4,1]{0,1:T(1,128)S(1)}, u32[]{:S(2)}, u32[]{:S(2)}) collective-permute-start(f32[4,1]{0,1:T(1,128)S(1)} %bitcast_select_fusion), channel_id=1, source_target_pairs={{0,5},{1,6},{2,7},{8,13},{9,14},{10,15},{16,21},{17,22},{18,23},{2... | collective-permute-start | bytes 56 | tf_op jit(solution)/shard_map/ppermute | solution.py:46
  89.6 16.0 %collective-permute-start.3 = (f32[4,1]{0,1:T(1,128)S(1)}, f32[4,1]{0,1:T(1,128)S(1)}, u32[]{:S(2)}, u32[]{:S(2)}) collective-permute-start(f32[4,1]{0,1:T(1,128)S(1)} %bitcast_select_fusion), channel_id=1, source_target_pairs={{0,2},{1,3},{2,4},{3,5},{4,6},{5,7},{8,10},{9,11},{10,12},{11,13},... | collective-permute-start | bytes 56 | tf_op jit(solution)/shard_map/ppermute | solution.py:46
  90.9 16.0 %collective-permute-start.5 = (f32[4,1]{0,1:T(1,128)S(1)}, f32[4,1]{0,1:T(1,128)S(1)}, u32[]{:S(2)}, u32[]{:S(2)}) collective-permute-start(f32[4,1]{0,1:T(1,128)S(1)} %bitcast_select_fusion), channel_id=1, source_target_pairs={{0,3},{1,4},{2,5},{3,6},{4,7},{8,11},{9,12},{10,13},{11,14},{12,15... | collective-permute-start | bytes 56 | tf_op jit(solution)/shard_map/ppermute | solution.py:46
  94.2 13.3 %collective-permute-start.7 = (f32[4,1]{0,1:T(1,128)S(1)}, f32[4,1]{0,1:T(1,128)S(1)}, u32[]{:S(2)}, u32[]{:S(2)}) collective-permute-start(f32[4,1]{0,1:T(1,128)S(1)} %bitcast_select_fusion), channel_id=1, source_target_pairs={{0,4},{1,5},{2,6},{3,7},{8,12},{9,13},{10,14},{11,15},{16,20},{17,... | collective-permute-start | bytes 56 | tf_op jit(solution)/shard_map/ppermute | solution.py:46
  102.3 63.0 %collective-permute-start.11 = (f32[4,1]{0,1:T(1,128)S(1)}, f32[4,1]{0,1:T(1,128)S(1)}, u32[]{:S(2)}, u32[]{:S(2)}) collective-permute-start(f32[4,1]{0,1:T(1,128)S(1)} %bitcast_select_fusion), channel_id=1, source_target_pairs={{0,6},{1,7},{8,14},{9,15},{16,22},{17,23},{24,30},{25,31},{32,38},... | collective-permute-start | bytes 56 | tf_op jit(solution)/shard_map/ppermute | solution.py:46
  103.6 68.8 %collective-permute-start = (f32[4,1,64,128]{3,2,0,1:T(8,128)S(1)}, f32[4,1,64,128]{3,2,0,1:T(8,128)S(1)}, u32[]{:S(2)}, u32[]{:S(2)}) collective-permute-start(f32[4,1,64,128]{3,2,0,1:T(8,128)S(1)} %convolution_bitcast_fusion.9), channel_id=1, source_target_pairs={{0,1},{1,2},{2,3},{3,4},{4,5},{5,6},{6,7},{8,9},{9,10},{10,11},{11... | collective-permute-start | bytes 393224 | tf_op jit(solution)/shard_map/ppermute | solution.py:46
  105.6 68.2 %collective-permute-start.10 = (f32[4,1,64,128]{3,2,0,1:T(8,128)S(1)}, f32[4,1,64,128]{3,2,0,1:T(8,128)S(1)}, u32[]{:S(2)}, u32[]{:S(2)}) collective-permute-start(f32[4,1,64,128]{3,2,0,1:T(8,128)S(1)} %convolution_bitcast_fusion.9), channel_id=1, source_target_pairs={{0,6},{1,7},{8,14},{9,15},{16,22},{17,23},{24,30},{25,31},{32,38},... | collective-permute-start | bytes 393224 | tf_op jit(solution)/shard_map/ppermute | solution.py:46
  106.9 70.2 %collective-permute-start.12 = (f32[4,1,64,128]{3,2,0,1:T(8,128)S(1)}, f32[4,1,64,128]{3,2,0,1:T(8,128)S(1)}, u32[]{:S(2)}, u32[]{:S(2)}) collective-permute-start(f32[4,1,64,128]{3,2,0,1:T(8,128)S(1)} %convolution_bitcast_fusion.9), channel_id=1, source_target_pairs={{0,7},{8,15},{16,23},{24,31},{32,39},{40,47},{48,55},{56,63},{64,7... | collective-permute-start | bytes 393224 | tf_op jit(solution)/shard_map/ppermute | solution.py:46
  107.6 5.1 %collective-permute-start.14 = (f32[4,1]{0,1:T(1,128)S(1)}, f32[4,1]{0,1:T(1,128)S(1)}, u32[]{:S(2)}, u32[]{:S(2)}) collective-permute-start(f32[4,1]{0,1:T(1,128)S(1)} %bitcast_select_fusion), channel_id=1, source_target_pairs={{1,0},{2,1},{3,2},{4,3},{5,4},{6,5},{7,6},{9,8},{10,9},{11,10},{12... | collective-permute-start | bytes 56 | tf_op jit(solution)/shard_map/ppermute | solution.py:46
  112.7 6.5 %collective-permute-start.22 = (f32[4,1]{0,1:T(1,128)S(1)}, f32[4,1]{0,1:T(1,128)S(1)}, u32[]{:S(2)}, u32[]{:S(2)}) collective-permute-start(f32[4,1]{0,1:T(1,128)S(1)} %bitcast_select_fusion), channel_id=1, source_target_pairs={{5,0},{6,1},{7,2},{13,8},{14,9},{15,10},{21,16},{22,17},{23,18},{2... | collective-permute-start | bytes 56 | tf_op jit(solution)/shard_map/ppermute | solution.py:46
  119.1 4.3 %collective-permute-start.16 = (f32[4,1]{0,1:T(1,128)S(1)}, f32[4,1]{0,1:T(1,128)S(1)}, u32[]{:S(2)}, u32[]{:S(2)}) collective-permute-start(f32[4,1]{0,1:T(1,128)S(1)} %bitcast_select_fusion), channel_id=1, source_target_pairs={{2,0},{3,1},{4,2},{5,3},{6,4},{7,5},{10,8},{11,9},{12,10},{13,11},... | collective-permute-start | bytes 56 | tf_op jit(solution)/shard_map/ppermute | solution.py:46
  123.4 6.4 %collective-permute-start.18 = (f32[4,1]{0,1:T(1,128)S(1)}, f32[4,1]{0,1:T(1,128)S(1)}, u32[]{:S(2)}, u32[]{:S(2)}) collective-permute-start(f32[4,1]{0,1:T(1,128)S(1)} %bitcast_select_fusion), channel_id=1, source_target_pairs={{3,0},{4,1},{5,2},{6,3},{7,4},{11,8},{12,9},{13,10},{14,11},{15,12... | collective-permute-start | bytes 56 | tf_op jit(solution)/shard_map/ppermute | solution.py:46
  129.8 5.8 %collective-permute-start.20 = (f32[4,1]{0,1:T(1,128)S(1)}, f32[4,1]{0,1:T(1,128)S(1)}, u32[]{:S(2)}, u32[]{:S(2)}) collective-permute-start(f32[4,1]{0,1:T(1,128)S(1)} %bitcast_select_fusion), channel_id=1, source_target_pairs={{4,0},{5,1},{6,2},{7,3},{12,8},{13,9},{14,10},{15,11},{20,16},{21,... | collective-permute-start | bytes 56 | tf_op jit(solution)/shard_map/ppermute | solution.py:46
  135.6 41.4 %collective-permute-start.2 = (f32[4,1,64,128]{3,2,0,1:T(8,128)S(1)}, f32[4,1,64,128]{3,2,0,1:T(8,128)S(1)}, u32[]{:S(2)}, u32[]{:S(2)}) collective-permute-start(f32[4,1,64,128]{3,2,0,1:T(8,128)S(1)} %convolution_bitcast_fusion.9), channel_id=1, source_target_pairs={{0,2},{1,3},{2,4},{3,5},{4,6},{5,7},{8,10},{9,11},{10,12},{11,13},... | collective-permute-start | bytes 393224 | tf_op jit(solution)/shard_map/ppermute | solution.py:46
  155.4 26.8 %all-to-all-start.1 = ((bf16[64,256,8]{1,2,0:T(8,128)(2,1)}), bf16[64,256,8]{1,2,0:T(8,128)(2,1)S(1)}, u32[]{:S(2)}, u32[]{:S(2)}) async-start(bf16[64,256,8]{1,2,0:T(8,128)(2,1)} %copy.140), calls=%async_computation.2 | async-start | bytes 524288 | tf_op jit(solution)/shard_map/all_to_all | solution.py:93
  165.3 5.8 %collective-permute-start.24 = (f32[4,1]{0,1:T(1,128)S(1)}, f32[4,1]{0,1:T(1,128)S(1)}, u32[]{:S(2)}, u32[]{:S(2)}) collective-permute-start(f32[4,1]{0,1:T(1,128)S(1)} %bitcast_select_fusion), channel_id=1, source_target_pairs={{6,0},{7,1},{14,8},{15,9},{22,16},{23,17},{30,24},{31,25},{38,32},... | collective-permute-start | bytes 56 | tf_op jit(solution)/shard_map/ppermute | solution.py:46
  171.1 5.9 %collective-permute-start.4 = (f32[4,1,64,128]{3,2,0,1:T(8,128)S(1)}, f32[4,1,64,128]{3,2,0,1:T(8,128)S(1)}, u32[]{:S(2)}, u32[]{:S(2)}) collective-permute-start(f32[4,1,64,128]{3,2,0,1:T(8,128)S(1)} %convolution_bitcast_fusion.9), channel_id=1, source_target_pairs={{0,3},{1,4},{2,5},{3,6},{4,7},{8,11},{9,12},{10,13},{11,14},{12,15... | collective-permute-start | bytes 393224 | tf_op jit(solution)/shard_map/ppermute | solution.py:46
  172.4 4.6 %collective-permute-start.6 = (f32[4,1,64,128]{3,2,0,1:T(8,128)S(1)}, f32[4,1,64,128]{3,2,0,1:T(8,128)S(1)}, u32[]{:S(2)}, u32[]{:S(2)}) collective-permute-start(f32[4,1,64,128]{3,2,0,1:T(8,128)S(1)} %convolution_bitcast_fusion.9), channel_id=1, source_target_pairs={{0,4},{1,5},{2,6},{3,7},{8,12},{9,13},{10,14},{11,15},{16,20},{17,... | collective-permute-start | bytes 393224 | tf_op jit(solution)/shard_map/ppermute | solution.py:46
  173.7 8.3 %collective-permute-start.8 = (f32[4,1,64,128]{3,2,0,1:T(8,128)S(1)}, f32[4,1,64,128]{3,2,0,1:T(8,128)S(1)}, u32[]{:S(2)}, u32[]{:S(2)}) collective-permute-start(f32[4,1,64,128]{3,2,0,1:T(8,128)S(1)} %convolution_bitcast_fusion.9), channel_id=1, source_target_pairs={{0,5},{1,6},{2,7},{8,13},{9,14},{10,15},{16,21},{17,22},{18,23},{2... | collective-permute-start | bytes 393224 | tf_op jit(solution)/shard_map/ppermute | solution.py:46
  187.6 10.4 %collective-permute-start.13 = (f32[4,1,128,64]{2,3,0,1:T(8,128)S(1)}, f32[4,1,128,64]{2,3,0,1:T(8,128)S(1)}, u32[]{:S(2)}, u32[]{:S(2)}) collective-permute-start(f32[4,1,128,64]{2,3,0,1:T(8,128)S(1)} %convolution_bitcast_fusion.8), channel_id=1, source_target_pairs={{1,0},{2,1},{3,2},{4,3},{5,4},{6,5},{7,6},{9,8},{10,9},{11,10},{12... | collective-permute-start | bytes 393224 | tf_op jit(solution)/shard_map/ppermute | solution.py:46
  189.5 9.8 %collective-permute-start.15 = (f32[4,1,128,64]{2,3,0,1:T(8,128)S(1)}, f32[4,1,128,64]{2,3,0,1:T(8,128)S(1)}, u32[]{:S(2)}, u32[]{:S(2)}) collective-permute-start(f32[4,1,128,64]{2,3,0,1:T(8,128)S(1)} %convolution_bitcast_fusion.8), channel_id=1, source_target_pairs={{2,0},{3,1},{4,2},{5,3},{6,4},{7,5},{10,8},{11,9},{12,10},{13,11},... | collective-permute-start | bytes 393224 | tf_op jit(solution)/shard_map/ppermute | solution.py:46
  190.8 9.6 %collective-permute-start.17 = (f32[4,1,128,64]{2,3,0,1:T(8,128)S(1)}, f32[4,1,128,64]{2,3,0,1:T(8,128)S(1)}, u32[]{:S(2)}, u32[]{:S(2)}) collective-permute-start(f32[4,1,128,64]{2,3,0,1:T(8,128)S(1)} %convolution_bitcast_fusion.8), channel_id=1, source_target_pairs={{3,0},{4,1},{5,2},{6,3},{7,4},{11,8},{12,9},{13,10},{14,11},{15,12... | collective-permute-start | bytes 393224 | tf_op jit(solution)/shard_map/ppermute | solution.py:46
  192.1 10.1 %collective-permute-start.19 = (f32[4,1,128,64]{2,3,0,1:T(8,128)S(1)}, f32[4,1,128,64]{2,3,0,1:T(8,128)S(1)}, u32[]{:S(2)}, u32[]{:S(2)}) collective-permute-start(f32[4,1,128,64]{2,3,0,1:T(8,128)S(1)} %convolution_bitcast_fusion.8), channel_id=1, source_target_pairs={{4,0},{5,1},{6,2},{7,3},{12,8},{13,9},{14,10},{15,11},{20,16},{21,... | collective-permute-start | bytes 393224 | tf_op jit(solution)/shard_map/ppermute | solution.py:46
  193.4 12.0 %collective-permute-start.21 = (f32[4,1,128,64]{2,3,0,1:T(8,128)S(1)}, f32[4,1,128,64]{2,3,0,1:T(8,128)S(1)}, u32[]{:S(2)}, u32[]{:S(2)}) collective-permute-start(f32[4,1,128,64]{2,3,0,1:T(8,128)S(1)} %convolution_bitcast_fusion.8), channel_id=1, source_target_pairs={{5,0},{6,1},{7,2},{13,8},{14,9},{15,10},{21,16},{22,17},{23,18},{2... | collective-permute-start | bytes 393224 | tf_op jit(solution)/shard_map/ppermute | solution.py:46
  198.0 10.8 %collective-permute-start.23 = (f32[4,1,128,64]{2,3,0,1:T(8,128)S(1)}, f32[4,1,128,64]{2,3,0,1:T(8,128)S(1)}, u32[]{:S(2)}, u32[]{:S(2)}) collective-permute-start(f32[4,1,128,64]{2,3,0,1:T(8,128)S(1)} %convolution_bitcast_fusion.8), channel_id=1, source_target_pairs={{6,0},{7,1},{14,8},{15,9},{22,16},{23,17},{30,24},{31,25},{38,32},... | collective-permute-start | bytes 393224 | tf_op jit(solution)/shard_map/ppermute | solution.py:46
  199.3 9.5 %collective-permute-start.25 = (f32[4,1,128,64]{2,3,0,1:T(8,128)S(1)}, f32[4,1,128,64]{2,3,0,1:T(8,128)S(1)}, u32[]{:S(2)}, u32[]{:S(2)}) collective-permute-start(f32[4,1,128,64]{2,3,0,1:T(8,128)S(1)} %convolution_bitcast_fusion.8), channel_id=1, source_target_pairs={{7,0},{15,8},{23,16},{31,24},{39,32},{47,40},{55,48},{63,56},{71,6... | collective-permute-start | bytes 393224 | tf_op jit(solution)/shard_map/ppermute | solution.py:46
Sparse Core Ops, SparseCore 0:
  29.3 44.6 all-gather.2
  79.1 40.4 reduce-scatter.1

commit v3 on v1

--- a/solution.py
+++ b/solution.py
@@ -50,12 +50,8 @@
     return jnp.where(live[:, None, None], weights, 0.0)
 
 
-def carried(local, through, axis, backward):
-    place = lax.axis_index(axis)
-    through_all = lax.all_gather(through, axis)
-    local_all = lax.all_gather(local, axis)
-    weights = chain_weights(through_all, place, backward)
-    return jnp.sum(weights[:, :, :, None, None] * local_all, axis=0)
+def combine(weights, local_all):
+    return jnp.sum(weights[:, :, :, None, None] * local_all.astype(jnp.float32), axis=0)
 
 
 def per_device(
@@ -122,7 +118,24 @@
     through = jnp.exp(log_sums[-1]) * (counts[-1] == 0).astype(jnp.float32)[:, None]
     inputs = step_size[..., None] * x_full
     local_state = jnp.einsum("jbh,jbhp,jbhn->bhpn", to_end, inputs, b_full, precision=HIGH)
-    state_in = carried(local_state, through, "seq", False)
+    place = lax.axis_index("seq")
+    through_hi = through.astype(jnp.bfloat16)
+    through_lo = (through - through_hi.astype(jnp.float32)).astype(jnp.bfloat16)
+    edge = local_state.shape[-1]
+    packed_state = jnp.concatenate(
+        [
+            local_state.astype(jnp.bfloat16),
+            jnp.broadcast_to(through_hi[:, :, None, None], through.shape + (1, edge)),
+            jnp.broadcast_to(through_lo[:, :, None, None], through.shape + (1, edge)),
+        ],
+        axis=2,
+    )
+    gathered = lax.all_gather(packed_state, "seq")
+    rows = local_state.shape[2]
+    through_all = gathered[:, :, :, rows, 0].astype(jnp.float32) + gathered[
+        :, :, :, rows + 1, 0
+    ].astype(jnp.float32)
+    state_in = combine(chain_weights(through_all, place, False), gathered[:, :, :, :rows])
     decay_mat = decay_matrix(log_sums, counts)
     scores = jnp.einsum("ibhn,jbhn->bhij", c_in, b_in, preferred_element_type=jnp.float32)
     mixing = decay_mat * scores
@@ -133,7 +146,8 @@
     output = output + skip_gain[None, None, :, None] * x_full
     residual = output - target.astype(jnp.float32)
     local_adjoint = jnp.einsum("ibh,ibhn,ibhp->bhnp", from_start, c_full, residual, precision=HIGH)
-    adjoint_in = carried(local_adjoint, through, "seq", True)
+    adjoint_all = lax.all_gather(local_adjoint.astype(jnp.bfloat16), "seq")
+    adjoint_in = combine(chain_weights(through_all, place, True), adjoint_all)
     grad_u = jnp.einsum("bhij,ibhp->jbhp", mixing, residual, precision=QUADRATIC)
     grad_u = grad_u + to_end[..., None] * jnp.einsum(
         "jbhn,bhnp->jbhp", b_full, adjoint_in, precision=HIGH

time: 202 us -> 187 us (0.926)
  waiting for transfers between devices: 88.4 us -> 56.1 us
  blocking collectives: 44.4 us -> 65.6 us
  other arithmetic: 13.1 us -> 10.5 us
    all_gather x2 -> x0, waiting for transfers between devices: 41.9 us -> none  [carried(): local_all = lax.all_gather(local, axis)]
    all_gather x1 -> x2, blocking collectives: 14.2 us -> 35.3 us  [the longest x1 17.7 us: per_device(): adjoint_all = lax.all_gather(local_adjoint.astype(jnp.bfloat16), 'seq')]
    all_to_all x1, waiting for transfers between devices: 0.01 us -> 11.6 us  [per_device(): lax.all_to_all(outgoing, TEACH, split_axis=0, concat_axis=0, tiled=True)]
    reduce_sum x2, other arithmetic: 2.74 us -> 0.33 us  [combine(): jnp.sum(weights[:, :, :, None, None] * local_all.astype(jnp.float32), axi...]
    unnamed x20 -> x22, local copies, waits for them, and re-layouts: 4.73 us -> 4.95 us
  transfers between devices with their start and end apart: 5 -> 3, of which waited for: 4 -> 2; matrix products, arithmetic and copies ran while one was open for 11% -> 7% of each run, Pallas kernels for 0% -> 0%
where the time goes in v3:
time: 187 us
  blocking collectives  65.6 us (35%)
  waiting for transfers between devices  56.1 us (30%)
  between operations  15.8 us (8%)
  matrix products  13.8 us (7%)
  local copies, waits for them, and re-layouts  13 us (7%)
  starting transfers between devices  11.8 us (6%)
  other arithmetic  10.5 us (6%)
    all_gather x1, waiting for transfers between devices, per_device(): received = lax.all_gather(by_family, 'tz')  44.5 us
    all_to_all x1, blocking collectives, per_device(): lax.all_to_all(packed, 'ty', split_axis=0, concat_axis=0, tiled=True)  18.1 us
    all_gather x1, blocking collectives, per_device(): adjoint_all = lax.all_gather(local_adjoint.astype(jnp.bfloat16), 'seq')  17.7 us
    all_gather x1, blocking collectives, per_device(): gathered = lax.all_gather(packed_state, 'seq')  17.6 us
    unnamed x1, blocking collectives  12.2 us
    all_to_all x1, starting transfers between devices, per_device(): lax.all_to_all(outgoing, TEACH, split_axis=0, concat_axis=0, tiled=True)  11.7 us
    all_to_all x1, waiting for transfers between devices, per_device(): lax.all_to_all(outgoing, TEACH, split_axis=0, concat_axis=0, tiled=True)  11.6 us
    dot_general x1, matrix products, per_device(): jnp.dot(received, weights, preferred_element_type=jnp.float32)  5.49 us
  transfers between devices with their start and end apart: 3, of which 2 were waited for; matrix products, arithmetic and copies ran while one was open for 7% of the time, Pallas kernels for 0%

profile of v3, /device:TPU:1, one launch (start us, length us, event | category | flops | bytes accessed | tf_op | source)
XLA Modules:
  0.0 186.7 jit_solution(14880902745041684816)
XLA Ops:
  7.2 1.2 copy.184
  8.4 0.6 reshape.554
  9.1 0.1 dynamic_slice.7
  9.2 0.1 fusion.57
  9.3 0.2 reduce_window_sum.81
  9.4 0.2 select_reduce_fusion.1
  9.6 0.1 multiply_add_fusion
  9.7 1.0 reshape.555
  10.7 0.4 convolution_convert_fusion
  11.0 18.1 %all_to_all.10 = bf16[8,32,640]{2,1,0:T(8,128)(2,1)} all-to-all(bf16[8,32,640]{2,1,0:T(8,128)(2,1)S(1)} %bitcast.246), channel_id=1, replica_groups=mesh['tz'=8,'ty'=8,'seq'=8] {'ty'}, dimensions={0} | all-to-all | bytes 655360 | tf_op jit(solution)/shard_map/all_to_all | solution.py:81
  29.2 0.3 copy.188
  29.5 44.5 %all-gather.5.cloned.1.call-done = bf16[64,32,640]{2,1,0:T(8,128)(2,1)} async-done(((bf16[8,32,640]{2,1,0:T(8,128)(2,1)}), bf16[64,32,640]{2,1,0:T(8,128)(2,1)}) %all-gather.5.cloned.1.call-update) | async-done | bytes 2621456 | tf_op jit(solution)/shard_map/all_gather | solution.py:82
  74.0 5.5 %fusion.23 = f32[8,256,64,8]{1,2,3,0:T(8,128)} fusion(bf16[8,256,640,1]{2,1,3,0:T(8,128)(2,1)} %bitcast.238, bf16[64,8,640]{2,1,0:T(8,128)(2,1)S(1)} %bitcast.251), kind=kOutput, calls=%fused_computation.41 | convolution fusion | flops 1342177280 | bytes 7471104 | tf_op jit(solution)/shard_map/dot_general | solution.py:86
  80.3 1.2 reduce-window.16
  81.5 0.1 slice.41
  81.6 0.1 copy.185
  81.7 2.5 %select_reduce_fusion = s32[8,128]{0,1:T(8,128)S(1)} fusion(s32[8,128]{0,1:T(8,128)S(1)} %copy.185), kind=kOutput, calls=%fused_computation.46 | output fusion | flops 1096704 | bytes 8192 | tf_op jit(solution)/shard_map/jit(cumsum)/reduce_window_sum | solution.py:23
  84.3 1.2 reduce-window.14
  85.5 0.1 slice.40
  85.6 0.1 copy.172
  85.7 0.1 copy.173
  85.8 0.1 copy.174
  86.0 0.1 copy.175
  86.1 0.1 broadcast.282
  86.3 0.2 slice_reduce_fusion
  86.4 0.2 slice_reduce_fusion.1
  86.6 0.1 copy_bitcast_fusion.2
  86.7 0.3 fusion.16
  87.2 17.6 %all-gather = bf16[32,1,66,128]{3,2,1,0:T(8,128)(2,1)S(1)} all-gather(bf16[4,1,66,128]{3,2,1,0:T(8,128)(2,1)S(1)} %maximum_bitcast_fusion), channel_id=2, replica_groups=mesh['tz'=8,'ty'=8,'seq'=8] {'seq'}, dimensions={0}, use_global_device_ids=true | all-gather | bytes 608256 | tf_op jit(solution)/shard_map/all_gather | solution.py:133
  104.9 0.1 copy.210
  105.0 0.1 copy.211
  105.1 0.2 select_reduce_fusion.2
  105.4 0.1 copy.182
  105.5 0.2 broadcast_in_dim.132
  105.6 0.1 copy.187
  106.4 0.1 copy.194
  106.5 1.3 dynamic-slice
  107.9 0.5 convolution_multiply_fusion.1
  108.3 2.4 %multiply_reduce_fusion = f32[64,32]{1,0:T(8,128)S(1)} fusion(bf16[64,32,640]{2,1,0:T(8,128)(2,1)} %all-gather.5.cloned.1.call-done), kind=kLoop, calls=%fused_computation.1 | loop fusion | flops 3930112 | bytes 2629632 | tf_op jit(solution)/shard_map/reduce_sum | solution.py:87
  110.7 0.1 reshape.557
  110.8 12.2 %all-reduce = f32[8,256]{1,0:T(8,128)S(1)} all-reduce(f32[8,256]{1,0:T(8,128)S(1)} %reshape.557), channel_id=6, replica_groups=mesh['tz'=8,'ty'=8,'seq'=8] {'seq'}, use_global_device_ids=true, to_apply=%region_12.13.clone | all-reduce | flops 2048 | bytes 16384
  123.0 0.7 fusion.62
  123.7 1.1 fusion.33
  124.8 0.9 copy.190
  125.6 11.7 %all-to-all-start.1 = ((bf16[64,256,8]{1,2,0:T(8,128)(2,1)}), bf16[64,256,8]{1,2,0:T(8,128)(2,1)S(1)}, u32[]{:S(2)}, u32[]{:S(2)}) async-start(bf16[64,256,8]{1,2,0:T(8,128)(2,1)} %copy.190), calls=%async_computation.2 | async-start | bytes 524288 | tf_op jit(solution)/shard_map/all_to_all | solution.py:96
  137.4 0.2 multiply_reduce_fusion.1
  137.5 0.6 convolution_bitcast_fusion.7
  138.2 11.6 %all-to-all-done.1 = bf16[64,256,8]{1,2,0:T(8,128)(2,1)S(1)} async-done(((bf16[64,256,8]{1,2,0:T(8,128)(2,1)}), bf16[64,256,8]{1,2,0:T(8,128)(2,1)S(1)}, u32[]{:S(2)}, u32[]{:S(2)}) %all-to-all-start.1) | async-done | bytes 262176 | tf_op jit(solution)/shard_map/all_to_all | solution.py:96
  149.9 0.3 copy.192
  150.2 3.2 %gather_fusion = bf16[1024,64]{1,0:T(8,128)(2,1)S(1)} fusion(bf16[2048,64]{1,0:T(8,128)(2,1)S(1)} %copy.192, s32[1024]{0:T(1024)S(1)} %broadcast_clamp_fusion), kind=kCustom, calls=%fused_computation | custom fusion | bytes 266240 | tf_op jit(solution)/shard_map/jit(_take)/gather | solution.py:107
  153.4 0.2 copy.193
  153.5 0.4 fusion.13
  154.0 1.0 convolution_multiply_fusion
  154.9 0.4 convolution_bitcast_fusion.1
  155.4 0.8 convolution_bitcast_fusion.3
  156.2 0.3 fusion.17
  156.4 0.4 convolution_bitcast_fusion.6
  156.9 1.1 fusion.4
  158.0 0.9 copy.204
  158.9 17.7 %all-gather.2 = bf16[32,128,64]{1,2,0:T(8,128)(2,1)S(1)} all-gather(bf16[4,128,64]{1,2,0:T(8,128)(2,1)S(1)} %fusion.17), channel_id=4, replica_groups=mesh['tz'=8,'ty'=8,'seq'=8] {'seq'}, dimensions={0}, use_global_device_ids=true | all-gather | bytes 589824 | tf_op jit(solution)/shard_map/all_gather | solution.py:149
  176.6 0.2 fusion.18
  176.8 1.1 fusion.5
  177.9 0.9 copy.203
  178.8 1.1 fusion.15
  (48 shorter events, 0.9 us)
Async XLA Ops:
  7.2 79.5 %copy-start = (bf16[256,4,1,128]{3,1,2,0:T(4,128)(2,1)S(1)}, bf16[256,4,1,128]{3,1,2,0:T(4,128)(2,1)}, u32[]{:S(2)}) copy-start(bf16[256,4,1,128]{3,1,2,0:T(4,128)(2,1)} %param.14) | copy-start | bytes 786436
  7.2 22.0 %copy-start.3 = (bf16[1,640,512]{2,1,0:T(8,128)(2,1)S(1)}, bf16[1,640,512]{2,1,0:T(8,128)(2,1)}, u32[]{:S(2)}) copy-start(bf16[1,640,512]{2,1,0:T(8,128)(2,1)} %param.11) | copy-start | bytes 1966084
  7.2 66.8 %all-gather.5.cloned.1.call-start = ((), (), s32[]{:S(2)}) async-start(), calls=%async_computation.4 | async-start | bytes 2949120 | tf_op jit(solution)/shard_map/all_gather | solution.py:82
  29.2 94.5 %reduce-scatter.2.cloned.1.call-start = ((), (), s32[]{:S(2)}) async-start(), calls=%async_computation.3 | async-start | bytes 4718592 | tf_op jit(solution)/shard_map/reduce_scatter | solution.py:90
  79.5 0.8 copy-start.4
  79.5 4.8 %copy-start.5 = (s32[256,4]{0,1:T(4,128)S(1)}, s32[256,4]{0,1:T(4,128)}, u32[]{:S(2)}) copy-start(s32[256,4]{0,1:T(4,128)} %param.17) | copy-start | bytes 12292
  79.5 7.2 %copy-start.2 = (bf16[256,4,1,64]{0,3,2,1:T(8,128)(2,1)S(1)}, bf16[256,4,1,64]{0,3,2,1:T(8,128)(2,1)}, u32[]{:S(2)}) copy-start(bf16[256,4,1,64]{0,3,2,1:T(8,128)(2,1)} %param.13) | copy-start | bytes 393220
  79.5 28.4 %copy-start.1 = (bf16[256,4,1,128]{3,1,2,0:T(4,128)(2,1)S(1)}, bf16[256,4,1,128]{3,1,2,0:T(4,128)(2,1)}, u32[]{:S(2)}) copy-start(bf16[256,4,1,128]{3,1,2,0:T(4,128)(2,1)} %param.15) | copy-start | bytes 786436
  125.6 24.1 %all-to-all-start.1 = ((bf16[64,256,8]{1,2,0:T(8,128)(2,1)}), bf16[64,256,8]{1,2,0:T(8,128)(2,1)S(1)}, u32[]{:S(2)}, u32[]{:S(2)}) async-start(bf16[64,256,8]{1,2,0:T(8,128)(2,1)} %copy.190), calls=%async_computation.2 | async-start | bytes 524288 | tf_op jit(solution)/shard_map/all_to_all | solution.py:96
Sparse Core Ops, SparseCore 0:
  29.3 44.6 all-gather.4
  79.6 43.5 reduce-scatter.1

commit v4 on v3

--- a/solution.py
+++ b/solution.py
@@ -80,33 +80,6 @@
     packed = packed.reshape(FAM, CAP, feat_width)
     by_family = lax.all_to_all(packed, "ty", split_axis=0, concat_axis=0, tiled=True)
     received = lax.all_gather(by_family, "tz")
-    slots_all = n_z * n_y * CAP
-    received = received.reshape(slots_all, feat_width)
-    weights = teacher_proj[0]
-    partial_value = jnp.dot(received, weights, preferred_element_type=jnp.float32)
-    sq_sums = jnp.sum(jnp.square(received.astype(jnp.float32)), axis=1)
-    partial_value = partial_value.reshape(n_z, n_y * CAP, heads_all, -1)
-    sq_sums = sq_sums.reshape(n_z, n_y * CAP)
-    summed = lax.psum_scatter(partial_value, "seq", scatter_dimension=0, tiled=True)[0]
-    totals = lax.psum_scatter(sq_sums, "seq", scatter_dimension=0, tiled=True)[0]
-    row_scale = lax.rsqrt(totals / TD + EPS)
-    scaled = (summed * row_scale[:, None, None]).astype(jnp.bfloat16)
-    cols = scaled.shape[-1]
-    outgoing = scaled.transpose(1, 0, 2)
-    arrived = lax.all_to_all(outgoing, TEACH, split_axis=0, concat_axis=0, tiled=True)
-    arrived = arrived.reshape(n_z, n_y, n_y * CAP, cols)
-    table = arrived.transpose(1, 2, 0, 3).reshape(n_y * n_y * CAP, n_z * cols)
-
-    shard_rows = n_y * block_rows
-    shard_fam = lax.dynamic_slice_in_dim(
-        fam_all, lax.axis_index("seq") * shard_rows, shard_rows
-    ).reshape(n_y, block_rows)
-    shard_slots = family_slots(shard_fam)
-    sources = jnp.arange(n_y, dtype=jnp.int32)[:, None]
-    row_index = ((shard_fam * n_y + sources) * CAP + shard_slots).reshape(shard_rows)
-    picked = jnp.take(table, row_index, axis=0)
-    target = picked.reshape(n_y * block_pos, batch_n, 1, P_SIZE)
-
     x_full = x_in.astype(jnp.float32)
     b_full = b_in.astype(jnp.float32)
     c_full = c_in.astype(jnp.float32)
@@ -135,6 +108,40 @@
     through_all = gathered[:, :, :, rows, 0].astype(jnp.float32) + gathered[
         :, :, :, rows + 1, 0
     ].astype(jnp.float32)
+    slots_all = n_z * n_y * CAP
+    received, gathered = lax.optimization_barrier((received, gathered))
+    received = received.reshape(slots_all, feat_width)
+    weights = teacher_proj[0]
+    partial_value = jnp.dot(received, weights, preferred_element_type=jnp.float32)
+    sq_sums = jnp.sum(jnp.square(received.astype(jnp.float32)), axis=1)
+    width = partial_value.shape[-1]
+    group = n_y * CAP
+    partial_value = partial_value.reshape(n_z, group, width)
+    sq_row = jnp.zeros((n_z, 1, width), jnp.float32).at[:, 0, :group].set(
+        sq_sums.reshape(n_z, group)
+    )
+    summed = lax.psum_scatter(
+        jnp.concatenate([partial_value, sq_row], axis=1), "seq", scatter_dimension=0, tiled=True
+    )[0]
+    row_scale = lax.rsqrt(summed[group, :group] / TD + EPS)
+    scaled = (summed[:group] * row_scale[:, None]).astype(jnp.bfloat16)
+    scaled = scaled.reshape(group, heads_all, -1)
+    cols = scaled.shape[-1]
+    outgoing = scaled.transpose(1, 0, 2)
+    arrived = lax.all_to_all(outgoing, TEACH, split_axis=0, concat_axis=0, tiled=True)
+    arrived = arrived.reshape(n_z, n_y, n_y * CAP, cols)
+    table = arrived.transpose(1, 2, 0, 3).reshape(n_y * n_y * CAP, n_z * cols)
+
+    shard_rows = n_y * block_rows
+    shard_fam = lax.dynamic_slice_in_dim(
+        fam_all, lax.axis_index("seq") * shard_rows, shard_rows
+    ).reshape(n_y, block_rows)
+    shard_slots = family_slots(shard_fam)
+    sources = jnp.arange(n_y, dtype=jnp.int32)[:, None]
+    row_index = ((shard_fam * n_y + sources) * CAP + shard_slots).reshape(shard_rows)
+    picked = jnp.take(table, row_index, axis=0)
+    target = picked.reshape(n_y * block_pos, batch_n, 1, P_SIZE)
+
     state_in = combine(chain_weights(through_all, place, False), gathered[:, :, :, :rows])
     decay_mat = decay_matrix(log_sums, counts)
     scores = jnp.einsum("ibhn,jbhn->bhij", c_in, b_in, preferred_element_type=jnp.float32)

time: 187 us -> 194 us (1.037)
  blocking collectives: 65.6 us -> 53 us
  waiting for transfers between devices: 56.1 us -> 67.3 us
  other arithmetic: 10.5 us -> 14.8 us
  local copies, waits for them, and re-layouts: 13 us -> 16.2 us
    reduce_scatter x1, waiting for transfers between devices: 0.02 us -> 36.3 us  [per_device(): lax.psum_scatter(jnp.concatenate([partial_value, sq_row], axis=1), 'seq',...]
    all_gather x1, waiting for transfers between devices: 44.5 us -> 21.5 us  [per_device(): received = lax.all_gather(by_family, 'tz')]
    unnamed x1 -> x0, blocking collectives: 12.2 us -> none
    slice x2, local copies, waits for them, and re-layouts: 0.18 us -> 3.1 us  [per_device(): scaled = (summed[:group] * row_scale[:, None]).astype(jnp.bfloat16)]
    concatenate x0 -> x1, other arithmetic: none -> 2.64 us  [per_device(): jnp.concatenate([partial_value, sq_row], axis=1)]
    all_to_all x1, waiting for transfers between devices: 11.6 us -> 9.4 us  [per_device(): lax.all_to_all(outgoing, TEACH, split_axis=0, concat_axis=0, tiled=True)]
    dot_general x1, matrix products: 5.49 us -> 3.54 us  [per_device(): jnp.dot(received, weights, preferred_element_type=jnp.float32)]
    unnamed x22 -> x28, local copies, waits for them, and re-layouts: 4.95 us -> 3.4 us
  transfers between devices with their start and end apart: 3 -> 3, of which waited for: 2 -> 3; matrix products, arithmetic and copies ran while one was open for 7% -> 7% of each run, Pallas kernels for 0% -> 0%
where the time goes in v4:
time: 194 us
  waiting for transfers between devices  67.3 us (35%)
  blocking collectives  53 us (27%)
  local copies, waits for them, and re-layouts  16.2 us (8%)
  between operations  15.7 us (8%)
  other arithmetic  14.8 us (8%)
  matrix products  14.3 us (7%)
  starting transfers between devices  12.4 us (6%)
    reduce_scatter x1, waiting for transfers between devices, per_device(): lax.psum_scatter(jnp.concatenate([partial_value, sq_row], axis=1), 'seq',...  36.3 us
    all_gather x1, waiting for transfers between devices, per_device(): received = lax.all_gather(by_family, 'tz')  21.5 us
    all_to_all x1, blocking collectives, per_device(): lax.all_to_all(packed, 'ty', split_axis=0, concat_axis=0, tiled=True)  18.1 us
    all_gather x1, blocking collectives, per_device(): adjoint_all = lax.all_gather(local_adjoint.astype(jnp.bfloat16), 'seq')  17.9 us
    all_gather x1, blocking collectives, per_device(): gathered = lax.all_gather(packed_state, 'seq')  17 us
    all_to_all x1, starting transfers between devices, per_device(): lax.all_to_all(outgoing, TEACH, split_axis=0, concat_axis=0, tiled=True)  12.3 us
    all_to_all x1, waiting for transfers between devices, per_device(): lax.all_to_all(outgoing, TEACH, split_axis=0, concat_axis=0, tiled=True)  9.4 us
  transfers between devices with their start and end apart: 3, of which 3 were waited for; matrix products, arithmetic and copies ran while one was open for 7% of the time, Pallas kernels for 0%

profile of v4, /device:TPU:1, one launch (start us, length us, event | category | flops | bytes accessed | tf_op | source)
XLA Modules:
  0.0 193.7 jit_solution(5746349697366819120)
XLA Ops:
  7.3 1.2 copy.176
  8.5 0.6 reshape.607
  9.1 0.1 dynamic_slice.6
  9.2 0.1 fusion.56
  9.3 0.2 reduce_window_sum.80
  9.5 0.2 select_reduce_fusion.1
  9.6 0.1 multiply_add_fusion
  9.7 1.0 reshape.608
  10.7 0.4 convolution_convert_fusion
  11.1 18.1 %all_to_all.10 = bf16[8,32,640]{2,1,0:T(8,128)(2,1)} all-to-all(bf16[8,32,640]{2,1,0:T(8,128)(2,1)S(1)} %bitcast.236), channel_id=1, replica_groups=mesh['tz'=8,'ty'=8,'seq'=8] {'ty'}, dimensions={0} | all-to-all | bytes 655360 | tf_op jit(solution)/shard_map/all_to_all | solution.py:81
  29.9 0.7 negate_multiply_fusion
  30.6 1.2 reduce-window.16
  31.9 0.7 reshape.595
  32.6 1.2 reduce-window.14
  33.9 0.1 copy.165
  34.0 0.1 copy.166
  34.1 0.1 copy.167
  34.2 0.1 copy.168
  34.5 0.2 slice_reduce_fusion
  34.7 0.2 slice_reduce_fusion.1
  34.9 0.1 copy_bitcast_fusion.2
  35.0 0.3 fusion.16
  35.5 17.0 %all-gather = bf16[32,1,66,128]{3,2,1,0:T(8,128)(2,1)S(1)} all-gather(bf16[4,1,66,128]{3,2,1,0:T(8,128)(2,1)S(1)} %maximum_bitcast_fusion), channel_id=2, replica_groups=mesh['tz'=8,'ty'=8,'seq'=8] {'seq'}, dimensions={0}, use_global_device_ids=true | all-gather | bytes 608256 | tf_op jit(solution)/shard_map/all_gather | solution.py:106
  52.5 21.5 %all-gather.5.cloned.1.call-done = bf16[64,32,640]{2,1,0:T(8,128)(2,1)} async-done(((bf16[8,32,640]{2,1,0:T(8,128)(2,1)}), bf16[64,32,640]{2,1,0:T(8,128)(2,1)}) %all-gather.5.cloned.1.call-update) | async-done | bytes 2621456 | tf_op jit(solution)/shard_map/all_gather | solution.py:82
  74.0 2.3 %multiply_reduce_fusion = f32[8,8,32]{2,1,0:T(8,128)S(1)} fusion(bf16[8,8,32,640]{3,2,1,0:T(8,128)(2,1)} %bitcast.227), kind=kLoop, calls=%fused_computation.1 | loop fusion | flops 3930112 | bytes 2629632 | tf_op jit(solution)/shard_map/reduce_sum | solution.py:116
  76.3 0.1 reshape.610
  76.4 3.5 %fusion.23 = f32[8,256,512]{2,1,0:T(8,128)S(1)} fusion(bf16[8,256,640]{2,1,0:T(8,128)(2,1)} %bitcast.228, bf16[1,640,512]{2,1,0:T(8,128)(2,1)S(1)} %copy-done), kind=kOutput, calls=%fused_computation.43 | convolution fusion | flops 1342177280 | bytes 7471104 | tf_op jit(solution)/shard_map/dot_general | solution.py:115
  80.0 2.6 %select_maximum_fusion = f32[8,257,512]{2,1,0:T(8,128)} fusion(f32[8,1,256]{2,1,0:T(1,128)S(1)} %reshape.610, f32[8,256,512]{2,1,0:T(8,128)S(1)} %fusion.23), kind=kLoop, calls=%fused_computation.2 | loop fusion | flops 3158016 | bytes 8413184 | tf_op jit(solution)/shard_map/concatenate | solution.py:124
  82.7 0.1 copy.178
  82.8 2.5 %select_reduce_fusion = s32[8,128]{0,1:T(8,128)S(1)} fusion(s32[8,128]{0,1:T(8,128)S(1)} %copy.178), kind=kOutput, calls=%fused_computation.47 | output fusion | flops 1096704 | bytes 8192 | tf_op jit(solution)/shard_map/jit(cumsum)/reduce_window_sum | solution.py:23
  85.4 0.1 copy.200
  85.5 0.1 copy.201
  85.7 0.2 select_reduce_fusion.2
  85.9 0.7 copy.175
  86.6 0.2 broadcast_in_dim.133
  86.7 0.7 copy.180
  88.1 0.7 copy.185
  88.9 0.5 convolution_multiply_fusion.1
  89.4 36.3 %reduce-scatter.2.cloned.1.call-done = f32[1,257,512]{2,1,0:T(8,128)} async-done(((f32[8,257,512]{2,1,0:T(8,128)}), f32[1,257,512]{2,1,0:T(8,128)}) %reduce-scatter.2.cloned.1.call-update) | async-done | bytes 526352 | tf_op jit(solution)/shard_map/reduce_scatter | solution.py:123
  125.7 1.9 slice.81
  127.5 1.2 copy.181
  128.8 0.7 fusion.61
  129.5 0.7 fusion.32
  130.2 12.3 %all-to-all-start.1 = ((bf16[64,256,8]{1,2,0:T(8,128)(2,1)}), bf16[64,256,8]{1,2,0:T(8,128)(2,1)S(1)}, u32[]{:S(2)}, u32[]{:S(2)}) async-start(bf16[64,256,8]{1,2,0:T(8,128)(2,1)} %fusion.32), calls=%async_computation.2 | async-start | bytes 524288 | tf_op jit(solution)/shard_map/all_to_all | solution.py:131
  142.6 1.3 convolution_bitcast_fusion.7
  143.9 0.7 broadcast_clamp_fusion
  144.6 0.9 multiply_reduce_fusion.1
  145.5 9.4 %all-to-all-done.1 = bf16[64,256,8]{1,2,0:T(8,128)(2,1)S(1)} async-done(((bf16[64,256,8]{1,2,0:T(8,128)(2,1)}), bf16[64,256,8]{1,2,0:T(8,128)(2,1)S(1)}, u32[]{:S(2)}, u32[]{:S(2)}) %all-to-all-start.1) | async-done | bytes 262176 | tf_op jit(solution)/shard_map/all_to_all | solution.py:131
  155.0 0.3 copy.183
  155.3 3.2 %gather_fusion = bf16[1024,64]{1,0:T(8,128)(2,1)S(1)} fusion(bf16[2048,64]{1,0:T(8,128)(2,1)S(1)} %copy.183, s32[1024]{0:T(1024)S(1)} %broadcast_clamp_fusion), kind=kCustom, calls=%fused_computation | custom fusion | bytes 266240 | tf_op jit(solution)/shard_map/jit(_take)/gather | solution.py:142
  158.5 0.2 copy.184
  158.6 1.4 fusion.13
  160.0 1.7 convolution_multiply_fusion
  161.8 0.5 convolution_bitcast_fusion.1
  162.2 0.8 convolution_bitcast_fusion.3
  163.0 0.3 fusion.17
  163.3 0.4 convolution_bitcast_fusion.6
  163.7 1.1 fusion.4
  164.8 0.9 copy.195
  165.7 17.9 %all-gather.2 = bf16[32,128,64]{1,2,0:T(8,128)(2,1)S(1)} all-gather(bf16[4,128,64]{1,2,0:T(8,128)(2,1)S(1)} %fusion.17), channel_id=4, replica_groups=mesh['tz'=8,'ty'=8,'seq'=8] {'seq'}, dimensions={0}, use_global_device_ids=true | all-gather | bytes 589824 | tf_op jit(solution)/shard_map/all_gather | solution.py:156
  183.6 0.2 fusion.18
  183.8 1.1 fusion.5
  184.9 0.9 copy.194
  185.8 1.1 fusion.15
  (55 shorter events, 1.1 us)
Async XLA Ops:
  7.2 69.3 %copy-start = (bf16[1,640,512]{2,1,0:T(8,128)(2,1)S(1)}, bf16[1,640,512]{2,1,0:T(8,128)(2,1)}, u32[]{:S(2)}) copy-start(bf16[1,640,512]{2,1,0:T(8,128)(2,1)} %param.13) | copy-start | bytes 1966084
  7.2 27.7 %copy-start.6 = (f32[256,4,1]{0,2,1:T(1,128)S(1)}, f32[256,4,1]{0,2,1:T(1,128)}, u32[]{:S(2)}) copy-start(f32[256,4,1]{0,2,1:T(1,128)} %param.18) | copy-start | bytes 12292
  7.2 27.8 %copy-start.3 = (bf16[256,4,1,128]{3,1,2,0:T(4,128)(2,1)S(1)}, bf16[256,4,1,128]{3,1,2,0:T(4,128)(2,1)}, u32[]{:S(2)}) copy-start(bf16[256,4,1,128]{3,1,2,0:T(4,128)(2,1)} %param.16) | copy-start | bytes 786436
  7.2 27.8 %copy-start.2 = (bf16[256,4,1,64]{0,3,2,1:T(8,128)(2,1)S(1)}, bf16[256,4,1,64]{0,3,2,1:T(8,128)(2,1)}, u32[]{:S(2)}) copy-start(bf16[256,4,1,64]{0,3,2,1:T(8,128)(2,1)} %param.15) | copy-start | bytes 393220
  7.2 66.8 %all-gather.5.cloned.1.call-start = ((), (), s32[]{:S(2)}) async-start(), calls=%async_computation.4 | async-start | bytes 2949120 | tf_op jit(solution)/shard_map/all_gather | solution.py:82
  9.1 77.5 %copy-start.4 = (s32[8192]{0:T(1024)}, s32[8192]{0:T(1024)S(1)}, u32[]{:S(2)}) copy-start(s32[8192]{0:T(1024)S(1)} %reshape.607) | copy-start | bytes 98308
  29.2 96.5 %reduce-scatter.2.cloned.1.call-start = ((), (), s32[]{:S(2)}) async-start(), calls=%async_computation.3 | async-start | bytes 4866048 | tf_op jit(solution)/shard_map/reduce_scatter | solution.py:123
  34.5 54.4 %copy-start.7 = (s32[1,4,2,128]{3,1,2,0:T(4,128)}, s32[1,4,2,128]{3,1,2,0:T(4,128)S(1)}, u32[]{:S(2)}) copy-start(s32[1,4,2,128]{3,1,2,0:T(4,128)S(1)} %copy.234) | copy-start | bytes 12292
  82.6 6.3 %copy-start.1 = (bf16[256,4,1,128]{3,1,2,0:T(4,128)(2,1)S(1)}, bf16[256,4,1,128]{3,1,2,0:T(4,128)(2,1)}, u32[]{:S(2)}) copy-start(bf16[256,4,1,128]{3,1,2,0:T(4,128)(2,1)} %param.17) | copy-start | bytes 786436
  88.9 36.8 %copy-start.9 = (f32[4,256]{1,0:T(4,128)}, f32[4,256]{1,0:T(4,128)S(1)}, u32[]{:S(2)}) copy-start(f32[4,256]{1,0:T(4,128)S(1)} %bitcast_add_fusion) | copy-start | bytes 12292
  130.2 24.6 %all-to-all-start.1 = ((bf16[64,256,8]{1,2,0:T(8,128)(2,1)}), bf16[64,256,8]{1,2,0:T(8,128)(2,1)S(1)}, u32[]{:S(2)}, u32[]{:S(2)}) async-start(bf16[64,256,8]{1,2,0:T(8,128)(2,1)} %fusion.32), calls=%async_computation.2 | async-start | bytes 524288 | tf_op jit(solution)/shard_map/all_to_all | solution.py:131
  144.6 14.0 %copy-start.8 = (pred[256,4]{0,1:T(4,128)(4,1)S(1)}, pred[256,4]{0,1:T(4,128)(4,1)}, u32[]{:S(2)}) copy-start(pred[256,4]{0,1:T(4,128)(4,1)} %copy.180) | copy-start | bytes 3076
  161.8 21.9 %copy-start.5 = (f32[8,4]{1,0:T(8,128)S(1)}, f32[8,4]{1,0:T(8,128)}, u32[]{:S(2)}) copy-start(f32[8,4]{1,0:T(8,128)} %copy.185) | copy-start | bytes 388
Sparse Core Ops, SparseCore 0:
  29.3 44.6 all-gather.4
  82.8 42.8 reduce-scatter.1

commit v5 on v4

--- a/solution.py
+++ b/solution.py
@@ -117,13 +117,16 @@
     width = partial_value.shape[-1]
     group = n_y * CAP
     partial_value = partial_value.reshape(n_z, group, width)
-    sq_row = jnp.zeros((n_z, 1, width), jnp.float32).at[:, 0, :group].set(
-        sq_sums.reshape(n_z, group)
-    )
-    summed = lax.psum_scatter(
-        jnp.concatenate([partial_value, sq_row], axis=1), "seq", scatter_dimension=0, tiled=True
-    )[0]
-    row_scale = lax.rsqrt(summed[group, :group] / TD + EPS)
+    sq_all = sq_sums.reshape(n_z, group)
+    sq_hi = sq_all.astype(jnp.bfloat16)
+    sq_lo = (sq_all - sq_hi.astype(jnp.float32)).astype(jnp.bfloat16)
+    sq_row = jnp.zeros((n_z, 1, width), jnp.bfloat16)
+    sq_row = sq_row.at[:, 0, :group].set(sq_hi).at[:, 0, group : 2 * group].set(sq_lo)
+    outbound = jnp.concatenate([partial_value.astype(jnp.bfloat16), sq_row], axis=1)
+    inbound = lax.all_to_all(outbound, "seq", split_axis=0, concat_axis=0, tiled=True)
+    summed = jnp.sum(inbound.astype(jnp.float32), axis=0)
+    sq_total = summed[group, :group] + summed[group, group : 2 * group]
+    row_scale = lax.rsqrt(sq_total / TD + EPS)
     scaled = (summed[:group] * row_scale[:, None]).astype(jnp.bfloat16)
     scaled = scaled.reshape(group, heads_all, -1)
     cols = scaled.shape[-1]

time: 194 us -> 180 us (0.928)
  waiting for transfers between devices: 67.3 us -> 40.1 us
  starting transfers between devices: 12.4 us -> 18.3 us
  other arithmetic: 14.8 us -> 20.2 us
  local copies, waits for them, and re-layouts: 16.2 us -> 19.6 us
    reduce_scatter x1 -> x0, waiting for transfers between devices: 36.3 us -> none  [per_device(): lax.psum_scatter(jnp.concatenate([partial_value, sq_row], axis=1), 'seq',...]
    all_to_all x0 -> x1, waiting for transfers between devices: none -> 14.1 us  [per_device(): lax.all_to_all(outbound, 'seq', split_axis=0, concat_axis=0, tiled=True)]
    all_to_all x0 -> x1, starting transfers between devices: none -> 8.19 us  [per_device(): lax.all_to_all(outbound, 'seq', split_axis=0, concat_axis=0, tiled=True)]
    all_gather x1, waiting for transfers between devices: 21.5 us -> 16.2 us  [per_device(): received = lax.all_gather(by_family, 'tz')]
    unnamed x28 -> x53, local copies, waits for them, and re-layouts: 3.4 us -> 6.96 us
    slice x2 -> x0, local copies, waits for them, and re-layouts: 3.1 us -> none  [per_device(): scaled = (summed[:group] * row_scale[:, None]).astype(jnp.bfloat16)]
    all_to_all x1, starting transfers between devices: 12.3 us -> 10.1 us  [per_device(): lax.all_to_all(outgoing, TEACH, split_axis=0, concat_axis=0, tiled=True)]
    another operation x5 -> x8, other arithmetic: 2.5 us -> 4.67 us
  transfers between devices with their start and end apart: 3 -> 3, of which waited for: 3 -> 3; matrix products, arithmetic and copies ran while one was open for 7% -> 14% of each run, Pallas kernels for 0% -> 0%
where the time goes in v5:
time: 180 us
  blocking collectives  51.2 us (28%)
  waiting for transfers between devices  40.1 us (22%)
  other arithmetic  20.2 us (11%)
  local copies, waits for them, and re-layouts  19.6 us (11%)
  starting transfers between devices  18.3 us (10%)
  between operations  15.8 us (9%)
  matrix products  14.4 us (8%)
    all_to_all x1, blocking collectives, per_device(): lax.all_to_all(packed, 'ty', split_axis=0, concat_axis=0, tiled=True)  18.1 us
    all_gather x1, blocking collectives, per_device(): gathered = lax.all_gather(packed_state, 'seq')  17 us
    all_gather x1, waiting for transfers between devices, per_device(): received = lax.all_gather(by_family, 'tz')  16.2 us
    all_gather x1, blocking collectives, per_device(): adjoint_all = lax.all_gather(local_adjoint.astype(jnp.bfloat16), 'seq')  16.1 us
    all_to_all x1, waiting for transfers between devices, per_device(): lax.all_to_all(outbound, 'seq', split_axis=0, concat_axis=0, tiled=True)  14.1 us
    all_to_all x1, starting transfers between devices, per_device(): lax.all_to_all(outgoing, TEACH, split_axis=0, concat_axis=0, tiled=True)  10.1 us
    all_to_all x1, waiting for transfers between devices, per_device(): lax.all_to_all(outgoing, TEACH, split_axis=0, concat_axis=0, tiled=True)  9.76 us
    all_to_all x1, starting transfers between devices, per_device(): lax.all_to_all(outbound, 'seq', split_axis=0, concat_axis=0, tiled=True)  8.19 us
  transfers between devices with their start and end apart: 3, of which 3 were waited for; matrix products, arithmetic and copies ran while one was open for 14% of the time, Pallas kernels for 0%

profile of v5, /device:TPU:1, one launch (start us, length us, event | category | flops | bytes accessed | tf_op | source)
XLA Modules:
  0.0 179.6 jit_solution(8377318958917601374)
XLA Ops:
  7.3 1.2 copy.169
  8.5 0.6 reshape.662
  9.3 0.2 reduce_window_sum.80
  9.5 0.2 select_reduce_fusion.1
  9.8 1.0 reshape.663
  10.7 0.4 convolution_convert_fusion.1
  11.1 18.1 %all_to_all.15 = bf16[8,32,640]{2,1,0:T(8,128)(2,1)} all-to-all(bf16[8,32,640]{2,1,0:T(8,128)(2,1)S(1)} %bitcast.227), channel_id=1, replica_groups=mesh['tz'=8,'ty'=8,'seq'=8] {'ty'}, dimensions={0} | all-to-all | bytes 655360 | tf_op jit(solution)/shard_map/all_to_all | solution.py:81
  29.9 1.2 reduce-window.16
  31.3 1.2 reduce-window.14
  33.2 0.7 slice.97
  34.0 0.6 iota_compare_fusion.8
  34.6 0.2 slice_reduce_fusion
  34.8 0.2 slice_reduce_fusion.1
  34.9 0.7 and_reduce_fusion
  35.8 0.3 fusion.16
  36.2 0.6 fusion.56
  36.8 17.0 %all-gather = bf16[32,1,66,128]{3,2,1,0:T(8,128)(2,1)S(1)} all-gather(bf16[4,1,66,128]{3,2,1,0:T(8,128)(2,1)S(1)} %maximum_bitcast_fusion), channel_id=2, replica_groups=mesh['tz'=8,'ty'=8,'seq'=8] {'seq'}, dimensions={0}, use_global_device_ids=true | all-gather | bytes 608256 | tf_op jit(solution)/shard_map/all_gather | solution.py:106
  53.8 0.8 copy-done.4
  54.7 0.6 fusion.61
  55.3 2.5 %select_reduce_fusion = s32[8,128]{0,1:T(8,128)S(1)} fusion(s32[8,128]{0,1:T(8,128)S(1)} %copy.171), kind=kOutput, calls=%fused_computation.47 | output fusion | flops 1096704 | bytes 8192 | tf_op jit(solution)/shard_map/jit(cumsum)/reduce_window_sum | solution.py:23
  57.8 16.2 %all-gather.5.cloned.1.call-done = bf16[64,32,640]{2,1,0:T(8,128)(2,1)} async-done(((bf16[8,32,640]{2,1,0:T(8,128)(2,1)}), bf16[64,32,640]{2,1,0:T(8,128)(2,1)}) %all-gather.5.cloned.1.call-update) | async-done | bytes 2621456 | tf_op jit(solution)/shard_map/all_gather | solution.py:82
  74.1 2.5 %multiply_reduce_fusion = f32[8,8,32]{2,1,0:T(8,128)S(1)} fusion(bf16[8,8,32,640]{3,2,1,0:T(8,128)(2,1)} %bitcast.218), kind=kLoop, calls=%fused_computation.1 | loop fusion | flops 3930112 | bytes 2629632 | tf_op jit(solution)/shard_map/reduce_sum | solution.py:116
  76.7 3.1 %convolution_convert_fusion = bf16[8,256,512]{2,1,0:T(8,128)(2,1)} fusion(bf16[8,256,640]{2,1,0:T(8,128)(2,1)S(1)} %bitcast.219, bf16[1,640,512]{2,1,0:T(8,128)(2,1)S(1)} %copy-done), kind=kOutput, calls=%fused_computation.4 | convolution fusion | flops 1343225856 | bytes 5373952 | tf_op jit(solution)/shard_map/dot_general | solution.py:115
  79.8 1.4 broadcast_select_fusion
  81.2 0.9 scatter.9
  82.2 3.2 %pad_maximum_fusion = bf16[8,257,512]{2,1,0:T(8,128)(2,1)} fusion(bf16[8,1,512]{2,1,0:T(2,128)(2,1)S(1)} %scatter.9, bf16[8,256,512]{2,1,0:T(8,128)(2,1)} %convolution_convert_fusion), kind=kLoop, calls=%fused_computation.3 | loop fusion | flops 4210688 | bytes 4210688 | tf_op jit(solution)/shard_map/concatenate | solution.py:125
  85.3 8.2 %all-to-all-start.1 = ((bf16[8,257,512]{2,1,0:T(8,128)(2,1)}), bf16[8,257,512]{2,1,0:T(8,128)(2,1)S(1)}, u32[]{:S(2)}, u32[]{:S(2)}) async-start(bf16[8,257,512]{2,1,0:T(8,128)(2,1)} %pad_maximum_fusion), calls=%async_computation.1 | async-start | bytes 4325376 | tf_op jit(solution)/shard_map/all_to_all | solution.py:126
  93.5 1.2 fusion.57
  94.7 0.7 copy.172
  95.4 0.8 copy.192
  96.2 0.8 copy.193
  97.1 0.9 select_reduce_fusion.2
  98.0 0.6 broadcast_select_fusion.2
  98.5 0.7 copy.168
  99.2 0.7 compare_and_fusion.1
  100.1 0.7 copy.173
  101.4 0.7 broadcast_select_fusion.1
  102.1 0.7 copy.177
  102.8 0.8 broadcast_bitcast_fusion
  103.5 0.6 copy-done.18
  104.1 2.2 %convolution_multiply_fusion.1 = f32[4,256,256]{2,1,0:T(8,128)} fusion(f32[4,256]{1,0:T(4,128)S(1)} %bitcast_add_fusion, s32[4,256]{1,0:T(4,128)} %bitcast.236, pred[256,256]{1,0:T(8,128)(4,1)S(1)} %iota_compare_fusion.2, bf16[256,4,128]{2,1,0:T(4,128)(2,1)S(1)} %bitcast.231, bf16[256,4,128]{2,1,0:T(4,128)(2,1)S(1)} %bitcast.220), kind=kOutput, calls=%fused_computation.6 | convolution fusion | flops 68681728 | bytes 1646592 | tf_op jit(solution)/shard_map/ibhn,jbhn->bhij/dot_general | solution.py:150
  106.3 14.1 %all-to-all-done.1 = bf16[8,257,512]{2,1,0:T(8,128)(2,1)S(1)} async-done(((bf16[8,257,512]{2,1,0:T(8,128)(2,1)}), bf16[8,257,512]{2,1,0:T(8,128)(2,1)S(1)}, u32[]{:S(2)}, u32[]{:S(2)}) %all-to-all-start.1) | async-done | bytes 2105376 | tf_op jit(solution)/shard_map/all_to_all | solution.py:126
  120.4 0.3 convert_reduce_fusion
  120.9 0.8 copy.174
  121.7 10.1 %all-to-all-start.2 = ((bf16[64,256,8]{1,2,0:T(8,128)(2,1)}), bf16[64,256,8]{1,2,0:T(8,128)(2,1)S(1)}, u32[]{:S(2)}, u32[]{:S(2)}) async-start(bf16[64,256,8]{1,2,0:T(8,128)(2,1)} %bitcast.37), calls=%async_computation.2 | async-start | bytes 524288 | tf_op jit(solution)/shard_map/all_to_all | solution.py:134
  131.8 1.8 %convolution_bitcast_fusion.7 = f32[256,4,1,64]{0,3,1,2:T(8,128)S(1)} fusion(f32[4,256,256]{2,1,0:T(8,128)} %convolution_multiply_fusion.1, bf16[256,4,1,64]{0,3,2,1:T(8,128)(2,1)S(1)} %copy-done.6, f32[256,4]{0,1:T(4,128)S(1)} %get-tuple-element.59), kind=kOutput, calls=%fused_computation.27 | convolution fusion | flops 100794368 | bytes 1445888 | tf_op jit(solution)/shard_map/bhij,jbhp->ibhp/dot_general | solution.py:152
  133.7 0.7 broadcast_clamp_fusion
  134.4 0.2 multiply_reduce_fusion.1
  134.6 9.8 %all-to-all-done.2 = bf16[64,256,8]{1,2,0:T(8,128)(2,1)S(1)} async-done(((bf16[64,256,8]{1,2,0:T(8,128)(2,1)}), bf16[64,256,8]{1,2,0:T(8,128)(2,1)S(1)}, u32[]{:S(2)}, u32[]{:S(2)}) %all-to-all-start.2) | async-done | bytes 262176 | tf_op jit(solution)/shard_map/all_to_all | solution.py:134
  144.3 0.3 copy.175
  144.6 3.2 %gather_fusion = bf16[1024,64]{1,0:T(8,128)(2,1)S(1)} fusion(bf16[2048,64]{1,0:T(8,128)(2,1)S(1)} %copy.175, s32[1024]{0:T(1024)S(1)} %broadcast_clamp_fusion), kind=kCustom, calls=%fused_computation | custom fusion | bytes 266240 | tf_op jit(solution)/shard_map/jit(_take)/gather | solution.py:145
  148.0 0.4 fusion.13
  148.4 1.0 convolution_multiply_fusion
  149.4 0.5 convolution_bitcast_fusion.1
  149.9 0.8 convolution_bitcast_fusion.3
  150.7 0.3 fusion.17
  151.0 0.4 convolution_bitcast_fusion.6
  151.4 1.1 fusion.4
  152.5 0.9 copy.187
  153.4 16.1 %all-gather.2 = bf16[32,128,64]{1,2,0:T(8,128)(2,1)S(1)} all-gather(bf16[4,128,64]{1,2,0:T(8,128)(2,1)S(1)} %fusion.17), channel_id=4, replica_groups=mesh['tz'=8,'ty'=8,'seq'=8] {'seq'}, dimensions={0}, use_global_device_ids=true | all-gather | bytes 589824 | tf_op jit(solution)/shard_map/all_gather | solution.py:159
  169.5 0.2 fusion.18
  169.7 1.1 fusion.5
  170.8 0.9 copy.186
  171.7 1.1 fusion.15
  (85 shorter events, 2.2 us)
Async XLA Ops:
  7.2 69.5 %copy-start = (bf16[1,640,512]{2,1,0:T(8,128)(2,1)S(1)}, bf16[1,640,512]{2,1,0:T(8,128)(2,1)}, u32[]{:S(2)}) copy-start(bf16[1,640,512]{2,1,0:T(8,128)(2,1)} %param.15) | copy-start | bytes 1966084
  7.2 27.8 %copy-start.22 = (s32[3]{0:T(128)S(1)}, s32[3]{0:T(128)}, u32[]{:S(2)}) copy-start(s32[3]{0:T(128)} %constant.121.clone.1) | copy-start | bytes 40
  7.2 22.7 %copy-start.14 = (f32[256,4,1]{0,2,1:T(1,128)S(1)}, f32[256,4,1]{0,2,1:T(1,128)}, u32[]{:S(2)}) copy-start(f32[256,4,1]{0,2,1:T(1,128)} %param.20) | copy-start | bytes 12292
  7.2 24.0 %copy-start.20 = (s32[256,4]{0,1:T(4,128)S(1)}, s32[256,4]{0,1:T(4,128)}, u32[]{:S(2)}) copy-start(s32[256,4]{0,1:T(4,128)} %param.21) | copy-start | bytes 12292
  7.2 28.5 %copy-start.7 = (bf16[256,4,1,128]{3,1,2,0:T(4,128)(2,1)S(1)}, bf16[256,4,1,128]{3,1,2,0:T(4,128)(2,1)}, u32[]{:S(2)}) copy-start(bf16[256,4,1,128]{3,1,2,0:T(4,128)(2,1)} %param.18) | copy-start | bytes 786436
  7.2 28.5 %copy-start.6 = (bf16[256,4,1,64]{0,3,2,1:T(8,128)(2,1)S(1)}, bf16[256,4,1,64]{0,3,2,1:T(8,128)(2,1)}, u32[]{:S(2)}) copy-start(bf16[256,4,1,64]{0,3,2,1:T(8,128)(2,1)} %param.17) | copy-start | bytes 393220
  7.2 66.9 %all-gather.5.cloned.1.call-start = ((), (), s32[]{:S(2)}) async-start(), calls=%async_computation.3 | async-start | bytes 2949120 | tf_op jit(solution)/shard_map/all_gather | solution.py:82
  9.2 48.7 %copy-start.9 = (s32[8192]{0:T(1024)}, s32[8192]{0:T(1024)S(1)}, u32[]{:S(2)}) copy-start(s32[8192]{0:T(1024)S(1)} %reshape.662) | copy-start | bytes 98308
  33.0 0.8 copy-start.11
  33.2 24.6 %copy-start.15 = (s32[1,4,2,128]{3,1,2,0:T(4,128)}, s32[1,4,2,128]{3,1,2,0:T(4,128)S(1)}, u32[]{:S(2)}) copy-start(s32[1,4,2,128]{3,1,2,0:T(4,128)S(1)} %copy.223) | copy-start | bytes 12292
  34.6 1.7 copy-start.21
  53.8 0.8 copy-start.4
  74.1 2.6 %copy-start.2 = (bf16[64,32,640]{2,1,0:T(8,128)(2,1)S(1)}, bf16[64,32,640]{2,1,0:T(8,128)(2,1)}, u32[]{:S(2)}) copy-start(bf16[64,32,640]{2,1,0:T(8,128)(2,1)} %all-gather.5.cloned.1.call-done) | copy-start | bytes 7864324
  85.3 18.8 %copy-start.3 = (bf16[256,4,1,128]{3,1,2,0:T(4,128)(2,1)S(1)}, bf16[256,4,1,128]{3,1,2,0:T(4,128)(2,1)}, u32[]{:S(2)}) copy-start(bf16[256,4,1,128]{3,1,2,0:T(4,128)(2,1)} %param.19) | copy-start | bytes 786436
  85.3 18.8 %copy-start.8 = (bf16[256,4,1,128]{3,1,2,0:T(4,128)(2,1)S(1)}, bf16[256,4,1,128]{3,1,2,0:T(4,128)(2,1)}, u32[]{:S(2)}) copy-start(bf16[256,4,1,128]{3,1,2,0:T(4,128)(2,1)} %param.18) | copy-start | bytes 786436
  85.3 35.1 %all-to-all-start.1 = ((bf16[8,257,512]{2,1,0:T(8,128)(2,1)}), bf16[8,257,512]{2,1,0:T(8,128)(2,1)S(1)}, u32[]{:S(2)}, u32[]{:S(2)}) async-start(bf16[8,257,512]{2,1,0:T(8,128)(2,1)} %pad_maximum_fusion), calls=%async_computation.1 | async-start | bytes 4325376 | tf_op jit(solution)/shard_map/all_to_all | solution.py:126
  103.5 0.6 copy-start.18
  106.3 27.3 %copy-start.10 = (s32[8,128]{1,0:T(8,128)S(1)}, s32[8,128]{1,0:T(8,128)}, u32[]{:S(2)}) copy-start(s32[8,128]{1,0:T(8,128)} %copy.172) | copy-start | bytes 12292
  120.7 13.6 %copy-start.5 = (bf16[32,1,66,128]{3,2,1,0:T(8,128)(2,1)S(1)}, bf16[32,1,66,128]{3,2,1,0:T(8,128)(2,1)}, u32[]{:S(2)}) copy-start(bf16[32,1,66,128]{3,2,1,0:T(8,128)(2,1)} %copy-done.4) | copy-start | bytes 1622020
  120.7 13.6 %copy-start.13 = (f32[8,4]{1,0:T(8,128)S(1)}, f32[8,4]{1,0:T(8,128)}, u32[]{:S(2)}) copy-start(f32[8,4]{1,0:T(8,128)} %copy.168) | copy-start | bytes 388
  121.7 22.6 %all-to-all-start.2 = ((bf16[64,256,8]{1,2,0:T(8,128)(2,1)}), bf16[64,256,8]{1,2,0:T(8,128)(2,1)S(1)}, u32[]{:S(2)}, u32[]{:S(2)}) async-start(bf16[64,256,8]{1,2,0:T(8,128)(2,1)} %bitcast.37), calls=%async_computation.2 | async-start | bytes 524288 | tf_op jit(solution)/shard_map/all_to_all | solution.py:134
  131.8 16.2 %copy-start.17 = (pred[256,4]{0,1:T(4,128)(4,1)S(1)}, pred[256,4]{0,1:T(4,128)(4,1)}, u32[]{:S(2)}) copy-start(pred[256,4]{0,1:T(4,128)(4,1)} %copy.173) | copy-start | bytes 3076
  134.4 14.0 %copy-start.16 = (s32[1,4,2,128]{3,1,2,0:T(4,128)S(1)}, s32[1,4,2,128]{3,1,2,0:T(4,128)}, u32[]{:S(2)}) copy-start(s32[1,4,2,128]{3,1,2,0:T(4,128)} %copy-done.15) | copy-start | bytes 12292
  134.4 14.0 %copy-start.19 = (f32[4,256]{1,0:T(4,128)S(1)}, f32[4,256]{1,0:T(4,128)}, u32[]{:S(2)}) copy-start(f32[4,256]{1,0:T(4,128)} %copy-done.18) | copy-start | bytes 12292
  149.4 1.5 copy-start.1
  150.7 18.8 %copy-start.12 = (f32[8,4]{1,0:T(8,128)S(1)}, f32[8,4]{1,0:T(8,128)}, u32[]{:S(2)}) copy-start(f32[8,4]{1,0:T(8,128)} %copy.177) | copy-start | bytes 388
Sparse Core Ops, SparseCore 0:
  29.4 44.6 all-gather.4

commit v6 on v5

--- a/solution.py
+++ b/solution.py
@@ -120,8 +120,7 @@
     sq_all = sq_sums.reshape(n_z, group)
     sq_hi = sq_all.astype(jnp.bfloat16)
     sq_lo = (sq_all - sq_hi.astype(jnp.float32)).astype(jnp.bfloat16)
-    sq_row = jnp.zeros((n_z, 1, width), jnp.bfloat16)
-    sq_row = sq_row.at[:, 0, :group].set(sq_hi).at[:, 0, group : 2 * group].set(sq_lo)
+    sq_row = jnp.concatenate([sq_hi, sq_lo], axis=1)[:, None, :]
     outbound = jnp.concatenate([partial_value.astype(jnp.bfloat16), sq_row], axis=1)
     inbound = lax.all_to_all(outbound, "seq", split_axis=0, concat_axis=0, tiled=True)
     summed = jnp.sum(inbound.astype(jnp.float32), axis=0)
@@ -156,7 +155,13 @@
     output = output + skip_gain[None, None, :, None] * x_full
     residual = output - target.astype(jnp.float32)
     local_adjoint = jnp.einsum("ibh,ibhn,ibhp->bhnp", from_start, c_full, residual, precision=HIGH)
-    adjoint_all = lax.all_gather(local_adjoint.astype(jnp.bfloat16), "seq")
+    adjoint_all = lax.all_to_all(
+        jnp.broadcast_to(local_adjoint.astype(jnp.bfloat16)[None], (seq_n,) + local_adjoint.shape),
+        "seq",
+        split_axis=0,
+        concat_axis=0,
+        tiled=True,
+    )
     adjoint_in = combine(chain_weights(through_all, place, True), adjoint_all)
     grad_u = jnp.einsum("bhij,ibhp->jbhp", mixing, residual, precision=QUADRATIC)
     grad_u = grad_u + to_end[..., None] * jnp.einsum(

time: 180 us -> 177 us (0.983)
  blocking collectives: 51.2 us -> 35.1 us
  starting transfers between devices: 18.3 us -> 25.5 us
  waiting for transfers between devices: 40.1 us -> 46.2 us
  matrix products: 14.4 us -> 17.7 us
  other arithmetic: 20.2 us -> 17.3 us
    all_gather x1 -> x0, blocking collectives: 16.1 us -> none  [per_device(): adjoint_all = lax.all_gather(local_adjoint.astype(jnp.bfloat16), 'seq')]
    all_to_all x0 -> x1, starting transfers between devices: none -> 7.2 us  [per_device(): lax.all_to_all(jnp.broadcast_to(local_adjoint.astype(jnp.bfloat16)[None],...]
    all_to_all x0 -> x1, waiting for transfers between devices: none -> 4.49 us  [per_device(): lax.all_to_all(jnp.broadcast_to(local_adjoint.astype(jnp.bfloat16)[None],...]
    another operation x8 -> x5, other arithmetic: 4.67 us -> 2.53 us
    dot_general x1, matrix products: 0.45 us -> 2.31 us  [per_device(): grad_c = jnp.einsum('bhij,jbhn->ibhn', pair, b_full, precision=QUADRATIC)]
    unnamed x53 -> x57, local copies, waits for them, and re-layouts: 6.96 us -> 6.88 us
  transfers between devices with their start and end apart: 3 -> 4, of which waited for: 3 -> 4; matrix products, arithmetic and copies ran while one was open for 14% -> 16% of each run, Pallas kernels for 0% -> 0%
where the time goes in v6:
time: 177 us; the launch traced here: 176 us
  waiting for transfers between devices  46.2 us (26%)
  blocking collectives  35.1 us (20%)
  starting transfers between devices  25.5 us (14%)
  local copies, waits for them, and re-layouts  18.8 us (11%)
  matrix products  17.7 us (10%)
  other arithmetic  17.3 us (10%)
  between operations  15.8 us (9%)
    all_to_all x1, blocking collectives, per_device(): lax.all_to_all(packed, 'ty', split_axis=0, concat_axis=0, tiled=True)  18.1 us
    all_gather x1, waiting for transfers between devices, per_device(): received = lax.all_gather(by_family, 'tz')  17.7 us
    all_gather x1, blocking collectives, per_device(): gathered = lax.all_gather(packed_state, 'seq')  17 us
    all_to_all x1, waiting for transfers between devices, per_device(): lax.all_to_all(outbound, 'seq', split_axis=0, concat_axis=0, tiled=True)  14.2 us
    all_to_all x1, starting transfers between devices, per_device(): lax.all_to_all(outgoing, TEACH, split_axis=0, concat_axis=0, tiled=True)  10.1 us
    all_to_all x1, waiting for transfers between devices, per_device(): lax.all_to_all(outgoing, TEACH, split_axis=0, concat_axis=0, tiled=True)  9.74 us
    all_to_all x1, starting transfers between devices, per_device(): lax.all_to_all(outbound, 'seq', split_axis=0, concat_axis=0, tiled=True)  8.19 us
    all_to_all x1, starting transfers between devices, per_device(): lax.all_to_all(jnp.broadcast_to(local_adjoint.astype(jnp.bfloat16)[None],...  7.2 us
  transfers between devices with their start and end apart: 4, of which 4 were waited for; matrix products, arithmetic and copies ran while one was open for 16% of the time, Pallas kernels for 0%

profile of v6, /device:TPU:1, one launch (start us, length us, event | category | flops | bytes accessed | tf_op | source)
XLA Modules:
  0.0 176.4 jit_solution(9183473259507592521)
XLA Ops:
  7.3 1.2 copy.176
  8.5 0.6 reshape.573
  9.3 0.2 reduce_window_sum.80
  9.5 0.2 select_reduce_fusion.1
  9.7 1.0 reshape.574
  10.7 0.4 convolution_convert_fusion.1
  11.1 18.1 %all_to_all.20 = bf16[8,32,640]{2,1,0:T(8,128)(2,1)} all-to-all(bf16[8,32,640]{2,1,0:T(8,128)(2,1)S(1)} %bitcast.225), channel_id=1, replica_groups=mesh['tz'=8,'ty'=8,'seq'=8] {'ty'}, dimensions={0} | all-to-all | bytes 655360 | tf_op jit(solution)/shard_map/all_to_all | solution.py:81
  29.9 1.2 reduce-window.16
  31.2 1.2 reduce-window.14
  33.2 0.5 iota_compare_fusion.8
  33.8 0.2 slice_reduce_fusion
  34.0 0.2 slice_reduce_fusion.1
  34.3 0.3 fusion.16
  34.7 0.5 fusion.55
  35.3 17.0 %all-gather = bf16[32,1,66,128]{3,2,1,0:T(8,128)(2,1)S(1)} all-gather(bf16[4,1,66,128]{3,2,1,0:T(8,128)(2,1)S(1)} %maximum_bitcast_fusion), channel_id=2, replica_groups=mesh['tz'=8,'ty'=8,'seq'=8] {'seq'}, dimensions={0}, use_global_device_ids=true | all-gather | bytes 608256 | tf_op jit(solution)/shard_map/all_gather | solution.py:106
  52.3 0.8 copy-done.4
  53.1 0.6 fusion.60
  53.8 2.5 %select_reduce_fusion = s32[8,128]{0,1:T(8,128)S(1)} fusion(s32[8,128]{0,1:T(8,128)S(1)} %copy.178), kind=kOutput, calls=%fused_computation.46 | output fusion | flops 1096704 | bytes 8192 | tf_op jit(solution)/shard_map/jit(cumsum)/reduce_window_sum | solution.py:23
  56.3 17.7 %all-gather.4.cloned.1.call-done = bf16[64,32,640]{2,1,0:T(8,128)(2,1)} async-done(((bf16[8,32,640]{2,1,0:T(8,128)(2,1)}), bf16[64,32,640]{2,1,0:T(8,128)(2,1)}) %all-gather.4.cloned.1.call-update) | async-done | bytes 2621456 | tf_op jit(solution)/shard_map/all_gather | solution.py:82
  74.1 2.5 %multiply_reduce_fusion = f32[8,8,32]{2,1,0:T(8,128)S(1)} fusion(bf16[8,8,32,640]{3,2,1,0:T(8,128)(2,1)} %bitcast.217), kind=kLoop, calls=%fused_computation.1 | loop fusion | flops 3930112 | bytes 2629632 | tf_op jit(solution)/shard_map/reduce_sum | solution.py:116
  76.6 1.8 %convolution_convert_fusion = bf16[8,256,512]{2,1,0:T(8,128)(2,1)S(1)} fusion(bf16[8,256,640]{2,1,0:T(8,128)(2,1)S(1)} %bitcast.218, bf16[1,640,512]{2,1,0:T(8,128)(2,1)S(1)} %copy-done), kind=kOutput, calls=%fused_computation.4 | convolution fusion | flops 1343225856 | bytes 5373952 | tf_op jit(solution)/shard_map/dot_general | solution.py:115
  78.4 1.5 pad_maximum_fusion
  80.0 8.2 %all-to-all-start.1 = ((bf16[8,257,512]{2,1,0:T(8,128)(2,1)}), bf16[8,257,512]{2,1,0:T(8,128)(2,1)S(1)}, u32[]{:S(2)}, u32[]{:S(2)}) async-start(bf16[8,257,512]{2,1,0:T(8,128)(2,1)} %pad_maximum_fusion), calls=%async_computation.1 | async-start | bytes 4325376 | tf_op jit(solution)/shard_map/all_to_all | solution.py:125
  88.2 1.2 fusion.56
  89.3 0.7 copy.179
  90.0 0.8 copy.200
  90.8 0.8 copy.201
  91.6 0.8 select_reduce_fusion.2
  92.5 0.6 broadcast_select_fusion.1
  93.1 0.7 copy.175
  93.8 0.7 compare_and_fusion.1
  94.5 0.2 broadcast_in_dim.141
  94.7 0.6 copy.180
  95.9 0.6 broadcast_select_fusion
  96.6 0.7 copy.185
  97.3 0.7 broadcast_bitcast_fusion
  98.0 0.6 copy-done.21
  98.6 2.2 %convolution_multiply_fusion.1 = f32[4,256,256]{2,1,0:T(8,128)} fusion(f32[4,256]{1,0:T(4,128)S(1)} %bitcast_add_fusion, s32[4,256]{1,0:T(4,128)} %bitcast.234, pred[256,256]{1,0:T(8,128)(4,1)S(1)} %iota_compare_fusion.2, bf16[256,4,128]{2,1,0:T(4,128)(2,1)S(1)} %bitcast.230, bf16[256,4,128]{2,1,0:T(4,128)(2,1)S(1)} %bitcast.219), kind=kOutput, calls=%fused_computation.6 | convolution fusion | flops 68681728 | bytes 1646592 | tf_op jit(solution)/shard_map/ibhn,jbhn->bhij/dot_general | solution.py:149
  100.8 14.2 %all-to-all-done.1 = bf16[8,257,512]{2,1,0:T(8,128)(2,1)S(1)} async-done(((bf16[8,257,512]{2,1,0:T(8,128)(2,1)}), bf16[8,257,512]{2,1,0:T(8,128)(2,1)S(1)}, u32[]{:S(2)}, u32[]{:S(2)}) %all-to-all-start.1) | async-done | bytes 2105376 | tf_op jit(solution)/shard_map/all_to_all | solution.py:125
  115.1 0.3 convert_reduce_fusion
  115.5 0.8 copy.182
  116.4 10.1 %all-to-all-start.2 = ((bf16[64,256,8]{1,2,0:T(8,128)(2,1)}), bf16[64,256,8]{1,2,0:T(8,128)(2,1)S(1)}, u32[]{:S(2)}, u32[]{:S(2)}) async-start(bf16[64,256,8]{1,2,0:T(8,128)(2,1)} %bitcast.37), calls=%async_computation.2 | async-start | bytes 524288 | tf_op jit(solution)/shard_map/all_to_all | solution.py:133
  126.5 1.8 %convolution_bitcast_fusion.7 = f32[256,4,1,64]{0,3,1,2:T(8,128)S(1)} fusion(f32[4,256,256]{2,1,0:T(8,128)} %convolution_multiply_fusion.1, bf16[256,4,1,64]{0,3,2,1:T(8,128)(2,1)S(1)} %copy-done.6, f32[256,4]{0,1:T(4,128)S(1)} %get-tuple-element.37), kind=kOutput, calls=%fused_computation.27 | convolution fusion | flops 100794368 | bytes 1445888 | tf_op jit(solution)/shard_map/bhij,jbhp->ibhp/dot_general | solution.py:151
  128.3 0.7 broadcast_clamp_fusion
  129.1 0.2 multiply_reduce_fusion.2
  129.2 9.7 %all-to-all-done.2 = bf16[64,256,8]{1,2,0:T(8,128)(2,1)S(1)} async-done(((bf16[64,256,8]{1,2,0:T(8,128)(2,1)}), bf16[64,256,8]{1,2,0:T(8,128)(2,1)S(1)}, u32[]{:S(2)}, u32[]{:S(2)}) %all-to-all-start.2) | async-done | bytes 262176 | tf_op jit(solution)/shard_map/all_to_all | solution.py:133
  139.0 0.3 copy.183
  139.3 3.2 %gather_fusion = bf16[1024,64]{1,0:T(8,128)(2,1)S(1)} fusion(bf16[2048,64]{1,0:T(8,128)(2,1)S(1)} %copy.183, s32[1024]{0:T(1024)S(1)} %broadcast_clamp_fusion), kind=kCustom, calls=%fused_computation | custom fusion | bytes 266240 | tf_op jit(solution)/shard_map/jit(_take)/gather | solution.py:144
  142.5 0.2 copy.184
  142.6 0.4 fusion.13
  143.1 1.0 convolution_multiply_fusion
  144.1 0.3 fusion.17
  144.4 2.3 %convolution_bitcast_fusion.1 = f32[256,4,1,128]{3,0,1,2:T(8,128)} fusion(f32[4,256,256]{2,1,0:T(8,128)S(1)} %convolution_multiply_fusion, bf16[256,4,128]{2,1,0:T(4,128)(2,1)} %bitcast.228), kind=kOutput, calls=%fused_computation.8 | convolution fusion | flops 201326592 | bytes 1835008 | tf_op jit(solution)/shard_map/bhij,jbhn->ibhn/dot_general | solution.py:176
  146.7 0.9 broadcast_in_dim.148
  147.6 7.2 %all-to-all-start.3 = ((bf16[8,4,1,128,64]{3,4,2,1,0:T(8,128)(2,1)}), bf16[8,4,1,128,64]{3,4,2,1,0:T(8,128)(2,1)}, u32[]{:S(2)}, u32[]{:S(2)}) async-start(bf16[8,4,1,128,64]{3,4,2,1,0:T(8,128)(2,1)} %broadcast_in_dim.148), calls=%async_computation.3 | async-start | bytes 1048576 | tf_op jit(solution)/shard_map/all_to_all | solution.py:158
  154.8 2.1 %fusion.4 = bf16[256,4,1,128]{3,0,1,2:T(8,128)(2,1)S(1)} fusion(f32[256,4,1,128]{3,0,1,2:T(8,128)} %convolution_bitcast_fusion.1, f32[4,64,128]{2,1,0:T(8,128)S(1)} %multiply_reduce_fusion.2, f32[256,4,1,64]{0,3,1,2:T(8,128)S(1)} %fusion.13, f32[256,4]{0,1:T(4,128)S(1)} %get-tuple-element.27), kind=kOutput, calls=%fused_computation.16 | convolution fusion | flops 101056512 | bytes 1183744 | tf_op jit(solution)/shard_map/ibhp,bhpn->ibhn/dot_general | solution.py:177
  157.0 0.9 copy.195
  157.9 1.1 convolution_bitcast_fusion.6
  159.0 0.8 convolution_bitcast_fusion.3
  159.8 4.5 %all-to-all-done.3 = bf16[8,4,1,128,64]{3,4,2,1,0:T(8,128)(2,1)} async-done(((bf16[8,4,1,128,64]{3,4,2,1,0:T(8,128)(2,1)}), bf16[8,4,1,128,64]{3,4,2,1,0:T(8,128)(2,1)}, u32[]{:S(2)}, u32[]{:S(2)}) %all-to-all-start.3) | async-done | bytes 524320 | tf_op jit(solution)/shard_map/all_to_all | solution.py:158
  164.3 1.2 multiply_reduce_fusion.1
  165.5 1.1 fusion.5
  166.6 0.9 copy.194
  167.5 2.0 %fusion.15 = bf16[256,4,1,64]{0,3,2,1:T(8,128)(2,1)} fusion(f32[256,4,1,64]{0,3,1,2:T(8,128)} %convolution_bitcast_fusion.6, f32[4,128,64]{1,2,0:T(8,128)S(1)} %multiply_reduce_fusion.1, f32[256,4,1,64]{0,3,1,2:T(8,128)S(1)} %fusion.13, bf16[256,4,128]{2,1,0:T(4,128)(2,1)S(1)} %bitcast.231, f32[256,4]{0,1:T(4,128)S(1)} %get-tuple-element.38, f32[]{:T(128)} %bitcast.216, ...), kind=kOutput, calls=%fused_computation.31 | convolution fusion | flops 101056512 | bytes 1056772 | tf_op jit(solution)/shard_map/jbhn,bhnp->jbhp/dot_general | solution.py:167
  (87 shorter events, 1.8 us)
Async XLA Ops:
  7.2 69.5 %copy-start = (bf16[1,640,512]{2,1,0:T(8,128)(2,1)S(1)}, bf16[1,640,512]{2,1,0:T(8,128)(2,1)}, u32[]{:S(2)}) copy-start(bf16[1,640,512]{2,1,0:T(8,128)(2,1)} %param.11) | copy-start | bytes 1966084
  7.2 22.7 %copy-start.17 = (f32[256,4,1]{0,2,1:T(1,128)S(1)}, f32[256,4,1]{0,2,1:T(1,128)}, u32[]{:S(2)}) copy-start(f32[256,4,1]{0,2,1:T(1,128)} %param.16) | copy-start | bytes 12292
  7.2 24.0 %copy-start.23 = (s32[256,4]{0,1:T(4,128)S(1)}, s32[256,4]{0,1:T(4,128)}, u32[]{:S(2)}) copy-start(s32[256,4]{0,1:T(4,128)} %param.17) | copy-start | bytes 12292
  7.2 27.1 %copy-start.7 = (bf16[256,4,1,128]{3,1,2,0:T(4,128)(2,1)S(1)}, bf16[256,4,1,128]{3,1,2,0:T(4,128)(2,1)}, u32[]{:S(2)}) copy-start(bf16[256,4,1,128]{3,1,2,0:T(4,128)(2,1)} %param.14) | copy-start | bytes 786436
  7.2 27.0 %copy-start.6 = (bf16[256,4,1,64]{0,3,2,1:T(8,128)(2,1)S(1)}, bf16[256,4,1,64]{0,3,2,1:T(8,128)(2,1)}, u32[]{:S(2)}) copy-start(bf16[256,4,1,64]{0,3,2,1:T(8,128)(2,1)} %param.13) | copy-start | bytes 393220
  7.2 66.8 %all-gather.4.cloned.1.call-start = ((), (), s32[]{:S(2)}) async-start(), calls=%async_computation.4 | async-start | bytes 2949120 | tf_op jit(solution)/shard_map/all_gather | solution.py:82
  9.1 47.2 %copy-start.12 = (s32[8192]{0:T(1024)}, s32[8192]{0:T(1024)S(1)}, u32[]{:S(2)}) copy-start(s32[8192]{0:T(1024)S(1)} %reshape.573) | copy-start | bytes 98308
  33.0 1.0 copy-start.14
  33.1 1.5 copy-start.18
  33.8 22.5 %copy-start.24 = (pred[8]{0:T(512)(128)(4,1)}, pred[8]{0:T(512)(128)(4,1)S(1)}, u32[]{:S(2)}) copy-start(pred[8]{0:T(512)(128)(4,1)S(1)} %get-tuple-element.40) | copy-start | bytes 28
  52.3 0.8 copy-start.4
  74.1 2.6 %copy-start.2 = (bf16[64,32,640]{2,1,0:T(8,128)(2,1)S(1)}, bf16[64,32,640]{2,1,0:T(8,128)(2,1)}, u32[]{:S(2)}) copy-start(bf16[64,32,640]{2,1,0:T(8,128)(2,1)} %all-gather.4.cloned.1.call-done) | copy-start | bytes 7864324
  80.0 18.6 %copy-start.3 = (bf16[256,4,1,128]{3,1,2,0:T(4,128)(2,1)S(1)}, bf16[256,4,1,128]{3,1,2,0:T(4,128)(2,1)}, u32[]{:S(2)}) copy-start(bf16[256,4,1,128]{3,1,2,0:T(4,128)(2,1)} %param.15) | copy-start | bytes 786436
  80.0 18.6 %copy-start.8 = (bf16[256,4,1,128]{3,1,2,0:T(4,128)(2,1)S(1)}, bf16[256,4,1,128]{3,1,2,0:T(4,128)(2,1)}, u32[]{:S(2)}) copy-start(bf16[256,4,1,128]{3,1,2,0:T(4,128)(2,1)} %param.14) | copy-start | bytes 786436
  80.0 35.1 %all-to-all-start.1 = ((bf16[8,257,512]{2,1,0:T(8,128)(2,1)}), bf16[8,257,512]{2,1,0:T(8,128)(2,1)S(1)}, u32[]{:S(2)}, u32[]{:S(2)}) async-start(bf16[8,257,512]{2,1,0:T(8,128)(2,1)} %pad_maximum_fusion), calls=%async_computation.1 | async-start | bytes 4325376 | tf_op jit(solution)/shard_map/all_to_all | solution.py:125
  97.3 18.1 %copy-start.10 = (pred[256,256]{1,0:T(8,128)(4,1)}, pred[256,256]{1,0:T(8,128)(4,1)S(1)}, u32[]{:S(2)}) copy-start(pred[256,256]{1,0:T(8,128)(4,1)S(1)} %iota_compare_fusion.2) | copy-start | bytes 196612
  98.0 0.6 copy-start.21
  100.8 27.5 %copy-start.13 = (s32[8,128]{1,0:T(8,128)S(1)}, s32[8,128]{1,0:T(8,128)}, u32[]{:S(2)}) copy-start(s32[8,128]{1,0:T(8,128)} %copy.179) | copy-start | bytes 12292
  100.8 28.2 %copy-start.16 = (f32[8,4]{1,0:T(8,128)S(1)}, f32[8,4]{1,0:T(8,128)}, u32[]{:S(2)}) copy-start(f32[8,4]{1,0:T(8,128)} %copy.175) | copy-start | bytes 388
  115.4 13.6 %copy-start.5 = (bf16[32,1,66,128]{3,2,1,0:T(8,128)(2,1)S(1)}, bf16[32,1,66,128]{3,2,1,0:T(8,128)(2,1)}, u32[]{:S(2)}) copy-start(bf16[32,1,66,128]{3,2,1,0:T(8,128)(2,1)} %copy-done.4) | copy-start | bytes 1622020
  116.4 22.6 %all-to-all-start.2 = ((bf16[64,256,8]{1,2,0:T(8,128)(2,1)}), bf16[64,256,8]{1,2,0:T(8,128)(2,1)S(1)}, u32[]{:S(2)}, u32[]{:S(2)}) async-start(bf16[64,256,8]{1,2,0:T(8,128)(2,1)} %bitcast.37), calls=%async_computation.2 | async-start | bytes 524288 | tf_op jit(solution)/shard_map/all_to_all | solution.py:133
  126.5 16.2 %copy-start.20 = (pred[256,4]{0,1:T(4,128)(4,1)S(1)}, pred[256,4]{0,1:T(4,128)(4,1)}, u32[]{:S(2)}) copy-start(pred[256,4]{0,1:T(4,128)(4,1)} %copy.180) | copy-start | bytes 3076
  129.0 14.0 %copy-start.11 = (pred[256,256]{1,0:T(8,128)(4,1)S(1)}, pred[256,256]{1,0:T(8,128)(4,1)}, u32[]{:S(2)}) copy-start(pred[256,256]{1,0:T(8,128)(4,1)} %copy-done.10) | copy-start | bytes 196612
  129.0 14.0 %copy-start.19 = (s32[1,4,2,128]{3,1,2,0:T(4,128)S(1)}, s32[1,4,2,128]{3,1,2,0:T(4,128)}, u32[]{:S(2)}) copy-start(s32[1,4,2,128]{3,1,2,0:T(4,128)} %copy-done.18) | copy-start | bytes 12292
  129.1 14.0 %copy-start.22 = (f32[4,256]{1,0:T(4,128)S(1)}, f32[4,256]{1,0:T(4,128)}, u32[]{:S(2)}) copy-start(f32[4,256]{1,0:T(4,128)} %copy-done.21) | copy-start | bytes 12292
  144.3 13.5 %copy-start.1 = (f32[4,256,256]{2,1,0:T(8,128)S(1)}, f32[4,256,256]{2,1,0:T(8,128)}, u32[]{:S(2)}) copy-start(f32[4,256,256]{2,1,0:T(8,128)} %convolution_multiply_fusion.1) | copy-start | bytes 3145732
  147.6 16.7 %all-to-all-start.3 = ((bf16[8,4,1,128,64]{3,4,2,1,0:T(8,128)(2,1)}), bf16[8,4,1,128,64]{3,4,2,1,0:T(8,128)(2,1)}, u32[]{:S(2)}, u32[]{:S(2)}) async-start(bf16[8,4,1,128,64]{3,4,2,1,0:T(8,128)(2,1)} %broadcast_in_dim.148), calls=%async_computation.3 | async-start | bytes 1048576 | tf_op jit(solution)/shard_map/all_to_all | solution.py:158
  154.8 9.5 %copy-start.15 = (f32[8,4]{1,0:T(8,128)S(1)}, f32[8,4]{1,0:T(8,128)}, u32[]{:S(2)}) copy-start(f32[8,4]{1,0:T(8,128)} %copy.185) | copy-start | bytes 388
  159.0 8.5 %copy-start.9 = (bf16[256,4,1,128]{3,1,2,0:T(4,128)(2,1)S(1)}, bf16[256,4,1,128]{3,1,2,0:T(4,128)(2,1)}, u32[]{:S(2)}) copy-start(bf16[256,4,1,128]{3,1,2,0:T(4,128)(2,1)} %param.14) | copy-start | bytes 786436
Sparse Core Ops, SparseCore 0:
  29.3 44.6 all-gather.3

commit v7 on v6

--- a/solution.py
+++ b/solution.py
@@ -54,6 +54,26 @@
     return jnp.sum(weights[:, :, :, None, None] * local_all.astype(jnp.float32), axis=0)
 
 
+def ring_gather(x, axis):
+    count = lax.axis_size(axis)
+    ahead = [(i, (i + 1) % count) for i in range(count)]
+    behind = [(i, (i - 1) % count) for i in range(count)]
+    later = [None] * count
+    later[0] = x
+    cw = x
+    ccw = x
+    for hop in range(1, count // 2 + 1):
+        cw = lax.ppermute(cw, axis, ahead)
+        later[count - hop] = cw
+        if hop < count - hop:
+            ccw = lax.ppermute(ccw, axis, behind)
+            later[hop] = ccw
+    rel = jnp.stack(later)
+    place = lax.axis_index(axis)
+    doubled = jnp.concatenate([rel, rel])
+    return lax.dynamic_slice_in_dim(doubled, (count - place) % count, count)
+
+
 def per_device(
     teacher_in, teacher_proj, family, x_in, b_in, c_in, step_size, doc_start, a_rate, skip_gain
 ):
@@ -79,7 +99,7 @@
     packed = jnp.dot(select.T, own_rows, preferred_element_type=jnp.float32).astype(jnp.bfloat16)
     packed = packed.reshape(FAM, CAP, feat_width)
     by_family = lax.all_to_all(packed, "ty", split_axis=0, concat_axis=0, tiled=True)
-    received = lax.all_gather(by_family, "tz")
+    received = ring_gather(by_family, "tz")
     x_full = x_in.astype(jnp.float32)
     b_full = b_in.astype(jnp.float32)
     c_full = c_in.astype(jnp.float32)

time: 177 us -> 180 us (1.017)
  starting transfers between devices: 25.5 us -> 59.8 us
  blocking collectives: 35.1 us -> 15.8 us
  between operations: 15.8 us -> 2.47 us
  waiting for transfers between devices: 46.2 us -> 43.1 us
  matrix products: 17.7 us -> 20.2 us
    ppermute x0 -> x7, starting transfers between devices: none -> 30 us  [the longest x3 18.9 us: ring_gather(): ccw = lax.ppermute(ccw, axis, behind)]
    all_to_all x1 -> x0, blocking collectives: 18.1 us -> none  [per_device(): lax.all_to_all(packed, 'ty', split_axis=0, concat_axis=0, tiled=True)]
    all_gather x1 -> x0, waiting for transfers between devices: 17.7 us -> none  [per_device(): received = lax.all_gather(by_family, 'tz')]
    ppermute x0 -> x7, waiting for transfers between devices: none -> 15.7 us  [the longest x3 10.2 us: ring_gather(): ccw = lax.ppermute(ccw, axis, behind)]
    all_to_all x0 -> x1, starting transfers between devices: none -> 7.64 us  [per_device(): lax.all_to_all(packed, 'ty', split_axis=0, concat_axis=0, tiled=True)]
    reduce_sum x1, other arithmetic: 2.45 us -> 0.56 us  [per_device(): sq_sums = jnp.sum(jnp.square(received.astype(jnp.float32)), axis=1)]
    all_to_all x1, starting transfers between devices: 10.1 us -> 8.24 us  [per_device(): lax.all_to_all(outgoing, TEACH, split_axis=0, concat_axis=0, tiled=True)]
    unnamed x57 -> x54, local copies, waits for them, and re-layouts: 6.88 us -> 6.86 us
  transfers between devices with their start and end apart: 4 -> 11, of which waited for: 4 -> 8; matrix products, arithmetic and copies ran while one was open for 16% -> 18% of each run, Pallas kernels for 0% -> 0%
where the time goes in v7:
time: 180 us; the launch traced here: 179 us
  starting transfers between devices  59.8 us (33%)
  waiting for transfers between devices  43.1 us (24%)
  matrix products  20.2 us (11%)
  local copies, waits for them, and re-layouts  19.7 us (11%)
  other arithmetic  17.9 us (10%)
  blocking collectives  15.8 us (9%)
  between operations  2.47 us (1%)
    ppermute x3, starting transfers between devices, ring_gather(): ccw = lax.ppermute(ccw, axis, behind)  18.9 us
    all_gather x1, blocking collectives, per_device(): gathered = lax.all_gather(packed_state, 'seq')  15.8 us
    all_to_all x1, waiting for transfers between devices, per_device(): lax.all_to_all(outbound, 'seq', split_axis=0, concat_axis=0, tiled=True)  14.1 us
    ppermute x4, starting transfers between devices, ring_gather(): cw = lax.ppermute(cw, axis, ahead)  11 us
    ppermute x3, waiting for transfers between devices, ring_gather(): ccw = lax.ppermute(ccw, axis, behind)  10.2 us
    all_to_all x1, waiting for transfers between devices, per_device(): lax.all_to_all(outgoing, TEACH, split_axis=0, concat_axis=0, tiled=True)  8.72 us
    all_to_all x1, starting transfers between devices, per_device(): lax.all_to_all(outgoing, TEACH, split_axis=0, concat_axis=0, tiled=True)  8.24 us
    all_to_all x1, starting transfers between devices, per_device(): lax.all_to_all(packed, 'ty', split_axis=0, concat_axis=0, tiled=True)  7.64 us
  transfers between devices with their start and end apart: 11, of which 8 were waited for; matrix products, arithmetic and copies ran while one was open for 18% of the time, Pallas kernels for 0%

profile of v7, /device:TPU:1, one launch (start us, length us, event | category | flops | bytes accessed | tf_op | source)
XLA Modules:
  0.0 179.0 jit_solution(8001379312179771145)
XLA Ops:
  0.7 1.2 copy.176
  1.8 0.6 reshape.573
  3.1 1.0 reshape.574
  4.1 1.1 convolution_convert_fusion.1
  5.1 7.6 %all-to-all-start = ((bf16[8,32,640]{2,1,0:T(8,128)(2,1)}), bf16[8,32,640]{2,1,0:T(8,128)(2,1)S(1)}, u32[]{:S(2)}, u32[]{:S(2)}) async-start(bf16[8,32,640]{2,1,0:T(8,128)(2,1)} %bitcast.23), calls=%async_computation | async-start | bytes 655360 | tf_op jit(solution)/shard_map/all_to_all | solution.py:101
  13.4 0.7 negate_multiply_fusion
  14.1 1.2 reduce-window.16
  15.4 0.7 reshape.561
  16.1 1.2 reduce-window.14
  18.8 0.8 copy_bitcast_fusion.1
  19.5 1.3 fusion.16
  21.0 2.5 %select_reduce_fusion = s32[8,128]{0,1:T(8,128)S(1)} fusion(s32[8,128]{0,1:T(8,128)S(1)} %copy.178), kind=kOutput, calls=%fused_computation.46 | output fusion | flops 1096704 | bytes 8192 | tf_op jit(solution)/shard_map/jit(cumsum)/reduce_window_sum | solution.py:23
  23.5 5.3 %collective-permute-start.3 = (bf16[8,32,640]{2,1,0:T(8,128)(2,1)S(1)}, bf16[8,32,640]{2,1,0:T(8,128)(2,1)S(1)}, u32[]{:S(2)}, u32[]{:S(2)}) collective-permute-start(bf16[8,32,640]{2,1,0:T(8,128)(2,1)S(1)} %all-to-all-done), channel_id=1, source_target_pairs={{0,64},{64,128},{128,192},{192,256},{256,320},{320,384},{384,448},... | collective-permute-start | bytes 983048 | tf_op jit(solution)/shard_map/ppermute | solution.py:66
  28.9 15.8 %all-gather = bf16[32,1,66,128]{3,2,1,0:T(8,128)(2,1)S(1)} all-gather(bf16[4,1,66,128]{3,2,1,0:T(8,128)(2,1)S(1)} %maximum_bitcast_fusion), channel_id=2, replica_groups=mesh['tz'=8,'ty'=8,'seq'=8] {'seq'}, dimensions={0}, use_global_device_ids=true | all-gather | bytes 608256 | tf_op jit(solution)/shard_map/all_gather | solution.py:126
  44.7 8.3 %collective-permute-start = (bf16[8,32,640]{2,1,0:T(8,128)(2,1)S(1)}, bf16[8,32,640]{2,1,0:T(8,128)(2,1)S(1)}, u32[]{:S(2)}, u32[]{:S(2)}) collective-permute-start(bf16[8,32,640]{2,1,0:T(8,128)(2,1)S(1)} %all-to-all-done), channel_id=1, source_target_pairs={{0,448},{64,0},{128,64},{192,128},{256,192},{320,256},{384,320},{4... | collective-permute-start | bytes 983048 | tf_op jit(solution)/shard_map/ppermute | solution.py:69
  53.0 0.6 fusion.60
  53.6 1.9 %collective-permute-start.4 = (bf16[8,32,640]{2,1,0:T(8,128)(2,1)S(1)}, bf16[8,32,640]{2,1,0:T(8,128)(2,1)S(1)}, u32[]{:S(2)}, u32[]{:S(2)}) collective-permute-start(bf16[8,32,640]{2,1,0:T(8,128)(2,1)S(1)} %collective-permute-done.3), channel_id=1, source_target_pairs={{0,64},{64,128},{128,192},{192,256},{256,320},{320,384},{384,448},... | collective-permute-start | bytes 983048 | tf_op jit(solution)/shard_map/ppermute | solution.py:66
  56.1 3.8 %collective-permute-done = bf16[8,32,640]{2,1,0:T(8,128)(2,1)S(1)} collective-permute-done((bf16[8,32,640]{2,1,0:T(8,128)(2,1)S(1)}, bf16[8,32,640]{2,1,0:T(8,128)(2,1)S(1)}, u32[]{:S(2)}, u32[]{:S(2)}) %collective-permute-start) | collective-permute-done | bytes 327712 | tf_op jit(solution)/shard_map/ppermute | solution.py:69
  59.9 5.3 %collective-permute-start.1 = (bf16[8,32,640]{2,1,0:T(8,128)(2,1)S(1)}, bf16[8,32,640]{2,1,0:T(8,128)(2,1)S(1)}, u32[]{:S(2)}, u32[]{:S(2)}) collective-permute-start(bf16[8,32,640]{2,1,0:T(8,128)(2,1)S(1)} %collective-permute-done), channel_id=1, source_target_pairs={{0,448},{64,0},{128,64},{192,128},{256,192},{320,256},{384,320},{4... | collective-permute-start | bytes 983048 | tf_op jit(solution)/shard_map/ppermute | solution.py:69
  65.7 1.9 %collective-permute-start.5 = (bf16[8,32,640]{2,1,0:T(8,128)(2,1)S(1)}, bf16[8,32,640]{2,1,0:T(8,128)(2,1)S(1)}, u32[]{:S(2)}, u32[]{:S(2)}) collective-permute-start(bf16[8,32,640]{2,1,0:T(8,128)(2,1)S(1)} %collective-permute-done.4), channel_id=1, source_target_pairs={{0,64},{64,128},{128,192},{192,256},{256,320},{320,384},{384,448},... | collective-permute-start | bytes 983048 | tf_op jit(solution)/shard_map/ppermute | solution.py:66
  67.7 3.5 %collective-permute-done.1 = bf16[8,32,640]{2,1,0:T(8,128)(2,1)S(1)} collective-permute-done((bf16[8,32,640]{2,1,0:T(8,128)(2,1)S(1)}, bf16[8,32,640]{2,1,0:T(8,128)(2,1)S(1)}, u32[]{:S(2)}, u32[]{:S(2)}) %collective-permute-start.1) | collective-permute-done | bytes 327712 | tf_op jit(solution)/shard_map/ppermute | solution.py:69
  71.2 5.3 %collective-permute-start.2 = (bf16[8,32,640]{2,1,0:T(8,128)(2,1)S(1)}, bf16[8,32,640]{2,1,0:T(8,128)(2,1)S(1)}, u32[]{:S(2)}, u32[]{:S(2)}) collective-permute-start(bf16[8,32,640]{2,1,0:T(8,128)(2,1)S(1)} %collective-permute-done.1), channel_id=1, source_target_pairs={{0,448},{64,0},{128,64},{192,128},{256,192},{320,256},{384,320},{4... | collective-permute-start | bytes 983048 | tf_op jit(solution)/shard_map/ppermute | solution.py:69
  76.8 1.9 %collective-permute-start.6 = (bf16[8,32,640]{2,1,0:T(8,128)(2,1)S(1)}, bf16[8,32,640]{2,1,0:T(8,128)(2,1)S(1)}, u32[]{:S(2)}, u32[]{:S(2)}) collective-permute-start(bf16[8,32,640]{2,1,0:T(8,128)(2,1)S(1)} %collective-permute-done.5), channel_id=1, source_target_pairs={{0,64},{64,128},{128,192},{192,256},{256,320},{320,384},{384,448},... | collective-permute-start | bytes 983048 | tf_op jit(solution)/shard_map/ppermute | solution.py:66
  78.8 2.9 %collective-permute-done.2 = bf16[8,32,640]{2,1,0:T(8,128)(2,1)S(1)} collective-permute-done((bf16[8,32,640]{2,1,0:T(8,128)(2,1)S(1)}, bf16[8,32,640]{2,1,0:T(8,128)(2,1)S(1)}, u32[]{:S(2)}, u32[]{:S(2)}) %collective-permute-start.2) | collective-permute-done | bytes 327712 | tf_op jit(solution)/shard_map/ppermute | solution.py:69
  81.7 5.3 %collective-permute-done.6 = bf16[8,32,640]{2,1,0:T(8,128)(2,1)S(1)} collective-permute-done((bf16[8,32,640]{2,1,0:T(8,128)(2,1)S(1)}, bf16[8,32,640]{2,1,0:T(8,128)(2,1)S(1)}, u32[]{:S(2)}, u32[]{:S(2)}) %collective-permute-start.6) | collective-permute-done | bytes 327712 | tf_op jit(solution)/shard_map/ppermute | solution.py:66
  87.8 0.6 multiply_reduce_fusion
  88.5 1.8 %convolution_convert_fusion = bf16[8,256,512]{2,1,0:T(8,128)(2,1)S(1)} fusion(bf16[8,256,640]{2,1,0:T(8,128)(2,1)S(1)} %bitcast.240, bf16[1,640,512]{2,1,0:T(8,128)(2,1)S(1)} %copy-done), kind=kOutput, calls=%fused_computation.4 | convolution fusion | flops 1343225856 | bytes 5373952 | tf_op jit(solution)/shard_map/dot_general | solution.py:135
  90.4 1.5 pad_maximum_fusion
  91.9 6.8 %all-to-all-start.1 = ((bf16[8,257,512]{2,1,0:T(8,128)(2,1)}), bf16[8,257,512]{2,1,0:T(8,128)(2,1)S(1)}, u32[]{:S(2)}, u32[]{:S(2)}) async-start(bf16[8,257,512]{2,1,0:T(8,128)(2,1)} %pad_maximum_fusion), calls=%async_computation.1 | async-start | bytes 4325376 | tf_op jit(solution)/shard_map/all_to_all | solution.py:145
  98.7 1.2 fusion.56
  99.9 0.7 copy.179
  100.5 0.8 copy.200
  101.4 0.8 copy.201
  102.2 0.9 select_reduce_fusion.2
  103.1 0.6 broadcast_select_fusion.1
  103.7 0.7 copy.175
  104.4 0.7 compare_and_fusion.1
  105.3 0.6 copy.180
  106.5 0.6 broadcast_select_fusion
  107.2 0.7 copy.185
  107.9 0.7 broadcast_bitcast_fusion
  108.6 0.6 copy-done.14
  109.2 2.2 %convolution_multiply_fusion.1 = f32[4,256,256]{2,1,0:T(8,128)} fusion(f32[4,256]{1,0:T(4,128)S(1)} %bitcast_add_fusion, s32[4,256]{1,0:T(4,128)} %bitcast.255, pred[256,256]{1,0:T(8,128)(4,1)S(1)} %iota_compare_fusion.2, bf16[256,4,128]{2,1,0:T(4,128)(2,1)S(1)} %bitcast.252, bf16[256,4,128]{2,1,0:T(4,128)(2,1)S(1)} %bitcast.241), kind=kOutput, calls=%fused_computation.6 | convolution fusion | flops 68681728 | bytes 1646592 | tf_op jit(solution)/shard_map/ibhn,jbhn->bhij/dot_general | solution.py:169
  111.5 14.1 %all-to-all-done.1 = bf16[8,257,512]{2,1,0:T(8,128)(2,1)S(1)} async-done(((bf16[8,257,512]{2,1,0:T(8,128)(2,1)}), bf16[8,257,512]{2,1,0:T(8,128)(2,1)S(1)}, u32[]{:S(2)}, u32[]{:S(2)}) %all-to-all-start.1) | async-done | bytes 2105376 | tf_op jit(solution)/shard_map/all_to_all | solution.py:145
  126.0 0.8 copy.182
  126.9 8.2 %all-to-all-start.2 = ((bf16[64,256,8]{1,2,0:T(8,128)(2,1)}), bf16[64,256,8]{1,2,0:T(8,128)(2,1)S(1)}, u32[]{:S(2)}, u32[]{:S(2)}) async-start(bf16[64,256,8]{1,2,0:T(8,128)(2,1)} %bitcast.44), calls=%async_computation.2 | async-start | bytes 524288 | tf_op jit(solution)/shard_map/all_to_all | solution.py:153
  135.1 1.8 %convolution_bitcast_fusion.7 = f32[256,4,1,64]{0,3,1,2:T(8,128)S(1)} fusion(f32[4,256,256]{2,1,0:T(8,128)} %convolution_multiply_fusion.1, bf16[256,4,1,64]{0,3,2,1:T(8,128)(2,1)S(1)} %copy-done.4, f32[256,4]{0,1:T(4,128)S(1)} %get-tuple-element.37), kind=kOutput, calls=%fused_computation.27 | convolution fusion | flops 100794368 | bytes 1445888 | tf_op jit(solution)/shard_map/bhij,jbhp->ibhp/dot_general | solution.py:171
  137.0 0.7 broadcast_clamp_fusion
  137.7 1.2 multiply_reduce_fusion.2
  138.9 8.7 %all-to-all-done.2 = bf16[64,256,8]{1,2,0:T(8,128)(2,1)S(1)} async-done(((bf16[64,256,8]{1,2,0:T(8,128)(2,1)}), bf16[64,256,8]{1,2,0:T(8,128)(2,1)S(1)}, u32[]{:S(2)}, u32[]{:S(2)}) %all-to-all-start.2) | async-done | bytes 262176 | tf_op jit(solution)/shard_map/all_to_all | solution.py:153
  147.9 3.2 %gather_fusion = bf16[1024,64]{1,0:T(8,128)(2,1)S(1)} fusion(bf16[2048,64]{1,0:T(8,128)(2,1)S(1)} %copy.183, s32[1024]{0:T(1024)S(1)} %broadcast_clamp_fusion), kind=kCustom, calls=%fused_computation | custom fusion | bytes 266240 | tf_op jit(solution)/shard_map/jit(_take)/gather | solution.py:164
  151.8 1.8 %convolution_multiply_fusion = f32[4,256,256]{2,1,0:T(8,128)S(1)} fusion(f32[4,256]{1,0:T(4,128)} %copy-done.14, s32[4,256]{1,0:T(4,128)} %bitcast.256, pred[256,256]{1,0:T(8,128)(4,1)} %copy-done.6, f32[256,4,1,64]{0,3,1,2:T(8,128)S(1)} %fusion.13, bf16[256,4,1,64]{0,3,2,1:T(8,128)(2,1)S(1)} %copy-done.4, f32[256,4]{0,1:T(4,128)S(1)} %get-tuple-element.37), kind=kOutput, calls=%fused_computation.5 | convolution fusion | flops 102367232 | bytes 1519616 | tf_op jit(solution)/shard_map/ibhp,jbhp->bhij/dot_general | solution.py:191
  153.9 2.2 %convolution_bitcast_fusion.1 = f32[256,4,1,128]{3,0,1,2:T(8,128)} fusion(f32[4,256,256]{2,1,0:T(8,128)S(1)} %convolution_multiply_fusion, bf16[256,4,128]{2,1,0:T(4,128)(2,1)} %bitcast.250), kind=kOutput, calls=%fused_computation.8 | convolution fusion | flops 201326592 | bytes 1835008 | tf_op jit(solution)/shard_map/bhij,jbhn->ibhn/dot_general | solution.py:196
  156.1 0.9 broadcast_in_dim.148
  157.0 7.2 %all-to-all-start.3 = ((bf16[8,4,1,128,64]{3,4,2,1,0:T(8,128)(2,1)}), bf16[8,4,1,128,64]{3,4,2,1,0:T(8,128)(2,1)}, u32[]{:S(2)}, u32[]{:S(2)}) async-start(bf16[8,4,1,128,64]{3,4,2,1,0:T(8,128)(2,1)} %broadcast_in_dim.148), calls=%async_computation.3 | async-start | bytes 1048576 | tf_op jit(solution)/shard_map/all_to_all | solution.py:178
  164.2 2.1 %fusion.4 = bf16[256,4,1,128]{3,0,1,2:T(8,128)(2,1)S(1)} fusion(f32[256,4,1,128]{3,0,1,2:T(8,128)} %convolution_bitcast_fusion.1, f32[4,64,128]{2,1,0:T(8,128)S(1)} %multiply_reduce_fusion.2, f32[256,4,1,64]{0,3,1,2:T(8,128)S(1)} %fusion.13, f32[256,4]{0,1:T(4,128)S(1)} %get-tuple-element.27), kind=kOutput, calls=%fused_computation.16 | convolution fusion | flops 101056512 | bytes 1183744 | tf_op jit(solution)/shard_map/ibhp,bhpn->ibhn/dot_general | solution.py:197
  166.4 0.9 copy.195
  167.3 1.1 convolution_bitcast_fusion.6
  168.4 0.8 convolution_bitcast_fusion.3
  169.2 4.5 %all-to-all-done.3 = bf16[8,4,1,128,64]{3,4,2,1,0:T(8,128)(2,1)} async-done(((bf16[8,4,1,128,64]{3,4,2,1,0:T(8,128)(2,1)}), bf16[8,4,1,128,64]{3,4,2,1,0:T(8,128)(2,1)}, u32[]{:S(2)}, u32[]{:S(2)}) %all-to-all-start.3) | async-done | bytes 524320 | tf_op jit(solution)/shard_map/all_to_all | solution.py:178
  173.7 1.2 multiply_reduce_fusion.1
  174.9 1.1 fusion.5
  176.1 0.9 copy.194
  177.0 2.1 %fusion.15 = bf16[256,4,1,64]{0,3,2,1:T(8,128)(2,1)} fusion(f32[256,4,1,64]{0,3,1,2:T(8,128)} %convolution_bitcast_fusion.6, f32[4,128,64]{1,2,0:T(8,128)S(1)} %multiply_reduce_fusion.1, f32[256,4,1,64]{0,3,1,2:T(8,128)S(1)} %fusion.13, bf16[256,4,128]{2,1,0:T(4,128)(2,1)} %bitcast.251, f32[256,4]{0,1:T(4,128)S(1)} %get-tuple-element.38, f32[]{:T(128)} %bitcast.239, ...), kind=kOutput, calls=%fused_computation.31 | convolution fusion | flops 101056512 | bytes 1056772 | tf_op jit(solution)/shard_map/jbhn,bhnp->jbhp/dot_general | solution.py:187
  (98 shorter events, 6.3 us)
Async XLA Ops:
  0.6 87.9 %copy-start = (bf16[1,640,512]{2,1,0:T(8,128)(2,1)S(1)}, bf16[1,640,512]{2,1,0:T(8,128)(2,1)}, u32[]{:S(2)}) copy-start(bf16[1,640,512]{2,1,0:T(8,128)(2,1)} %param.11) | copy-start | bytes 1966084
  2.5 26.4 %copy-start.7 = (s32[8192]{0:T(1024)}, s32[8192]{0:T(1024)S(1)}, u32[]{:S(2)}) copy-start(s32[8192]{0:T(1024)S(1)} %reshape.573) | copy-start | bytes 98308
  5.1 18.4 %all-to-all-start = ((bf16[8,32,640]{2,1,0:T(8,128)(2,1)}), bf16[8,32,640]{2,1,0:T(8,128)(2,1)S(1)}, u32[]{:S(2)}, u32[]{:S(2)}) async-start(bf16[8,32,640]{2,1,0:T(8,128)(2,1)} %bitcast.23), calls=%async_computation | async-start | bytes 655360 | tf_op jit(solution)/shard_map/all_to_all | solution.py:101
  18.0 0.6 copy-start.9
  18.1 0.6 copy-start.12
  23.5 30.1 %collective-permute-start.3 = (bf16[8,32,640]{2,1,0:T(8,128)(2,1)S(1)}, bf16[8,32,640]{2,1,0:T(8,128)(2,1)S(1)}, u32[]{:S(2)}, u32[]{:S(2)}) collective-permute-start(bf16[8,32,640]{2,1,0:T(8,128)(2,1)S(1)} %all-to-all-done), channel_id=1, source_target_pairs={{0,64},{64,128},{128,192},{192,256},{256,320},{320,384},{384,448},... | collective-permute-start | bytes 983048 | tf_op jit(solution)/shard_map/ppermute | solution.py:66
  44.7 15.2 %copy-start.3 = (bf16[32,1,66,128]{3,2,1,0:T(8,128)(2,1)}, bf16[32,1,66,128]{3,2,1,0:T(8,128)(2,1)S(1)}, u32[]{:S(2)}) copy-start(bf16[32,1,66,128]{3,2,1,0:T(8,128)(2,1)S(1)} %all-gather) | copy-start | bytes 1622020
  44.7 15.2 %collective-permute-start = (bf16[8,32,640]{2,1,0:T(8,128)(2,1)S(1)}, bf16[8,32,640]{2,1,0:T(8,128)(2,1)S(1)}, u32[]{:S(2)}, u32[]{:S(2)}) collective-permute-start(bf16[8,32,640]{2,1,0:T(8,128)(2,1)S(1)} %all-to-all-done), channel_id=1, source_target_pairs={{0,448},{64,0},{128,64},{192,128},{256,192},{320,256},{384,320},{4... | collective-permute-start | bytes 983048 | tf_op jit(solution)/shard_map/ppermute | solution.py:69
  53.6 12.1 %collective-permute-start.4 = (bf16[8,32,640]{2,1,0:T(8,128)(2,1)S(1)}, bf16[8,32,640]{2,1,0:T(8,128)(2,1)S(1)}, u32[]{:S(2)}, u32[]{:S(2)}) collective-permute-start(bf16[8,32,640]{2,1,0:T(8,128)(2,1)S(1)} %collective-permute-done.3), channel_id=1, source_target_pairs={{0,64},{64,128},{128,192},{192,256},{256,320},{320,384},{384,448},... | collective-permute-start | bytes 983048 | tf_op jit(solution)/shard_map/ppermute | solution.py:66
  56.1 31.5 %copy-start.15 = (pred[8]{0:T(512)(128)(4,1)}, pred[8]{0:T(512)(128)(4,1)S(1)}, u32[]{:S(2)}) copy-start(pred[8]{0:T(512)(128)(4,1)S(1)} %get-tuple-element.40) | copy-start | bytes 28
  59.9 11.3 %collective-permute-start.1 = (bf16[8,32,640]{2,1,0:T(8,128)(2,1)S(1)}, bf16[8,32,640]{2,1,0:T(8,128)(2,1)S(1)}, u32[]{:S(2)}, u32[]{:S(2)}) collective-permute-start(bf16[8,32,640]{2,1,0:T(8,128)(2,1)S(1)} %collective-permute-done), channel_id=1, source_target_pairs={{0,448},{64,0},{128,64},{192,128},{256,192},{320,256},{384,320},{4... | collective-permute-start | bytes 983048 | tf_op jit(solution)/shard_map/ppermute | solution.py:69
  65.7 11.1 %collective-permute-start.5 = (bf16[8,32,640]{2,1,0:T(8,128)(2,1)S(1)}, bf16[8,32,640]{2,1,0:T(8,128)(2,1)S(1)}, u32[]{:S(2)}, u32[]{:S(2)}) collective-permute-start(bf16[8,32,640]{2,1,0:T(8,128)(2,1)S(1)} %collective-permute-done.4), channel_id=1, source_target_pairs={{0,64},{64,128},{128,192},{192,256},{256,320},{320,384},{384,448},... | collective-permute-start | bytes 983048 | tf_op jit(solution)/shard_map/ppermute | solution.py:66
  71.2 10.5 %collective-permute-start.2 = (bf16[8,32,640]{2,1,0:T(8,128)(2,1)S(1)}, bf16[8,32,640]{2,1,0:T(8,128)(2,1)S(1)}, u32[]{:S(2)}, u32[]{:S(2)}) collective-permute-start(bf16[8,32,640]{2,1,0:T(8,128)(2,1)S(1)} %collective-permute-done.1), channel_id=1, source_target_pairs={{0,448},{64,0},{128,64},{192,128},{256,192},{320,256},{384,320},{4... | collective-permute-start | bytes 983048 | tf_op jit(solution)/shard_map/ppermute | solution.py:69
  76.8 10.2 %collective-permute-start.6 = (bf16[8,32,640]{2,1,0:T(8,128)(2,1)S(1)}, bf16[8,32,640]{2,1,0:T(8,128)(2,1)S(1)}, u32[]{:S(2)}, u32[]{:S(2)}) collective-permute-start(bf16[8,32,640]{2,1,0:T(8,128)(2,1)S(1)} %collective-permute-done.5), channel_id=1, source_target_pairs={{0,64},{64,128},{128,192},{192,256},{256,320},{320,384},{384,448},... | collective-permute-start | bytes 983048 | tf_op jit(solution)/shard_map/ppermute | solution.py:66
  90.3 18.9 %copy-start.2 = (bf16[256,4,1,128]{3,1,2,0:T(4,128)(2,1)S(1)}, bf16[256,4,1,128]{3,1,2,0:T(4,128)(2,1)}, u32[]{:S(2)}) copy-start(bf16[256,4,1,128]{3,1,2,0:T(4,128)(2,1)} %param.15) | copy-start | bytes 786436
  90.3 18.9 %copy-start.5 = (bf16[256,4,1,128]{3,1,2,0:T(4,128)(2,1)S(1)}, bf16[256,4,1,128]{3,1,2,0:T(4,128)(2,1)}, u32[]{:S(2)}) copy-start(bf16[256,4,1,128]{3,1,2,0:T(4,128)(2,1)} %param.14) | copy-start | bytes 786436
  91.9 43.3 %copy-start.4 = (bf16[256,4,1,64]{0,3,2,1:T(8,128)(2,1)S(1)}, bf16[256,4,1,64]{0,3,2,1:T(8,128)(2,1)}, u32[]{:S(2)}) copy-start(bf16[256,4,1,64]{0,3,2,1:T(8,128)(2,1)} %param.13) | copy-start | bytes 393220
  91.9 33.7 %all-to-all-start.1 = ((bf16[8,257,512]{2,1,0:T(8,128)(2,1)}), bf16[8,257,512]{2,1,0:T(8,128)(2,1)S(1)}, u32[]{:S(2)}, u32[]{:S(2)}) async-start(bf16[8,257,512]{2,1,0:T(8,128)(2,1)} %pad_maximum_fusion), calls=%async_computation.1 | async-start | bytes 4325376 | tf_op jit(solution)/shard_map/all_to_all | solution.py:145
  107.9 29.1 %copy-start.6 = (pred[256,256]{1,0:T(8,128)(4,1)}, pred[256,256]{1,0:T(8,128)(4,1)S(1)}, u32[]{:S(2)}) copy-start(pred[256,256]{1,0:T(8,128)(4,1)S(1)} %iota_compare_fusion.2) | copy-start | bytes 196612
  108.6 0.6 copy-start.14
  108.6 28.4 %copy-start.8 = (s32[8,128]{1,0:T(8,128)S(1)}, s32[8,128]{1,0:T(8,128)}, u32[]{:S(2)}) copy-start(s32[8,128]{1,0:T(8,128)} %copy.179) | copy-start | bytes 12292
  111.5 26.2 %copy-start.11 = (f32[8,4]{1,0:T(8,128)S(1)}, f32[8,4]{1,0:T(8,128)}, u32[]{:S(2)}) copy-start(f32[8,4]{1,0:T(8,128)} %copy.175) | copy-start | bytes 388
  111.5 39.9 %copy-start.13 = (pred[256,4]{0,1:T(4,128)(4,1)S(1)}, pred[256,4]{0,1:T(4,128)(4,1)}, u32[]{:S(2)}) copy-start(pred[256,4]{0,1:T(4,128)(4,1)} %copy.180) | copy-start | bytes 3076
  126.9 20.8 %all-to-all-start.2 = ((bf16[64,256,8]{1,2,0:T(8,128)(2,1)}), bf16[64,256,8]{1,2,0:T(8,128)(2,1)S(1)}, u32[]{:S(2)}, u32[]{:S(2)}) async-start(bf16[64,256,8]{1,2,0:T(8,128)(2,1)} %bitcast.44), calls=%async_computation.2 | async-start | bytes 524288 | tf_op jit(solution)/shard_map/all_to_all | solution.py:153
  151.2 16.1 %copy-start.1 = (f32[4,256,256]{2,1,0:T(8,128)S(1)}, f32[4,256,256]{2,1,0:T(8,128)}, u32[]{:S(2)}) copy-start(f32[4,256,256]{2,1,0:T(8,128)} %convolution_multiply_fusion.1) | copy-start | bytes 3145732
  151.8 22.0 %copy-start.10 = (f32[8,4]{1,0:T(8,128)S(1)}, f32[8,4]{1,0:T(8,128)}, u32[]{:S(2)}) copy-start(f32[8,4]{1,0:T(8,128)} %copy.185) | copy-start | bytes 388
  157.0 16.7 %all-to-all-start.3 = ((bf16[8,4,1,128,64]{3,4,2,1,0:T(8,128)(2,1)}), bf16[8,4,1,128,64]{3,4,2,1,0:T(8,128)(2,1)}, u32[]{:S(2)}, u32[]{:S(2)}) async-start(bf16[8,4,1,128,64]{3,4,2,1,0:T(8,128)(2,1)} %broadcast_in_dim.148), calls=%async_computation.3 | async-start | bytes 1048576 | tf_op jit(solution)/shard_map/all_to_all | solution.py:178

commit v8 on v7

--- a/solution.py
+++ b/solution.py
@@ -123,13 +123,13 @@
         ],
         axis=2,
     )
+    packed_state = lax.optimization_barrier((packed_state, received))[0]
     gathered = lax.all_gather(packed_state, "seq")
     rows = local_state.shape[2]
     through_all = gathered[:, :, :, rows, 0].astype(jnp.float32) + gathered[
         :, :, :, rows + 1, 0
     ].astype(jnp.float32)
     slots_all = n_z * n_y * CAP
-    received, gathered = lax.optimization_barrier((received, gathered))
     received = received.reshape(slots_all, feat_width)
     weights = teacher_proj[0]
     partial_value = jnp.dot(received, weights, preferred_element_type=jnp.float32)

time: 180 us -> 179 us (level)
  blocking collectives: 15.8 us -> 31.9 us
  waiting for transfers between devices: 43.1 us -> 34 us
  other arithmetic: 17.9 us -> 13.7 us
  local copies, waits for them, and re-layouts: 19.7 us -> 16.1 us
    all_gather x1, blocking collectives: 15.8 us -> 31.9 us  [per_device(): gathered = lax.all_gather(packed_state, 'seq')]
    all_to_all x1, waiting for transfers between devices: 14.1 us -> 0.01 us  [per_device(): lax.all_to_all(outbound, 'seq', split_axis=0, concat_axis=0, tiled=True)]
    ppermute x4, waiting for transfers between devices: 5.49 us -> 17.7 us  [ring_gather(): cw = lax.ppermute(cw, axis, ahead)]
    ppermute x3, waiting for transfers between devices: 10.2 us -> 0.01 us  [ring_gather(): ccw = lax.ppermute(ccw, axis, behind)]
    all_to_all x1, waiting for transfers between devices: 8.72 us -> 11.8 us  [per_device(): lax.all_to_all(outgoing, TEACH, split_axis=0, concat_axis=0, tiled=True)]
    all_to_all x1, starting transfers between devices: 6.82 us -> 9.16 us  [per_device(): lax.all_to_all(outbound, 'seq', split_axis=0, concat_axis=0, tiled=True)]
    unnamed x54 -> x44, local copies, waits for them, and re-layouts: 6.86 us -> 5.75 us
  transfers between devices with their start and end apart: 11 -> 11, of which waited for: 8 -> 6; matrix products, arithmetic and copies ran while one was open for 18% -> 12% of each run, Pallas kernels for 0% -> 0%
where the time goes in v8:
time: 179 us; the launch traced here: 178 us
  starting transfers between devices  60.7 us (34%)
  waiting for transfers between devices  34 us (19%)
  blocking collectives  31.9 us (18%)
  matrix products  18.8 us (11%)
  local copies, waits for them, and re-layouts  16.1 us (9%)
  other arithmetic  13.7 us (8%)
  between operations  2.53 us (1%)
    all_gather x1, blocking collectives, per_device(): gathered = lax.all_gather(packed_state, 'seq')  31.9 us
    ppermute x3, starting transfers between devices, ring_gather(): ccw = lax.ppermute(ccw, axis, behind)  17.7 us
    ppermute x4, waiting for transfers between devices, ring_gather(): cw = lax.ppermute(cw, axis, ahead)  17.7 us
    all_to_all x1, waiting for transfers between devices, per_device(): lax.all_to_all(outgoing, TEACH, split_axis=0, concat_axis=0, tiled=True)  11.8 us
    all_to_all x1, starting transfers between devices, per_device(): lax.all_to_all(outgoing, TEACH, split_axis=0, concat_axis=0, tiled=True)  10 us
    ppermute x4, starting transfers between devices, ring_gather(): cw = lax.ppermute(cw, axis, ahead)  9.72 us
    all_to_all x1, starting transfers between devices, per_device(): lax.all_to_all(outbound, 'seq', split_axis=0, concat_axis=0, tiled=True)  9.16 us
    all_to_all x1, starting transfers between devices, per_device(): lax.all_to_all(packed, 'ty', split_axis=0, concat_axis=0, tiled=True)  7.64 us
  transfers between devices with their start and end apart: 11, of which 6 were waited for; matrix products, arithmetic and copies ran while one was open for 12% of the time, Pallas kernels for 0%

profile of v8, /device:TPU:1, one launch (start us, length us, event | category | flops | bytes accessed | tf_op | source)
XLA Modules:
  0.0 177.7 jit_solution(16514646502350003951)
XLA Ops:
  0.7 1.2 copy.172
  1.8 0.6 reshape.573
  2.7 0.2 reduce_window_sum.80
  2.8 0.2 select_reduce_fusion.1
  3.1 1.0 reshape.574
  4.1 1.1 convolution_convert_fusion.1
  5.1 7.6 %all-to-all-start = ((bf16[8,32,640]{2,1,0:T(8,128)(2,1)}), bf16[8,32,640]{2,1,0:T(8,128)(2,1)S(1)}, u32[]{:S(2)}, u32[]{:S(2)}) async-start(bf16[8,32,640]{2,1,0:T(8,128)(2,1)} %bitcast.20), calls=%async_computation | async-start | bytes 655360 | tf_op jit(solution)/shard_map/all_to_all | solution.py:101
  13.4 0.7 negate_multiply_fusion
  14.1 1.2 reduce-window.16
  15.5 2.5 %select_reduce_fusion = s32[8,128]{0,1:T(8,128)S(1)} fusion(s32[8,128]{0,1:T(8,128)S(1)} %copy.178), kind=kOutput, calls=%fused_computation.46 | output fusion | flops 1096704 | bytes 8192 | tf_op jit(solution)/shard_map/jit(cumsum)/reduce_window_sum | solution.py:23
  18.1 0.7 reshape.561
  18.8 1.2 reduce-window.14
  20.8 0.2 slice_reduce_fusion
  21.0 0.2 slice_reduce_fusion.1
  21.1 0.8 copy_bitcast_fusion.1
  21.9 0.2 broadcast_in_dim.141
  22.1 0.7 copy.180
  23.4 1.3 fusion.16
  24.9 0.6 pad_maximum_fusion.1
  25.6 4.0 %collective-permute-start.3 = (bf16[8,32,640]{2,1,0:T(8,128)(2,1)S(1)}, bf16[8,32,640]{2,1,0:T(8,128)(2,1)S(1)}, u32[]{:S(2)}, u32[]{:S(2)}) collective-permute-start(bf16[8,32,640]{2,1,0:T(8,128)(2,1)S(1)} %all-to-all-done), channel_id=1, source_target_pairs={{0,64},{64,128},{128,192},{192,256},{256,320},{320,384},{384,448},... | collective-permute-start | bytes 983048 | tf_op jit(solution)/shard_map/ppermute | solution.py:66
  29.6 8.6 %collective-permute-start = (bf16[8,32,640]{2,1,0:T(8,128)(2,1)S(1)}, bf16[8,32,640]{2,1,0:T(8,128)(2,1)S(1)}, u32[]{:S(2)}, u32[]{:S(2)}) collective-permute-start(bf16[8,32,640]{2,1,0:T(8,128)(2,1)S(1)} %all-to-all-done), channel_id=1, source_target_pairs={{0,448},{64,0},{128,64},{192,128},{256,192},{320,256},{384,320},{4... | collective-permute-start | bytes 983048 | tf_op jit(solution)/shard_map/ppermute | solution.py:69
  38.2 0.7 iota_compare_fusion.2
  38.9 4.0 %collective-permute-done.3 = bf16[8,32,640]{2,1,0:T(8,128)(2,1)S(1)} collective-permute-done((bf16[8,32,640]{2,1,0:T(8,128)(2,1)S(1)}, bf16[8,32,640]{2,1,0:T(8,128)(2,1)S(1)}, u32[]{:S(2)}, u32[]{:S(2)}) %collective-permute-start.3) | collective-permute-done | bytes 327712 | tf_op jit(solution)/shard_map/ppermute | solution.py:66
  42.9 1.9 %collective-permute-start.4 = (bf16[8,32,640]{2,1,0:T(8,128)(2,1)S(1)}, bf16[8,32,640]{2,1,0:T(8,128)(2,1)S(1)}, u32[]{:S(2)}, u32[]{:S(2)}) collective-permute-start(bf16[8,32,640]{2,1,0:T(8,128)(2,1)S(1)} %collective-permute-done.3), channel_id=1, source_target_pairs={{0,64},{64,128},{128,192},{192,256},{256,320},{320,384},{384,448},... | collective-permute-start | bytes 983048 | tf_op jit(solution)/shard_map/ppermute | solution.py:66
  44.8 4.6 %collective-permute-start.1 = (bf16[8,32,640]{2,1,0:T(8,128)(2,1)S(1)}, bf16[8,32,640]{2,1,0:T(8,128)(2,1)S(1)}, u32[]{:S(2)}, u32[]{:S(2)}) collective-permute-start(bf16[8,32,640]{2,1,0:T(8,128)(2,1)S(1)} %collective-permute-done), channel_id=1, source_target_pairs={{0,448},{64,0},{128,64},{192,128},{256,192},{320,256},{384,320},{4... | collective-permute-start | bytes 983048 | tf_op jit(solution)/shard_map/ppermute | solution.py:69
  49.4 3.8 %collective-permute-done.4 = bf16[8,32,640]{2,1,0:T(8,128)(2,1)S(1)} collective-permute-done((bf16[8,32,640]{2,1,0:T(8,128)(2,1)S(1)}, bf16[8,32,640]{2,1,0:T(8,128)(2,1)S(1)}, u32[]{:S(2)}, u32[]{:S(2)}) %collective-permute-start.4) | collective-permute-done | bytes 327712 | tf_op jit(solution)/shard_map/ppermute | solution.py:66
  53.2 1.9 %collective-permute-start.5 = (bf16[8,32,640]{2,1,0:T(8,128)(2,1)S(1)}, bf16[8,32,640]{2,1,0:T(8,128)(2,1)S(1)}, u32[]{:S(2)}, u32[]{:S(2)}) collective-permute-start(bf16[8,32,640]{2,1,0:T(8,128)(2,1)S(1)} %collective-permute-done.4), channel_id=1, source_target_pairs={{0,64},{64,128},{128,192},{192,256},{256,320},{320,384},{384,448},... | collective-permute-start | bytes 983048 | tf_op jit(solution)/shard_map/ppermute | solution.py:66
  55.2 4.6 %collective-permute-start.2 = (bf16[8,32,640]{2,1,0:T(8,128)(2,1)S(1)}, bf16[8,32,640]{2,1,0:T(8,128)(2,1)S(1)}, u32[]{:S(2)}, u32[]{:S(2)}) collective-permute-start(bf16[8,32,640]{2,1,0:T(8,128)(2,1)S(1)} %collective-permute-done.1), channel_id=1, source_target_pairs={{0,448},{64,0},{128,64},{192,128},{256,192},{320,256},{384,320},{4... | collective-permute-start | bytes 983048 | tf_op jit(solution)/shard_map/ppermute | solution.py:69
  59.8 2.9 %collective-permute-done.5 = bf16[8,32,640]{2,1,0:T(8,128)(2,1)S(1)} collective-permute-done((bf16[8,32,640]{2,1,0:T(8,128)(2,1)S(1)}, bf16[8,32,640]{2,1,0:T(8,128)(2,1)S(1)}, u32[]{:S(2)}, u32[]{:S(2)}) %collective-permute-start.5) | collective-permute-done | bytes 327712 | tf_op jit(solution)/shard_map/ppermute | solution.py:66
  62.7 1.9 %collective-permute-start.6 = (bf16[8,32,640]{2,1,0:T(8,128)(2,1)S(1)}, bf16[8,32,640]{2,1,0:T(8,128)(2,1)S(1)}, u32[]{:S(2)}, u32[]{:S(2)}) collective-permute-start(bf16[8,32,640]{2,1,0:T(8,128)(2,1)S(1)} %collective-permute-done.5), channel_id=1, source_target_pairs={{0,64},{64,128},{128,192},{192,256},{256,320},{320,384},{384,448},... | collective-permute-start | bytes 983048 | tf_op jit(solution)/shard_map/ppermute | solution.py:66
  64.7 7.0 %collective-permute-done.6 = bf16[8,32,640]{2,1,0:T(8,128)(2,1)S(1)} collective-permute-done((bf16[8,32,640]{2,1,0:T(8,128)(2,1)S(1)}, bf16[8,32,640]{2,1,0:T(8,128)(2,1)S(1)}, u32[]{:S(2)}, u32[]{:S(2)}) %collective-permute-start.6) | collective-permute-done | bytes 327712 | tf_op jit(solution)/shard_map/ppermute | solution.py:66
  72.3 0.6 multiply_reduce_fusion
  73.1 1.8 %convolution_convert_fusion = bf16[8,256,512]{2,1,0:T(8,128)(2,1)S(1)} fusion(bf16[8,256,640]{2,1,0:T(8,128)(2,1)S(1)} %bitcast.239, bf16[1,640,512]{2,1,0:T(8,128)(2,1)S(1)} %copy-done), kind=kOutput, calls=%fused_computation.4 | convolution fusion | flops 1343225856 | bytes 5373952 | tf_op jit(solution)/shard_map/dot_general | solution.py:135
  74.9 1.5 pad_maximum_fusion
  76.4 9.2 %all-to-all-start.1 = ((bf16[8,257,512]{2,1,0:T(8,128)(2,1)}), bf16[8,257,512]{2,1,0:T(8,128)(2,1)S(1)}, u32[]{:S(2)}, u32[]{:S(2)}) async-start(bf16[8,257,512]{2,1,0:T(8,128)(2,1)} %pad_maximum_fusion), calls=%async_computation.1 | async-start | bytes 4325376 | tf_op jit(solution)/shard_map/all_to_all | solution.py:145
  85.6 1.3 convolution_multiply_fusion.1
  87.0 1.0 copy-done.1
  87.9 1.3 convolution_bitcast_fusion.7
  89.3 31.9 %all-gather = bf16[32,1,66,128]{3,2,1,0:T(8,128)(2,1)S(1)} all-gather(bf16[4,1,66,128]{3,2,1,0:T(8,128)(2,1)} %bitcast.252), channel_id=2, replica_groups=mesh['tz'=8,'ty'=8,'seq'=8] {'seq'}, dimensions={0}, use_global_device_ids=true | all-gather | bytes 608256 | tf_op jit(solution)/shard_map/all_gather | solution.py:127
  121.2 0.8 copy-done.4
  122.3 0.2 select_reduce_fusion.2
  122.5 0.3 convert_reduce_fusion
  122.9 0.8 copy.182
  123.8 10.0 %all-to-all-start.2 = ((bf16[64,256,8]{1,2,0:T(8,128)(2,1)}), bf16[64,256,8]{1,2,0:T(8,128)(2,1)S(1)}, u32[]{:S(2)}, u32[]{:S(2)}) async-start(bf16[64,256,8]{1,2,0:T(8,128)(2,1)} %bitcast.44), calls=%async_computation.2 | async-start | bytes 524288 | tf_op jit(solution)/shard_map/all_to_all | solution.py:153
  134.0 1.2 multiply_reduce_fusion.2
  135.2 11.8 %all-to-all-done.2 = bf16[64,256,8]{1,2,0:T(8,128)(2,1)S(1)} async-done(((bf16[64,256,8]{1,2,0:T(8,128)(2,1)}), bf16[64,256,8]{1,2,0:T(8,128)(2,1)S(1)}, u32[]{:S(2)}, u32[]{:S(2)}) %all-to-all-start.2) | async-done | bytes 262176 | tf_op jit(solution)/shard_map/all_to_all | solution.py:153
  147.1 0.3 copy.183
  147.3 3.2 %gather_fusion = bf16[1024,64]{1,0:T(8,128)(2,1)S(1)} fusion(bf16[2048,64]{1,0:T(8,128)(2,1)S(1)} %copy.183, s32[1024]{0:T(1024)S(1)} %broadcast_clamp_fusion), kind=kCustom, calls=%fused_computation | custom fusion | bytes 266240 | tf_op jit(solution)/shard_map/jit(_take)/gather | solution.py:164
  150.6 0.2 copy.184
  150.7 0.4 fusion.13
  151.2 1.8 %convolution_multiply_fusion = f32[4,256,256]{2,1,0:T(8,128)S(1)} fusion(f32[4,256]{1,0:T(4,128)} %copy-done.10, s32[4,256]{1,0:T(4,128)} %bitcast.256, pred[256,256]{1,0:T(8,128)(4,1)} %iota_compare_fusion.2, f32[256,4,1,64]{0,3,1,2:T(8,128)S(1)} %fusion.13, bf16[256,4,1,64]{0,3,2,1:T(8,128)(2,1)S(1)} %copy-done.5, f32[256,4]{0,1:T(4,128)S(1)} %get-tuple-element.37), kind=kOutput, calls=%fused_computation.5 | convolution fusion | flops 102367232 | bytes 1519616 | tf_op jit(solution)/shard_map/ibhp,jbhp->bhij/dot_general | solution.py:191
  153.0 0.3 fusion.17
  153.3 2.2 %convolution_bitcast_fusion.1 = f32[256,4,1,128]{3,0,1,2:T(8,128)} fusion(f32[4,256,256]{2,1,0:T(8,128)S(1)} %convolution_multiply_fusion, bf16[256,4,128]{2,1,0:T(4,128)(2,1)} %bitcast.249), kind=kOutput, calls=%fused_computation.8 | convolution fusion | flops 201326592 | bytes 1835008 | tf_op jit(solution)/shard_map/bhij,jbhn->ibhn/dot_general | solution.py:196
  155.5 0.9 broadcast_in_dim.148
  156.4 6.5 %all-to-all-start.3 = ((bf16[8,4,1,128,64]{3,4,2,1,0:T(8,128)(2,1)}), bf16[8,4,1,128,64]{3,4,2,1,0:T(8,128)(2,1)}, u32[]{:S(2)}, u32[]{:S(2)}) async-start(bf16[8,4,1,128,64]{3,4,2,1,0:T(8,128)(2,1)} %broadcast_in_dim.148), calls=%async_computation.3 | async-start | bytes 1048576 | tf_op jit(solution)/shard_map/all_to_all | solution.py:178
  162.9 2.1 %fusion.4 = bf16[256,4,1,128]{3,0,1,2:T(8,128)(2,1)S(1)} fusion(f32[256,4,1,128]{3,0,1,2:T(8,128)} %convolution_bitcast_fusion.1, f32[4,64,128]{2,1,0:T(8,128)S(1)} %multiply_reduce_fusion.2, f32[256,4,1,64]{0,3,1,2:T(8,128)S(1)} %fusion.13, f32[256,4]{0,1:T(4,128)S(1)} %get-tuple-element.25), kind=kOutput, calls=%fused_computation.16 | convolution fusion | flops 101056512 | bytes 1183744 | tf_op jit(solution)/shard_map/ibhp,bhpn->ibhn/dot_general | solution.py:197
  165.1 0.9 copy.195
  166.0 1.1 convolution_bitcast_fusion.6
  167.1 0.8 convolution_bitcast_fusion.3
  167.9 4.5 %all-to-all-done.3 = bf16[8,4,1,128,64]{3,4,2,1,0:T(8,128)(2,1)} async-done(((bf16[8,4,1,128,64]{3,4,2,1,0:T(8,128)(2,1)}), bf16[8,4,1,128,64]{3,4,2,1,0:T(8,128)(2,1)}, u32[]{:S(2)}, u32[]{:S(2)}) %all-to-all-start.3) | async-done | bytes 524320 | tf_op jit(solution)/shard_map/all_to_all | solution.py:178
  172.4 1.2 multiply_reduce_fusion.1
  173.6 1.1 fusion.5
  174.7 0.9 copy.194
  175.6 2.1 %fusion.15 = bf16[256,4,1,64]{0,3,2,1:T(8,128)(2,1)} fusion(f32[256,4,1,64]{0,3,1,2:T(8,128)} %convolution_bitcast_fusion.6, f32[4,128,64]{1,2,0:T(8,128)S(1)} %multiply_reduce_fusion.1, f32[256,4,1,64]{0,3,1,2:T(8,128)S(1)} %fusion.13, bf16[256,4,128]{2,1,0:T(4,128)(2,1)} %bitcast.250, f32[256,4]{0,1:T(4,128)S(1)} %get-tuple-element.38, f32[]{:T(128)} %bitcast.238, ...), kind=kOutput, calls=%fused_computation.31 | convolution fusion | flops 101056512 | bytes 1056772 | tf_op jit(solution)/shard_map/jbhn,bhnp->jbhp/dot_general | solution.py:187
  (87 shorter events, 2.9 us)
Async XLA Ops:
  0.6 72.4 %copy-start = (bf16[1,640,512]{2,1,0:T(8,128)(2,1)S(1)}, bf16[1,640,512]{2,1,0:T(8,128)(2,1)}, u32[]{:S(2)}) copy-start(bf16[1,640,512]{2,1,0:T(8,128)(2,1)} %param.11) | copy-start | bytes 1966084
  5.1 20.4 %all-to-all-start = ((bf16[8,32,640]{2,1,0:T(8,128)(2,1)}), bf16[8,32,640]{2,1,0:T(8,128)(2,1)S(1)}, u32[]{:S(2)}, u32[]{:S(2)}) async-start(bf16[8,32,640]{2,1,0:T(8,128)(2,1)} %bitcast.20), calls=%async_computation | async-start | bytes 655360 | tf_op jit(solution)/shard_map/all_to_all | solution.py:101
  20.7 64.8 %copy-start.8 = (s32[1,4,2,128]{3,1,2,0:T(4,128)}, s32[1,4,2,128]{3,1,2,0:T(4,128)S(1)}, u32[]{:S(2)}) copy-start(s32[1,4,2,128]{3,1,2,0:T(4,128)S(1)} %copy.231) | copy-start | bytes 12292
  25.6 17.3 %collective-permute-start.3 = (bf16[8,32,640]{2,1,0:T(8,128)(2,1)S(1)}, bf16[8,32,640]{2,1,0:T(8,128)(2,1)S(1)}, u32[]{:S(2)}, u32[]{:S(2)}) collective-permute-start(bf16[8,32,640]{2,1,0:T(8,128)(2,1)S(1)} %all-to-all-done), channel_id=1, source_target_pairs={{0,64},{64,128},{128,192},{192,256},{256,320},{320,384},{384,448},... | collective-permute-start | bytes 983048 | tf_op jit(solution)/shard_map/ppermute | solution.py:66
  29.6 15.2 %collective-permute-start = (bf16[8,32,640]{2,1,0:T(8,128)(2,1)S(1)}, bf16[8,32,640]{2,1,0:T(8,128)(2,1)S(1)}, u32[]{:S(2)}, u32[]{:S(2)}) collective-permute-start(bf16[8,32,640]{2,1,0:T(8,128)(2,1)S(1)} %all-to-all-done), channel_id=1, source_target_pairs={{0,448},{64,0},{128,64},{192,128},{256,192},{320,256},{384,320},{4... | collective-permute-start | bytes 983048 | tf_op jit(solution)/shard_map/ppermute | solution.py:69
  42.9 10.3 %collective-permute-start.4 = (bf16[8,32,640]{2,1,0:T(8,128)(2,1)S(1)}, bf16[8,32,640]{2,1,0:T(8,128)(2,1)S(1)}, u32[]{:S(2)}, u32[]{:S(2)}) collective-permute-start(bf16[8,32,640]{2,1,0:T(8,128)(2,1)S(1)} %collective-permute-done.3), channel_id=1, source_target_pairs={{0,64},{64,128},{128,192},{192,256},{256,320},{320,384},{384,448},... | collective-permute-start | bytes 983048 | tf_op jit(solution)/shard_map/ppermute | solution.py:66
  44.8 40.8 %copy-start.10 = (f32[4,256]{1,0:T(4,128)}, f32[4,256]{1,0:T(4,128)S(1)}, u32[]{:S(2)}) copy-start(f32[4,256]{1,0:T(4,128)S(1)} %bitcast_add_fusion) | copy-start | bytes 12292
  44.8 10.4 %collective-permute-start.1 = (bf16[8,32,640]{2,1,0:T(8,128)(2,1)S(1)}, bf16[8,32,640]{2,1,0:T(8,128)(2,1)S(1)}, u32[]{:S(2)}, u32[]{:S(2)}) collective-permute-start(bf16[8,32,640]{2,1,0:T(8,128)(2,1)S(1)} %collective-permute-done), channel_id=1, source_target_pairs={{0,448},{64,0},{128,64},{192,128},{256,192},{320,256},{384,320},{4... | collective-permute-start | bytes 983048 | tf_op jit(solution)/shard_map/ppermute | solution.py:69
  53.2 9.5 %collective-permute-start.5 = (bf16[8,32,640]{2,1,0:T(8,128)(2,1)S(1)}, bf16[8,32,640]{2,1,0:T(8,128)(2,1)S(1)}, u32[]{:S(2)}, u32[]{:S(2)}) collective-permute-start(bf16[8,32,640]{2,1,0:T(8,128)(2,1)S(1)} %collective-permute-done.4), channel_id=1, source_target_pairs={{0,64},{64,128},{128,192},{192,256},{256,320},{320,384},{384,448},... | collective-permute-start | bytes 983048 | tf_op jit(solution)/shard_map/ppermute | solution.py:66
  55.2 9.5 %collective-permute-start.2 = (bf16[8,32,640]{2,1,0:T(8,128)(2,1)S(1)}, bf16[8,32,640]{2,1,0:T(8,128)(2,1)S(1)}, u32[]{:S(2)}, u32[]{:S(2)}) collective-permute-start(bf16[8,32,640]{2,1,0:T(8,128)(2,1)S(1)} %collective-permute-done.1), channel_id=1, source_target_pairs={{0,448},{64,0},{128,64},{192,128},{256,192},{320,256},{384,320},{4... | collective-permute-start | bytes 983048 | tf_op jit(solution)/shard_map/ppermute | solution.py:69
  62.7 9.0 %collective-permute-start.6 = (bf16[8,32,640]{2,1,0:T(8,128)(2,1)S(1)}, bf16[8,32,640]{2,1,0:T(8,128)(2,1)S(1)}, u32[]{:S(2)}, u32[]{:S(2)}) collective-permute-start(bf16[8,32,640]{2,1,0:T(8,128)(2,1)S(1)} %collective-permute-done.5), channel_id=1, source_target_pairs={{0,64},{64,128},{128,192},{192,256},{256,320},{320,384},{384,448},... | collective-permute-start | bytes 983048 | tf_op jit(solution)/shard_map/ppermute | solution.py:66
  74.9 10.7 %copy-start.3 = (bf16[256,4,1,128]{3,1,2,0:T(4,128)(2,1)S(1)}, bf16[256,4,1,128]{3,1,2,0:T(4,128)(2,1)}, u32[]{:S(2)}) copy-start(bf16[256,4,1,128]{3,1,2,0:T(4,128)(2,1)} %param.15) | copy-start | bytes 786436
  74.9 10.7 %copy-start.6 = (bf16[256,4,1,128]{3,1,2,0:T(4,128)(2,1)S(1)}, bf16[256,4,1,128]{3,1,2,0:T(4,128)(2,1)}, u32[]{:S(2)}) copy-start(bf16[256,4,1,128]{3,1,2,0:T(4,128)(2,1)} %param.14) | copy-start | bytes 786436
  74.9 13.1 %copy-start.5 = (bf16[256,4,1,64]{0,3,2,1:T(8,128)(2,1)S(1)}, bf16[256,4,1,64]{0,3,2,1:T(8,128)(2,1)}, u32[]{:S(2)}) copy-start(bf16[256,4,1,64]{0,3,2,1:T(8,128)(2,1)} %param.13) | copy-start | bytes 393220
  76.4 46.1 %all-to-all-start.1 = ((bf16[8,257,512]{2,1,0:T(8,128)(2,1)}), bf16[8,257,512]{2,1,0:T(8,128)(2,1)S(1)}, u32[]{:S(2)}, u32[]{:S(2)}) async-start(bf16[8,257,512]{2,1,0:T(8,128)(2,1)} %pad_maximum_fusion), calls=%async_computation.1 | async-start | bytes 4325376 | tf_op jit(solution)/shard_map/all_to_all | solution.py:145
  86.9 1.0 copy-start.1
  87.9 62.8 %copy-start.9 = (pred[256,4]{0,1:T(4,128)(4,1)S(1)}, pred[256,4]{0,1:T(4,128)(4,1)}, u32[]{:S(2)}) copy-start(pred[256,4]{0,1:T(4,128)(4,1)} %copy.180) | copy-start | bytes 3076
  121.2 0.8 copy-start.4
  122.8 27.9 %copy-start.7 = (f32[256,4,1,64]{0,3,1,2:T(8,128)S(1)}, f32[256,4,1,64]{0,3,1,2:T(8,128)}, u32[]{:S(2)}) copy-start(f32[256,4,1,64]{0,3,1,2:T(8,128)} %convolution_bitcast_fusion.7) | copy-start | bytes 786436
  123.8 23.3 %all-to-all-start.2 = ((bf16[64,256,8]{1,2,0:T(8,128)(2,1)}), bf16[64,256,8]{1,2,0:T(8,128)(2,1)S(1)}, u32[]{:S(2)}, u32[]{:S(2)}) async-start(bf16[64,256,8]{1,2,0:T(8,128)(2,1)} %bitcast.44), calls=%async_computation.2 | async-start | bytes 524288 | tf_op jit(solution)/shard_map/all_to_all | solution.py:153
  150.6 15.4 %copy-start.2 = (f32[4,256,256]{2,1,0:T(8,128)S(1)}, f32[4,256,256]{2,1,0:T(8,128)}, u32[]{:S(2)}) copy-start(f32[4,256,256]{2,1,0:T(8,128)} %copy-done.1) | copy-start | bytes 3145732
  156.4 16.0 %all-to-all-start.3 = ((bf16[8,4,1,128,64]{3,4,2,1,0:T(8,128)(2,1)}), bf16[8,4,1,128,64]{3,4,2,1,0:T(8,128)(2,1)}, u32[]{:S(2)}, u32[]{:S(2)}) async-start(bf16[8,4,1,128,64]{3,4,2,1,0:T(8,128)(2,1)} %broadcast_in_dim.148), calls=%async_computation.3 | async-start | bytes 1048576 | tf_op jit(solution)/shard_map/all_to_all | solution.py:178

commit v9 on v8

--- a/solution.py
+++ b/solution.py
@@ -123,8 +123,13 @@
         ],
         axis=2,
     )
-    packed_state = lax.optimization_barrier((packed_state, received))[0]
-    gathered = lax.all_gather(packed_state, "seq")
+    gathered = lax.all_to_all(
+        jnp.broadcast_to(packed_state[None], (seq_n,) + packed_state.shape),
+        "seq",
+        split_axis=0,
+        concat_axis=0,
+        tiled=True,
+    )
     rows = local_state.shape[2]
     through_all = gathered[:, :, :, rows, 0].astype(jnp.float32) + gathered[
         :, :, :, rows + 1, 0

time: 179 us -> 176 us (0.983)
  blocking collectives: 31.9 us -> 0 us
  waiting for transfers between devices: 34 us -> 55.2 us
  starting transfers between devices: 60.7 us -> 65.3 us
  other arithmetic: 13.7 us -> 16.3 us
    all_gather x1 -> x0, blocking collectives: 31.9 us -> none  [per_device(): gathered = lax.all_gather(packed_state, 'seq')]
    all_to_all x1, waiting for transfers between devices: 0.01 us -> 21.5 us  [per_device(): lax.all_to_all(outbound, 'seq', split_axis=0, concat_axis=0, tiled=True)]
    all_to_all x0 -> x1, starting transfers between devices: none -> 7.86 us  [per_device(): lax.all_to_all(jnp.broadcast_to(packed_state[None], (seq_n,) + packed_sta...]
    all_to_all x1, starting transfers between devices: 10 us -> 7.03 us  [per_device(): lax.all_to_all(outgoing, TEACH, split_axis=0, concat_axis=0, tiled=True)]
    all_to_all x1, starting transfers between devices: 9.16 us -> 6.66 us  [per_device(): lax.all_to_all(outbound, 'seq', split_axis=0, concat_axis=0, tiled=True)]
    all_to_all x1, waiting for transfers between devices: 11.8 us -> 9.66 us  [per_device(): lax.all_to_all(outgoing, TEACH, split_axis=0, concat_axis=0, tiled=True)]
    unnamed x44 -> x46, local copies, waits for them, and re-layouts: 5.75 us -> 4.96 us
  transfers between devices with their start and end apart: 11 -> 12, of which waited for: 6 -> 9; matrix products, arithmetic and copies ran while one was open for 12% -> 17% of each run, Pallas kernels for 0% -> 0%
where the time goes in v9:
time: 176 us; the launch traced here: 174 us
  starting transfers between devices  65.3 us (37%)
  waiting for transfers between devices  55.2 us (31%)
  matrix products  18.2 us (10%)
  local copies, waits for them, and re-layouts  16.8 us (10%)
  other arithmetic  16.3 us (9%)
  between operations  2.51 us (1%)
    all_to_all x1, waiting for transfers between devices, per_device(): lax.all_to_all(outbound, 'seq', split_axis=0, concat_axis=0, tiled=True)  21.5 us
    ppermute x3, starting transfers between devices, ring_gather(): ccw = lax.ppermute(ccw, axis, behind)  19.2 us
    ppermute x4, waiting for transfers between devices, ring_gather(): cw = lax.ppermute(cw, axis, ahead)  19.1 us
    ppermute x4, starting transfers between devices, ring_gather(): cw = lax.ppermute(cw, axis, ahead)  9.71 us
    all_to_all x1, waiting for transfers between devices, per_device(): lax.all_to_all(outgoing, TEACH, split_axis=0, concat_axis=0, tiled=True)  9.66 us
    all_to_all x1, starting transfers between devices, per_device(): lax.all_to_all(jnp.broadcast_to(packed_state[None], (seq_n,) + packed_sta...  7.86 us
    all_to_all x1, starting transfers between devices, per_device(): lax.all_to_all(packed, 'ty', split_axis=0, concat_axis=0, tiled=True)  7.64 us
    all_to_all x1, starting transfers between devices, per_device(): lax.all_to_all(jnp.broadcast_to(local_adjoint.astype(jnp.bfloat16)[None],...  7.19 us
  transfers between devices with their start and end apart: 12, of which 9 were waited for; matrix products, arithmetic and copies ran while one was open for 17% of the time, Pallas kernels for 0%

profile of v9, /device:TPU:1, one launch (start us, length us, event | category | flops | bytes accessed | tf_op | source)
XLA Modules:
  0.0 174.3 jit_solution(2244613188238560363)
XLA Ops:
  0.7 1.2 copy.217
  1.8 0.6 reshape.568
  3.1 1.0 reshape.569
  4.1 1.1 convolution_convert_fusion.1
  5.1 7.6 %all-to-all-start.1 = ((bf16[8,32,640]{2,1,0:T(8,128)(2,1)}), bf16[8,32,640]{2,1,0:T(8,128)(2,1)S(1)}, u32[]{:S(2)}, u32[]{:S(2)}) async-start(bf16[8,32,640]{2,1,0:T(8,128)(2,1)} %bitcast.28), calls=%async_computation.1 | async-start | bytes 655360 | tf_op jit(solution)/shard_map/all_to_all | solution.py:101
  13.4 0.7 negate_multiply_fusion
  14.1 1.2 reduce-window.16
  15.5 2.5 %select_reduce_fusion = s32[8,128]{0,1:T(8,128)S(1)} fusion(s32[8,128]{0,1:T(8,128)S(1)} %copy.218), kind=kOutput, calls=%fused_computation.46 | output fusion | flops 1096704 | bytes 8192 | tf_op jit(solution)/shard_map/jit(cumsum)/reduce_window_sum | solution.py:23
  18.0 0.7 reshape.556
  18.7 1.2 reduce-window.14
  21.1 0.8 copy_bitcast_fusion.1
  21.9 1.3 fusion.16
  23.4 0.9 broadcast_in_dim.147
  24.4 7.9 %all-to-all-start = ((bf16[8,4,1,66,128]{4,1,3,2,0:T(4,128)(2,1)}), bf16[8,4,1,66,128]{4,1,3,2,0:T(4,128)(2,1)}, u32[]{:S(2)}, u32[]{:S(2)}) async-start(bf16[8,4,1,66,128]{4,1,3,2,0:T(4,128)(2,1)} %broadcast_in_dim.147), calls=%async_computation | async-start | bytes 1081344 | tf_op jit(solution)/shard_map/all_to_all | solution.py:126
  32.2 4.0 %collective-permute-start.3 = (bf16[8,32,640]{2,1,0:T(8,128)(2,1)S(1)}, bf16[8,32,640]{2,1,0:T(8,128)(2,1)S(1)}, u32[]{:S(2)}, u32[]{:S(2)}) collective-permute-start(bf16[8,32,640]{2,1,0:T(8,128)(2,1)S(1)} %all-to-all-done.1), channel_id=1, source_target_pairs={{0,64},{64,128},{128,192},{192,256},{256,320},{320,384},{384,448},... | collective-permute-start | bytes 983048 | tf_op jit(solution)/shard_map/ppermute | solution.py:66
  36.4 0.6 copy.220
  37.7 8.6 %collective-permute-start = (bf16[8,32,640]{2,1,0:T(8,128)(2,1)S(1)}, bf16[8,32,640]{2,1,0:T(8,128)(2,1)S(1)}, u32[]{:S(2)}, u32[]{:S(2)}) collective-permute-start(bf16[8,32,640]{2,1,0:T(8,128)(2,1)S(1)} %all-to-all-done.1), channel_id=1, source_target_pairs={{0,448},{64,0},{128,64},{192,128},{256,192},{320,256},{384,320},{4... | collective-permute-start | bytes 983048 | tf_op jit(solution)/shard_map/ppermute | solution.py:69
  46.3 0.7 iota_compare_fusion.2
  46.9 4.0 %collective-permute-done.3 = bf16[8,32,640]{2,1,0:T(8,128)(2,1)S(1)} collective-permute-done((bf16[8,32,640]{2,1,0:T(8,128)(2,1)S(1)}, bf16[8,32,640]{2,1,0:T(8,128)(2,1)S(1)}, u32[]{:S(2)}, u32[]{:S(2)}) %collective-permute-start.3) | collective-permute-done | bytes 327712 | tf_op jit(solution)/shard_map/ppermute | solution.py:66
  51.0 1.9 %collective-permute-start.4 = (bf16[8,32,640]{2,1,0:T(8,128)(2,1)S(1)}, bf16[8,32,640]{2,1,0:T(8,128)(2,1)S(1)}, u32[]{:S(2)}, u32[]{:S(2)}) collective-permute-start(bf16[8,32,640]{2,1,0:T(8,128)(2,1)S(1)} %collective-permute-done.3), channel_id=1, source_target_pairs={{0,64},{64,128},{128,192},{192,256},{256,320},{320,384},{384,448},... | collective-permute-start | bytes 983048 | tf_op jit(solution)/shard_map/ppermute | solution.py:66
  53.0 0.4 collective-permute-done
  53.3 5.3 %collective-permute-start.1 = (bf16[8,32,640]{2,1,0:T(8,128)(2,1)S(1)}, bf16[8,32,640]{2,1,0:T(8,128)(2,1)S(1)}, u32[]{:S(2)}, u32[]{:S(2)}) collective-permute-start(bf16[8,32,640]{2,1,0:T(8,128)(2,1)S(1)} %collective-permute-done), channel_id=1, source_target_pairs={{0,448},{64,0},{128,64},{192,128},{256,192},{320,256},{384,320},{4... | collective-permute-start | bytes 983048 | tf_op jit(solution)/shard_map/ppermute | solution.py:69
  58.6 0.6 iota_compare_fusion.8
  59.2 3.5 %collective-permute-done.4 = bf16[8,32,640]{2,1,0:T(8,128)(2,1)S(1)} collective-permute-done((bf16[8,32,640]{2,1,0:T(8,128)(2,1)S(1)}, bf16[8,32,640]{2,1,0:T(8,128)(2,1)S(1)}, u32[]{:S(2)}, u32[]{:S(2)}) %collective-permute-start.4) | collective-permute-done | bytes 327712 | tf_op jit(solution)/shard_map/ppermute | solution.py:66
  62.8 1.9 %collective-permute-start.5 = (bf16[8,32,640]{2,1,0:T(8,128)(2,1)S(1)}, bf16[8,32,640]{2,1,0:T(8,128)(2,1)S(1)}, u32[]{:S(2)}, u32[]{:S(2)}) collective-permute-start(bf16[8,32,640]{2,1,0:T(8,128)(2,1)S(1)} %collective-permute-done.4), channel_id=1, source_target_pairs={{0,64},{64,128},{128,192},{192,256},{256,320},{320,384},{384,448},... | collective-permute-start | bytes 983048 | tf_op jit(solution)/shard_map/ppermute | solution.py:66
  64.8 5.3 %collective-permute-start.2 = (bf16[8,32,640]{2,1,0:T(8,128)(2,1)S(1)}, bf16[8,32,640]{2,1,0:T(8,128)(2,1)S(1)}, u32[]{:S(2)}, u32[]{:S(2)}) collective-permute-start(bf16[8,32,640]{2,1,0:T(8,128)(2,1)S(1)} %collective-permute-done.1), channel_id=1, source_target_pairs={{0,448},{64,0},{128,64},{192,128},{256,192},{320,256},{384,320},{4... | collective-permute-start | bytes 983048 | tf_op jit(solution)/shard_map/ppermute | solution.py:69
  70.2 3.5 %collective-permute-done.5 = bf16[8,32,640]{2,1,0:T(8,128)(2,1)S(1)} collective-permute-done((bf16[8,32,640]{2,1,0:T(8,128)(2,1)S(1)}, bf16[8,32,640]{2,1,0:T(8,128)(2,1)S(1)}, u32[]{:S(2)}, u32[]{:S(2)}) %collective-permute-start.5) | collective-permute-done | bytes 327712 | tf_op jit(solution)/shard_map/ppermute | solution.py:66
  73.7 1.9 %collective-permute-start.6 = (bf16[8,32,640]{2,1,0:T(8,128)(2,1)S(1)}, bf16[8,32,640]{2,1,0:T(8,128)(2,1)S(1)}, u32[]{:S(2)}, u32[]{:S(2)}) collective-permute-start(bf16[8,32,640]{2,1,0:T(8,128)(2,1)S(1)} %collective-permute-done.5), channel_id=1, source_target_pairs={{0,64},{64,128},{128,192},{192,256},{256,320},{320,384},{384,448},... | collective-permute-start | bytes 983048 | tf_op jit(solution)/shard_map/ppermute | solution.py:66
  75.7 8.0 %collective-permute-done.6 = bf16[8,32,640]{2,1,0:T(8,128)(2,1)S(1)} collective-permute-done((bf16[8,32,640]{2,1,0:T(8,128)(2,1)S(1)}, bf16[8,32,640]{2,1,0:T(8,128)(2,1)S(1)}, u32[]{:S(2)}, u32[]{:S(2)}) %collective-permute-start.6) | collective-permute-done | bytes 327712 | tf_op jit(solution)/shard_map/ppermute | solution.py:66
  84.3 0.6 multiply_reduce_fusion
  85.1 1.8 %convolution_convert_fusion = bf16[8,256,512]{2,1,0:T(8,128)(2,1)S(1)} fusion(bf16[8,256,640]{2,1,0:T(8,128)(2,1)S(1)} %bitcast.237, bf16[1,640,512]{2,1,0:T(8,128)(2,1)S(1)} %copy-done), kind=kOutput, calls=%fused_computation.4 | convolution fusion | flops 1343225856 | bytes 5373952 | tf_op jit(solution)/shard_map/dot_general | solution.py:140
  86.9 1.5 pad_maximum_fusion
  88.5 6.7 %all-to-all-start.2 = ((bf16[8,257,512]{2,1,0:T(8,128)(2,1)}), bf16[8,257,512]{2,1,0:T(8,128)(2,1)S(1)}, u32[]{:S(2)}, u32[]{:S(2)}) async-start(bf16[8,257,512]{2,1,0:T(8,128)(2,1)} %pad_maximum_fusion), calls=%async_computation.2 | async-start | bytes 4325376 | tf_op jit(solution)/shard_map/all_to_all | solution.py:150
  95.2 1.3 convolution_multiply_fusion.1
  96.5 1.0 copy-done.1
  97.5 0.6 convolution_bitcast_fusion.7
  98.1 0.6 fusion.58
  98.7 0.7 fusion.62
  99.7 0.9 select_reduce_fusion.2
  100.6 21.5 %all-to-all-done.2 = bf16[8,257,512]{2,1,0:T(8,128)(2,1)S(1)} async-done(((bf16[8,257,512]{2,1,0:T(8,128)(2,1)}), bf16[8,257,512]{2,1,0:T(8,128)(2,1)S(1)}, u32[]{:S(2)}, u32[]{:S(2)}) %all-to-all-start.2) | async-done | bytes 2105376 | tf_op jit(solution)/shard_map/all_to_all | solution.py:150
  122.1 0.3 convert_reduce_fusion
  122.5 0.8 copy.222
  123.3 7.0 %all-to-all-start.3 = ((bf16[64,256,8]{1,2,0:T(8,128)(2,1)}), bf16[64,256,8]{1,2,0:T(8,128)(2,1)S(1)}, u32[]{:S(2)}, u32[]{:S(2)}) async-start(bf16[64,256,8]{1,2,0:T(8,128)(2,1)} %bitcast.43), calls=%async_computation.3 | async-start | bytes 524288 | tf_op jit(solution)/shard_map/all_to_all | solution.py:158
  130.4 0.6 broadcast_select_fusion.1
  131.1 0.7 broadcast_select_fusion
  131.8 1.4 multiply_reduce_fusion.2
  133.2 9.7 %all-to-all-done.3 = bf16[64,256,8]{1,2,0:T(8,128)(2,1)S(1)} async-done(((bf16[64,256,8]{1,2,0:T(8,128)(2,1)}), bf16[64,256,8]{1,2,0:T(8,128)(2,1)S(1)}, u32[]{:S(2)}, u32[]{:S(2)}) %all-to-all-start.3) | async-done | bytes 262176 | tf_op jit(solution)/shard_map/all_to_all | solution.py:158
  142.9 0.3 copy.223
  143.2 3.2 %gather_fusion = bf16[1024,64]{1,0:T(8,128)(2,1)S(1)} fusion(bf16[2048,64]{1,0:T(8,128)(2,1)S(1)} %copy.223, s32[1024]{0:T(1024)S(1)} %broadcast_clamp_fusion), kind=kCustom, calls=%fused_computation | custom fusion | bytes 266240 | tf_op jit(solution)/shard_map/jit(_take)/gather | solution.py:169
  146.6 0.4 fusion.13
  147.0 1.9 %convolution_multiply_fusion = f32[4,256,256]{2,1,0:T(8,128)S(1)} fusion(f32[4,256]{1,0:T(4,128)} %copy-done.9, s32[4,256]{1,0:T(4,128)} %bitcast.250, pred[256,256]{1,0:T(8,128)(4,1)} %iota_compare_fusion.2, f32[256,4,1,64]{0,3,1,2:T(8,128)S(1)} %fusion.13, bf16[256,4,1,64]{0,3,2,1:T(8,128)(2,1)S(1)} %copy-done.4, f32[256,4]{0,1:T(4,128)S(1)} %get-tuple-element.40), kind=kOutput, calls=%fused_computation.5 | convolution fusion | flops 102367232 | bytes 1519616 | tf_op jit(solution)/shard_map/ibhp,jbhp->bhij/dot_general | solution.py:196
  148.9 0.3 fusion.17
  149.1 2.2 %convolution_bitcast_fusion.1 = f32[256,4,1,128]{3,0,1,2:T(8,128)} fusion(f32[4,256,256]{2,1,0:T(8,128)S(1)} %convolution_multiply_fusion, bf16[256,4,128]{2,1,0:T(4,128)(2,1)} %bitcast.245), kind=kOutput, calls=%fused_computation.8 | convolution fusion | flops 201326592 | bytes 1835008 | tf_op jit(solution)/shard_map/bhij,jbhn->ibhn/dot_general | solution.py:201
  151.3 0.9 broadcast_in_dim.158
  152.3 7.2 %all-to-all-start.4 = ((bf16[8,4,1,128,64]{3,4,2,1,0:T(8,128)(2,1)}), bf16[8,4,1,128,64]{3,4,2,1,0:T(8,128)(2,1)}, u32[]{:S(2)}, u32[]{:S(2)}) async-start(bf16[8,4,1,128,64]{3,4,2,1,0:T(8,128)(2,1)} %broadcast_in_dim.158), calls=%async_computation.4 | async-start | bytes 1048576 | tf_op jit(solution)/shard_map/all_to_all | solution.py:183
  159.5 2.1 %fusion.4 = bf16[256,4,1,128]{3,0,1,2:T(8,128)(2,1)S(1)} fusion(f32[256,4,1,128]{3,0,1,2:T(8,128)} %convolution_bitcast_fusion.1, f32[256,4,1,64]{0,3,1,2:T(8,128)S(1)} %fusion.13, f32[256,4]{0,1:T(4,128)S(1)} %get-tuple-element.26, f32[4,64,128]{2,0,1:T(4,128)S(1)} %multiply_reduce_fusion.2), kind=kOutput, calls=%fused_computation.16 | convolution fusion | flops 101056512 | bytes 1183744 | tf_op jit(solution)/shard_map/ibhp,bhpn->ibhn/dot_general | solution.py:202
  161.6 0.9 copy.236
  162.5 1.1 convolution_bitcast_fusion.6
  163.7 0.8 convolution_bitcast_fusion.3
  164.5 4.5 %all-to-all-done.4 = bf16[8,4,1,128,64]{3,4,2,1,0:T(8,128)(2,1)} async-done(((bf16[8,4,1,128,64]{3,4,2,1,0:T(8,128)(2,1)}), bf16[8,4,1,128,64]{3,4,2,1,0:T(8,128)(2,1)}, u32[]{:S(2)}, u32[]{:S(2)}) %all-to-all-start.4) | async-done | bytes 524320 | tf_op jit(solution)/shard_map/all_to_all | solution.py:183
  169.0 1.2 multiply_reduce_fusion.1
  170.2 1.1 fusion.5
  171.3 0.9 copy.235
  172.2 2.1 %fusion.15 = bf16[256,4,1,64]{0,3,2,1:T(8,128)(2,1)} fusion(f32[256,4,1,64]{0,3,1,2:T(8,128)} %convolution_bitcast_fusion.6, f32[4,128,64]{1,2,0:T(8,128)S(1)} %multiply_reduce_fusion.1, f32[256,4,1,64]{0,3,1,2:T(8,128)S(1)} %fusion.13, bf16[256,4,128]{2,1,0:T(4,128)(2,1)} %bitcast.246, f32[256,4]{0,1:T(4,128)S(1)} %get-tuple-element.41, f32[]{:T(128)} %bitcast.236, ...), kind=kOutput, calls=%fused_computation.31 | convolution fusion | flops 101056512 | bytes 1056772 | tf_op jit(solution)/shard_map/jbhn,bhnp->jbhp/dot_general | solution.py:192
  (92 shorter events, 4.0 us)
Async XLA Ops:
  0.6 84.4 %copy-start = (bf16[1,640,512]{2,1,0:T(8,128)(2,1)S(1)}, bf16[1,640,512]{2,1,0:T(8,128)(2,1)}, u32[]{:S(2)}) copy-start(bf16[1,640,512]{2,1,0:T(8,128)(2,1)} %param.11) | copy-start | bytes 1966084
  5.1 18.3 %all-to-all-start.1 = ((bf16[8,32,640]{2,1,0:T(8,128)(2,1)}), bf16[8,32,640]{2,1,0:T(8,128)(2,1)S(1)}, u32[]{:S(2)}, u32[]{:S(2)}) async-start(bf16[8,32,640]{2,1,0:T(8,128)(2,1)} %bitcast.28), calls=%async_computation.1 | async-start | bytes 655360 | tf_op jit(solution)/shard_map/all_to_all | solution.py:101
  20.7 1.2 copy-start.6
  24.4 64.1 %all-to-all-start = ((bf16[8,4,1,66,128]{4,1,3,2,0:T(4,128)(2,1)}), bf16[8,4,1,66,128]{4,1,3,2,0:T(4,128)(2,1)}, u32[]{:S(2)}, u32[]{:S(2)}) async-start(bf16[8,4,1,66,128]{4,1,3,2,0:T(4,128)(2,1)} %broadcast_in_dim.147), calls=%async_computation | async-start | bytes 1081344 | tf_op jit(solution)/shard_map/all_to_all | solution.py:126
  32.2 18.7 %collective-permute-start.3 = (bf16[8,32,640]{2,1,0:T(8,128)(2,1)S(1)}, bf16[8,32,640]{2,1,0:T(8,128)(2,1)S(1)}, u32[]{:S(2)}, u32[]{:S(2)}) collective-permute-start(bf16[8,32,640]{2,1,0:T(8,128)(2,1)S(1)} %all-to-all-done.1), channel_id=1, source_target_pairs={{0,64},{64,128},{128,192},{192,256},{256,320},{320,384},{384,448},... | collective-permute-start | bytes 983048 | tf_op jit(solution)/shard_map/ppermute | solution.py:66
  37.7 15.6 %collective-permute-start = (bf16[8,32,640]{2,1,0:T(8,128)(2,1)S(1)}, bf16[8,32,640]{2,1,0:T(8,128)(2,1)S(1)}, u32[]{:S(2)}, u32[]{:S(2)}) collective-permute-start(bf16[8,32,640]{2,1,0:T(8,128)(2,1)S(1)} %all-to-all-done.1), channel_id=1, source_target_pairs={{0,448},{64,0},{128,64},{192,128},{256,192},{320,256},{384,320},{4... | collective-permute-start | bytes 983048 | tf_op jit(solution)/shard_map/ppermute | solution.py:69
  51.0 11.8 %collective-permute-start.4 = (bf16[8,32,640]{2,1,0:T(8,128)(2,1)S(1)}, bf16[8,32,640]{2,1,0:T(8,128)(2,1)S(1)}, u32[]{:S(2)}, u32[]{:S(2)}) collective-permute-start(bf16[8,32,640]{2,1,0:T(8,128)(2,1)S(1)} %collective-permute-done.3), channel_id=1, source_target_pairs={{0,64},{64,128},{128,192},{192,256},{256,320},{320,384},{384,448},... | collective-permute-start | bytes 983048 | tf_op jit(solution)/shard_map/ppermute | solution.py:66
  53.3 11.5 %collective-permute-start.1 = (bf16[8,32,640]{2,1,0:T(8,128)(2,1)S(1)}, bf16[8,32,640]{2,1,0:T(8,128)(2,1)S(1)}, u32[]{:S(2)}, u32[]{:S(2)}) collective-permute-start(bf16[8,32,640]{2,1,0:T(8,128)(2,1)S(1)} %collective-permute-done), channel_id=1, source_target_pairs={{0,448},{64,0},{128,64},{192,128},{256,192},{320,256},{384,320},{4... | collective-permute-start | bytes 983048 | tf_op jit(solution)/shard_map/ppermute | solution.py:69
  62.8 10.9 %collective-permute-start.5 = (bf16[8,32,640]{2,1,0:T(8,128)(2,1)S(1)}, bf16[8,32,640]{2,1,0:T(8,128)(2,1)S(1)}, u32[]{:S(2)}, u32[]{:S(2)}) collective-permute-start(bf16[8,32,640]{2,1,0:T(8,128)(2,1)S(1)} %collective-permute-done.4), channel_id=1, source_target_pairs={{0,64},{64,128},{128,192},{192,256},{256,320},{320,384},{384,448},... | collective-permute-start | bytes 983048 | tf_op jit(solution)/shard_map/ppermute | solution.py:66
  64.8 10.8 %collective-permute-start.2 = (bf16[8,32,640]{2,1,0:T(8,128)(2,1)S(1)}, bf16[8,32,640]{2,1,0:T(8,128)(2,1)S(1)}, u32[]{:S(2)}, u32[]{:S(2)}) collective-permute-start(bf16[8,32,640]{2,1,0:T(8,128)(2,1)S(1)} %collective-permute-done.1), channel_id=1, source_target_pairs={{0,448},{64,0},{128,64},{192,128},{256,192},{320,256},{384,320},{4... | collective-permute-start | bytes 983048 | tf_op jit(solution)/shard_map/ppermute | solution.py:69
  73.7 10.1 %collective-permute-start.6 = (bf16[8,32,640]{2,1,0:T(8,128)(2,1)S(1)}, bf16[8,32,640]{2,1,0:T(8,128)(2,1)S(1)}, u32[]{:S(2)}, u32[]{:S(2)}) collective-permute-start(bf16[8,32,640]{2,1,0:T(8,128)(2,1)S(1)} %collective-permute-done.5), channel_id=1, source_target_pairs={{0,64},{64,128},{128,192},{192,256},{256,320},{320,384},{384,448},... | collective-permute-start | bytes 983048 | tf_op jit(solution)/shard_map/ppermute | solution.py:66
  86.9 8.2 %copy-start.3 = (bf16[256,4,1,128]{3,1,2,0:T(4,128)(2,1)S(1)}, bf16[256,4,1,128]{3,1,2,0:T(4,128)(2,1)}, u32[]{:S(2)}) copy-start(bf16[256,4,1,128]{3,1,2,0:T(4,128)(2,1)} %param.15) | copy-start | bytes 786436
  86.9 8.2 %copy-start.5 = (bf16[256,4,1,128]{3,1,2,0:T(4,128)(2,1)S(1)}, bf16[256,4,1,128]{3,1,2,0:T(4,128)(2,1)}, u32[]{:S(2)}) copy-start(bf16[256,4,1,128]{3,1,2,0:T(4,128)(2,1)} %param.14) | copy-start | bytes 786436
  86.9 8.2 %copy-start.7 = (s32[1,4,2,128]{3,1,2,0:T(4,128)S(1)}, s32[1,4,2,128]{3,1,2,0:T(4,128)}, u32[]{:S(2)}) copy-start(s32[1,4,2,128]{3,1,2,0:T(4,128)} %copy-done.6) | copy-start | bytes 12292
  86.9 10.6 %copy-start.4 = (bf16[256,4,1,64]{0,3,2,1:T(8,128)(2,1)S(1)}, bf16[256,4,1,64]{0,3,2,1:T(8,128)(2,1)}, u32[]{:S(2)}) copy-start(bf16[256,4,1,64]{0,3,2,1:T(8,128)(2,1)} %param.13) | copy-start | bytes 393220
  88.5 9.7 %copy-start.11 = (pred[8]{0:T(512)(128)(4,1)S(1)}, pred[8]{0:T(512)(128)(4,1)}, u32[]{:S(2)}) copy-start(pred[8]{0:T(512)(128)(4,1)} %get-tuple-element.39) | copy-start | bytes 28
  88.5 9.7 %copy-start.10 = (pred[8]{0:T(512)(128)(4,1)S(1)}, pred[8]{0:T(512)(128)(4,1)}, u32[]{:S(2)}) copy-start(pred[8]{0:T(512)(128)(4,1)} %get-tuple-element.38) | copy-start | bytes 28
  88.5 33.6 %all-to-all-start.2 = ((bf16[8,257,512]{2,1,0:T(8,128)(2,1)}), bf16[8,257,512]{2,1,0:T(8,128)(2,1)S(1)}, u32[]{:S(2)}, u32[]{:S(2)}) async-start(bf16[8,257,512]{2,1,0:T(8,128)(2,1)} %pad_maximum_fusion), calls=%async_computation.2 | async-start | bytes 4325376 | tf_op jit(solution)/shard_map/all_to_all | solution.py:150
  95.1 48.0 %copy-start.9 = (f32[4,256]{1,0:T(4,128)}, f32[4,256]{1,0:T(4,128)S(1)}, u32[]{:S(2)}) copy-start(f32[4,256]{1,0:T(4,128)S(1)} %bitcast_add_fusion) | copy-start | bytes 12292
  96.5 1.0 copy-start.1
  97.5 49.1 %copy-start.8 = (pred[256,4]{0,1:T(4,128)(4,1)S(1)}, pred[256,4]{0,1:T(4,128)(4,1)}, u32[]{:S(2)}) copy-start(pred[256,4]{0,1:T(4,128)(4,1)} %copy.220) | copy-start | bytes 3076
  123.3 19.6 %all-to-all-start.3 = ((bf16[64,256,8]{1,2,0:T(8,128)(2,1)}), bf16[64,256,8]{1,2,0:T(8,128)(2,1)S(1)}, u32[]{:S(2)}, u32[]{:S(2)}) async-start(bf16[64,256,8]{1,2,0:T(8,128)(2,1)} %bitcast.43), calls=%async_computation.3 | async-start | bytes 524288 | tf_op jit(solution)/shard_map/all_to_all | solution.py:158
  146.4 16.1 %copy-start.2 = (f32[4,256,256]{2,1,0:T(8,128)S(1)}, f32[4,256,256]{2,1,0:T(8,128)}, u32[]{:S(2)}) copy-start(f32[4,256,256]{2,1,0:T(8,128)} %copy-done.1) | copy-start | bytes 3145732
  152.3 16.7 %all-to-all-start.4 = ((bf16[8,4,1,128,64]{3,4,2,1,0:T(8,128)(2,1)}), bf16[8,4,1,128,64]{3,4,2,1,0:T(8,128)(2,1)}, u32[]{:S(2)}, u32[]{:S(2)}) async-start(bf16[8,4,1,128,64]{3,4,2,1,0:T(8,128)(2,1)} %broadcast_in_dim.158), calls=%async_computation.4 | async-start | bytes 1048576 | tf_op jit(solution)/shard_map/all_to_all | solution.py:183

commit v10 on v9

--- a/solution.py
+++ b/solution.py
@@ -157,7 +157,7 @@
     outgoing = scaled.transpose(1, 0, 2)
     arrived = lax.all_to_all(outgoing, TEACH, split_axis=0, concat_axis=0, tiled=True)
     arrived = arrived.reshape(n_z, n_y, n_y * CAP, cols)
-    table = arrived.transpose(1, 2, 0, 3).reshape(n_y * n_y * CAP, n_z * cols)
+    table = arrived.reshape(n_z, n_y * n_y * CAP, cols)
 
     shard_rows = n_y * block_rows
     shard_fam = lax.dynamic_slice_in_dim(
@@ -166,7 +166,10 @@
     shard_slots = family_slots(shard_fam)
     sources = jnp.arange(n_y, dtype=jnp.int32)[:, None]
     row_index = ((shard_fam * n_y + sources) * CAP + shard_slots).reshape(shard_rows)
-    picked = jnp.take(table, row_index, axis=0)
+    chooser = (row_index[:, None] == jnp.arange(table.shape[1], dtype=jnp.int32)[None, :]).astype(
+        jnp.bfloat16
+    )
+    picked = jnp.einsum("rq,jqc->rjc", chooser, table, preferred_element_type=jnp.float32)
     target = picked.reshape(n_y * block_pos, batch_n, 1, P_SIZE)
 
     state_in = combine(chain_weights(through_all, place, False), gathered[:, :, :, :rows])

time: 176 us -> 171 us (0.972)
  other arithmetic: 16.3 us -> 12.5 us
  local copies, waits for them, and re-layouts: 16.8 us -> 13.3 us
  waiting for transfers between devices: 55.2 us -> 58.4 us
  matrix products: 18.2 us -> 20 us
  starting transfers between devices: 65.3 us -> 63.5 us
    ppermute x4, waiting for transfers between devices: 19.1 us -> 15.5 us  [ring_gather(): cw = lax.ppermute(cw, axis, ahead)]
    gather x2 -> x0, local copies, waits for them, and re-layouts: 3.37 us -> none  [per_device(): picked = jnp.take(table, row_index, axis=0)]
    all_to_all x1, starting transfers between devices: 7.03 us -> 4.8 us  [per_device(): lax.all_to_all(outgoing, TEACH, split_axis=0, concat_axis=0, tiled=True)]
    all_to_all x1, waiting for transfers between devices: 0.01 us -> 2.14 us  [per_device(): lax.all_to_all(packed, 'ty', split_axis=0, concat_axis=0, tiled=True)]
    ppermute x3, waiting for transfers between devices: 0.49 us -> 2.57 us  [ring_gather(): ccw = lax.ppermute(ccw, axis, behind)]
    dot_general x0 -> x1, matrix products: none -> 1.84 us  [per_device(): jnp.einsum('rq,jqc->rjc', chooser, table, preferred_element_type=jnp.floa...]
    unnamed x46 -> x39, local copies, waits for them, and re-layouts: 4.96 us -> 5.63 us
  transfers between devices with their start and end apart: 12 -> 12, of which waited for: 9 -> 11; matrix products, arithmetic and copies ran while one was open for 17% -> 15% of each run, Pallas kernels for 0% -> 0%
where the time goes in v10:
time: 171 us; the launch traced here: 170 us
  starting transfers between devices  63.5 us (37%)
  waiting for transfers between devices  58.4 us (34%)
  matrix products  20 us (12%)
  local copies, waits for them, and re-layouts  13.3 us (8%)
  other arithmetic  12.5 us (7%)
  between operations  2.48 us (1%)
    all_to_all x1, waiting for transfers between devices, per_device(): lax.all_to_all(outbound, 'seq', split_axis=0, concat_axis=0, tiled=True)  22.7 us
    ppermute x3, starting transfers between devices, ring_gather(): ccw = lax.ppermute(ccw, axis, behind)  19.2 us
    ppermute x4, waiting for transfers between devices, ring_gather(): cw = lax.ppermute(cw, axis, ahead)  15.5 us
    all_to_all x1, waiting for transfers between devices, per_device(): lax.all_to_all(outgoing, TEACH, split_axis=0, concat_axis=0, tiled=True)  11 us
    ppermute x4, starting transfers between devices, ring_gather(): cw = lax.ppermute(cw, axis, ahead)  9.71 us
    all_to_all x1, starting transfers between devices, per_device(): lax.all_to_all(jnp.broadcast_to(packed_state[None], (seq_n,) + packed_sta...  8.42 us
    all_to_all x1, starting transfers between devices, per_device(): lax.all_to_all(packed, 'ty', split_axis=0, concat_axis=0, tiled=True)  7.64 us
    all_to_all x1, starting transfers between devices, per_device(): lax.all_to_all(jnp.broadcast_to(local_adjoint.astype(jnp.bfloat16)[None],...  7.09 us
  transfers between devices with their start and end apart: 12, of which 11 were waited for; matrix products, arithmetic and copies ran while one was open for 15% of the time, Pallas kernels for 0%

profile of v10, /device:TPU:1, one launch (start us, length us, event | category | flops | bytes accessed | tf_op | source)
XLA Modules:
  0.0 170.3 jit_solution(17106788183459088909)
XLA Ops:
  0.7 1.2 copy.207
  1.8 0.6 reshape.574
  2.7 0.2 reduce_window_sum.81
  2.8 0.2 select_reduce_fusion.1
  3.1 1.0 reshape.575
  4.1 1.1 convolution_convert_fusion.1
  5.1 7.6 %all-to-all-start.1 = ((bf16[8,32,640]{2,1,0:T(8,128)(2,1)}), bf16[8,32,640]{2,1,0:T(8,128)(2,1)S(1)}, u32[]{:S(2)}, u32[]{:S(2)}) async-start(bf16[8,32,640]{2,1,0:T(8,128)(2,1)} %bitcast.29), calls=%async_computation.1 | async-start | bytes 655360 | tf_op jit(solution)/shard_map/all_to_all | solution.py:101
  13.4 0.7 negate_multiply_fusion
  14.1 1.2 reduce-window.16
  15.4 0.7 reshape.562
  16.1 1.2 reduce-window.14
  18.1 0.2 slice_reduce_fusion
  18.3 0.2 slice_reduce_fusion.1
  18.5 0.7 copy.266
  19.2 1.3 fusion.23
  20.7 2.1 %all-to-all-done.1 = bf16[8,32,640]{2,1,0:T(8,128)(2,1)S(1)} async-done(((bf16[8,32,640]{2,1,0:T(8,128)(2,1)}), bf16[8,32,640]{2,1,0:T(8,128)(2,1)S(1)}, u32[]{:S(2)}, u32[]{:S(2)}) %all-to-all-start.1) | async-done | bytes 327712 | tf_op jit(solution)/shard_map/all_to_all | solution.py:101
  22.9 0.9 broadcast_in_dim.78
  23.8 8.4 %all-to-all-start = ((bf16[8,4,1,66,128]{4,1,3,2,0:T(4,128)(2,1)}), bf16[8,4,1,66,128]{4,1,3,2,0:T(4,128)(2,1)}, u32[]{:S(2)}, u32[]{:S(2)}) async-start(bf16[8,4,1,66,128]{4,1,3,2,0:T(4,128)(2,1)} %broadcast_in_dim.78), calls=%async_computation | async-start | bytes 1081344 | tf_op jit(solution)/shard_map/all_to_all | solution.py:126
  32.2 4.0 %collective-permute-start.3 = (bf16[8,32,640]{2,1,0:T(8,128)(2,1)S(1)}, bf16[8,32,640]{2,1,0:T(8,128)(2,1)S(1)}, u32[]{:S(2)}, u32[]{:S(2)}) collective-permute-start(bf16[8,32,640]{2,1,0:T(8,128)(2,1)S(1)} %all-to-all-done.1), channel_id=1, source_target_pairs={{0,64},{64,128},{128,192},{192,256},{256,320},{320,384},{384,448},... | collective-permute-start | bytes 983048 | tf_op jit(solution)/shard_map/ppermute | solution.py:66
  36.4 2.5 %select_reduce_fusion = s32[8,128]{0,1:T(8,128)S(1)} fusion(s32[8,128]{0,1:T(8,128)S(1)} %copy.208), kind=kOutput, calls=%fused_computation.50 | output fusion | flops 1096704 | bytes 8192 | tf_op jit(solution)/shard_map/jit(cumsum)/reduce_window_sum | solution.py:23
  38.9 8.6 %collective-permute-start = (bf16[8,32,640]{2,1,0:T(8,128)(2,1)S(1)}, bf16[8,32,640]{2,1,0:T(8,128)(2,1)S(1)}, u32[]{:S(2)}, u32[]{:S(2)}) collective-permute-start(bf16[8,32,640]{2,1,0:T(8,128)(2,1)S(1)} %all-to-all-done.1), channel_id=1, source_target_pairs={{0,448},{64,0},{128,64},{192,128},{256,192},{320,256},{384,320},{4... | collective-permute-start | bytes 983048 | tf_op jit(solution)/shard_map/ppermute | solution.py:69
  47.5 3.4 %collective-permute-done.3 = bf16[8,32,640]{2,1,0:T(8,128)(2,1)S(1)} collective-permute-done((bf16[8,32,640]{2,1,0:T(8,128)(2,1)S(1)}, bf16[8,32,640]{2,1,0:T(8,128)(2,1)S(1)}, u32[]{:S(2)}, u32[]{:S(2)}) %collective-permute-start.3) | collective-permute-done | bytes 327712 | tf_op jit(solution)/shard_map/ppermute | solution.py:66
  51.0 1.9 %collective-permute-start.4 = (bf16[8,32,640]{2,1,0:T(8,128)(2,1)S(1)}, bf16[8,32,640]{2,1,0:T(8,128)(2,1)S(1)}, u32[]{:S(2)}, u32[]{:S(2)}) collective-permute-start(bf16[8,32,640]{2,1,0:T(8,128)(2,1)S(1)} %collective-permute-done.3), channel_id=1, source_target_pairs={{0,64},{64,128},{128,192},{192,256},{256,320},{320,384},{384,448},... | collective-permute-start | bytes 983048 | tf_op jit(solution)/shard_map/ppermute | solution.py:66
  53.8 0.7 iota_compare_fusion.3
  54.6 5.3 %collective-permute-start.1 = (bf16[8,32,640]{2,1,0:T(8,128)(2,1)S(1)}, bf16[8,32,640]{2,1,0:T(8,128)(2,1)S(1)}, u32[]{:S(2)}, u32[]{:S(2)}) collective-permute-start(bf16[8,32,640]{2,1,0:T(8,128)(2,1)S(1)} %collective-permute-done), channel_id=1, source_target_pairs={{0,448},{64,0},{128,64},{192,128},{256,192},{320,256},{384,320},{4... | collective-permute-start | bytes 983048 | tf_op jit(solution)/shard_map/ppermute | solution.py:69
  59.9 2.8 %collective-permute-done.4 = bf16[8,32,640]{2,1,0:T(8,128)(2,1)S(1)} collective-permute-done((bf16[8,32,640]{2,1,0:T(8,128)(2,1)S(1)}, bf16[8,32,640]{2,1,0:T(8,128)(2,1)S(1)}, u32[]{:S(2)}, u32[]{:S(2)}) %collective-permute-start.4) | collective-permute-done | bytes 327712 | tf_op jit(solution)/shard_map/ppermute | solution.py:66
  62.8 1.9 %collective-permute-start.5 = (bf16[8,32,640]{2,1,0:T(8,128)(2,1)S(1)}, bf16[8,32,640]{2,1,0:T(8,128)(2,1)S(1)}, u32[]{:S(2)}, u32[]{:S(2)}) collective-permute-start(bf16[8,32,640]{2,1,0:T(8,128)(2,1)S(1)} %collective-permute-done.4), channel_id=1, source_target_pairs={{0,64},{64,128},{128,192},{192,256},{256,320},{320,384},{384,448},... | collective-permute-start | bytes 983048 | tf_op jit(solution)/shard_map/ppermute | solution.py:66
  64.7 1.4 collective-permute-done.1
  66.1 5.3 %collective-permute-start.2 = (bf16[8,32,640]{2,1,0:T(8,128)(2,1)S(1)}, bf16[8,32,640]{2,1,0:T(8,128)(2,1)S(1)}, u32[]{:S(2)}, u32[]{:S(2)}) collective-permute-start(bf16[8,32,640]{2,1,0:T(8,128)(2,1)S(1)} %collective-permute-done.1), channel_id=1, source_target_pairs={{0,448},{64,0},{128,64},{192,128},{256,192},{320,256},{384,320},{4... | collective-permute-start | bytes 983048 | tf_op jit(solution)/shard_map/ppermute | solution.py:69
  71.4 2.2 %collective-permute-done.5 = bf16[8,32,640]{2,1,0:T(8,128)(2,1)S(1)} collective-permute-done((bf16[8,32,640]{2,1,0:T(8,128)(2,1)S(1)}, bf16[8,32,640]{2,1,0:T(8,128)(2,1)S(1)}, u32[]{:S(2)}, u32[]{:S(2)}) %collective-permute-start.5) | collective-permute-done | bytes 327712 | tf_op jit(solution)/shard_map/ppermute | solution.py:66
  73.7 1.9 %collective-permute-start.6 = (bf16[8,32,640]{2,1,0:T(8,128)(2,1)S(1)}, bf16[8,32,640]{2,1,0:T(8,128)(2,1)S(1)}, u32[]{:S(2)}, u32[]{:S(2)}) collective-permute-start(bf16[8,32,640]{2,1,0:T(8,128)(2,1)S(1)} %collective-permute-done.5), channel_id=1, source_target_pairs={{0,64},{64,128},{128,192},{192,256},{256,320},{320,384},{384,448},... | collective-permute-start | bytes 983048 | tf_op jit(solution)/shard_map/ppermute | solution.py:66
  75.6 1.1 collective-permute-done.2
  76.8 7.0 %collective-permute-done.6 = bf16[8,32,640]{2,1,0:T(8,128)(2,1)S(1)} collective-permute-done((bf16[8,32,640]{2,1,0:T(8,128)(2,1)S(1)}, bf16[8,32,640]{2,1,0:T(8,128)(2,1)S(1)}, u32[]{:S(2)}, u32[]{:S(2)}) %collective-permute-start.6) | collective-permute-done | bytes 327712 | tf_op jit(solution)/shard_map/ppermute | solution.py:66
  84.3 0.6 multiply_reduce_fusion
  85.1 1.8 %convolution_convert_fusion = bf16[8,256,512]{2,1,0:T(8,128)(2,1)S(1)} fusion(bf16[8,256,640]{2,1,0:T(8,128)(2,1)S(1)} %bitcast.237, bf16[1,640,512]{2,1,0:T(8,128)(2,1)S(1)} %copy-done), kind=kOutput, calls=%fused_computation.7 | convolution fusion | flops 1343225856 | bytes 5373952 | tf_op jit(solution)/shard_map/dot_general | solution.py:140
  86.9 1.5 pad_maximum_fusion
  88.4 6.7 %all-to-all-start.2 = ((bf16[8,257,512]{2,1,0:T(8,128)(2,1)}), bf16[8,257,512]{2,1,0:T(8,128)(2,1)S(1)}, u32[]{:S(2)}, u32[]{:S(2)}) async-start(bf16[8,257,512]{2,1,0:T(8,128)(2,1)} %pad_maximum_fusion), calls=%async_computation.2 | async-start | bytes 4325376 | tf_op jit(solution)/shard_map/all_to_all | solution.py:150
  95.2 1.3 convolution_multiply_fusion.1
  96.5 1.0 copy-done.1
  97.5 0.6 convolution_bitcast_fusion.7
  98.2 0.7 fusion.69
  99.1 0.2 select_reduce_fusion.2
  99.4 22.7 %all-to-all-done.2 = bf16[8,257,512]{2,1,0:T(8,128)(2,1)S(1)} async-done(((bf16[8,257,512]{2,1,0:T(8,128)(2,1)}), bf16[8,257,512]{2,1,0:T(8,128)(2,1)S(1)}, u32[]{:S(2)}, u32[]{:S(2)}) %all-to-all-start.2) | async-done | bytes 2105376 | tf_op jit(solution)/shard_map/all_to_all | solution.py:150
  122.0 0.3 convert_reduce_fusion
  122.5 0.8 copy.212
  123.3 4.8 %all-to-all-start.3 = ((bf16[64,256,8]{1,2,0:T(8,128)(2,1)}), bf16[64,256,8]{1,2,0:T(8,128)(2,1)S(1)}, u32[]{:S(2)}, u32[]{:S(2)}) async-start(bf16[64,256,8]{1,2,0:T(8,128)(2,1)} %bitcast.44), calls=%async_computation.3 | async-start | bytes 524288 | tf_op jit(solution)/shard_map/all_to_all | solution.py:158
  128.3 1.4 multiply_reduce_fusion.2
  129.7 11.0 %all-to-all-done.3 = bf16[64,256,8]{1,2,0:T(8,128)(2,1)S(1)} async-done(((bf16[64,256,8]{1,2,0:T(8,128)(2,1)}), bf16[64,256,8]{1,2,0:T(8,128)(2,1)S(1)}, u32[]{:S(2)}, u32[]{:S(2)}) %all-to-all-start.3) | async-done | bytes 262176 | tf_op jit(solution)/shard_map/all_to_all | solution.py:158
  140.8 1.8 %fusion.16 = f32[256,4,1,64]{0,3,1,2:T(8,128)S(1)} fusion(bf16[64,2048,1]{1,0,2:T(8,128)(2,1)S(1)} %bitcast.246, s32[256,4]{0,1:T(4,128)S(1)} %copy.210), kind=kOutput, calls=%fused_computation.29 | convolution fusion | flops 270532608 | bytes 528384 | tf_op jit(solution)/shard_map/rq,jqc->rjc/dot_general | solution.py:172
  142.6 0.4 fusion.20
  143.0 1.9 %convolution_multiply_fusion = f32[4,256,256]{2,1,0:T(8,128)S(1)} fusion(f32[4,256]{1,0:T(4,128)} %copy-done.7, s32[4,256]{1,0:T(4,128)} %bitcast.255, pred[256,256]{1,0:T(8,128)(4,1)} %iota_compare_fusion.3, f32[256,4,1,64]{0,3,1,2:T(8,128)S(1)} %fusion.20, bf16[256,4,1,64]{0,3,2,1:T(8,128)(2,1)S(1)} %copy-done.4, f32[256,4]{0,1:T(4,128)S(1)} %bitcast.249), kind=kOutput, calls=%fused_computation.8 | convolution fusion | flops 102367232 | bytes 1519616 | tf_op jit(solution)/shard_map/ibhp,jbhp->bhij/dot_general | solution.py:199
  144.9 0.3 fusion.24
  145.2 2.2 %convolution_bitcast_fusion.1 = f32[256,4,1,128]{3,0,1,2:T(8,128)} fusion(f32[4,256,256]{2,1,0:T(8,128)S(1)} %convolution_multiply_fusion, bf16[256,4,128]{2,1,0:T(4,128)(2,1)} %bitcast.243), kind=kOutput, calls=%fused_computation.11 | convolution fusion | flops 201326592 | bytes 1835008 | tf_op jit(solution)/shard_map/bhij,jbhn->ibhn/dot_general | solution.py:204
  147.4 0.9 broadcast_in_dim.141
  148.3 7.1 %all-to-all-start.4 = ((bf16[8,4,1,128,64]{3,4,2,1,0:T(8,128)(2,1)}), bf16[8,4,1,128,64]{3,4,2,1,0:T(8,128)(2,1)}, u32[]{:S(2)}, u32[]{:S(2)}) async-start(bf16[8,4,1,128,64]{3,4,2,1,0:T(8,128)(2,1)} %broadcast_in_dim.141), calls=%async_computation.4 | async-start | bytes 1048576 | tf_op jit(solution)/shard_map/all_to_all | solution.py:186
  155.4 2.1 %fusion.8 = bf16[256,4,1,128]{3,0,1,2:T(8,128)(2,1)S(1)} fusion(f32[256,4,1,128]{3,0,1,2:T(8,128)} %convolution_bitcast_fusion.1, f32[256,4,1,64]{0,3,1,2:T(8,128)S(1)} %fusion.20, f32[256,4]{0,1:T(4,128)S(1)} %get-tuple-element.26, f32[4,64,128]{2,0,1:T(4,128)S(1)} %multiply_reduce_fusion.2), kind=kOutput, calls=%fused_computation.19 | convolution fusion | flops 101056512 | bytes 1183744 | tf_op jit(solution)/shard_map/ibhp,bhpn->ibhn/dot_general | solution.py:205
  157.6 0.9 copy.224
  158.5 1.1 convolution_bitcast_fusion.6
  159.6 0.8 convolution_bitcast_fusion.3
  160.4 4.5 %all-to-all-done.4 = bf16[8,4,1,128,64]{3,4,2,1,0:T(8,128)(2,1)} async-done(((bf16[8,4,1,128,64]{3,4,2,1,0:T(8,128)(2,1)}), bf16[8,4,1,128,64]{3,4,2,1,0:T(8,128)(2,1)}, u32[]{:S(2)}, u32[]{:S(2)}) %all-to-all-start.4) | async-done | bytes 524320 | tf_op jit(solution)/shard_map/all_to_all | solution.py:186
  164.9 1.2 multiply_reduce_fusion.1
  166.1 1.1 fusion.9
  167.3 0.9 copy.223
  168.2 2.1 %fusion.22 = bf16[256,4,1,64]{0,3,2,1:T(8,128)(2,1)} fusion(f32[256,4,1,64]{0,3,1,2:T(8,128)} %convolution_bitcast_fusion.6, f32[4,128,64]{1,2,0:T(8,128)S(1)} %multiply_reduce_fusion.1, f32[256,4,1,64]{0,3,1,2:T(8,128)S(1)} %fusion.20, bf16[256,4,128]{2,1,0:T(4,128)(2,1)} %bitcast.244, f32[256,4]{0,1:T(4,128)S(1)} %select_bitcast_fusion, f32[]{:T(128)} %bitcast.236, ...), kind=kOutput, calls=%fused_computation.35 | convolution fusion | flops 101056512 | bytes 1056772 | tf_op jit(solution)/shard_map/jbhn,bhnp->jbhp/dot_general | solution.py:195
  (82 shorter events, 3.3 us)
Async XLA Ops:
  0.6 84.4 %copy-start = (bf16[1,640,512]{2,1,0:T(8,128)(2,1)S(1)}, bf16[1,640,512]{2,1,0:T(8,128)(2,1)}, u32[]{:S(2)}) copy-start(bf16[1,640,512]{2,1,0:T(8,128)(2,1)} %param.11) | copy-start | bytes 1966084
  5.1 17.7 %all-to-all-start.1 = ((bf16[8,32,640]{2,1,0:T(8,128)(2,1)}), bf16[8,32,640]{2,1,0:T(8,128)(2,1)S(1)}, u32[]{:S(2)}, u32[]{:S(2)}) async-start(bf16[8,32,640]{2,1,0:T(8,128)(2,1)} %bitcast.29), calls=%async_computation.1 | async-start | bytes 655360 | tf_op jit(solution)/shard_map/all_to_all | solution.py:101
  18.0 77.1 %copy-start.6 = (s32[1,4,2,128]{3,1,2,0:T(4,128)}, s32[1,4,2,128]{3,1,2,0:T(4,128)S(1)}, u32[]{:S(2)}) copy-start(s32[1,4,2,128]{3,1,2,0:T(4,128)S(1)} %copy.267) | copy-start | bytes 12292
  23.8 64.6 %all-to-all-start = ((bf16[8,4,1,66,128]{4,1,3,2,0:T(4,128)(2,1)}), bf16[8,4,1,66,128]{4,1,3,2,0:T(4,128)(2,1)}, u32[]{:S(2)}, u32[]{:S(2)}) async-start(bf16[8,4,1,66,128]{4,1,3,2,0:T(4,128)(2,1)} %broadcast_in_dim.78), calls=%async_computation | async-start | bytes 1081344 | tf_op jit(solution)/shard_map/all_to_all | solution.py:126
  32.2 18.7 %collective-permute-start.3 = (bf16[8,32,640]{2,1,0:T(8,128)(2,1)S(1)}, bf16[8,32,640]{2,1,0:T(8,128)(2,1)S(1)}, u32[]{:S(2)}, u32[]{:S(2)}) collective-permute-start(bf16[8,32,640]{2,1,0:T(8,128)(2,1)S(1)} %all-to-all-done.1), channel_id=1, source_target_pairs={{0,64},{64,128},{128,192},{192,256},{256,320},{320,384},{384,448},... | collective-permute-start | bytes 983048 | tf_op jit(solution)/shard_map/ppermute | solution.py:66
  38.9 15.6 %collective-permute-start = (bf16[8,32,640]{2,1,0:T(8,128)(2,1)S(1)}, bf16[8,32,640]{2,1,0:T(8,128)(2,1)S(1)}, u32[]{:S(2)}, u32[]{:S(2)}) collective-permute-start(bf16[8,32,640]{2,1,0:T(8,128)(2,1)S(1)} %all-to-all-done.1), channel_id=1, source_target_pairs={{0,448},{64,0},{128,64},{192,128},{256,192},{320,256},{384,320},{4... | collective-permute-start | bytes 983048 | tf_op jit(solution)/shard_map/ppermute | solution.py:69
  51.0 11.8 %collective-permute-start.4 = (bf16[8,32,640]{2,1,0:T(8,128)(2,1)S(1)}, bf16[8,32,640]{2,1,0:T(8,128)(2,1)S(1)}, u32[]{:S(2)}, u32[]{:S(2)}) collective-permute-start(bf16[8,32,640]{2,1,0:T(8,128)(2,1)S(1)} %collective-permute-done.3), channel_id=1, source_target_pairs={{0,64},{64,128},{128,192},{192,256},{256,320},{320,384},{384,448},... | collective-permute-start | bytes 983048 | tf_op jit(solution)/shard_map/ppermute | solution.py:66
  54.6 11.5 %collective-permute-start.1 = (bf16[8,32,640]{2,1,0:T(8,128)(2,1)S(1)}, bf16[8,32,640]{2,1,0:T(8,128)(2,1)S(1)}, u32[]{:S(2)}, u32[]{:S(2)}) collective-permute-start(bf16[8,32,640]{2,1,0:T(8,128)(2,1)S(1)} %collective-permute-done), channel_id=1, source_target_pairs={{0,448},{64,0},{128,64},{192,128},{256,192},{320,256},{384,320},{4... | collective-permute-start | bytes 983048 | tf_op jit(solution)/shard_map/ppermute | solution.py:69
  62.8 10.9 %collective-permute-start.5 = (bf16[8,32,640]{2,1,0:T(8,128)(2,1)S(1)}, bf16[8,32,640]{2,1,0:T(8,128)(2,1)S(1)}, u32[]{:S(2)}, u32[]{:S(2)}) collective-permute-start(bf16[8,32,640]{2,1,0:T(8,128)(2,1)S(1)} %collective-permute-done.4), channel_id=1, source_target_pairs={{0,64},{64,128},{128,192},{192,256},{256,320},{320,384},{384,448},... | collective-permute-start | bytes 983048 | tf_op jit(solution)/shard_map/ppermute | solution.py:66
  66.1 10.6 %collective-permute-start.2 = (bf16[8,32,640]{2,1,0:T(8,128)(2,1)S(1)}, bf16[8,32,640]{2,1,0:T(8,128)(2,1)S(1)}, u32[]{:S(2)}, u32[]{:S(2)}) collective-permute-start(bf16[8,32,640]{2,1,0:T(8,128)(2,1)S(1)} %collective-permute-done.1), channel_id=1, source_target_pairs={{0,448},{64,0},{128,64},{192,128},{256,192},{320,256},{384,320},{4... | collective-permute-start | bytes 983048 | tf_op jit(solution)/shard_map/ppermute | solution.py:69
  73.7 10.1 %collective-permute-start.6 = (bf16[8,32,640]{2,1,0:T(8,128)(2,1)S(1)}, bf16[8,32,640]{2,1,0:T(8,128)(2,1)S(1)}, u32[]{:S(2)}, u32[]{:S(2)}) collective-permute-start(bf16[8,32,640]{2,1,0:T(8,128)(2,1)S(1)} %collective-permute-done.5), channel_id=1, source_target_pairs={{0,64},{64,128},{128,192},{192,256},{256,320},{320,384},{384,448},... | collective-permute-start | bytes 983048 | tf_op jit(solution)/shard_map/ppermute | solution.py:66
  86.9 8.3 %copy-start.3 = (bf16[256,4,1,128]{3,1,2,0:T(4,128)(2,1)S(1)}, bf16[256,4,1,128]{3,1,2,0:T(4,128)(2,1)}, u32[]{:S(2)}) copy-start(bf16[256,4,1,128]{3,1,2,0:T(4,128)(2,1)} %param.15) | copy-start | bytes 786436
  86.9 8.3 %copy-start.5 = (bf16[256,4,1,128]{3,1,2,0:T(4,128)(2,1)S(1)}, bf16[256,4,1,128]{3,1,2,0:T(4,128)(2,1)}, u32[]{:S(2)}) copy-start(bf16[256,4,1,128]{3,1,2,0:T(4,128)(2,1)} %param.14) | copy-start | bytes 786436
  86.9 10.6 %copy-start.4 = (bf16[256,4,1,64]{0,3,2,1:T(8,128)(2,1)S(1)}, bf16[256,4,1,64]{0,3,2,1:T(8,128)(2,1)}, u32[]{:S(2)}) copy-start(bf16[256,4,1,64]{0,3,2,1:T(8,128)(2,1)} %param.13) | copy-start | bytes 393220
  88.4 33.6 %all-to-all-start.2 = ((bf16[8,257,512]{2,1,0:T(8,128)(2,1)}), bf16[8,257,512]{2,1,0:T(8,128)(2,1)S(1)}, u32[]{:S(2)}, u32[]{:S(2)}) async-start(bf16[8,257,512]{2,1,0:T(8,128)(2,1)} %pad_maximum_fusion), calls=%async_computation.2 | async-start | bytes 4325376 | tf_op jit(solution)/shard_map/all_to_all | solution.py:150
  95.2 47.4 %copy-start.7 = (f32[4,256]{1,0:T(4,128)}, f32[4,256]{1,0:T(4,128)S(1)}, u32[]{:S(2)}) copy-start(f32[4,256]{1,0:T(4,128)S(1)} %bitcast_add_fusion) | copy-start | bytes 12292
  96.5 1.0 copy-start.1
  123.3 17.5 %all-to-all-start.3 = ((bf16[64,256,8]{1,2,0:T(8,128)(2,1)}), bf16[64,256,8]{1,2,0:T(8,128)(2,1)S(1)}, u32[]{:S(2)}, u32[]{:S(2)}) async-start(bf16[64,256,8]{1,2,0:T(8,128)(2,1)} %bitcast.44), calls=%async_computation.3 | async-start | bytes 524288 | tf_op jit(solution)/shard_map/all_to_all | solution.py:158
  142.6 15.9 %copy-start.2 = (f32[4,256,256]{2,1,0:T(8,128)S(1)}, f32[4,256,256]{2,1,0:T(8,128)}, u32[]{:S(2)}) copy-start(f32[4,256,256]{2,1,0:T(8,128)} %copy-done.1) | copy-start | bytes 3145732
  148.3 16.6 %all-to-all-start.4 = ((bf16[8,4,1,128,64]{3,4,2,1,0:T(8,128)(2,1)}), bf16[8,4,1,128,64]{3,4,2,1,0:T(8,128)(2,1)}, u32[]{:S(2)}, u32[]{:S(2)}) async-start(bf16[8,4,1,128,64]{3,4,2,1,0:T(8,128)(2,1)} %broadcast_in_dim.141), calls=%async_computation.4 | async-start | bytes 1048576 | tf_op jit(solution)/shard_map/all_to_all | solution.py:186

commit v11 on v10

--- a/solution.py
+++ b/solution.py
@@ -123,17 +123,6 @@
         ],
         axis=2,
     )
-    gathered = lax.all_to_all(
-        jnp.broadcast_to(packed_state[None], (seq_n,) + packed_state.shape),
-        "seq",
-        split_axis=0,
-        concat_axis=0,
-        tiled=True,
-    )
-    rows = local_state.shape[2]
-    through_all = gathered[:, :, :, rows, 0].astype(jnp.float32) + gathered[
-        :, :, :, rows + 1, 0
-    ].astype(jnp.float32)
     slots_all = n_z * n_y * CAP
     received = received.reshape(slots_all, feat_width)
     weights = teacher_proj[0]
@@ -146,9 +135,17 @@
     sq_hi = sq_all.astype(jnp.bfloat16)
     sq_lo = (sq_all - sq_hi.astype(jnp.float32)).astype(jnp.bfloat16)
     sq_row = jnp.concatenate([sq_hi, sq_lo], axis=1)[:, None, :]
-    outbound = jnp.concatenate([partial_value.astype(jnp.bfloat16), sq_row], axis=1)
+    state_rows = jnp.broadcast_to(
+        packed_state.reshape(1, -1, width), (n_z, packed_state.size // width, width)
+    )
+    outbound = jnp.concatenate([partial_value.astype(jnp.bfloat16), sq_row, state_rows], axis=1)
     inbound = lax.all_to_all(outbound, "seq", split_axis=0, concat_axis=0, tiled=True)
-    summed = jnp.sum(inbound.astype(jnp.float32), axis=0)
+    summed = jnp.sum(inbound[:, : group + 1].astype(jnp.float32), axis=0)
+    gathered = inbound[:, group + 1 :].reshape((seq_n,) + packed_state.shape)
+    rows = local_state.shape[2]
+    through_all = gathered[:, :, :, rows, 0].astype(jnp.float32) + gathered[
+        :, :, :, rows + 1, 0
+    ].astype(jnp.float32)
     sq_total = summed[group, :group] + summed[group, group : 2 * group]
     row_scale = lax.rsqrt(sq_total / TD + EPS)
     scaled = (summed[:group] * row_scale[:, None]).astype(jnp.bfloat16)

time: 171 us -> 170 us (level)
  waiting for transfers between devices: 58.4 us -> 49.4 us
  other arithmetic: 12.5 us -> 16.9 us
  local copies, waits for them, and re-layouts: 13.3 us -> 16.7 us
    all_to_all x1 -> x0, starting transfers between devices: 8.42 us -> none  [per_device(): lax.all_to_all(jnp.broadcast_to(packed_state[None], (seq_n,) + packed_sta...]
    all_to_all x1, waiting for transfers between devices: 22.7 us -> 18.4 us  [per_device(): lax.all_to_all(outbound, 'seq', split_axis=0, concat_axis=0, tiled=True)]
    all_to_all x1, starting transfers between devices: 6.66 us -> 10.3 us  [per_device(): lax.all_to_all(outbound, 'seq', split_axis=0, concat_axis=0, tiled=True)]
    ppermute x3, waiting for transfers between devices: 2.57 us -> 0.01 us  [ring_gather(): ccw = lax.ppermute(ccw, axis, behind)]
    all_to_all x1, waiting for transfers between devices: 11 us -> 8.74 us  [per_device(): lax.all_to_all(outgoing, TEACH, split_axis=0, concat_axis=0, tiled=True)]
    eq x2, local copies, waits for them, and re-layouts: 0.2 us -> 2.36 us  [per_device(): row_index[:, None] == jnp.arange(table.shape[1], dtype=jnp.int32)[None, :]]
    all_to_all x1, waiting for transfers between devices: 2.14 us -> 4.24 us  [per_device(): lax.all_to_all(packed, 'ty', split_axis=0, concat_axis=0, tiled=True)]
    all_to_all x1, starting transfers between devices: 4.8 us -> 6.79 us  [per_device(): lax.all_to_all(outgoing, TEACH, split_axis=0, concat_axis=0, tiled=True)]
  transfers between devices with their start and end apart: 12 -> 11, of which waited for: 11 -> 8; matrix products, arithmetic and copies ran while one was open for 15% -> 18% of each run, Pallas kernels for 0% -> 0%
where the time goes in v11:
time: 170 us; the launch traced here: 169 us
  starting transfers between devices  62 us (36%)
  waiting for transfers between devices  49.4 us (29%)
  matrix products  21.5 us (13%)
  other arithmetic  16.9 us (10%)
  local copies, waits for them, and re-layouts  16.7 us (10%)
  between operations  2.51 us (1%)
    all_to_all x1, waiting for transfers between devices, per_device(): lax.all_to_all(outbound, 'seq', split_axis=0, concat_axis=0, tiled=True)  18.4 us
    ppermute x3, starting transfers between devices, ring_gather(): ccw = lax.ppermute(ccw, axis, behind)  18.3 us
    ppermute x4, waiting for transfers between devices, ring_gather(): cw = lax.ppermute(cw, axis, ahead)  13.6 us
    ppermute x4, starting transfers between devices, ring_gather(): cw = lax.ppermute(cw, axis, ahead)  11.7 us
    all_to_all x1, starting transfers between devices, per_device(): lax.all_to_all(outbound, 'seq', split_axis=0, concat_axis=0, tiled=True)  10.3 us
    all_to_all x1, waiting for transfers between devices, per_device(): lax.all_to_all(outgoing, TEACH, split_axis=0, concat_axis=0, tiled=True)  8.74 us
    all_to_all x1, starting transfers between devices, per_device(): lax.all_to_all(packed, 'ty', split_axis=0, concat_axis=0, tiled=True)  7.64 us
    all_to_all x1, starting transfers between devices, per_device(): lax.all_to_all(jnp.broadcast_to(local_adjoint.astype(jnp.bfloat16)[None],...  7.2 us
  transfers between devices with their start and end apart: 11, of which 8 were waited for; matrix products, arithmetic and copies ran while one was open for 18% of the time, Pallas kernels for 0%

profile of v11, /device:TPU:1, one launch (start us, length us, event | category | flops | bytes accessed | tf_op | source)
XLA Modules:
  0.0 169.0 jit_solution(6562008353358903982)
XLA Ops:
  0.7 1.2 copy.161
  1.8 0.6 reshape.583
  3.1 1.0 reshape.584
  4.1 1.1 convolution_convert_fusion.1
  5.1 7.6 %all-to-all-start = ((bf16[8,32,640]{2,1,0:T(8,128)(2,1)}), bf16[8,32,640]{2,1,0:T(8,128)(2,1)S(1)}, u32[]{:S(2)}, u32[]{:S(2)}) async-start(bf16[8,32,640]{2,1,0:T(8,128)(2,1)} %bitcast.17), calls=%async_computation | async-start | bytes 655360 | tf_op jit(solution)/shard_map/all_to_all | solution.py:101
  13.4 0.7 negate_multiply_fusion
  14.1 1.2 reduce-window.16
  15.4 0.7 reshape.572
  16.1 1.2 reduce-window.14
  18.6 4.2 %all-to-all-done = bf16[8,32,640]{2,1,0:T(8,128)(2,1)S(1)} async-done(((bf16[8,32,640]{2,1,0:T(8,128)(2,1)}), bf16[8,32,640]{2,1,0:T(8,128)(2,1)S(1)}, u32[]{:S(2)}, u32[]{:S(2)}) %all-to-all-start) | async-done | bytes 327712 | tf_op jit(solution)/shard_map/all_to_all | solution.py:101
  22.9 6.0 %collective-permute-start.3 = (bf16[8,32,640]{2,1,0:T(8,128)(2,1)S(1)}, bf16[8,32,640]{2,1,0:T(8,128)(2,1)S(1)}, u32[]{:S(2)}, u32[]{:S(2)}) collective-permute-start(bf16[8,32,640]{2,1,0:T(8,128)(2,1)S(1)} %all-to-all-done), channel_id=1, source_target_pairs={{0,64},{64,128},{128,192},{192,256},{256,320},{320,384},{384,448},... | collective-permute-start | bytes 983048 | tf_op jit(solution)/shard_map/ppermute | solution.py:66
  28.9 0.8 copy_bitcast_fusion.1
  29.6 8.6 %collective-permute-start = (bf16[8,32,640]{2,1,0:T(8,128)(2,1)S(1)}, bf16[8,32,640]{2,1,0:T(8,128)(2,1)S(1)}, u32[]{:S(2)}, u32[]{:S(2)}) collective-permute-start(bf16[8,32,640]{2,1,0:T(8,128)(2,1)S(1)} %all-to-all-done), channel_id=1, source_target_pairs={{0,448},{64,0},{128,64},{192,128},{256,192},{320,256},{384,320},{4... | collective-permute-start | bytes 983048 | tf_op jit(solution)/shard_map/ppermute | solution.py:69
  38.2 1.3 fusion.23
  39.5 1.9 %collective-permute-done.3 = bf16[8,32,640]{2,1,0:T(8,128)(2,1)S(1)} collective-permute-done((bf16[8,32,640]{2,1,0:T(8,128)(2,1)S(1)}, bf16[8,32,640]{2,1,0:T(8,128)(2,1)S(1)}, u32[]{:S(2)}, u32[]{:S(2)}) %collective-permute-start.3) | collective-permute-done | bytes 327712 | tf_op jit(solution)/shard_map/ppermute | solution.py:66
  41.5 1.9 %collective-permute-start.4 = (bf16[8,32,640]{2,1,0:T(8,128)(2,1)S(1)}, bf16[8,32,640]{2,1,0:T(8,128)(2,1)S(1)}, u32[]{:S(2)}, u32[]{:S(2)}) collective-permute-start(bf16[8,32,640]{2,1,0:T(8,128)(2,1)S(1)} %collective-permute-done.3), channel_id=1, source_target_pairs={{0,64},{64,128},{128,192},{192,256},{256,320},{320,384},{384,448},... | collective-permute-start | bytes 983048 | tf_op jit(solution)/shard_map/ppermute | solution.py:66
  43.4 5.0 %collective-permute-start.1 = (bf16[8,32,640]{2,1,0:T(8,128)(2,1)S(1)}, bf16[8,32,640]{2,1,0:T(8,128)(2,1)S(1)}, u32[]{:S(2)}, u32[]{:S(2)}) collective-permute-start(bf16[8,32,640]{2,1,0:T(8,128)(2,1)S(1)} %collective-permute-done), channel_id=1, source_target_pairs={{0,448},{64,0},{128,64},{192,128},{256,192},{320,256},{384,320},{4... | collective-permute-start | bytes 983048 | tf_op jit(solution)/shard_map/ppermute | solution.py:69
  48.7 2.4 %collective-permute-done.4 = bf16[8,32,640]{2,1,0:T(8,128)(2,1)S(1)} collective-permute-done((bf16[8,32,640]{2,1,0:T(8,128)(2,1)S(1)}, bf16[8,32,640]{2,1,0:T(8,128)(2,1)S(1)}, u32[]{:S(2)}, u32[]{:S(2)}) %collective-permute-start.4) | collective-permute-done | bytes 327712 | tf_op jit(solution)/shard_map/ppermute | solution.py:66
  51.1 1.9 %collective-permute-start.5 = (bf16[8,32,640]{2,1,0:T(8,128)(2,1)S(1)}, bf16[8,32,640]{2,1,0:T(8,128)(2,1)S(1)}, u32[]{:S(2)}, u32[]{:S(2)}) collective-permute-start(bf16[8,32,640]{2,1,0:T(8,128)(2,1)S(1)} %collective-permute-done.4), channel_id=1, source_target_pairs={{0,64},{64,128},{128,192},{192,256},{256,320},{320,384},{384,448},... | collective-permute-start | bytes 983048 | tf_op jit(solution)/shard_map/ppermute | solution.py:66
  53.1 4.7 %collective-permute-start.2 = (bf16[8,32,640]{2,1,0:T(8,128)(2,1)S(1)}, bf16[8,32,640]{2,1,0:T(8,128)(2,1)S(1)}, u32[]{:S(2)}, u32[]{:S(2)}) collective-permute-start(bf16[8,32,640]{2,1,0:T(8,128)(2,1)S(1)} %collective-permute-done.1), channel_id=1, source_target_pairs={{0,448},{64,0},{128,64},{192,128},{256,192},{320,256},{384,320},{4... | collective-permute-start | bytes 983048 | tf_op jit(solution)/shard_map/ppermute | solution.py:69
  57.9 2.3 %collective-permute-done.5 = bf16[8,32,640]{2,1,0:T(8,128)(2,1)S(1)} collective-permute-done((bf16[8,32,640]{2,1,0:T(8,128)(2,1)S(1)}, bf16[8,32,640]{2,1,0:T(8,128)(2,1)S(1)}, u32[]{:S(2)}, u32[]{:S(2)}) %collective-permute-start.5) | collective-permute-done | bytes 327712 | tf_op jit(solution)/shard_map/ppermute | solution.py:66
  60.1 1.9 %collective-permute-start.6 = (bf16[8,32,640]{2,1,0:T(8,128)(2,1)S(1)}, bf16[8,32,640]{2,1,0:T(8,128)(2,1)S(1)}, u32[]{:S(2)}, u32[]{:S(2)}) collective-permute-start(bf16[8,32,640]{2,1,0:T(8,128)(2,1)S(1)} %collective-permute-done.5), channel_id=1, source_target_pairs={{0,64},{64,128},{128,192},{192,256},{256,320},{320,384},{384,448},... | collective-permute-start | bytes 983048 | tf_op jit(solution)/shard_map/ppermute | solution.py:66
  62.2 7.0 %collective-permute-done.6 = bf16[8,32,640]{2,1,0:T(8,128)(2,1)S(1)} collective-permute-done((bf16[8,32,640]{2,1,0:T(8,128)(2,1)S(1)}, bf16[8,32,640]{2,1,0:T(8,128)(2,1)S(1)}, u32[]{:S(2)}, u32[]{:S(2)}) %collective-permute-start.6) | collective-permute-done | bytes 327712 | tf_op jit(solution)/shard_map/ppermute | solution.py:66
  69.7 0.6 multiply_reduce_fusion
  70.5 1.8 %convolution_convert_fusion = bf16[8,256,512]{2,1,0:T(8,128)(2,1)S(1)} fusion(bf16[8,256,640]{2,1,0:T(8,128)(2,1)S(1)} %bitcast.237, bf16[1,640,512]{2,1,0:T(8,128)(2,1)S(1)} %copy-done), kind=kOutput, calls=%fused_computation.7 | convolution fusion | flops 1343225856 | bytes 5373952 | tf_op jit(solution)/shard_map/dot_general | solution.py:129
  72.3 1.8 %pad_maximum_fusion = bf16[8,323,512]{2,1,0:T(8,128)(2,1)} fusion(bf16[8,66,512]{2,1,0:T(8,128)(2,1)S(1)} %broadcast_in_dim.134, bf16[8,1,512]{2,1,0:T(2,128)(2,1)S(1)} %copy.163, bf16[8,256,512]{2,1,0:T(8,128)(2,1)S(1)} %convolution_convert_fusion), kind=kLoop, calls=%fused_computation.6 | loop fusion | flops 7938048 | bytes 5292032 | tf_op jit(solution)/shard_map/concatenate | solution.py:141
  74.1 10.3 %all-to-all-start.1 = ((bf16[8,323,512]{2,1,0:T(8,128)(2,1)}), bf16[8,323,512]{2,1,0:T(8,128)(2,1)S(1)}, u32[]{:S(2)}, u32[]{:S(2)}) async-start(bf16[8,323,512]{2,1,0:T(8,128)(2,1)} %pad_maximum_fusion), calls=%async_computation.1 | async-start | bytes 5373952 | tf_op jit(solution)/shard_map/all_to_all | solution.py:142
  84.4 1.3 dynamic-slice_bitcast_fusion
  85.7 0.8 copy.166
  86.5 3.2 %select_reduce_fusion = s32[8,128]{0,1:T(8,128)} fusion(s32[8,128]{0,1:T(8,128)S(1)} %copy.166), kind=kOutput, calls=%fused_computation.50 | output fusion | flops 1096704 | bytes 8192 | tf_op jit(solution)/shard_map/jit(cumsum)/reduce_window_sum | solution.py:23
  89.7 0.9 copy.167
  90.5 0.7 bitcast_add_fusion.1
  91.3 0.8 eq.146
  92.0 1.6 copy.168
  94.4 0.8 broadcast_bitcast_fusion
  95.1 1.5 convolution_multiply_fusion.1
  96.7 1.3 convolution_bitcast_fusion.7
  98.0 0.6 fusion.62
  98.6 18.4 %all-to-all-done.1 = bf16[8,323,512]{2,1,0:T(8,128)(2,1)S(1)} async-done(((bf16[8,323,512]{2,1,0:T(8,128)(2,1)}), bf16[8,323,512]{2,1,0:T(8,128)(2,1)S(1)}, u32[]{:S(2)}, u32[]{:S(2)}) %all-to-all-start.1) | async-done | bytes 2646048 | tf_op jit(solution)/shard_map/all_to_all | solution.py:142
  117.3 0.8 copy-done.4
  118.1 0.3 convert_reduce_fusion
  118.6 0.8 copy.169
  119.5 6.8 %all-to-all-start.2 = ((bf16[64,256,8]{1,2,0:T(8,128)(2,1)}), bf16[64,256,8]{1,2,0:T(8,128)(2,1)S(1)}, u32[]{:S(2)}, u32[]{:S(2)}) async-start(bf16[64,256,8]{1,2,0:T(8,128)(2,1)} %bitcast.43), calls=%async_computation.2 | async-start | bytes 524288 | tf_op jit(solution)/shard_map/all_to_all | solution.py:155
  126.2 0.9 select_reduce_fusion.2
  127.1 0.6 broadcast_select_fusion
  127.8 0.7 broadcast_select_fusion.1
  128.5 1.5 multiply_reduce_fusion.2
  130.0 8.7 %all-to-all-done.2 = bf16[64,256,8]{1,2,0:T(8,128)(2,1)S(1)} async-done(((bf16[64,256,8]{1,2,0:T(8,128)(2,1)}), bf16[64,256,8]{1,2,0:T(8,128)(2,1)S(1)}, u32[]{:S(2)}, u32[]{:S(2)}) %all-to-all-start.2) | async-done | bytes 262176 | tf_op jit(solution)/shard_map/all_to_all | solution.py:155
  138.8 2.5 %fusion.16 = f32[256,4,1,64]{0,3,1,2:T(8,128)S(1)} fusion(bf16[64,2048,1]{1,0,2:T(8,128)(2,1)S(1)} %bitcast.248, s32[256,4]{0,1:T(4,128)} %copy.168), kind=kOutput, calls=%fused_computation.29 | convolution fusion | flops 270532608 | bytes 528384 | tf_op jit(solution)/shard_map/rq,jqc->rjc/dot_general | solution.py:169
  141.3 0.4 fusion.20
  141.7 1.8 %convolution_multiply_fusion = f32[4,256,256]{2,1,0:T(8,128)S(1)} fusion(f32[4,256]{1,0:T(4,128)} %copy-done.11, s32[4,256]{1,0:T(4,128)} %bitcast.252, pred[256,256]{1,0:T(8,128)(4,1)} %copy-done.7, f32[256,4,1,64]{0,3,1,2:T(8,128)S(1)} %fusion.20, bf16[256,4,1,64]{0,3,2,1:T(8,128)(2,1)S(1)} %copy-done.5, f32[256,4]{0,1:T(4,128)S(1)} %get-tuple-element.33), kind=kOutput, calls=%fused_computation.8 | convolution fusion | flops 102367232 | bytes 1519616 | tf_op jit(solution)/shard_map/ibhp,jbhp->bhij/dot_general | solution.py:196
  143.6 0.3 fusion.24
  143.8 2.2 %convolution_bitcast_fusion.1 = f32[256,4,1,128]{3,0,1,2:T(8,128)} fusion(f32[4,256,256]{2,1,0:T(8,128)S(1)} %convolution_multiply_fusion, bf16[256,4,128]{2,1,0:T(4,128)(2,1)} %bitcast.246), kind=kOutput, calls=%fused_computation.11 | convolution fusion | flops 201326592 | bytes 1835008 | tf_op jit(solution)/shard_map/bhij,jbhn->ibhn/dot_general | solution.py:201
  146.1 0.9 broadcast_in_dim.140
  147.0 7.2 %all-to-all-start.3 = ((bf16[8,4,1,128,64]{3,4,2,1,0:T(8,128)(2,1)}), bf16[8,4,1,128,64]{3,4,2,1,0:T(8,128)(2,1)}, u32[]{:S(2)}, u32[]{:S(2)}) async-start(bf16[8,4,1,128,64]{3,4,2,1,0:T(8,128)(2,1)} %broadcast_in_dim.140), calls=%async_computation.3 | async-start | bytes 1048576 | tf_op jit(solution)/shard_map/all_to_all | solution.py:183
  154.2 2.1 %fusion.8 = bf16[256,4,1,128]{3,0,1,2:T(8,128)(2,1)S(1)} fusion(f32[256,4,1,128]{3,0,1,2:T(8,128)} %convolution_bitcast_fusion.1, f32[4,64,128]{2,1,0:T(8,128)S(1)} %multiply_reduce_fusion.2, f32[256,4,1,64]{0,3,1,2:T(8,128)S(1)} %fusion.20, f32[256,4]{0,1:T(4,128)S(1)} %get-tuple-element.23), kind=kOutput, calls=%fused_computation.19 | convolution fusion | flops 101056512 | bytes 1183744 | tf_op jit(solution)/shard_map/ibhp,bhpn->ibhn/dot_general | solution.py:202
  156.3 0.9 copy.180
  157.2 1.1 convolution_bitcast_fusion.6
  158.4 0.8 convolution_bitcast_fusion.3
  159.2 4.5 %all-to-all-done.3 = bf16[8,4,1,128,64]{3,4,2,1,0:T(8,128)(2,1)} async-done(((bf16[8,4,1,128,64]{3,4,2,1,0:T(8,128)(2,1)}), bf16[8,4,1,128,64]{3,4,2,1,0:T(8,128)(2,1)}, u32[]{:S(2)}, u32[]{:S(2)}) %all-to-all-start.3) | async-done | bytes 524320 | tf_op jit(solution)/shard_map/all_to_all | solution.py:183
  163.7 1.2 multiply_reduce_fusion.1
  164.9 1.1 fusion.9
  166.0 0.9 copy.179
  166.9 2.1 %fusion.22 = bf16[256,4,1,64]{0,3,2,1:T(8,128)(2,1)} fusion(f32[256,4,1,64]{0,3,1,2:T(8,128)} %convolution_bitcast_fusion.6, f32[4,128,64]{1,2,0:T(8,128)S(1)} %multiply_reduce_fusion.1, f32[256,4,1,64]{0,3,1,2:T(8,128)S(1)} %fusion.20, bf16[256,4,128]{2,1,0:T(4,128)(2,1)} %bitcast.247, f32[256,4]{0,1:T(4,128)S(1)} %get-tuple-element.34, f32[]{:T(128)} %bitcast.236, ...), kind=kOutput, calls=%fused_computation.35 | convolution fusion | flops 101056512 | bytes 1056772 | tf_op jit(solution)/shard_map/jbhn,bhnp->jbhp/dot_general | solution.py:192
  (89 shorter events, 3.7 us)
Async XLA Ops:
  0.6 69.8 %copy-start = (bf16[1,640,512]{2,1,0:T(8,128)(2,1)S(1)}, bf16[1,640,512]{2,1,0:T(8,128)(2,1)}, u32[]{:S(2)}) copy-start(bf16[1,640,512]{2,1,0:T(8,128)(2,1)} %param.11) | copy-start | bytes 1966084
  2.5 26.4 %copy-start.8 = (s32[8192]{0:T(1024)}, s32[8192]{0:T(1024)S(1)}, u32[]{:S(2)}) copy-start(s32[8192]{0:T(1024)S(1)} %reshape.583) | copy-start | bytes 98308
  5.1 17.8 %all-to-all-start = ((bf16[8,32,640]{2,1,0:T(8,128)(2,1)}), bf16[8,32,640]{2,1,0:T(8,128)(2,1)S(1)}, u32[]{:S(2)}, u32[]{:S(2)}) async-start(bf16[8,32,640]{2,1,0:T(8,128)(2,1)} %bitcast.17), calls=%async_computation | async-start | bytes 655360 | tf_op jit(solution)/shard_map/all_to_all | solution.py:101
  17.9 0.6 copy-start.9
  18.1 0.6 copy-start.10
  22.9 18.6 %collective-permute-start.3 = (bf16[8,32,640]{2,1,0:T(8,128)(2,1)S(1)}, bf16[8,32,640]{2,1,0:T(8,128)(2,1)S(1)}, u32[]{:S(2)}, u32[]{:S(2)}) collective-permute-start(bf16[8,32,640]{2,1,0:T(8,128)(2,1)S(1)} %all-to-all-done), channel_id=1, source_target_pairs={{0,64},{64,128},{128,192},{192,256},{256,320},{320,384},{384,448},... | collective-permute-start | bytes 983048 | tf_op jit(solution)/shard_map/ppermute | solution.py:66
  29.6 13.8 %collective-permute-start = (bf16[8,32,640]{2,1,0:T(8,128)(2,1)S(1)}, bf16[8,32,640]{2,1,0:T(8,128)(2,1)S(1)}, u32[]{:S(2)}, u32[]{:S(2)}) collective-permute-start(bf16[8,32,640]{2,1,0:T(8,128)(2,1)S(1)} %all-to-all-done), channel_id=1, source_target_pairs={{0,448},{64,0},{128,64},{192,128},{256,192},{320,256},{384,320},{4... | collective-permute-start | bytes 983048 | tf_op jit(solution)/shard_map/ppermute | solution.py:69
  41.5 9.6 %collective-permute-start.4 = (bf16[8,32,640]{2,1,0:T(8,128)(2,1)S(1)}, bf16[8,32,640]{2,1,0:T(8,128)(2,1)S(1)}, u32[]{:S(2)}, u32[]{:S(2)}) collective-permute-start(bf16[8,32,640]{2,1,0:T(8,128)(2,1)S(1)} %collective-permute-done.3), channel_id=1, source_target_pairs={{0,64},{64,128},{128,192},{192,256},{256,320},{320,384},{384,448},... | collective-permute-start | bytes 983048 | tf_op jit(solution)/shard_map/ppermute | solution.py:66
  43.4 9.7 %collective-permute-start.1 = (bf16[8,32,640]{2,1,0:T(8,128)(2,1)S(1)}, bf16[8,32,640]{2,1,0:T(8,128)(2,1)S(1)}, u32[]{:S(2)}, u32[]{:S(2)}) collective-permute-start(bf16[8,32,640]{2,1,0:T(8,128)(2,1)S(1)} %collective-permute-done), channel_id=1, source_target_pairs={{0,448},{64,0},{128,64},{192,128},{256,192},{320,256},{384,320},{4... | collective-permute-start | bytes 983048 | tf_op jit(solution)/shard_map/ppermute | solution.py:69
  51.1 9.0 %collective-permute-start.5 = (bf16[8,32,640]{2,1,0:T(8,128)(2,1)S(1)}, bf16[8,32,640]{2,1,0:T(8,128)(2,1)S(1)}, u32[]{:S(2)}, u32[]{:S(2)}) collective-permute-start(bf16[8,32,640]{2,1,0:T(8,128)(2,1)S(1)} %collective-permute-done.4), channel_id=1, source_target_pairs={{0,64},{64,128},{128,192},{192,256},{256,320},{320,384},{384,448},... | collective-permute-start | bytes 983048 | tf_op jit(solution)/shard_map/ppermute | solution.py:66
  53.1 9.0 %collective-permute-start.2 = (bf16[8,32,640]{2,1,0:T(8,128)(2,1)S(1)}, bf16[8,32,640]{2,1,0:T(8,128)(2,1)S(1)}, u32[]{:S(2)}, u32[]{:S(2)}) collective-permute-start(bf16[8,32,640]{2,1,0:T(8,128)(2,1)S(1)} %collective-permute-done.1), channel_id=1, source_target_pairs={{0,448},{64,0},{128,64},{192,128},{256,192},{320,256},{384,320},{4... | collective-permute-start | bytes 983048 | tf_op jit(solution)/shard_map/ppermute | solution.py:69
  60.1 9.0 %collective-permute-start.6 = (bf16[8,32,640]{2,1,0:T(8,128)(2,1)S(1)}, bf16[8,32,640]{2,1,0:T(8,128)(2,1)S(1)}, u32[]{:S(2)}, u32[]{:S(2)}) collective-permute-start(bf16[8,32,640]{2,1,0:T(8,128)(2,1)S(1)} %collective-permute-done.5), channel_id=1, source_target_pairs={{0,64},{64,128},{128,192},{192,256},{256,320},{320,384},{384,448},... | collective-permute-start | bytes 983048 | tf_op jit(solution)/shard_map/ppermute | solution.py:66
  74.1 22.5 %copy-start.5 = (bf16[256,4,1,64]{0,3,2,1:T(8,128)(2,1)S(1)}, bf16[256,4,1,64]{0,3,2,1:T(8,128)(2,1)}, u32[]{:S(2)}) copy-start(bf16[256,4,1,64]{0,3,2,1:T(8,128)(2,1)} %param.13) | copy-start | bytes 393220
  74.1 42.8 %all-to-all-start.1 = ((bf16[8,323,512]{2,1,0:T(8,128)(2,1)}), bf16[8,323,512]{2,1,0:T(8,128)(2,1)S(1)}, u32[]{:S(2)}, u32[]{:S(2)}) async-start(bf16[8,323,512]{2,1,0:T(8,128)(2,1)} %pad_maximum_fusion), calls=%async_computation.1 | async-start | bytes 5373952 | tf_op jit(solution)/shard_map/all_to_all | solution.py:142
  94.3 3.7 %copy-start.12 = (pred[8]{0:T(512)(128)(4,1)}, pred[8]{0:T(512)(128)(4,1)S(1)}, u32[]{:S(2)}) copy-start(pred[8]{0:T(512)(128)(4,1)S(1)} %iota_compare_fusion.10) | copy-start | bytes 28
  94.3 3.7 %copy-start.13 = (pred[8]{0:T(512)(128)(4,1)}, pred[8]{0:T(512)(128)(4,1)S(1)}, u32[]{:S(2)}) copy-start(pred[8]{0:T(512)(128)(4,1)S(1)} %iota_compare_fusion.9) | copy-start | bytes 28
  94.3 25.1 %copy-start.7 = (pred[256,256]{1,0:T(8,128)(4,1)}, pred[256,256]{1,0:T(8,128)(4,1)S(1)}, u32[]{:S(2)}) copy-start(pred[256,256]{1,0:T(8,128)(4,1)S(1)} %iota_compare_fusion.3) | copy-start | bytes 196612
  95.1 2.9 %copy-start.11 = (f32[4,256]{1,0:T(4,128)}, f32[4,256]{1,0:T(4,128)S(1)}, u32[]{:S(2)}) copy-start(f32[4,256]{1,0:T(4,128)S(1)} %bitcast_add_fusion) | copy-start | bytes 12292
  96.7 1.3 copy-start.1
  117.3 0.8 copy-start.4
  118.5 22.8 %copy-start.3 = (bf16[256,4,1,128]{3,1,2,0:T(4,128)(2,1)S(1)}, bf16[256,4,1,128]{3,1,2,0:T(4,128)(2,1)}, u32[]{:S(2)}) copy-start(bf16[256,4,1,128]{3,1,2,0:T(4,128)(2,1)} %param.15) | copy-start | bytes 786436
  118.5 22.8 %copy-start.6 = (f32[256,4,1,64]{0,3,1,2:T(8,128)S(1)}, f32[256,4,1,64]{0,3,1,2:T(8,128)}, u32[]{:S(2)}) copy-start(f32[256,4,1,64]{0,3,1,2:T(8,128)} %convolution_bitcast_fusion.7) | copy-start | bytes 786436
  119.5 19.3 %all-to-all-start.2 = ((bf16[64,256,8]{1,2,0:T(8,128)(2,1)}), bf16[64,256,8]{1,2,0:T(8,128)(2,1)S(1)}, u32[]{:S(2)}, u32[]{:S(2)}) async-start(bf16[64,256,8]{1,2,0:T(8,128)(2,1)} %bitcast.43), calls=%async_computation.2 | async-start | bytes 524288 | tf_op jit(solution)/shard_map/all_to_all | solution.py:155
  141.3 16.0 %copy-start.2 = (f32[4,256,256]{2,1,0:T(8,128)S(1)}, f32[4,256,256]{2,1,0:T(8,128)}, u32[]{:S(2)}) copy-start(f32[4,256,256]{2,1,0:T(8,128)} %copy-done.1) | copy-start | bytes 3145732
  147.0 16.7 %all-to-all-start.3 = ((bf16[8,4,1,128,64]{3,4,2,1,0:T(8,128)(2,1)}), bf16[8,4,1,128,64]{3,4,2,1,0:T(8,128)(2,1)}, u32[]{:S(2)}, u32[]{:S(2)}) async-start(bf16[8,4,1,128,64]{3,4,2,1,0:T(8,128)(2,1)} %broadcast_in_dim.140), calls=%async_computation.3 | async-start | bytes 1048576 | tf_op jit(solution)/shard_map/all_to_all | solution.py:183

commit v12 on v11

--- a/solution.py
+++ b/solution.py
@@ -151,10 +151,9 @@
     scaled = (summed[:group] * row_scale[:, None]).astype(jnp.bfloat16)
     scaled = scaled.reshape(group, heads_all, -1)
     cols = scaled.shape[-1]
-    outgoing = scaled.transpose(1, 0, 2)
+    outgoing = scaled.transpose(1, 2, 0)
     arrived = lax.all_to_all(outgoing, TEACH, split_axis=0, concat_axis=0, tiled=True)
-    arrived = arrived.reshape(n_z, n_y, n_y * CAP, cols)
-    table = arrived.reshape(n_z, n_y * n_y * CAP, cols)
+    table = arrived.reshape(n_z, n_y, cols, n_y * CAP)
 
     shard_rows = n_y * block_rows
     shard_fam = lax.dynamic_slice_in_dim(
@@ -163,10 +162,11 @@
     shard_slots = family_slots(shard_fam)
     sources = jnp.arange(n_y, dtype=jnp.int32)[:, None]
     row_index = ((shard_fam * n_y + sources) * CAP + shard_slots).reshape(shard_rows)
-    chooser = (row_index[:, None] == jnp.arange(table.shape[1], dtype=jnp.int32)[None, :]).astype(
+    chooser = (row_index[:, None] == jnp.arange(n_y * n_y * CAP, dtype=jnp.int32)[None, :]).astype(
         jnp.bfloat16
     )
-    picked = jnp.einsum("rq,jqc->rjc", chooser, table, preferred_element_type=jnp.float32)
+    chooser = chooser.reshape(shard_rows, n_y, n_y * CAP)
+    picked = jnp.einsum("rfq,jfcq->rjc", chooser, table, preferred_element_type=jnp.float32)
     target = picked.reshape(n_y * block_pos, batch_n, 1, P_SIZE)
 
     state_in = combine(chain_weights(through_all, place, False), gathered[:, :, :, :rows])

time: 170 us -> 170 us (level)
    unnamed x48 -> x46, local copies, waits for them, and re-layouts: 5.43 us -> 4.65 us
where the time goes in v12:
time: 170 us; the launch traced here: 168 us
  starting transfers between devices  62.2 us (37%)
  waiting for transfers between devices  47.9 us (28%)
  matrix products  21.8 us (13%)
  other arithmetic  17.1 us (10%)
  local copies, waits for them, and re-layouts  16.9 us (10%)
  between operations  2.46 us (1%)
    ppermute x3, starting transfers between devices, ring_gather(): ccw = lax.ppermute(ccw, axis, behind)  18.3 us
    all_to_all x1, waiting for transfers between devices, per_device(): lax.all_to_all(outbound, 'seq', split_axis=0, concat_axis=0, tiled=True)  17.8 us
    ppermute x4, waiting for transfers between devices, ring_gather(): cw = lax.ppermute(cw, axis, ahead)  13.6 us
    ppermute x4, starting transfers between devices, ring_gather(): cw = lax.ppermute(cw, axis, ahead)  11.7 us
    all_to_all x1, starting transfers between devices, per_device(): lax.all_to_all(outbound, 'seq', split_axis=0, concat_axis=0, tiled=True)  10.3 us
    all_to_all x1, waiting for transfers between devices, per_device(): lax.all_to_all(outgoing, TEACH, split_axis=0, concat_axis=0, tiled=True)  7.83 us
    all_to_all x1, starting transfers between devices, per_device(): lax.all_to_all(packed, 'ty', split_axis=0, concat_axis=0, tiled=True)  7.64 us
    all_to_all x1, starting transfers between devices, per_device(): lax.all_to_all(jnp.broadcast_to(local_adjoint.astype(jnp.bfloat16)[None],...  7.19 us
  transfers between devices with their start and end apart: 11, of which 8 were waited for; matrix products, arithmetic and copies ran while one was open for 18% of the time, Pallas kernels for 0%

profile of v12, /device:TPU:1, one launch (start us, length us, event | category | flops | bytes accessed | tf_op | source)
XLA Modules:
  0.0 168.3 jit_solution(3307019597714916666)
XLA Ops:
  0.7 1.2 copy.165
  1.8 0.6 reshape.598
  3.1 1.0 reshape.599
  4.1 1.1 convolution_convert_fusion.1
  5.1 7.6 %all-to-all-start = ((bf16[8,32,640]{2,1,0:T(8,128)(2,1)}), bf16[8,32,640]{2,1,0:T(8,128)(2,1)S(1)}, u32[]{:S(2)}, u32[]{:S(2)}) async-start(bf16[8,32,640]{2,1,0:T(8,128)(2,1)} %bitcast.17), calls=%async_computation | async-start | bytes 655360 | tf_op jit(solution)/shard_map/all_to_all | solution.py:101
  13.4 0.7 negate_multiply_fusion
  14.1 1.2 reduce-window.16
  15.4 0.7 reshape.587
  16.1 1.2 reduce-window.14
  18.7 4.2 %all-to-all-done = bf16[8,32,640]{2,1,0:T(8,128)(2,1)S(1)} async-done(((bf16[8,32,640]{2,1,0:T(8,128)(2,1)}), bf16[8,32,640]{2,1,0:T(8,128)(2,1)S(1)}, u32[]{:S(2)}, u32[]{:S(2)}) %all-to-all-start) | async-done | bytes 327712 | tf_op jit(solution)/shard_map/all_to_all | solution.py:101
  22.9 6.0 %collective-permute-start.3 = (bf16[8,32,640]{2,1,0:T(8,128)(2,1)S(1)}, bf16[8,32,640]{2,1,0:T(8,128)(2,1)S(1)}, u32[]{:S(2)}, u32[]{:S(2)}) collective-permute-start(bf16[8,32,640]{2,1,0:T(8,128)(2,1)S(1)} %all-to-all-done), channel_id=1, source_target_pairs={{0,64},{64,128},{128,192},{192,256},{256,320},{320,384},{384,448},... | collective-permute-start | bytes 983048 | tf_op jit(solution)/shard_map/ppermute | solution.py:66
  28.9 0.8 copy_bitcast_fusion.1
  29.6 8.6 %collective-permute-start = (bf16[8,32,640]{2,1,0:T(8,128)(2,1)S(1)}, bf16[8,32,640]{2,1,0:T(8,128)(2,1)S(1)}, u32[]{:S(2)}, u32[]{:S(2)}) collective-permute-start(bf16[8,32,640]{2,1,0:T(8,128)(2,1)S(1)} %all-to-all-done), channel_id=1, source_target_pairs={{0,448},{64,0},{128,64},{192,128},{256,192},{320,256},{384,320},{4... | collective-permute-start | bytes 983048 | tf_op jit(solution)/shard_map/ppermute | solution.py:69
  38.2 1.3 fusion.25
  39.5 1.9 %collective-permute-done.3 = bf16[8,32,640]{2,1,0:T(8,128)(2,1)S(1)} collective-permute-done((bf16[8,32,640]{2,1,0:T(8,128)(2,1)S(1)}, bf16[8,32,640]{2,1,0:T(8,128)(2,1)S(1)}, u32[]{:S(2)}, u32[]{:S(2)}) %collective-permute-start.3) | collective-permute-done | bytes 327712 | tf_op jit(solution)/shard_map/ppermute | solution.py:66
  41.5 1.9 %collective-permute-start.4 = (bf16[8,32,640]{2,1,0:T(8,128)(2,1)S(1)}, bf16[8,32,640]{2,1,0:T(8,128)(2,1)S(1)}, u32[]{:S(2)}, u32[]{:S(2)}) collective-permute-start(bf16[8,32,640]{2,1,0:T(8,128)(2,1)S(1)} %collective-permute-done.3), channel_id=1, source_target_pairs={{0,64},{64,128},{128,192},{192,256},{256,320},{320,384},{384,448},... | collective-permute-start | bytes 983048 | tf_op jit(solution)/shard_map/ppermute | solution.py:66
  43.4 5.0 %collective-permute-start.1 = (bf16[8,32,640]{2,1,0:T(8,128)(2,1)S(1)}, bf16[8,32,640]{2,1,0:T(8,128)(2,1)S(1)}, u32[]{:S(2)}, u32[]{:S(2)}) collective-permute-start(bf16[8,32,640]{2,1,0:T(8,128)(2,1)S(1)} %collective-permute-done), channel_id=1, source_target_pairs={{0,448},{64,0},{128,64},{192,128},{256,192},{320,256},{384,320},{4... | collective-permute-start | bytes 983048 | tf_op jit(solution)/shard_map/ppermute | solution.py:69
  48.7 2.4 %collective-permute-done.4 = bf16[8,32,640]{2,1,0:T(8,128)(2,1)S(1)} collective-permute-done((bf16[8,32,640]{2,1,0:T(8,128)(2,1)S(1)}, bf16[8,32,640]{2,1,0:T(8,128)(2,1)S(1)}, u32[]{:S(2)}, u32[]{:S(2)}) %collective-permute-start.4) | collective-permute-done | bytes 327712 | tf_op jit(solution)/shard_map/ppermute | solution.py:66
  51.1 1.9 %collective-permute-start.5 = (bf16[8,32,640]{2,1,0:T(8,128)(2,1)S(1)}, bf16[8,32,640]{2,1,0:T(8,128)(2,1)S(1)}, u32[]{:S(2)}, u32[]{:S(2)}) collective-permute-start(bf16[8,32,640]{2,1,0:T(8,128)(2,1)S(1)} %collective-permute-done.4), channel_id=1, source_target_pairs={{0,64},{64,128},{128,192},{192,256},{256,320},{320,384},{384,448},... | collective-permute-start | bytes 983048 | tf_op jit(solution)/shard_map/ppermute | solution.py:66
  53.1 4.7 %collective-permute-start.2 = (bf16[8,32,640]{2,1,0:T(8,128)(2,1)S(1)}, bf16[8,32,640]{2,1,0:T(8,128)(2,1)S(1)}, u32[]{:S(2)}, u32[]{:S(2)}) collective-permute-start(bf16[8,32,640]{2,1,0:T(8,128)(2,1)S(1)} %collective-permute-done.1), channel_id=1, source_target_pairs={{0,448},{64,0},{128,64},{192,128},{256,192},{320,256},{384,320},{4... | collective-permute-start | bytes 983048 | tf_op jit(solution)/shard_map/ppermute | solution.py:69
  57.9 2.3 %collective-permute-done.5 = bf16[8,32,640]{2,1,0:T(8,128)(2,1)S(1)} collective-permute-done((bf16[8,32,640]{2,1,0:T(8,128)(2,1)S(1)}, bf16[8,32,640]{2,1,0:T(8,128)(2,1)S(1)}, u32[]{:S(2)}, u32[]{:S(2)}) %collective-permute-start.5) | collective-permute-done | bytes 327712 | tf_op jit(solution)/shard_map/ppermute | solution.py:66
  60.1 1.9 %collective-permute-start.6 = (bf16[8,32,640]{2,1,0:T(8,128)(2,1)S(1)}, bf16[8,32,640]{2,1,0:T(8,128)(2,1)S(1)}, u32[]{:S(2)}, u32[]{:S(2)}) collective-permute-start(bf16[8,32,640]{2,1,0:T(8,128)(2,1)S(1)} %collective-permute-done.5), channel_id=1, source_target_pairs={{0,64},{64,128},{128,192},{192,256},{256,320},{320,384},{384,448},... | collective-permute-start | bytes 983048 | tf_op jit(solution)/shard_map/ppermute | solution.py:66
  62.2 7.0 %collective-permute-done.6 = bf16[8,32,640]{2,1,0:T(8,128)(2,1)S(1)} collective-permute-done((bf16[8,32,640]{2,1,0:T(8,128)(2,1)S(1)}, bf16[8,32,640]{2,1,0:T(8,128)(2,1)S(1)}, u32[]{:S(2)}, u32[]{:S(2)}) %collective-permute-start.6) | collective-permute-done | bytes 327712 | tf_op jit(solution)/shard_map/ppermute | solution.py:66
  69.7 0.6 multiply_reduce_fusion
  70.5 1.8 %convolution_convert_fusion = bf16[8,256,512]{2,1,0:T(8,128)(2,1)S(1)} fusion(bf16[8,256,640]{2,1,0:T(8,128)(2,1)S(1)} %bitcast.234, bf16[1,640,512]{2,1,0:T(8,128)(2,1)S(1)} %copy-done), kind=kOutput, calls=%fused_computation.7 | convolution fusion | flops 1343225856 | bytes 5373952 | tf_op jit(solution)/shard_map/dot_general | solution.py:129
  72.3 1.8 %pad_maximum_fusion = bf16[8,323,512]{2,1,0:T(8,128)(2,1)} fusion(bf16[8,66,512]{2,1,0:T(8,128)(2,1)S(1)} %broadcast_in_dim.134, bf16[8,1,512]{2,1,0:T(2,128)(2,1)S(1)} %copy.167, bf16[8,256,512]{2,1,0:T(8,128)(2,1)S(1)} %convolution_convert_fusion), kind=kLoop, calls=%fused_computation.6 | loop fusion | flops 7938048 | bytes 5292032 | tf_op jit(solution)/shard_map/concatenate | solution.py:141
  74.1 10.3 %all-to-all-start.1 = ((bf16[8,323,512]{2,1,0:T(8,128)(2,1)}), bf16[8,323,512]{2,1,0:T(8,128)(2,1)S(1)}, u32[]{:S(2)}, u32[]{:S(2)}) async-start(bf16[8,323,512]{2,1,0:T(8,128)(2,1)} %pad_maximum_fusion), calls=%async_computation.1 | async-start | bytes 5373952 | tf_op jit(solution)/shard_map/all_to_all | solution.py:142
  85.1 1.3 dynamic-slice_bitcast_fusion
  86.4 0.8 copy.170
  87.2 3.2 %select_reduce_fusion = s32[8,128]{0,1:T(8,128)} fusion(s32[8,128]{0,1:T(8,128)S(1)} %copy.170), kind=kOutput, calls=%fused_computation.50 | output fusion | flops 1096704 | bytes 8192 | tf_op jit(solution)/shard_map/jit(cumsum)/reduce_window_sum | solution.py:23
  90.3 0.9 copy.171
  91.2 0.7 bitcast_add_fusion.1
  91.9 0.8 eq.142
  92.7 1.6 copy.172
  94.3 0.6 multiply_add_fusion
  94.9 0.8 broadcast_bitcast_fusion
  95.7 1.5 convolution_multiply_fusion.1
  97.3 1.3 convolution_bitcast_fusion.7
  98.6 0.6 fusion.66
  99.2 17.8 %all-to-all-done.1 = bf16[8,323,512]{2,1,0:T(8,128)(2,1)S(1)} async-done(((bf16[8,323,512]{2,1,0:T(8,128)(2,1)}), bf16[8,323,512]{2,1,0:T(8,128)(2,1)S(1)}, u32[]{:S(2)}, u32[]{:S(2)}) %all-to-all-start.1) | async-done | bytes 2646048 | tf_op jit(solution)/shard_map/all_to_all | solution.py:142
  117.0 0.3 convert_reduce_fusion
  117.3 0.8 fusion.32
  118.1 1.8 %copy.173 = bf16[256,512]{0,1:T(8,128)(2,1)} copy(bf16[256,512]{1,0:T(8,128)(2,1)} %fusion.32) | data formatting | bytes 524288 | tf_op jit(solution)/shard_map/convert_element_type | solution.py:151
  119.9 7.0 %all-to-all-start.2 = ((bf16[64,8,256]{2,1,0:T(8,128)(2,1)}), bf16[64,8,256]{2,1,0:T(8,128)(2,1)}, u32[]{:S(2)}, u32[]{:S(2)}) async-start(bf16[64,8,256]{2,1,0:T(8,128)(2,1)} %bitcast.245), calls=%async_computation.2 | async-start | bytes 524288 | tf_op jit(solution)/shard_map/all_to_all | solution.py:155
  127.4 0.9 select_reduce_fusion.2
  128.2 0.6 broadcast_select_fusion
  129.0 0.6 broadcast_select_fusion.1
  129.6 0.5 multiply_reduce_fusion.2
  130.0 1.4 fusion.14
  131.5 7.8 %all-to-all-done.2 = bf16[64,8,256]{2,1,0:T(8,128)(2,1)} async-done(((bf16[64,8,256]{2,1,0:T(8,128)(2,1)}), bf16[64,8,256]{2,1,0:T(8,128)(2,1)}, u32[]{:S(2)}, u32[]{:S(2)}) %all-to-all-start.2) | async-done | bytes 262176 | tf_op jit(solution)/shard_map/all_to_all | solution.py:155
  139.3 2.7 %fusion.19 = f32[256,4,1,64]{0,3,1,2:T(8,128)S(1)} fusion(f32[256,4,1,64]{0,3,1,2:T(8,128)S(1)} %fusion.14, s32[8,256]{1,0:T(8,128)} %multiply_add_fusion, s32[256,4]{0,1:T(4,128)} %copy.172, bf16[8,8,8,256]{3,1,2,0:T(8,128)(2,1)} %bitcast.44), kind=kOutput, calls=%fused_computation.30 | convolution fusion | flops 270598144 | bytes 798720 | tf_op jit(solution)/shard_map/rfq,jfcq->rjc/dot_general | solution.py:169
  142.0 1.8 %convolution_multiply_fusion = f32[4,256,256]{2,1,0:T(8,128)S(1)} fusion(f32[4,256]{1,0:T(4,128)} %copy-done.10, s32[4,256]{1,0:T(4,128)} %bitcast.249, pred[256,256]{1,0:T(8,128)(4,1)} %copy-done.6, f32[256,4,1,64]{0,3,1,2:T(8,128)S(1)} %fusion.19, bf16[256,4,1,64]{0,3,2,1:T(8,128)(2,1)S(1)} %copy-done.4, f32[256,4]{0,1:T(4,128)S(1)} %get-tuple-element.33), kind=kOutput, calls=%fused_computation.8 | convolution fusion | flops 102367232 | bytes 1519616 | tf_op jit(solution)/shard_map/ibhp,jbhp->bhij/dot_general | solution.py:196
  144.1 1.3 convolution_bitcast_fusion.1
  145.4 0.9 broadcast_in_dim.140
  146.3 7.2 %all-to-all-start.3 = ((bf16[8,4,1,128,64]{3,4,2,1,0:T(8,128)(2,1)}), bf16[8,4,1,128,64]{3,4,2,1,0:T(8,128)(2,1)}, u32[]{:S(2)}, u32[]{:S(2)}) async-start(bf16[8,4,1,128,64]{3,4,2,1,0:T(8,128)(2,1)} %broadcast_in_dim.140), calls=%async_computation.3 | async-start | bytes 1048576 | tf_op jit(solution)/shard_map/all_to_all | solution.py:183
  153.5 2.1 %fusion.8 = bf16[256,4,1,128]{3,0,1,2:T(8,128)(2,1)S(1)} fusion(f32[256,4,1,128]{3,0,1,2:T(8,128)} %convolution_bitcast_fusion.1, f32[4,64,128]{2,1,0:T(8,128)S(1)} %multiply_reduce_fusion.2, f32[256,4,1,64]{0,3,1,2:T(8,128)S(1)} %fusion.19, f32[256,4]{0,1:T(4,128)S(1)} %get-tuple-element.23), kind=kOutput, calls=%fused_computation.19 | convolution fusion | flops 101056512 | bytes 1183744 | tf_op jit(solution)/shard_map/ibhp,bhpn->ibhn/dot_general | solution.py:202
  155.7 0.9 copy.185
  156.6 1.1 convolution_bitcast_fusion.6
  157.7 0.8 convolution_bitcast_fusion.3
  158.5 4.5 %all-to-all-done.3 = bf16[8,4,1,128,64]{3,4,2,1,0:T(8,128)(2,1)} async-done(((bf16[8,4,1,128,64]{3,4,2,1,0:T(8,128)(2,1)}), bf16[8,4,1,128,64]{3,4,2,1,0:T(8,128)(2,1)}, u32[]{:S(2)}, u32[]{:S(2)}) %all-to-all-start.3) | async-done | bytes 524320 | tf_op jit(solution)/shard_map/all_to_all | solution.py:183
  163.0 1.2 multiply_reduce_fusion.1
  164.2 1.1 fusion.9
  165.3 0.9 copy.184
  166.2 2.1 %fusion.24 = bf16[256,4,1,64]{0,3,2,1:T(8,128)(2,1)} fusion(f32[256,4,1,64]{0,3,1,2:T(8,128)} %convolution_bitcast_fusion.6, f32[4,128,64]{1,2,0:T(8,128)S(1)} %multiply_reduce_fusion.1, f32[256,4,1,64]{0,3,1,2:T(8,128)S(1)} %fusion.19, bf16[256,4,128]{2,1,0:T(4,128)(2,1)} %bitcast.243, f32[256,4]{0,1:T(4,128)S(1)} %get-tuple-element.34, f32[]{:T(128)} %bitcast.233, ...), kind=kOutput, calls=%fused_computation.35 | convolution fusion | flops 101056512 | bytes 1056772 | tf_op jit(solution)/shard_map/jbhn,bhnp->jbhp/dot_general | solution.py:192
  (88 shorter events, 3.9 us)
Async XLA Ops:
  0.6 69.8 %copy-start = (bf16[1,640,512]{2,1,0:T(8,128)(2,1)S(1)}, bf16[1,640,512]{2,1,0:T(8,128)(2,1)}, u32[]{:S(2)}) copy-start(bf16[1,640,512]{2,1,0:T(8,128)(2,1)} %param.11) | copy-start | bytes 1966084
  2.5 26.4 %copy-start.7 = (s32[8192]{0:T(1024)}, s32[8192]{0:T(1024)S(1)}, u32[]{:S(2)}) copy-start(s32[8192]{0:T(1024)S(1)} %reshape.598) | copy-start | bytes 98308
  5.1 17.8 %all-to-all-start = ((bf16[8,32,640]{2,1,0:T(8,128)(2,1)}), bf16[8,32,640]{2,1,0:T(8,128)(2,1)S(1)}, u32[]{:S(2)}, u32[]{:S(2)}) async-start(bf16[8,32,640]{2,1,0:T(8,128)(2,1)} %bitcast.17), calls=%async_computation | async-start | bytes 655360 | tf_op jit(solution)/shard_map/all_to_all | solution.py:101
  17.9 0.6 copy-start.8
  18.1 0.6 copy-start.9
  22.9 18.6 %collective-permute-start.3 = (bf16[8,32,640]{2,1,0:T(8,128)(2,1)S(1)}, bf16[8,32,640]{2,1,0:T(8,128)(2,1)S(1)}, u32[]{:S(2)}, u32[]{:S(2)}) collective-permute-start(bf16[8,32,640]{2,1,0:T(8,128)(2,1)S(1)} %all-to-all-done), channel_id=1, source_target_pairs={{0,64},{64,128},{128,192},{192,256},{256,320},{320,384},{384,448},... | collective-permute-start | bytes 983048 | tf_op jit(solution)/shard_map/ppermute | solution.py:66
  29.6 13.8 %collective-permute-start = (bf16[8,32,640]{2,1,0:T(8,128)(2,1)S(1)}, bf16[8,32,640]{2,1,0:T(8,128)(2,1)S(1)}, u32[]{:S(2)}, u32[]{:S(2)}) collective-permute-start(bf16[8,32,640]{2,1,0:T(8,128)(2,1)S(1)} %all-to-all-done), channel_id=1, source_target_pairs={{0,448},{64,0},{128,64},{192,128},{256,192},{320,256},{384,320},{4... | collective-permute-start | bytes 983048 | tf_op jit(solution)/shard_map/ppermute | solution.py:69
  41.5 9.6 %collective-permute-start.4 = (bf16[8,32,640]{2,1,0:T(8,128)(2,1)S(1)}, bf16[8,32,640]{2,1,0:T(8,128)(2,1)S(1)}, u32[]{:S(2)}, u32[]{:S(2)}) collective-permute-start(bf16[8,32,640]{2,1,0:T(8,128)(2,1)S(1)} %collective-permute-done.3), channel_id=1, source_target_pairs={{0,64},{64,128},{128,192},{192,256},{256,320},{320,384},{384,448},... | collective-permute-start | bytes 983048 | tf_op jit(solution)/shard_map/ppermute | solution.py:66
  43.4 9.7 %collective-permute-start.1 = (bf16[8,32,640]{2,1,0:T(8,128)(2,1)S(1)}, bf16[8,32,640]{2,1,0:T(8,128)(2,1)S(1)}, u32[]{:S(2)}, u32[]{:S(2)}) collective-permute-start(bf16[8,32,640]{2,1,0:T(8,128)(2,1)S(1)} %collective-permute-done), channel_id=1, source_target_pairs={{0,448},{64,0},{128,64},{192,128},{256,192},{320,256},{384,320},{4... | collective-permute-start | bytes 983048 | tf_op jit(solution)/shard_map/ppermute | solution.py:69
  51.1 9.0 %collective-permute-start.5 = (bf16[8,32,640]{2,1,0:T(8,128)(2,1)S(1)}, bf16[8,32,640]{2,1,0:T(8,128)(2,1)S(1)}, u32[]{:S(2)}, u32[]{:S(2)}) collective-permute-start(bf16[8,32,640]{2,1,0:T(8,128)(2,1)S(1)} %collective-permute-done.4), channel_id=1, source_target_pairs={{0,64},{64,128},{128,192},{192,256},{256,320},{320,384},{384,448},... | collective-permute-start | bytes 983048 | tf_op jit(solution)/shard_map/ppermute | solution.py:66
  53.1 9.0 %collective-permute-start.2 = (bf16[8,32,640]{2,1,0:T(8,128)(2,1)S(1)}, bf16[8,32,640]{2,1,0:T(8,128)(2,1)S(1)}, u32[]{:S(2)}, u32[]{:S(2)}) collective-permute-start(bf16[8,32,640]{2,1,0:T(8,128)(2,1)S(1)} %collective-permute-done.1), channel_id=1, source_target_pairs={{0,448},{64,0},{128,64},{192,128},{256,192},{320,256},{384,320},{4... | collective-permute-start | bytes 983048 | tf_op jit(solution)/shard_map/ppermute | solution.py:69
  60.1 9.0 %collective-permute-start.6 = (bf16[8,32,640]{2,1,0:T(8,128)(2,1)S(1)}, bf16[8,32,640]{2,1,0:T(8,128)(2,1)S(1)}, u32[]{:S(2)}, u32[]{:S(2)}) collective-permute-start(bf16[8,32,640]{2,1,0:T(8,128)(2,1)S(1)} %collective-permute-done.5), channel_id=1, source_target_pairs={{0,64},{64,128},{128,192},{192,256},{256,320},{320,384},{384,448},... | collective-permute-start | bytes 983048 | tf_op jit(solution)/shard_map/ppermute | solution.py:66
  74.1 23.1 %copy-start.4 = (bf16[256,4,1,64]{0,3,2,1:T(8,128)(2,1)S(1)}, bf16[256,4,1,64]{0,3,2,1:T(8,128)(2,1)}, u32[]{:S(2)}) copy-start(bf16[256,4,1,64]{0,3,2,1:T(8,128)(2,1)} %param.13) | copy-start | bytes 393220
  74.1 42.8 %all-to-all-start.1 = ((bf16[8,323,512]{2,1,0:T(8,128)(2,1)}), bf16[8,323,512]{2,1,0:T(8,128)(2,1)S(1)}, u32[]{:S(2)}, u32[]{:S(2)}) async-start(bf16[8,323,512]{2,1,0:T(8,128)(2,1)} %pad_maximum_fusion), calls=%async_computation.1 | async-start | bytes 5373952 | tf_op jit(solution)/shard_map/all_to_all | solution.py:142
  94.3 4.3 %copy-start.12 = (pred[8]{0:T(512)(128)(4,1)}, pred[8]{0:T(512)(128)(4,1)S(1)}, u32[]{:S(2)}) copy-start(pred[8]{0:T(512)(128)(4,1)S(1)} %iota_compare_fusion.8) | copy-start | bytes 28
  94.3 4.3 %copy-start.11 = (pred[8]{0:T(512)(128)(4,1)}, pred[8]{0:T(512)(128)(4,1)S(1)}, u32[]{:S(2)}) copy-start(pred[8]{0:T(512)(128)(4,1)S(1)} %iota_compare_fusion.9) | copy-start | bytes 28
  94.9 32.3 %copy-start.6 = (pred[256,256]{1,0:T(8,128)(4,1)}, pred[256,256]{1,0:T(8,128)(4,1)S(1)}, u32[]{:S(2)}) copy-start(pred[256,256]{1,0:T(8,128)(4,1)S(1)} %iota_compare_fusion.2) | copy-start | bytes 196612
  95.7 2.9 %copy-start.10 = (f32[4,256]{1,0:T(4,128)}, f32[4,256]{1,0:T(4,128)S(1)}, u32[]{:S(2)}) copy-start(f32[4,256]{1,0:T(4,128)S(1)} %bitcast_add_fusion) | copy-start | bytes 12292
  97.3 1.3 copy-start.1
  119.9 19.4 %all-to-all-start.2 = ((bf16[64,8,256]{2,1,0:T(8,128)(2,1)}), bf16[64,8,256]{2,1,0:T(8,128)(2,1)}, u32[]{:S(2)}, u32[]{:S(2)}) async-start(bf16[64,8,256]{2,1,0:T(8,128)(2,1)} %bitcast.245), calls=%async_computation.2 | async-start | bytes 524288 | tf_op jit(solution)/shard_map/all_to_all | solution.py:155
  127.1 16.7 %copy-start.3 = (bf16[256,4,1,128]{3,1,2,0:T(4,128)(2,1)S(1)}, bf16[256,4,1,128]{3,1,2,0:T(4,128)(2,1)}, u32[]{:S(2)}) copy-start(bf16[256,4,1,128]{3,1,2,0:T(4,128)(2,1)} %param.15) | copy-start | bytes 786436
  139.3 4.8 %copy-start.5 = (bf16[256,4,1,128]{3,1,2,0:T(4,128)(2,1)S(1)}, bf16[256,4,1,128]{3,1,2,0:T(4,128)(2,1)}, u32[]{:S(2)}) copy-start(bf16[256,4,1,128]{3,1,2,0:T(4,128)(2,1)} %param.14) | copy-start | bytes 786436
  139.3 17.3 %copy-start.2 = (f32[4,256,256]{2,1,0:T(8,128)S(1)}, f32[4,256,256]{2,1,0:T(8,128)}, u32[]{:S(2)}) copy-start(f32[4,256,256]{2,1,0:T(8,128)} %copy-done.1) | copy-start | bytes 3145732
  146.3 16.7 %all-to-all-start.3 = ((bf16[8,4,1,128,64]{3,4,2,1,0:T(8,128)(2,1)}), bf16[8,4,1,128,64]{3,4,2,1,0:T(8,128)(2,1)}, u32[]{:S(2)}, u32[]{:S(2)}) async-start(bf16[8,4,1,128,64]{3,4,2,1,0:T(8,128)(2,1)} %broadcast_in_dim.140), calls=%async_computation.3 | async-start | bytes 1048576 | tf_op jit(solution)/shard_map/all_to_all | solution.py:183

commit v13 on v12

--- a/solution.py
+++ b/solution.py
@@ -87,10 +87,9 @@
     feat_width = teacher_in.shape[2]
     block_rows = block_pos * batch_n
     source = lax.axis_index("tz") * n_y + lax.axis_index("ty")
-    fam_all = family.reshape(family.shape[0] * family.shape[1])
 
     own_rows = teacher_in.reshape(block_rows, feat_width)
-    own_fam = lax.dynamic_slice_in_dim(fam_all, source * block_rows, block_rows)
+    own_fam = lax.dynamic_slice_in_dim(family, source * block_pos, block_pos).reshape(block_rows)
     slot_ids = family_slots(own_fam.reshape(1, block_rows))[0]
     dest_cols = own_fam * CAP + slot_ids
     select = (dest_cols[:, None] == jnp.arange(FAM * CAP, dtype=jnp.int32)[None, :]).astype(
@@ -157,7 +156,7 @@
 
     shard_rows = n_y * block_rows
     shard_fam = lax.dynamic_slice_in_dim(
-        fam_all, lax.axis_index("seq") * shard_rows, shard_rows
+        family, lax.axis_index("seq") * (n_y * block_pos), n_y * block_pos
     ).reshape(n_y, block_rows)
     shard_slots = family_slots(shard_fam)
     sources = jnp.arange(n_y, dtype=jnp.int32)[:, None]

time: 170 us -> 169 us (level)
  waiting for transfers between devices: 47.9 us -> 44.3 us
    all_to_all x1, waiting for transfers between devices: 17.8 us -> 14 us  [per_device(): lax.all_to_all(outbound, 'seq', split_axis=0, concat_axis=0, tiled=True)]
    add x0 -> x3, local copies, waits for them, and re-layouts: none -> 2.36 us  [the longest x1 1.57 us: per_device(): (shard_fam * n_y + sources) * CAP + shard_slots]
    eq x2 -> x0, local copies, waits for them, and re-layouts: 2.36 us -> none  [per_device(): row_index[:, None] == jnp.arange(n_y * n_y * CAP, dtype=jnp.int32)[None, :]]
    unnamed x46 -> x44, local copies, waits for them, and re-layouts: 4.65 us -> 4.2 us
  transfers between devices with their start and end apart: 11 -> 11, of which waited for: 8 -> 8; matrix products, arithmetic and copies ran while one was open for 18% -> 20% of each run, Pallas kernels for 0% -> 0%
where the time goes in v13:
time: 169 us; the launch traced here: 167 us
  starting transfers between devices  62 us (37%)
  waiting for transfers between devices  44.3 us (26%)
  matrix products  22.9 us (14%)
  other arithmetic  18 us (11%)
  local copies, waits for them, and re-layouts  17.6 us (10%)
  between operations  2.47 us (1%)
    ppermute x3, starting transfers between devices, ring_gather(): ccw = lax.ppermute(ccw, axis, behind)  18.3 us
    all_to_all x1, waiting for transfers between devices, per_device(): lax.all_to_all(outbound, 'seq', split_axis=0, concat_axis=0, tiled=True)  14 us
    ppermute x4, waiting for transfers between devices, ring_gather(): cw = lax.ppermute(cw, axis, ahead)  13.7 us
    ppermute x4, starting transfers between devices, ring_gather(): cw = lax.ppermute(cw, axis, ahead)  11.7 us
    all_to_all x1, starting transfers between devices, per_device(): lax.all_to_all(outbound, 'seq', split_axis=0, concat_axis=0, tiled=True)  10.1 us
    all_to_all x1, waiting for transfers between devices, per_device(): lax.all_to_all(outgoing, TEACH, split_axis=0, concat_axis=0, tiled=True)  7.82 us
    all_to_all x1, starting transfers between devices, per_device(): lax.all_to_all(packed, 'ty', split_axis=0, concat_axis=0, tiled=True)  7.64 us
    all_to_all x1, starting transfers between devices, per_device(): lax.all_to_all(jnp.broadcast_to(local_adjoint.astype(jnp.bfloat16)[None],...  7.2 us
  transfers between devices with their start and end apart: 11, of which 8 were waited for; matrix products, arithmetic and copies ran while one was open for 20% of the time, Pallas kernels for 0%

profile of v13, /device:TPU:1, one launch (start us, length us, event | category | flops | bytes accessed | tf_op | source)
XLA Modules:
  0.0 167.2 jit_solution(16646826982981456044)
XLA Ops:
  0.7 0.8 constant_dynamic-slice_fusion.2
  2.1 1.0 reshape.634
  3.1 1.1 convolution_convert_fusion.1
  4.2 7.6 %all-to-all-start = ((bf16[8,32,640]{2,1,0:T(8,128)(2,1)}), bf16[8,32,640]{2,1,0:T(8,128)(2,1)S(1)}, u32[]{:S(2)}, u32[]{:S(2)}) async-start(bf16[8,32,640]{2,1,0:T(8,128)(2,1)} %bitcast.17), calls=%async_computation | async-start | bytes 655360 | tf_op jit(solution)/shard_map/all_to_all | solution.py:100
  12.5 0.7 negate_multiply_fusion
  13.2 1.2 reduce-window.16
  14.5 0.7 reshape.622
  15.2 1.2 reduce-window.14
  17.7 4.2 %all-to-all-done = bf16[8,32,640]{2,1,0:T(8,128)(2,1)S(1)} async-done(((bf16[8,32,640]{2,1,0:T(8,128)(2,1)}), bf16[8,32,640]{2,1,0:T(8,128)(2,1)S(1)}, u32[]{:S(2)}, u32[]{:S(2)}) %all-to-all-start) | async-done | bytes 327712 | tf_op jit(solution)/shard_map/all_to_all | solution.py:100
  21.9 6.0 %collective-permute-start.3 = (bf16[8,32,640]{2,1,0:T(8,128)(2,1)S(1)}, bf16[8,32,640]{2,1,0:T(8,128)(2,1)S(1)}, u32[]{:S(2)}, u32[]{:S(2)}) collective-permute-start(bf16[8,32,640]{2,1,0:T(8,128)(2,1)S(1)} %all-to-all-done), channel_id=1, source_target_pairs={{0,64},{64,128},{128,192},{192,256},{256,320},{320,384},{384,448},... | collective-permute-start | bytes 983048 | tf_op jit(solution)/shard_map/ppermute | solution.py:66
  27.9 0.8 copy_bitcast_fusion.1
  28.7 8.6 %collective-permute-start = (bf16[8,32,640]{2,1,0:T(8,128)(2,1)S(1)}, bf16[8,32,640]{2,1,0:T(8,128)(2,1)S(1)}, u32[]{:S(2)}, u32[]{:S(2)}) collective-permute-start(bf16[8,32,640]{2,1,0:T(8,128)(2,1)S(1)} %all-to-all-done), channel_id=1, source_target_pairs={{0,448},{64,0},{128,64},{192,128},{256,192},{320,256},{384,320},{4... | collective-permute-start | bytes 983048 | tf_op jit(solution)/shard_map/ppermute | solution.py:69
  37.3 1.3 fusion.25
  38.6 2.0 %collective-permute-done.3 = bf16[8,32,640]{2,1,0:T(8,128)(2,1)S(1)} collective-permute-done((bf16[8,32,640]{2,1,0:T(8,128)(2,1)S(1)}, bf16[8,32,640]{2,1,0:T(8,128)(2,1)S(1)}, u32[]{:S(2)}, u32[]{:S(2)}) %collective-permute-start.3) | collective-permute-done | bytes 327712 | tf_op jit(solution)/shard_map/ppermute | solution.py:66
  40.5 1.9 %collective-permute-start.4 = (bf16[8,32,640]{2,1,0:T(8,128)(2,1)S(1)}, bf16[8,32,640]{2,1,0:T(8,128)(2,1)S(1)}, u32[]{:S(2)}, u32[]{:S(2)}) collective-permute-start(bf16[8,32,640]{2,1,0:T(8,128)(2,1)S(1)} %collective-permute-done.3), channel_id=1, source_target_pairs={{0,64},{64,128},{128,192},{192,256},{256,320},{320,384},{384,448},... | collective-permute-start | bytes 983048 | tf_op jit(solution)/shard_map/ppermute | solution.py:66
  42.5 5.0 %collective-permute-start.1 = (bf16[8,32,640]{2,1,0:T(8,128)(2,1)S(1)}, bf16[8,32,640]{2,1,0:T(8,128)(2,1)S(1)}, u32[]{:S(2)}, u32[]{:S(2)}) collective-permute-start(bf16[8,32,640]{2,1,0:T(8,128)(2,1)S(1)} %collective-permute-done), channel_id=1, source_target_pairs={{0,448},{64,0},{128,64},{192,128},{256,192},{320,256},{384,320},{4... | collective-permute-start | bytes 983048 | tf_op jit(solution)/shard_map/ppermute | solution.py:69
  47.8 2.4 %collective-permute-done.4 = bf16[8,32,640]{2,1,0:T(8,128)(2,1)S(1)} collective-permute-done((bf16[8,32,640]{2,1,0:T(8,128)(2,1)S(1)}, bf16[8,32,640]{2,1,0:T(8,128)(2,1)S(1)}, u32[]{:S(2)}, u32[]{:S(2)}) %collective-permute-start.4) | collective-permute-done | bytes 327712 | tf_op jit(solution)/shard_map/ppermute | solution.py:66
  50.2 1.9 %collective-permute-start.5 = (bf16[8,32,640]{2,1,0:T(8,128)(2,1)S(1)}, bf16[8,32,640]{2,1,0:T(8,128)(2,1)S(1)}, u32[]{:S(2)}, u32[]{:S(2)}) collective-permute-start(bf16[8,32,640]{2,1,0:T(8,128)(2,1)S(1)} %collective-permute-done.4), channel_id=1, source_target_pairs={{0,64},{64,128},{128,192},{192,256},{256,320},{320,384},{384,448},... | collective-permute-start | bytes 983048 | tf_op jit(solution)/shard_map/ppermute | solution.py:66
  52.2 4.7 %collective-permute-start.2 = (bf16[8,32,640]{2,1,0:T(8,128)(2,1)S(1)}, bf16[8,32,640]{2,1,0:T(8,128)(2,1)S(1)}, u32[]{:S(2)}, u32[]{:S(2)}) collective-permute-start(bf16[8,32,640]{2,1,0:T(8,128)(2,1)S(1)} %collective-permute-done.1), channel_id=1, source_target_pairs={{0,448},{64,0},{128,64},{192,128},{256,192},{320,256},{384,320},{4... | collective-permute-start | bytes 983048 | tf_op jit(solution)/shard_map/ppermute | solution.py:69
  57.0 2.3 %collective-permute-done.5 = bf16[8,32,640]{2,1,0:T(8,128)(2,1)S(1)} collective-permute-done((bf16[8,32,640]{2,1,0:T(8,128)(2,1)S(1)}, bf16[8,32,640]{2,1,0:T(8,128)(2,1)S(1)}, u32[]{:S(2)}, u32[]{:S(2)}) %collective-permute-start.5) | collective-permute-done | bytes 327712 | tf_op jit(solution)/shard_map/ppermute | solution.py:66
  59.2 1.9 %collective-permute-start.6 = (bf16[8,32,640]{2,1,0:T(8,128)(2,1)S(1)}, bf16[8,32,640]{2,1,0:T(8,128)(2,1)S(1)}, u32[]{:S(2)}, u32[]{:S(2)}) collective-permute-start(bf16[8,32,640]{2,1,0:T(8,128)(2,1)S(1)} %collective-permute-done.5), channel_id=1, source_target_pairs={{0,64},{64,128},{128,192},{192,256},{256,320},{320,384},{384,448},... | collective-permute-start | bytes 983048 | tf_op jit(solution)/shard_map/ppermute | solution.py:66
  61.3 7.0 %collective-permute-done.6 = bf16[8,32,640]{2,1,0:T(8,128)(2,1)S(1)} collective-permute-done((bf16[8,32,640]{2,1,0:T(8,128)(2,1)S(1)}, bf16[8,32,640]{2,1,0:T(8,128)(2,1)S(1)}, u32[]{:S(2)}, u32[]{:S(2)}) %collective-permute-start.6) | collective-permute-done | bytes 327712 | tf_op jit(solution)/shard_map/ppermute | solution.py:66
  68.8 0.6 multiply_reduce_fusion
  69.6 1.8 %convolution_convert_fusion = bf16[8,256,512]{2,1,0:T(8,128)(2,1)S(1)} fusion(bf16[8,256,640]{2,1,0:T(8,128)(2,1)S(1)} %bitcast.232, bf16[1,640,512]{2,1,0:T(8,128)(2,1)S(1)} %copy-done), kind=kOutput, calls=%fused_computation.7 | convolution fusion | flops 1343225856 | bytes 5373952 | tf_op jit(solution)/shard_map/dot_general | solution.py:128
  71.4 1.8 %pad_maximum_fusion = bf16[8,323,512]{2,1,0:T(8,128)(2,1)} fusion(bf16[8,66,512]{2,1,0:T(8,128)(2,1)S(1)} %broadcast_in_dim.134, bf16[8,1,512]{2,1,0:T(2,128)(2,1)S(1)} %copy.143, bf16[8,256,512]{2,1,0:T(8,128)(2,1)S(1)} %convolution_convert_fusion), kind=kLoop, calls=%fused_computation.6 | loop fusion | flops 7938048 | bytes 5292032 | tf_op jit(solution)/shard_map/concatenate | solution.py:140
  73.2 10.1 %all-to-all-start.1 = ((bf16[8,323,512]{2,1,0:T(8,128)(2,1)}), bf16[8,323,512]{2,1,0:T(8,128)(2,1)S(1)}, u32[]{:S(2)}, u32[]{:S(2)}) async-start(bf16[8,323,512]{2,1,0:T(8,128)(2,1)} %pad_maximum_fusion), calls=%async_computation.1 | async-start | bytes 5373952 | tf_op jit(solution)/shard_map/all_to_all | solution.py:141
  84.0 0.7 constant_dynamic-slice_fusion
  84.8 0.7 eq.136
  85.5 0.8 copy.147
  86.3 3.2 %select_reduce_fusion = s32[8,128]{0,1:T(8,128)} fusion(s32[8,128]{0,1:T(8,128)S(1)} %copy.147), kind=kOutput, calls=%fused_computation.50 | output fusion | flops 1096704 | bytes 8192 | tf_op jit(solution)/shard_map/jit(cumsum)/reduce_window_sum | solution.py:23
  89.5 0.9 copy.148
  90.4 0.8 reduce_sum.60
  91.2 0.8 add.108
  92.0 1.6 fusion.54
  93.6 1.6 copy.149
  95.2 0.6 multiply_add_fusion
  95.8 0.8 broadcast_bitcast_fusion
  96.6 0.6 copy-done.9
  97.2 1.5 convolution_multiply_fusion.1
  98.8 2.5 %convolution_bitcast_fusion.7 = f32[256,4,1,64]{0,3,1,2:T(8,128)} fusion(f32[4,256,256]{2,1,0:T(8,128)S(1)} %convolution_multiply_fusion.1, bf16[256,4,1,64]{0,3,2,1:T(8,128)(2,1)} %param.13, f32[256,4]{0,1:T(4,128)S(1)} %get-tuple-element.30), kind=kOutput, calls=%fused_computation.32 | convolution fusion | flops 100794368 | bytes 1445888 | tf_op jit(solution)/shard_map/bhij,jbhp->ibhp/dot_general | solution.py:175
  101.2 0.6 fusion.67
  101.8 14.0 %all-to-all-done.1 = bf16[8,323,512]{2,1,0:T(8,128)(2,1)S(1)} async-done(((bf16[8,323,512]{2,1,0:T(8,128)(2,1)}), bf16[8,323,512]{2,1,0:T(8,128)(2,1)S(1)}, u32[]{:S(2)}, u32[]{:S(2)}) %all-to-all-start.1) | async-done | bytes 2646048 | tf_op jit(solution)/shard_map/all_to_all | solution.py:141
  116.2 0.8 fusion.32
  117.0 1.8 %copy.150 = bf16[256,512]{0,1:T(8,128)(2,1)} copy(bf16[256,512]{1,0:T(8,128)(2,1)} %fusion.32) | data formatting | bytes 524288 | tf_op jit(solution)/shard_map/convert_element_type | solution.py:150
  118.8 7.1 %all-to-all-start.2 = ((bf16[64,8,256]{2,1,0:T(8,128)(2,1)}), bf16[64,8,256]{2,1,0:T(8,128)(2,1)}, u32[]{:S(2)}, u32[]{:S(2)}) async-start(bf16[64,8,256]{2,1,0:T(8,128)(2,1)} %bitcast.243), calls=%async_computation.2 | async-start | bytes 524288 | tf_op jit(solution)/shard_map/all_to_all | solution.py:154
  126.3 0.9 select_reduce_fusion.2
  127.1 0.6 broadcast_select_fusion
  127.9 0.6 broadcast_select_fusion.1
  128.9 1.4 fusion.14
  130.4 7.8 %all-to-all-done.2 = bf16[64,8,256]{2,1,0:T(8,128)(2,1)} async-done(((bf16[64,8,256]{2,1,0:T(8,128)(2,1)}), bf16[64,8,256]{2,1,0:T(8,128)(2,1)}, u32[]{:S(2)}, u32[]{:S(2)}) %all-to-all-start.2) | async-done | bytes 262176 | tf_op jit(solution)/shard_map/all_to_all | solution.py:154
  138.2 2.7 %fusion.19 = f32[256,4,1,64]{0,3,1,2:T(8,128)S(1)} fusion(f32[256,4,1,64]{0,3,1,2:T(8,128)S(1)} %fusion.14, s32[8,256]{1,0:T(8,128)} %multiply_add_fusion, s32[256,4]{0,1:T(4,128)} %copy.149, bf16[8,8,8,256]{3,1,2,0:T(8,128)(2,1)} %bitcast.42), kind=kOutput, calls=%fused_computation.30 | convolution fusion | flops 270598144 | bytes 798720 | tf_op jit(solution)/shard_map/rfq,jfcq->rjc/dot_general | solution.py:168
  140.9 1.8 %convolution_multiply_fusion = f32[4,256,256]{2,1,0:T(8,128)S(1)} fusion(f32[4,256]{1,0:T(4,128)} %copy-done.9, s32[4,256]{1,0:T(4,128)} %bitcast.247, pred[256,256]{1,0:T(8,128)(4,1)} %copy-done.6, f32[256,4,1,64]{0,3,1,2:T(8,128)S(1)} %fusion.19, bf16[256,4,1,64]{0,3,2,1:T(8,128)(2,1)S(1)} %copy-done.4, f32[256,4]{0,1:T(4,128)S(1)} %get-tuple-element.30), kind=kOutput, calls=%fused_computation.8 | convolution fusion | flops 102367232 | bytes 1519616 | tf_op jit(solution)/shard_map/ibhp,jbhp->bhij/dot_general | solution.py:195
  143.0 1.3 convolution_bitcast_fusion.1
  144.3 0.9 broadcast_in_dim.140
  145.2 7.2 %all-to-all-start.3 = ((bf16[8,4,1,128,64]{3,4,2,1,0:T(8,128)(2,1)}), bf16[8,4,1,128,64]{3,4,2,1,0:T(8,128)(2,1)}, u32[]{:S(2)}, u32[]{:S(2)}) async-start(bf16[8,4,1,128,64]{3,4,2,1,0:T(8,128)(2,1)} %broadcast_in_dim.140), calls=%async_computation.3 | async-start | bytes 1048576 | tf_op jit(solution)/shard_map/all_to_all | solution.py:182
  152.4 2.1 %fusion.8 = bf16[256,4,1,128]{3,0,1,2:T(8,128)(2,1)S(1)} fusion(f32[256,4,1,128]{3,0,1,2:T(8,128)} %convolution_bitcast_fusion.1, f32[4,64,128]{2,1,0:T(8,128)S(1)} %multiply_reduce_fusion.2, f32[256,4,1,64]{0,3,1,2:T(8,128)S(1)} %fusion.19, f32[256,4]{0,1:T(4,128)S(1)} %get-tuple-element.20), kind=kOutput, calls=%fused_computation.19 | convolution fusion | flops 101056512 | bytes 1183744 | tf_op jit(solution)/shard_map/ibhp,bhpn->ibhn/dot_general | solution.py:201
  154.6 0.9 copy.162
  155.5 1.1 convolution_bitcast_fusion.6
  156.6 0.8 convolution_bitcast_fusion.3
  157.4 4.5 %all-to-all-done.3 = bf16[8,4,1,128,64]{3,4,2,1,0:T(8,128)(2,1)} async-done(((bf16[8,4,1,128,64]{3,4,2,1,0:T(8,128)(2,1)}), bf16[8,4,1,128,64]{3,4,2,1,0:T(8,128)(2,1)}, u32[]{:S(2)}, u32[]{:S(2)}) %all-to-all-start.3) | async-done | bytes 524320 | tf_op jit(solution)/shard_map/all_to_all | solution.py:182
  161.9 1.2 multiply_reduce_fusion.1
  163.1 1.1 fusion.9
  164.2 0.9 copy.161
  165.2 2.1 %fusion.24 = bf16[256,4,1,64]{0,3,2,1:T(8,128)(2,1)} fusion(f32[256,4,1,64]{0,3,1,2:T(8,128)} %convolution_bitcast_fusion.6, f32[4,128,64]{1,2,0:T(8,128)S(1)} %multiply_reduce_fusion.1, f32[256,4,1,64]{0,3,1,2:T(8,128)S(1)} %fusion.19, bf16[256,4,128]{2,1,0:T(4,128)(2,1)} %bitcast.241, f32[256,4]{0,1:T(4,128)S(1)} %get-tuple-element.31, f32[]{:T(128)} %bitcast.231, ...), kind=kOutput, calls=%fused_computation.35 | convolution fusion | flops 101056512 | bytes 1056772 | tf_op jit(solution)/shard_map/jbhn,bhnp->jbhp/dot_general | solution.py:191
  (90 shorter events, 4.8 us)
Async XLA Ops:
  0.6 68.9 %copy-start = (bf16[1,640,512]{2,1,0:T(8,128)(2,1)S(1)}, bf16[1,640,512]{2,1,0:T(8,128)(2,1)}, u32[]{:S(2)}) copy-start(bf16[1,640,512]{2,1,0:T(8,128)(2,1)} %param.11) | copy-start | bytes 1966084
  4.2 17.8 %all-to-all-start = ((bf16[8,32,640]{2,1,0:T(8,128)(2,1)}), bf16[8,32,640]{2,1,0:T(8,128)(2,1)S(1)}, u32[]{:S(2)}, u32[]{:S(2)}) async-start(bf16[8,32,640]{2,1,0:T(8,128)(2,1)} %bitcast.17), calls=%async_computation | async-start | bytes 655360 | tf_op jit(solution)/shard_map/all_to_all | solution.py:100
  16.9 0.6 copy-start.7
  17.1 0.6 copy-start.8
  21.9 18.6 %collective-permute-start.3 = (bf16[8,32,640]{2,1,0:T(8,128)(2,1)S(1)}, bf16[8,32,640]{2,1,0:T(8,128)(2,1)S(1)}, u32[]{:S(2)}, u32[]{:S(2)}) collective-permute-start(bf16[8,32,640]{2,1,0:T(8,128)(2,1)S(1)} %all-to-all-done), channel_id=1, source_target_pairs={{0,64},{64,128},{128,192},{192,256},{256,320},{320,384},{384,448},... | collective-permute-start | bytes 983048 | tf_op jit(solution)/shard_map/ppermute | solution.py:66
  28.7 13.8 %collective-permute-start = (bf16[8,32,640]{2,1,0:T(8,128)(2,1)S(1)}, bf16[8,32,640]{2,1,0:T(8,128)(2,1)S(1)}, u32[]{:S(2)}, u32[]{:S(2)}) collective-permute-start(bf16[8,32,640]{2,1,0:T(8,128)(2,1)S(1)} %all-to-all-done), channel_id=1, source_target_pairs={{0,448},{64,0},{128,64},{192,128},{256,192},{320,256},{384,320},{4... | collective-permute-start | bytes 983048 | tf_op jit(solution)/shard_map/ppermute | solution.py:69
  40.5 9.7 %collective-permute-start.4 = (bf16[8,32,640]{2,1,0:T(8,128)(2,1)S(1)}, bf16[8,32,640]{2,1,0:T(8,128)(2,1)S(1)}, u32[]{:S(2)}, u32[]{:S(2)}) collective-permute-start(bf16[8,32,640]{2,1,0:T(8,128)(2,1)S(1)} %collective-permute-done.3), channel_id=1, source_target_pairs={{0,64},{64,128},{128,192},{192,256},{256,320},{320,384},{384,448},... | collective-permute-start | bytes 983048 | tf_op jit(solution)/shard_map/ppermute | solution.py:66
  42.5 9.7 %collective-permute-start.1 = (bf16[8,32,640]{2,1,0:T(8,128)(2,1)S(1)}, bf16[8,32,640]{2,1,0:T(8,128)(2,1)S(1)}, u32[]{:S(2)}, u32[]{:S(2)}) collective-permute-start(bf16[8,32,640]{2,1,0:T(8,128)(2,1)S(1)} %collective-permute-done), channel_id=1, source_target_pairs={{0,448},{64,0},{128,64},{192,128},{256,192},{320,256},{384,320},{4... | collective-permute-start | bytes 983048 | tf_op jit(solution)/shard_map/ppermute | solution.py:69
  50.2 9.0 %collective-permute-start.5 = (bf16[8,32,640]{2,1,0:T(8,128)(2,1)S(1)}, bf16[8,32,640]{2,1,0:T(8,128)(2,1)S(1)}, u32[]{:S(2)}, u32[]{:S(2)}) collective-permute-start(bf16[8,32,640]{2,1,0:T(8,128)(2,1)S(1)} %collective-permute-done.4), channel_id=1, source_target_pairs={{0,64},{64,128},{128,192},{192,256},{256,320},{320,384},{384,448},... | collective-permute-start | bytes 983048 | tf_op jit(solution)/shard_map/ppermute | solution.py:66
  52.2 9.0 %collective-permute-start.2 = (bf16[8,32,640]{2,1,0:T(8,128)(2,1)S(1)}, bf16[8,32,640]{2,1,0:T(8,128)(2,1)S(1)}, u32[]{:S(2)}, u32[]{:S(2)}) collective-permute-start(bf16[8,32,640]{2,1,0:T(8,128)(2,1)S(1)} %collective-permute-done.1), channel_id=1, source_target_pairs={{0,448},{64,0},{128,64},{192,128},{256,192},{320,256},{384,320},{4... | collective-permute-start | bytes 983048 | tf_op jit(solution)/shard_map/ppermute | solution.py:69
  59.2 9.0 %collective-permute-start.6 = (bf16[8,32,640]{2,1,0:T(8,128)(2,1)S(1)}, bf16[8,32,640]{2,1,0:T(8,128)(2,1)S(1)}, u32[]{:S(2)}, u32[]{:S(2)}) collective-permute-start(bf16[8,32,640]{2,1,0:T(8,128)(2,1)S(1)} %collective-permute-done.5), channel_id=1, source_target_pairs={{0,64},{64,128},{128,192},{192,256},{256,320},{320,384},{384,448},... | collective-permute-start | bytes 983048 | tf_op jit(solution)/shard_map/ppermute | solution.py:66
  73.2 42.6 %all-to-all-start.1 = ((bf16[8,323,512]{2,1,0:T(8,128)(2,1)}), bf16[8,323,512]{2,1,0:T(8,128)(2,1)S(1)}, u32[]{:S(2)}, u32[]{:S(2)}) async-start(bf16[8,323,512]{2,1,0:T(8,128)(2,1)} %pad_maximum_fusion), calls=%async_computation.1 | async-start | bytes 5373952 | tf_op jit(solution)/shard_map/all_to_all | solution.py:141
  95.2 6.0 %copy-start.11 = (pred[8]{0:T(512)(128)(4,1)}, pred[8]{0:T(512)(128)(4,1)S(1)}, u32[]{:S(2)}) copy-start(pred[8]{0:T(512)(128)(4,1)S(1)} %iota_compare_fusion.8) | copy-start | bytes 28
  95.2 6.0 %copy-start.10 = (pred[8]{0:T(512)(128)(4,1)}, pred[8]{0:T(512)(128)(4,1)S(1)}, u32[]{:S(2)}) copy-start(pred[8]{0:T(512)(128)(4,1)S(1)} %iota_compare_fusion.9) | copy-start | bytes 28
  95.8 30.3 %copy-start.6 = (pred[256,256]{1,0:T(8,128)(4,1)}, pred[256,256]{1,0:T(8,128)(4,1)S(1)}, u32[]{:S(2)}) copy-start(pred[256,256]{1,0:T(8,128)(4,1)S(1)} %iota_compare_fusion.2) | copy-start | bytes 196612
  96.6 0.6 copy-start.9
  98.8 2.5 %copy-start.1 = (f32[4,256,256]{2,1,0:T(8,128)}, f32[4,256,256]{2,1,0:T(8,128)S(1)}, u32[]{:S(2)}) copy-start(f32[4,256,256]{2,1,0:T(8,128)S(1)} %convolution_multiply_fusion.1) | copy-start | bytes 3145732
  98.8 30.2 %copy-start.4 = (bf16[256,4,1,64]{0,3,2,1:T(8,128)(2,1)S(1)}, bf16[256,4,1,64]{0,3,2,1:T(8,128)(2,1)}, u32[]{:S(2)}) copy-start(bf16[256,4,1,64]{0,3,2,1:T(8,128)(2,1)} %param.13) | copy-start | bytes 393220
  118.8 19.4 %all-to-all-start.2 = ((bf16[64,8,256]{2,1,0:T(8,128)(2,1)}), bf16[64,8,256]{2,1,0:T(8,128)(2,1)}, u32[]{:S(2)}, u32[]{:S(2)}) async-start(bf16[64,8,256]{2,1,0:T(8,128)(2,1)} %bitcast.243), calls=%async_computation.2 | async-start | bytes 524288 | tf_op jit(solution)/shard_map/all_to_all | solution.py:154
  126.0 16.7 %copy-start.3 = (bf16[256,4,1,128]{3,1,2,0:T(4,128)(2,1)S(1)}, bf16[256,4,1,128]{3,1,2,0:T(4,128)(2,1)}, u32[]{:S(2)}) copy-start(bf16[256,4,1,128]{3,1,2,0:T(4,128)(2,1)} %param.15) | copy-start | bytes 786436
  138.2 4.8 %copy-start.5 = (bf16[256,4,1,128]{3,1,2,0:T(4,128)(2,1)S(1)}, bf16[256,4,1,128]{3,1,2,0:T(4,128)(2,1)}, u32[]{:S(2)}) copy-start(bf16[256,4,1,128]{3,1,2,0:T(4,128)(2,1)} %param.14) | copy-start | bytes 786436
  138.2 17.3 %copy-start.2 = (f32[4,256,256]{2,1,0:T(8,128)S(1)}, f32[4,256,256]{2,1,0:T(8,128)}, u32[]{:S(2)}) copy-start(f32[4,256,256]{2,1,0:T(8,128)} %copy-done.1) | copy-start | bytes 3145732
  145.2 16.7 %all-to-all-start.3 = ((bf16[8,4,1,128,64]{3,4,2,1,0:T(8,128)(2,1)}), bf16[8,4,1,128,64]{3,4,2,1,0:T(8,128)(2,1)}, u32[]{:S(2)}, u32[]{:S(2)}) async-start(bf16[8,4,1,128,64]{3,4,2,1,0:T(8,128)(2,1)} %broadcast_in_dim.140), calls=%async_computation.3 | async-start | bytes 1048576 | tf_op jit(solution)/shard_map/all_to_all | solution.py:182

commit v14 on v13

--- a/solution.py
+++ b/solution.py
@@ -88,14 +88,18 @@
     block_rows = block_pos * batch_n
     source = lax.axis_index("tz") * n_y + lax.axis_index("ty")
 
-    own_rows = teacher_in.reshape(block_rows, feat_width)
     own_fam = lax.dynamic_slice_in_dim(family, source * block_pos, block_pos).reshape(block_rows)
     slot_ids = family_slots(own_fam.reshape(1, block_rows))[0]
     dest_cols = own_fam * CAP + slot_ids
     select = (dest_cols[:, None] == jnp.arange(FAM * CAP, dtype=jnp.int32)[None, :]).astype(
         jnp.bfloat16
     )
-    packed = jnp.dot(select.T, own_rows, preferred_element_type=jnp.float32).astype(jnp.bfloat16)
+    packed = jnp.einsum(
+        "pbs,pbk->sk",
+        select.reshape(block_pos, batch_n, FAM * CAP),
+        teacher_in,
+        preferred_element_type=jnp.float32,
+    ).astype(jnp.bfloat16)
     packed = packed.reshape(FAM, CAP, feat_width)
     by_family = lax.all_to_all(packed, "ty", split_axis=0, concat_axis=0, tiled=True)
     received = ring_gather(by_family, "tz")

time: 169 us -> 169 us (level)
  no operation moved by 1% of the time
where the time goes in v14:
time: 169 us; the launch traced here: 167 us
  starting transfers between devices  62 us (37%)
  waiting for transfers between devices  44.3 us (26%)
  matrix products  23.8 us (14%)
  other arithmetic  18.8 us (11%)
  local copies, waits for them, and re-layouts  16 us (9%)
  between operations  2.47 us (1%)
    ppermute x3, starting transfers between devices, ring_gather(): ccw = lax.ppermute(ccw, axis, behind)  18.4 us
    all_to_all x1, waiting for transfers between devices, per_device(): lax.all_to_all(outbound, 'seq', split_axis=0, concat_axis=0, tiled=True)  14 us
    ppermute x4, waiting for transfers between devices, ring_gather(): cw = lax.ppermute(cw, axis, ahead)  13.7 us
    ppermute x4, starting transfers between devices, ring_gather(): cw = lax.ppermute(cw, axis, ahead)  11.7 us
    all_to_all x1, starting transfers between devices, per_device(): lax.all_to_all(outbound, 'seq', split_axis=0, concat_axis=0, tiled=True)  10.1 us
    all_to_all x1, waiting for transfers between devices, per_device(): lax.all_to_all(outgoing, TEACH, split_axis=0, concat_axis=0, tiled=True)  7.82 us
    all_to_all x1, starting transfers between devices, per_device(): lax.all_to_all(packed, 'ty', split_axis=0, concat_axis=0, tiled=True)  7.64 us
    all_to_all x1, starting transfers between devices, per_device(): lax.all_to_all(jnp.broadcast_to(local_adjoint.astype(jnp.bfloat16)[None],...  7.19 us
  transfers between devices with their start and end apart: 11, of which 8 were waited for; matrix products, arithmetic and copies ran while one was open for 20% of the time, Pallas kernels for 0%

profile of v14, /device:TPU:1, one launch (start us, length us, event | category | flops | bytes accessed | tf_op | source)
XLA Modules:
  0.0 167.4 jit_solution(11959726832561673189)
XLA Ops:
  0.7 0.8 broadcast_multiply_fusion
  2.3 2.0 %fusion.4 = bf16[256,640]{1,0:T(8,128)(2,1)} fusion(bf16[32,4,640]{2,1,0:T(4,128)(2,1)} %param.10, s32[32,4]{0,1:T(4,128)S(1)} %add.99), kind=kOutput, calls=%fused_computation.15 | convolution fusion | flops 42139648 | bytes 492032 | tf_op jit(solution)/shard_map/pbs,pbk->sk/dot_general | solution.py:97
  4.3 7.6 %all-to-all-start = ((bf16[8,32,640]{2,1,0:T(8,128)(2,1)}), bf16[8,32,640]{2,1,0:T(8,128)(2,1)S(1)}, u32[]{:S(2)}, u32[]{:S(2)}) async-start(bf16[8,32,640]{2,1,0:T(8,128)(2,1)} %bitcast.19), calls=%async_computation | async-start | bytes 655360 | tf_op jit(solution)/shard_map/all_to_all | solution.py:104
  12.6 0.7 negate_multiply_fusion
  13.3 1.2 reduce-window.16
  14.6 0.7 reshape.629
  15.3 1.2 reduce-window.14
  17.8 4.2 %all-to-all-done = bf16[8,32,640]{2,1,0:T(8,128)(2,1)S(1)} async-done(((bf16[8,32,640]{2,1,0:T(8,128)(2,1)}), bf16[8,32,640]{2,1,0:T(8,128)(2,1)S(1)}, u32[]{:S(2)}, u32[]{:S(2)}) %all-to-all-start) | async-done | bytes 327712 | tf_op jit(solution)/shard_map/all_to_all | solution.py:104
  22.1 6.0 %collective-permute-start.3 = (bf16[8,32,640]{2,1,0:T(8,128)(2,1)S(1)}, bf16[8,32,640]{2,1,0:T(8,128)(2,1)S(1)}, u32[]{:S(2)}, u32[]{:S(2)}) collective-permute-start(bf16[8,32,640]{2,1,0:T(8,128)(2,1)S(1)} %all-to-all-done), channel_id=1, source_target_pairs={{0,64},{64,128},{128,192},{192,256},{256,320},{320,384},{384,448},... | collective-permute-start | bytes 983048 | tf_op jit(solution)/shard_map/ppermute | solution.py:66
  28.0 0.8 copy_bitcast_fusion.1
  28.8 8.6 %collective-permute-start = (bf16[8,32,640]{2,1,0:T(8,128)(2,1)S(1)}, bf16[8,32,640]{2,1,0:T(8,128)(2,1)S(1)}, u32[]{:S(2)}, u32[]{:S(2)}) collective-permute-start(bf16[8,32,640]{2,1,0:T(8,128)(2,1)S(1)} %all-to-all-done), channel_id=1, source_target_pairs={{0,448},{64,0},{128,64},{192,128},{256,192},{320,256},{384,320},{4... | collective-permute-start | bytes 983048 | tf_op jit(solution)/shard_map/ppermute | solution.py:69
  37.4 1.3 fusion.26
  38.7 2.0 %collective-permute-done.3 = bf16[8,32,640]{2,1,0:T(8,128)(2,1)S(1)} collective-permute-done((bf16[8,32,640]{2,1,0:T(8,128)(2,1)S(1)}, bf16[8,32,640]{2,1,0:T(8,128)(2,1)S(1)}, u32[]{:S(2)}, u32[]{:S(2)}) %collective-permute-start.3) | collective-permute-done | bytes 327712 | tf_op jit(solution)/shard_map/ppermute | solution.py:66
  40.7 1.9 %collective-permute-start.4 = (bf16[8,32,640]{2,1,0:T(8,128)(2,1)S(1)}, bf16[8,32,640]{2,1,0:T(8,128)(2,1)S(1)}, u32[]{:S(2)}, u32[]{:S(2)}) collective-permute-start(bf16[8,32,640]{2,1,0:T(8,128)(2,1)S(1)} %collective-permute-done.3), channel_id=1, source_target_pairs={{0,64},{64,128},{128,192},{192,256},{256,320},{320,384},{384,448},... | collective-permute-start | bytes 983048 | tf_op jit(solution)/shard_map/ppermute | solution.py:66
  42.6 5.0 %collective-permute-start.1 = (bf16[8,32,640]{2,1,0:T(8,128)(2,1)S(1)}, bf16[8,32,640]{2,1,0:T(8,128)(2,1)S(1)}, u32[]{:S(2)}, u32[]{:S(2)}) collective-permute-start(bf16[8,32,640]{2,1,0:T(8,128)(2,1)S(1)} %collective-permute-done), channel_id=1, source_target_pairs={{0,448},{64,0},{128,64},{192,128},{256,192},{320,256},{384,320},{4... | collective-permute-start | bytes 983048 | tf_op jit(solution)/shard_map/ppermute | solution.py:69
  47.9 2.4 %collective-permute-done.4 = bf16[8,32,640]{2,1,0:T(8,128)(2,1)S(1)} collective-permute-done((bf16[8,32,640]{2,1,0:T(8,128)(2,1)S(1)}, bf16[8,32,640]{2,1,0:T(8,128)(2,1)S(1)}, u32[]{:S(2)}, u32[]{:S(2)}) %collective-permute-start.4) | collective-permute-done | bytes 327712 | tf_op jit(solution)/shard_map/ppermute | solution.py:66
  50.4 1.9 %collective-permute-start.5 = (bf16[8,32,640]{2,1,0:T(8,128)(2,1)S(1)}, bf16[8,32,640]{2,1,0:T(8,128)(2,1)S(1)}, u32[]{:S(2)}, u32[]{:S(2)}) collective-permute-start(bf16[8,32,640]{2,1,0:T(8,128)(2,1)S(1)} %collective-permute-done.4), channel_id=1, source_target_pairs={{0,64},{64,128},{128,192},{192,256},{256,320},{320,384},{384,448},... | collective-permute-start | bytes 983048 | tf_op jit(solution)/shard_map/ppermute | solution.py:66
  52.3 4.7 %collective-permute-start.2 = (bf16[8,32,640]{2,1,0:T(8,128)(2,1)S(1)}, bf16[8,32,640]{2,1,0:T(8,128)(2,1)S(1)}, u32[]{:S(2)}, u32[]{:S(2)}) collective-permute-start(bf16[8,32,640]{2,1,0:T(8,128)(2,1)S(1)} %collective-permute-done.1), channel_id=1, source_target_pairs={{0,448},{64,0},{128,64},{192,128},{256,192},{320,256},{384,320},{4... | collective-permute-start | bytes 983048 | tf_op jit(solution)/shard_map/ppermute | solution.py:69
  57.1 2.3 %collective-permute-done.5 = bf16[8,32,640]{2,1,0:T(8,128)(2,1)S(1)} collective-permute-done((bf16[8,32,640]{2,1,0:T(8,128)(2,1)S(1)}, bf16[8,32,640]{2,1,0:T(8,128)(2,1)S(1)}, u32[]{:S(2)}, u32[]{:S(2)}) %collective-permute-start.5) | collective-permute-done | bytes 327712 | tf_op jit(solution)/shard_map/ppermute | solution.py:66
  59.4 1.9 %collective-permute-start.6 = (bf16[8,32,640]{2,1,0:T(8,128)(2,1)S(1)}, bf16[8,32,640]{2,1,0:T(8,128)(2,1)S(1)}, u32[]{:S(2)}, u32[]{:S(2)}) collective-permute-start(bf16[8,32,640]{2,1,0:T(8,128)(2,1)S(1)} %collective-permute-done.5), channel_id=1, source_target_pairs={{0,64},{64,128},{128,192},{192,256},{256,320},{320,384},{384,448},... | collective-permute-start | bytes 983048 | tf_op jit(solution)/shard_map/ppermute | solution.py:66
  61.4 7.0 %collective-permute-done.6 = bf16[8,32,640]{2,1,0:T(8,128)(2,1)S(1)} collective-permute-done((bf16[8,32,640]{2,1,0:T(8,128)(2,1)S(1)}, bf16[8,32,640]{2,1,0:T(8,128)(2,1)S(1)}, u32[]{:S(2)}, u32[]{:S(2)}) %collective-permute-start.6) | collective-permute-done | bytes 327712 | tf_op jit(solution)/shard_map/ppermute | solution.py:66
  69.0 0.6 multiply_reduce_fusion
  69.7 1.8 %convolution_convert_fusion = bf16[8,256,512]{2,1,0:T(8,128)(2,1)S(1)} fusion(bf16[8,256,640]{2,1,0:T(8,128)(2,1)S(1)} %bitcast.236, bf16[1,640,512]{2,1,0:T(8,128)(2,1)S(1)} %copy-done), kind=kOutput, calls=%fused_computation.7 | convolution fusion | flops 1343225856 | bytes 5373952 | tf_op jit(solution)/shard_map/dot_general | solution.py:132
  71.6 1.8 %pad_maximum_fusion = bf16[8,323,512]{2,1,0:T(8,128)(2,1)} fusion(bf16[8,66,512]{2,1,0:T(8,128)(2,1)S(1)} %broadcast_in_dim.134, bf16[8,1,512]{2,1,0:T(2,128)(2,1)S(1)} %copy.153, bf16[8,256,512]{2,1,0:T(8,128)(2,1)S(1)} %convolution_convert_fusion), kind=kLoop, calls=%fused_computation.6 | loop fusion | flops 7938048 | bytes 5292032 | tf_op jit(solution)/shard_map/concatenate | solution.py:144
  73.4 10.1 %all-to-all-start.1 = ((bf16[8,323,512]{2,1,0:T(8,128)(2,1)}), bf16[8,323,512]{2,1,0:T(8,128)(2,1)S(1)}, u32[]{:S(2)}, u32[]{:S(2)}) async-start(bf16[8,323,512]{2,1,0:T(8,128)(2,1)} %pad_maximum_fusion), calls=%async_computation.1 | async-start | bytes 5373952 | tf_op jit(solution)/shard_map/all_to_all | solution.py:145
  84.2 0.7 constant_dynamic-slice_fusion
  85.0 0.7 eq.140
  85.7 0.8 copy.157
  86.5 3.2 %select_reduce_fusion = s32[8,128]{0,1:T(8,128)} fusion(s32[8,128]{0,1:T(8,128)S(1)} %copy.157), kind=kOutput, calls=%fused_computation.51 | output fusion | flops 1096704 | bytes 8192 | tf_op jit(solution)/shard_map/jit(cumsum)/reduce_window_sum | solution.py:23
  89.7 0.9 copy.158
  90.6 0.8 reduce_sum.63
  91.4 0.8 add.108
  92.2 1.6 fusion.56
  93.8 1.6 copy.159
  95.4 0.6 multiply_add_fusion
  96.0 0.8 broadcast_bitcast_fusion
  96.8 0.6 copy-done.9
  97.4 1.5 convolution_multiply_fusion.1
  99.0 2.5 %convolution_bitcast_fusion.8 = f32[256,4,1,64]{0,3,1,2:T(8,128)} fusion(f32[4,256,256]{2,1,0:T(8,128)S(1)} %convolution_multiply_fusion.1, bf16[256,4,1,64]{0,3,2,1:T(8,128)(2,1)} %param.13, f32[256,4]{0,1:T(4,128)S(1)} %get-tuple-element.32), kind=kOutput, calls=%fused_computation.33 | convolution fusion | flops 100794368 | bytes 1445888 | tf_op jit(solution)/shard_map/bhij,jbhp->ibhp/dot_general | solution.py:179
  101.4 0.6 fusion.69
  102.0 14.0 %all-to-all-done.1 = bf16[8,323,512]{2,1,0:T(8,128)(2,1)S(1)} async-done(((bf16[8,323,512]{2,1,0:T(8,128)(2,1)}), bf16[8,323,512]{2,1,0:T(8,128)(2,1)S(1)}, u32[]{:S(2)}, u32[]{:S(2)}) %all-to-all-start.1) | async-done | bytes 2646048 | tf_op jit(solution)/shard_map/all_to_all | solution.py:145
  116.4 0.8 fusion.33
  117.2 1.8 %copy.160 = bf16[256,512]{0,1:T(8,128)(2,1)} copy(bf16[256,512]{1,0:T(8,128)(2,1)} %fusion.33) | data formatting | bytes 524288 | tf_op jit(solution)/shard_map/convert_element_type | solution.py:154
  119.0 7.0 %all-to-all-start.2 = ((bf16[64,8,256]{2,1,0:T(8,128)(2,1)}), bf16[64,8,256]{2,1,0:T(8,128)(2,1)}, u32[]{:S(2)}, u32[]{:S(2)}) async-start(bf16[64,8,256]{2,1,0:T(8,128)(2,1)} %bitcast.247), calls=%async_computation.2 | async-start | bytes 524288 | tf_op jit(solution)/shard_map/all_to_all | solution.py:158
  126.4 0.9 select_reduce_fusion.2
  127.3 0.6 broadcast_select_fusion
  128.0 0.6 broadcast_select_fusion.1
  128.6 0.5 multiply_reduce_fusion.2
  129.1 1.4 fusion.15
  130.5 7.8 %all-to-all-done.2 = bf16[64,8,256]{2,1,0:T(8,128)(2,1)} async-done(((bf16[64,8,256]{2,1,0:T(8,128)(2,1)}), bf16[64,8,256]{2,1,0:T(8,128)(2,1)}, u32[]{:S(2)}, u32[]{:S(2)}) %all-to-all-start.2) | async-done | bytes 262176 | tf_op jit(solution)/shard_map/all_to_all | solution.py:158
  138.3 2.7 %fusion.20 = f32[256,4,1,64]{0,3,1,2:T(8,128)S(1)} fusion(f32[256,4,1,64]{0,3,1,2:T(8,128)S(1)} %fusion.15, s32[8,256]{1,0:T(8,128)} %multiply_add_fusion, s32[256,4]{0,1:T(4,128)} %copy.159, bf16[8,8,8,256]{3,1,2,0:T(8,128)(2,1)} %bitcast.44), kind=kOutput, calls=%fused_computation.31 | convolution fusion | flops 270598144 | bytes 798720 | tf_op jit(solution)/shard_map/rfq,jfcq->rjc/dot_general | solution.py:172
  141.0 1.8 %convolution_multiply_fusion = f32[4,256,256]{2,1,0:T(8,128)S(1)} fusion(f32[4,256]{1,0:T(4,128)} %copy-done.9, s32[4,256]{1,0:T(4,128)} %bitcast.251, pred[256,256]{1,0:T(8,128)(4,1)} %copy-done.6, f32[256,4,1,64]{0,3,1,2:T(8,128)S(1)} %fusion.20, bf16[256,4,1,64]{0,3,2,1:T(8,128)(2,1)S(1)} %copy-done.4, f32[256,4]{0,1:T(4,128)S(1)} %get-tuple-element.32), kind=kOutput, calls=%fused_computation.8 | convolution fusion | flops 102367232 | bytes 1519616 | tf_op jit(solution)/shard_map/ibhp,jbhp->bhij/dot_general | solution.py:199
  143.2 1.3 convolution_bitcast_fusion.2
  144.4 0.9 broadcast_in_dim.140
  145.4 7.2 %all-to-all-start.3 = ((bf16[8,4,1,128,64]{3,4,2,1,0:T(8,128)(2,1)}), bf16[8,4,1,128,64]{3,4,2,1,0:T(8,128)(2,1)}, u32[]{:S(2)}, u32[]{:S(2)}) async-start(bf16[8,4,1,128,64]{3,4,2,1,0:T(8,128)(2,1)} %broadcast_in_dim.140), calls=%async_computation.3 | async-start | bytes 1048576 | tf_op jit(solution)/shard_map/all_to_all | solution.py:186
  152.6 2.1 %fusion.9 = bf16[256,4,1,128]{3,0,1,2:T(8,128)(2,1)S(1)} fusion(f32[256,4,1,128]{3,0,1,2:T(8,128)} %convolution_bitcast_fusion.2, f32[4,64,128]{2,1,0:T(8,128)S(1)} %multiply_reduce_fusion.2, f32[256,4,1,64]{0,3,1,2:T(8,128)S(1)} %fusion.20, f32[256,4]{0,1:T(4,128)S(1)} %get-tuple-element.20), kind=kOutput, calls=%fused_computation.20 | convolution fusion | flops 101056512 | bytes 1183744 | tf_op jit(solution)/shard_map/ibhp,bhpn->ibhn/dot_general | solution.py:205
  154.7 0.9 copy.172
  155.6 1.1 convolution_bitcast_fusion.7
  156.8 0.8 convolution_bitcast_fusion.4
  157.5 4.5 %all-to-all-done.3 = bf16[8,4,1,128,64]{3,4,2,1,0:T(8,128)(2,1)} async-done(((bf16[8,4,1,128,64]{3,4,2,1,0:T(8,128)(2,1)}), bf16[8,4,1,128,64]{3,4,2,1,0:T(8,128)(2,1)}, u32[]{:S(2)}, u32[]{:S(2)}) %all-to-all-start.3) | async-done | bytes 524320 | tf_op jit(solution)/shard_map/all_to_all | solution.py:186
  162.0 1.2 multiply_reduce_fusion.1
  163.3 1.1 fusion.10
  164.4 0.9 copy.171
  165.3 2.1 %fusion.25 = bf16[256,4,1,64]{0,3,2,1:T(8,128)(2,1)} fusion(f32[256,4,1,64]{0,3,1,2:T(8,128)} %convolution_bitcast_fusion.7, f32[4,128,64]{1,2,0:T(8,128)S(1)} %multiply_reduce_fusion.1, f32[256,4,1,64]{0,3,1,2:T(8,128)S(1)} %fusion.20, bf16[256,4,128]{2,1,0:T(4,128)(2,1)} %bitcast.245, f32[256,4]{0,1:T(4,128)S(1)} %get-tuple-element.33, f32[]{:T(128)} %bitcast.235, ...), kind=kOutput, calls=%fused_computation.36 | convolution fusion | flops 101056512 | bytes 1056772 | tf_op jit(solution)/shard_map/jbhn,bhnp->jbhp/dot_general | solution.py:195
  (91 shorter events, 4.5 us)
Async XLA Ops:
  0.6 69.1 %copy-start = (bf16[1,640,512]{2,1,0:T(8,128)(2,1)S(1)}, bf16[1,640,512]{2,1,0:T(8,128)(2,1)}, u32[]{:S(2)}) copy-start(bf16[1,640,512]{2,1,0:T(8,128)(2,1)} %param.11) | copy-start | bytes 1966084
  4.3 17.8 %all-to-all-start = ((bf16[8,32,640]{2,1,0:T(8,128)(2,1)}), bf16[8,32,640]{2,1,0:T(8,128)(2,1)S(1)}, u32[]{:S(2)}, u32[]{:S(2)}) async-start(bf16[8,32,640]{2,1,0:T(8,128)(2,1)} %bitcast.19), calls=%async_computation | async-start | bytes 655360 | tf_op jit(solution)/shard_map/all_to_all | solution.py:104
  17.1 0.6 copy-start.7
  17.2 0.6 copy-start.8
  22.1 18.6 %collective-permute-start.3 = (bf16[8,32,640]{2,1,0:T(8,128)(2,1)S(1)}, bf16[8,32,640]{2,1,0:T(8,128)(2,1)S(1)}, u32[]{:S(2)}, u32[]{:S(2)}) collective-permute-start(bf16[8,32,640]{2,1,0:T(8,128)(2,1)S(1)} %all-to-all-done), channel_id=1, source_target_pairs={{0,64},{64,128},{128,192},{192,256},{256,320},{320,384},{384,448},... | collective-permute-start | bytes 983048 | tf_op jit(solution)/shard_map/ppermute | solution.py:66
  28.8 13.8 %collective-permute-start = (bf16[8,32,640]{2,1,0:T(8,128)(2,1)S(1)}, bf16[8,32,640]{2,1,0:T(8,128)(2,1)S(1)}, u32[]{:S(2)}, u32[]{:S(2)}) collective-permute-start(bf16[8,32,640]{2,1,0:T(8,128)(2,1)S(1)} %all-to-all-done), channel_id=1, source_target_pairs={{0,448},{64,0},{128,64},{192,128},{256,192},{320,256},{384,320},{4... | collective-permute-start | bytes 983048 | tf_op jit(solution)/shard_map/ppermute | solution.py:69
  40.7 9.7 %collective-permute-start.4 = (bf16[8,32,640]{2,1,0:T(8,128)(2,1)S(1)}, bf16[8,32,640]{2,1,0:T(8,128)(2,1)S(1)}, u32[]{:S(2)}, u32[]{:S(2)}) collective-permute-start(bf16[8,32,640]{2,1,0:T(8,128)(2,1)S(1)} %collective-permute-done.3), channel_id=1, source_target_pairs={{0,64},{64,128},{128,192},{192,256},{256,320},{320,384},{384,448},... | collective-permute-start | bytes 983048 | tf_op jit(solution)/shard_map/ppermute | solution.py:66
  42.6 9.7 %collective-permute-start.1 = (bf16[8,32,640]{2,1,0:T(8,128)(2,1)S(1)}, bf16[8,32,640]{2,1,0:T(8,128)(2,1)S(1)}, u32[]{:S(2)}, u32[]{:S(2)}) collective-permute-start(bf16[8,32,640]{2,1,0:T(8,128)(2,1)S(1)} %collective-permute-done), channel_id=1, source_target_pairs={{0,448},{64,0},{128,64},{192,128},{256,192},{320,256},{384,320},{4... | collective-permute-start | bytes 983048 | tf_op jit(solution)/shard_map/ppermute | solution.py:69
  50.4 9.0 %collective-permute-start.5 = (bf16[8,32,640]{2,1,0:T(8,128)(2,1)S(1)}, bf16[8,32,640]{2,1,0:T(8,128)(2,1)S(1)}, u32[]{:S(2)}, u32[]{:S(2)}) collective-permute-start(bf16[8,32,640]{2,1,0:T(8,128)(2,1)S(1)} %collective-permute-done.4), channel_id=1, source_target_pairs={{0,64},{64,128},{128,192},{192,256},{256,320},{320,384},{384,448},... | collective-permute-start | bytes 983048 | tf_op jit(solution)/shard_map/ppermute | solution.py:66
  52.3 9.0 %collective-permute-start.2 = (bf16[8,32,640]{2,1,0:T(8,128)(2,1)S(1)}, bf16[8,32,640]{2,1,0:T(8,128)(2,1)S(1)}, u32[]{:S(2)}, u32[]{:S(2)}) collective-permute-start(bf16[8,32,640]{2,1,0:T(8,128)(2,1)S(1)} %collective-permute-done.1), channel_id=1, source_target_pairs={{0,448},{64,0},{128,64},{192,128},{256,192},{320,256},{384,320},{4... | collective-permute-start | bytes 983048 | tf_op jit(solution)/shard_map/ppermute | solution.py:69
  59.4 9.0 %collective-permute-start.6 = (bf16[8,32,640]{2,1,0:T(8,128)(2,1)S(1)}, bf16[8,32,640]{2,1,0:T(8,128)(2,1)S(1)}, u32[]{:S(2)}, u32[]{:S(2)}) collective-permute-start(bf16[8,32,640]{2,1,0:T(8,128)(2,1)S(1)} %collective-permute-done.5), channel_id=1, source_target_pairs={{0,64},{64,128},{128,192},{192,256},{256,320},{320,384},{384,448},... | collective-permute-start | bytes 983048 | tf_op jit(solution)/shard_map/ppermute | solution.py:66
  73.4 42.7 %all-to-all-start.1 = ((bf16[8,323,512]{2,1,0:T(8,128)(2,1)}), bf16[8,323,512]{2,1,0:T(8,128)(2,1)S(1)}, u32[]{:S(2)}, u32[]{:S(2)}) async-start(bf16[8,323,512]{2,1,0:T(8,128)(2,1)} %pad_maximum_fusion), calls=%async_computation.1 | async-start | bytes 5373952 | tf_op jit(solution)/shard_map/all_to_all | solution.py:145
  95.4 6.0 %copy-start.11 = (pred[8]{0:T(512)(128)(4,1)}, pred[8]{0:T(512)(128)(4,1)S(1)}, u32[]{:S(2)}) copy-start(pred[8]{0:T(512)(128)(4,1)S(1)} %iota_compare_fusion.8) | copy-start | bytes 28
  95.4 6.0 %copy-start.10 = (pred[8]{0:T(512)(128)(4,1)}, pred[8]{0:T(512)(128)(4,1)S(1)}, u32[]{:S(2)}) copy-start(pred[8]{0:T(512)(128)(4,1)S(1)} %iota_compare_fusion.9) | copy-start | bytes 28
  96.0 30.3 %copy-start.6 = (pred[256,256]{1,0:T(8,128)(4,1)}, pred[256,256]{1,0:T(8,128)(4,1)S(1)}, u32[]{:S(2)}) copy-start(pred[256,256]{1,0:T(8,128)(4,1)S(1)} %iota_compare_fusion.2) | copy-start | bytes 196612
  96.8 0.6 copy-start.9
  98.9 2.5 %copy-start.1 = (f32[4,256,256]{2,1,0:T(8,128)}, f32[4,256,256]{2,1,0:T(8,128)S(1)}, u32[]{:S(2)}) copy-start(f32[4,256,256]{2,1,0:T(8,128)S(1)} %convolution_multiply_fusion.1) | copy-start | bytes 3145732
  99.0 30.1 %copy-start.4 = (bf16[256,4,1,64]{0,3,2,1:T(8,128)(2,1)S(1)}, bf16[256,4,1,64]{0,3,2,1:T(8,128)(2,1)}, u32[]{:S(2)}) copy-start(bf16[256,4,1,64]{0,3,2,1:T(8,128)(2,1)} %param.13) | copy-start | bytes 393220
  119.0 19.4 %all-to-all-start.2 = ((bf16[64,8,256]{2,1,0:T(8,128)(2,1)}), bf16[64,8,256]{2,1,0:T(8,128)(2,1)}, u32[]{:S(2)}, u32[]{:S(2)}) async-start(bf16[64,8,256]{2,1,0:T(8,128)(2,1)} %bitcast.247), calls=%async_computation.2 | async-start | bytes 524288 | tf_op jit(solution)/shard_map/all_to_all | solution.py:158
  126.1 16.7 %copy-start.3 = (bf16[256,4,1,128]{3,1,2,0:T(4,128)(2,1)S(1)}, bf16[256,4,1,128]{3,1,2,0:T(4,128)(2,1)}, u32[]{:S(2)}) copy-start(bf16[256,4,1,128]{3,1,2,0:T(4,128)(2,1)} %param.15) | copy-start | bytes 786436
  138.3 4.8 %copy-start.5 = (bf16[256,4,1,128]{3,1,2,0:T(4,128)(2,1)S(1)}, bf16[256,4,1,128]{3,1,2,0:T(4,128)(2,1)}, u32[]{:S(2)}) copy-start(bf16[256,4,1,128]{3,1,2,0:T(4,128)(2,1)} %param.14) | copy-start | bytes 786436
  138.3 17.3 %copy-start.2 = (f32[4,256,256]{2,1,0:T(8,128)S(1)}, f32[4,256,256]{2,1,0:T(8,128)}, u32[]{:S(2)}) copy-start(f32[4,256,256]{2,1,0:T(8,128)} %copy-done.1) | copy-start | bytes 3145732
  145.4 16.7 %all-to-all-start.3 = ((bf16[8,4,1,128,64]{3,4,2,1,0:T(8,128)(2,1)}), bf16[8,4,1,128,64]{3,4,2,1,0:T(8,128)(2,1)}, u32[]{:S(2)}, u32[]{:S(2)}) async-start(bf16[8,4,1,128,64]{3,4,2,1,0:T(8,128)(2,1)} %broadcast_in_dim.140), calls=%async_computation.3 | async-start | bytes 1048576 | tf_op jit(solution)/shard_map/all_to_all | solution.py:186

commit v15 on v13

--- a/solution.py
+++ b/solution.py
@@ -54,24 +54,28 @@
     return jnp.sum(weights[:, :, :, None, None] * local_all.astype(jnp.float32), axis=0)
 
 
-def ring_gather(x, axis):
+def ring_apply(x, axis, work):
     count = lax.axis_size(axis)
     ahead = [(i, (i + 1) % count) for i in range(count)]
     behind = [(i, (i - 1) % count) for i in range(count)]
     later = [None] * count
-    later[0] = x
+    later[0] = work(x)
     cw = x
     ccw = x
     for hop in range(1, count // 2 + 1):
         cw = lax.ppermute(cw, axis, ahead)
-        later[count - hop] = cw
+        later[count - hop] = work(cw)
         if hop < count - hop:
             ccw = lax.ppermute(ccw, axis, behind)
-            later[hop] = ccw
-    rel = jnp.stack(later)
+            later[hop] = work(ccw)
     place = lax.axis_index(axis)
-    doubled = jnp.concatenate([rel, rel])
-    return lax.dynamic_slice_in_dim(doubled, (count - place) % count, count)
+
+    def order(*parts):
+        rel = jnp.stack(parts)
+        doubled = jnp.concatenate([rel, rel])
+        return lax.dynamic_slice_in_dim(doubled, (count - place) % count, count)
+
+    return jax.tree.map(order, *later)
 
 
 def per_device(
@@ -98,7 +102,6 @@
     packed = jnp.dot(select.T, own_rows, preferred_element_type=jnp.float32).astype(jnp.bfloat16)
     packed = packed.reshape(FAM, CAP, feat_width)
     by_family = lax.all_to_all(packed, "ty", split_axis=0, concat_axis=0, tiled=True)
-    received = ring_gather(by_family, "tz")
     x_full = x_in.astype(jnp.float32)
     b_full = b_in.astype(jnp.float32)
     c_full = c_in.astype(jnp.float32)
@@ -122,11 +125,14 @@
         ],
         axis=2,
     )
-    slots_all = n_z * n_y * CAP
-    received = received.reshape(slots_all, feat_width)
     weights = teacher_proj[0]
-    partial_value = jnp.dot(received, weights, preferred_element_type=jnp.float32)
-    sq_sums = jnp.sum(jnp.square(received.astype(jnp.float32)), axis=1)
+
+    def project(block):
+        rows_in = block.reshape(-1, feat_width)
+        value = jnp.dot(rows_in, weights, preferred_element_type=jnp.float32).astype(jnp.bfloat16)
+        return value, jnp.sum(jnp.square(rows_in.astype(jnp.float32)), axis=1)
+
+    partial_value, sq_sums = ring_apply(by_family, "tz", project)
     width = partial_value.shape[-1]
     group = n_y * CAP
     partial_value = partial_value.reshape(n_z, group, width)
@@ -137,7 +143,7 @@
     state_rows = jnp.broadcast_to(
         packed_state.reshape(1, -1, width), (n_z, packed_state.size // width, width)
     )
-    outbound = jnp.concatenate([partial_value.astype(jnp.bfloat16), sq_row, state_rows], axis=1)
+    outbound = jnp.concatenate([partial_value, sq_row, state_rows], axis=1)
     inbound = lax.all_to_all(outbound, "seq", split_axis=0, concat_axis=0, tiled=True)
     summed = jnp.sum(inbound[:, : group + 1].astype(jnp.float32), axis=0)
     gathered = inbound[:, group + 1 :].reshape((seq_n,) + packed_state.shape)

time: 169 us -> 182 us (1.077)
  local copies, waits for them, and re-layouts: 17.6 us -> 25.5 us
  matrix products: 22.9 us -> 30.6 us
    dot_general x1 -> x8, matrix products: 1.8 us -> 8.62 us  [project(): jnp.dot(rows_in, weights, preferred_element_type=jnp.float32)]
    unnamed x44 -> x36, local copies, waits for them, and re-layouts: 4.2 us -> 8.95 us
    all_to_all x1, waiting for transfers between devices: 4.24 us -> 1.62 us  [per_device(): lax.all_to_all(packed, 'ty', split_axis=0, concat_axis=0, tiled=True)]
  transfers between devices with their start and end apart: 11 -> 11, of which waited for: 8 -> 9; matrix products, arithmetic and copies ran while one was open for 20% -> 22% of each run, Pallas kernels for 0% -> 0%
where the time goes in v15:
time: 182 us; the launch traced here: 181 us
  starting transfers between devices  61.5 us (34%)
  waiting for transfers between devices  42.6 us (23%)
  matrix products  30.6 us (17%)
  local copies, waits for them, and re-layouts  25.5 us (14%)
  other arithmetic  18.5 us (10%)
  between operations  2.42 us (1%)
    ppermute x3, starting transfers between devices, ring_apply(): ccw = lax.ppermute(ccw, axis, behind)  22.5 us
    all_to_all x1, waiting for transfers between devices, per_device(): lax.all_to_all(outbound, 'seq', split_axis=0, concat_axis=0, tiled=True)  14 us
    ppermute x4, waiting for transfers between devices, ring_apply(): cw = lax.ppermute(cw, axis, ahead)  12.1 us
    all_to_all x1, starting transfers between devices, per_device(): lax.all_to_all(outbound, 'seq', split_axis=0, concat_axis=0, tiled=True)  11 us
    unnamed x36, local copies, waits for them, and re-layouts  8.95 us
    dot_general x8, matrix products, project(): jnp.dot(rows_in, weights, preferred_element_type=jnp.float32)  8.62 us
    all_to_all x1, waiting for transfers between devices, per_device(): lax.all_to_all(outgoing, TEACH, split_axis=0, concat_axis=0, tiled=True)  7.9 us
    ppermute x4, starting transfers between devices, ring_apply(): cw = lax.ppermute(cw, axis, ahead)  7.64 us
  transfers between devices with their start and end apart: 11, of which 9 were waited for; matrix products, arithmetic and copies ran while one was open for 22% of the time, Pallas kernels for 0%

profile of v15, /device:TPU:1, one launch (start us, length us, event | category | flops | bytes accessed | tf_op | source)
XLA Modules:
  0.0 181.1 jit_solution(14657747022476758731)
XLA Ops:
  0.7 0.8 constant_dynamic-slice_fusion.2
  2.1 1.0 reshape.665
  3.1 1.1 convolution_convert_fusion
  4.2 7.6 %all-to-all-start = ((bf16[8,32,640]{2,1,0:T(8,128)(2,1)}), bf16[8,32,640]{2,1,0:T(8,128)(2,1)S(1)}, u32[]{:S(2)}, u32[]{:S(2)}) async-start(bf16[8,32,640]{2,1,0:T(8,128)(2,1)} %bitcast.17), calls=%async_computation | async-start | bytes 655360 | tf_op jit(solution)/shard_map/all_to_all | solution.py:104
  13.2 1.2 reduce-window.16
  15.2 1.2 reduce-window.14
  18.0 0.8 copy_bitcast_fusion.1
  18.7 1.3 fusion.33
  20.3 1.6 all-to-all-done
  21.9 12.7 %collective-permute-start = (bf16[8,32,640]{2,1,0:T(8,128)(2,1)S(1)}, bf16[8,32,640]{2,1,0:T(8,128)(2,1)S(1)}, u32[]{:S(2)}, u32[]{:S(2)}) collective-permute-start(bf16[8,32,640]{2,1,0:T(8,128)(2,1)S(1)} %all-to-all-done), channel_id=1, source_target_pairs={{0,448},{64,0},{128,64},{192,128},{256,192},{320,256},{384,320},{4... | collective-permute-start | bytes 983048 | tf_op jit(solution)/shard_map/ppermute | solution.py:69
  34.8 1.9 %collective-permute-start.3 = (bf16[8,32,640]{2,1,0:T(8,128)(2,1)S(1)}, bf16[8,32,640]{2,1,0:T(8,128)(2,1)S(1)}, u32[]{:S(2)}, u32[]{:S(2)}) collective-permute-start(bf16[8,32,640]{2,1,0:T(8,128)(2,1)S(1)} %all-to-all-done), channel_id=1, source_target_pairs={{0,64},{64,128},{128,192},{192,256},{256,320},{320,384},{384,448},... | collective-permute-start | bytes 983048 | tf_op jit(solution)/shard_map/ppermute | solution.py:66
  36.7 1.1 constant_dynamic-update-slice_fusion.15
  37.8 1.7 collective-permute-done
  39.7 5.3 %collective-permute-start.1 = (bf16[8,32,640]{2,1,0:T(8,128)(2,1)S(1)}, bf16[8,32,640]{2,1,0:T(8,128)(2,1)S(1)}, u32[]{:S(2)}, u32[]{:S(2)}) collective-permute-start(bf16[8,32,640]{2,1,0:T(8,128)(2,1)S(1)} %collective-permute-done), channel_id=1, source_target_pairs={{0,448},{64,0},{128,64},{192,128},{256,192},{320,256},{384,320},{4... | collective-permute-start | bytes 983048 | tf_op jit(solution)/shard_map/ppermute | solution.py:69
  45.3 1.9 %collective-permute-start.4 = (bf16[8,32,640]{2,1,0:T(8,128)(2,1)S(1)}, bf16[8,32,640]{2,1,0:T(8,128)(2,1)S(1)}, u32[]{:S(2)}, u32[]{:S(2)}) collective-permute-start(bf16[8,32,640]{2,1,0:T(8,128)(2,1)S(1)} %collective-permute-done.3), channel_id=1, source_target_pairs={{0,64},{64,128},{128,192},{192,256},{256,320},{320,384},{384,448},... | collective-permute-start | bytes 983048 | tf_op jit(solution)/shard_map/ppermute | solution.py:66
  47.2 1.1 constant_dynamic-update-slice_fusion.14
  48.3 0.8 collective-permute-done.1
  49.3 5.0 %collective-permute-done.4 = bf16[8,32,640]{2,1,0:T(8,128)(2,1)S(1)} collective-permute-done((bf16[8,32,640]{2,1,0:T(8,128)(2,1)S(1)}, bf16[8,32,640]{2,1,0:T(8,128)(2,1)S(1)}, u32[]{:S(2)}, u32[]{:S(2)}) %collective-permute-start.4) | collective-permute-done | bytes 327712 | tf_op jit(solution)/shard_map/ppermute | solution.py:66
  54.3 1.9 %collective-permute-start.5 = (bf16[8,32,640]{2,1,0:T(8,128)(2,1)S(1)}, bf16[8,32,640]{2,1,0:T(8,128)(2,1)S(1)}, u32[]{:S(2)}, u32[]{:S(2)}) collective-permute-start(bf16[8,32,640]{2,1,0:T(8,128)(2,1)S(1)} %collective-permute-done.4), channel_id=1, source_target_pairs={{0,64},{64,128},{128,192},{192,256},{256,320},{320,384},{384,448},... | collective-permute-start | bytes 983048 | tf_op jit(solution)/shard_map/ppermute | solution.py:66
  56.4 4.6 %collective-permute-start.2 = (bf16[8,32,640]{2,1,0:T(8,128)(2,1)S(1)}, bf16[8,32,640]{2,1,0:T(8,128)(2,1)S(1)}, u32[]{:S(2)}, u32[]{:S(2)}) collective-permute-start(bf16[8,32,640]{2,1,0:T(8,128)(2,1)S(1)} %collective-permute-done.1), channel_id=1, source_target_pairs={{0,448},{64,0},{128,64},{192,128},{256,192},{320,256},{384,320},{4... | collective-permute-start | bytes 983048 | tf_op jit(solution)/shard_map/ppermute | solution.py:69
  61.0 1.1 constant_dynamic-update-slice_fusion.13
  62.1 1.2 collective-permute-done.5
  63.5 1.9 %collective-permute-start.6 = (bf16[8,32,640]{2,1,0:T(8,128)(2,1)S(1)}, bf16[8,32,640]{2,1,0:T(8,128)(2,1)S(1)}, u32[]{:S(2)}, u32[]{:S(2)}) collective-permute-start(bf16[8,32,640]{2,1,0:T(8,128)(2,1)S(1)} %collective-permute-done.5), channel_id=1, source_target_pairs={{0,64},{64,128},{128,192},{192,256},{256,320},{320,384},{384,448},... | collective-permute-start | bytes 983048 | tf_op jit(solution)/shard_map/ppermute | solution.py:66
  65.7 1.1 constant_dynamic-update-slice_fusion.12
  66.8 5.8 %collective-permute-done.6 = bf16[8,32,640]{2,1,0:T(8,128)(2,1)S(1)} collective-permute-done((bf16[8,32,640]{2,1,0:T(8,128)(2,1)S(1)}, bf16[8,32,640]{2,1,0:T(8,128)(2,1)S(1)}, u32[]{:S(2)}, u32[]{:S(2)}) %collective-permute-start.6) | collective-permute-done | bytes 327712 | tf_op jit(solution)/shard_map/ppermute | solution.py:66
  72.8 1.1 constant_dynamic-update-slice_fusion.11
  73.9 1.1 constant_dynamic-update-slice_fusion.10
  75.0 1.1 constant_dynamic-update-slice_fusion.9
  76.0 1.1 constant_dynamic-update-slice_fusion.8
  77.1 0.7 constant_dynamic-update-slice_fusion.7
  82.9 1.8 constant_dynamic-slice_fusion.1
  84.9 1.8 %pad_maximum_fusion = bf16[8,323,512]{2,1,0:T(8,128)(2,1)} fusion(bf16[8,66,512]{2,1,0:T(8,128)(2,1)S(1)} %broadcast_in_dim.134, bf16[8,1,512]{2,1,0:T(2,128)(2,1)S(1)} %copy.143, bf16[8,256,512]{2,1,0:T(8,128)(2,1)S(1)} %constant_dynamic-slice_fusion.1), kind=kLoop, calls=%fused_computation.5 | loop fusion | flops 7938048 | bytes 5292032 | tf_op jit(solution)/shard_map/concatenate | solution.py:146
  86.8 11.0 %all-to-all-start.1 = ((bf16[8,323,512]{2,1,0:T(8,128)(2,1)}), bf16[8,323,512]{2,1,0:T(8,128)(2,1)S(1)}, u32[]{:S(2)}, u32[]{:S(2)}) async-start(bf16[8,323,512]{2,1,0:T(8,128)(2,1)} %pad_maximum_fusion), calls=%async_computation.1 | async-start | bytes 5373952 | tf_op jit(solution)/shard_map/all_to_all | solution.py:147
  99.9 0.8 copy.147
  100.7 3.2 %select_reduce_fusion = s32[8,128]{0,1:T(8,128)} fusion(s32[8,128]{0,1:T(8,128)S(1)} %copy.147), kind=kOutput, calls=%fused_computation.79 | output fusion | flops 1096704 | bytes 8192 | tf_op jit(solution)/shard_map/jit(cumsum)/reduce_window_sum | solution.py:23
  103.9 0.9 copy.148
  104.8 0.8 reduce_sum.130
  105.6 0.8 add.110
  106.4 1.6 fusion.69
  108.0 1.6 copy.149
  110.3 0.8 broadcast_bitcast_fusion
  111.6 1.5 convolution_multiply_fusion.1
  113.2 2.5 %convolution_bitcast_fusion.7 = f32[256,4,1,64]{0,3,1,2:T(8,128)} fusion(f32[4,256,256]{2,1,0:T(8,128)S(1)} %convolution_multiply_fusion.1, bf16[256,4,1,64]{0,3,2,1:T(8,128)(2,1)} %param.13, f32[256,4]{0,1:T(4,128)S(1)} %get-tuple-element.44), kind=kOutput, calls=%fused_computation.46 | convolution fusion | flops 100794368 | bytes 1445888 | tf_op jit(solution)/shard_map/bhij,jbhp->ibhp/dot_general | solution.py:181
  116.2 14.0 %all-to-all-done.1 = bf16[8,323,512]{2,1,0:T(8,128)(2,1)S(1)} async-done(((bf16[8,323,512]{2,1,0:T(8,128)(2,1)}), bf16[8,323,512]{2,1,0:T(8,128)(2,1)S(1)}, u32[]{:S(2)}, u32[]{:S(2)}) %all-to-all-start.1) | async-done | bytes 2646048 | tf_op jit(solution)/shard_map/all_to_all | solution.py:147
  130.6 0.8 fusion.47
  131.4 1.8 copy.150
  133.2 5.6 %all-to-all-start.2 = ((bf16[64,8,256]{2,1,0:T(8,128)(2,1)}), bf16[64,8,256]{2,1,0:T(8,128)(2,1)}, u32[]{:S(2)}, u32[]{:S(2)}) async-start(bf16[64,8,256]{2,1,0:T(8,128)(2,1)} %bitcast.285), calls=%async_computation.2 | async-start | bytes 524288 | tf_op jit(solution)/shard_map/all_to_all | solution.py:160
  139.3 0.9 select_reduce_fusion.2
  142.0 1.4 fusion.22
  143.4 7.9 %all-to-all-done.2 = bf16[64,8,256]{2,1,0:T(8,128)(2,1)} async-done(((bf16[64,8,256]{2,1,0:T(8,128)(2,1)}), bf16[64,8,256]{2,1,0:T(8,128)(2,1)}, u32[]{:S(2)}, u32[]{:S(2)}) %all-to-all-start.2) | async-done | bytes 262176 | tf_op jit(solution)/shard_map/all_to_all | solution.py:160
  151.3 2.6 %fusion.27 = f32[256,4,1,64]{0,3,1,2:T(8,128)S(1)} fusion(f32[256,4,1,64]{0,3,1,2:T(8,128)S(1)} %fusion.22, s32[8,256]{1,0:T(8,128)} %multiply_add_fusion, s32[256,4]{0,1:T(4,128)} %copy.149, bf16[8,8,8,256]{3,1,2,0:T(8,128)(2,1)} %bitcast.48), kind=kOutput, calls=%fused_computation.44 | convolution fusion | flops 270598144 | bytes 798720 | tf_op jit(solution)/shard_map/rfq,jfcq->rjc/dot_general | solution.py:174
  153.9 1.9 %convolution_multiply_fusion = f32[4,256,256]{2,1,0:T(8,128)S(1)} fusion(f32[4,256]{1,0:T(4,128)} %copy-done.9, s32[4,256]{1,0:T(4,128)} %bitcast.289, pred[256,256]{1,0:T(8,128)(4,1)} %copy-done.6, f32[256,4,1,64]{0,3,1,2:T(8,128)S(1)} %fusion.27, bf16[256,4,1,64]{0,3,2,1:T(8,128)(2,1)S(1)} %copy-done.4, f32[256,4]{0,1:T(4,128)S(1)} %get-tuple-element.44), kind=kOutput, calls=%fused_computation.6 | convolution fusion | flops 102367232 | bytes 1519616 | tf_op jit(solution)/shard_map/ibhp,jbhp->bhij/dot_general | solution.py:201
  156.1 2.2 %convolution_bitcast_fusion.1 = f32[256,4,1,128]{3,0,1,2:T(8,128)} fusion(f32[4,256,256]{2,1,0:T(8,128)S(1)} %convolution_multiply_fusion, bf16[256,4,128]{2,1,0:T(4,128)(2,1)} %bitcast.283), kind=kOutput, calls=%fused_computation.9 | convolution fusion | flops 201326592 | bytes 1835008 | tf_op jit(solution)/shard_map/bhij,jbhn->ibhn/dot_general | solution.py:206
  158.3 0.9 broadcast_in_dim.140
  159.3 7.1 %all-to-all-start.3 = ((bf16[8,4,1,128,64]{3,4,2,1,0:T(8,128)(2,1)}), bf16[8,4,1,128,64]{3,4,2,1,0:T(8,128)(2,1)}, u32[]{:S(2)}, u32[]{:S(2)}) async-start(bf16[8,4,1,128,64]{3,4,2,1,0:T(8,128)(2,1)} %broadcast_in_dim.140), calls=%async_computation.3 | async-start | bytes 1048576 | tf_op jit(solution)/shard_map/all_to_all | solution.py:188
  166.4 2.1 %fusion.8 = bf16[256,4,1,128]{3,0,1,2:T(8,128)(2,1)S(1)} fusion(f32[256,4,1,128]{3,0,1,2:T(8,128)} %convolution_bitcast_fusion.1, f32[4,64,128]{2,1,0:T(8,128)S(1)} %multiply_reduce_fusion.1, f32[256,4,1,64]{0,3,1,2:T(8,128)S(1)} %fusion.27, f32[256,4]{0,1:T(4,128)S(1)} %get-tuple-element.20), kind=kOutput, calls=%fused_computation.17 | convolution fusion | flops 101056512 | bytes 1183744 | tf_op jit(solution)/shard_map/ibhp,bhpn->ibhn/dot_general | solution.py:207
  168.5 0.9 copy.162
  169.4 1.1 convolution_bitcast_fusion.6
  170.6 0.8 convolution_bitcast_fusion.3
  171.4 4.5 %all-to-all-done.3 = bf16[8,4,1,128,64]{3,4,2,1,0:T(8,128)(2,1)} async-done(((bf16[8,4,1,128,64]{3,4,2,1,0:T(8,128)(2,1)}), bf16[8,4,1,128,64]{3,4,2,1,0:T(8,128)(2,1)}, u32[]{:S(2)}, u32[]{:S(2)}) %all-to-all-start.3) | async-done | bytes 524320 | tf_op jit(solution)/shard_map/all_to_all | solution.py:188
  175.8 1.2 multiply_reduce_fusion
  177.1 1.1 fusion.9
  178.2 0.9 copy.161
  179.1 2.0 %fusion.32 = bf16[256,4,1,64]{0,3,2,1:T(8,128)(2,1)} fusion(f32[256,4,1,64]{0,3,1,2:T(8,128)} %convolution_bitcast_fusion.6, f32[4,128,64]{1,2,0:T(8,128)S(1)} %multiply_reduce_fusion, f32[256,4,1,64]{0,3,1,2:T(8,128)S(1)} %fusion.27, bf16[256,4,128]{2,1,0:T(4,128)(2,1)S(1)} %bitcast.284, f32[256,4]{0,1:T(4,128)S(1)} %get-tuple-element.45, f32[]{:T(128)} %bitcast.266, ...), kind=kOutput, calls=%fused_computation.49 | convolution fusion | flops 101056512 | bytes 1056772 | tf_op jit(solution)/shard_map/jbhn,bhnp->jbhp/dot_general | solution.py:197
  (105 shorter events, 17.1 us)
Async XLA Ops:
  0.6 36.1 %copy-start = (bf16[1,640,512]{2,1,0:T(8,128)(2,1)S(1)}, bf16[1,640,512]{2,1,0:T(8,128)(2,1)}, u32[]{:S(2)}) copy-start(bf16[1,640,512]{2,1,0:T(8,128)(2,1)} %param.11) | copy-start | bytes 1966084
  4.2 17.8 %all-to-all-start = ((bf16[8,32,640]{2,1,0:T(8,128)(2,1)}), bf16[8,32,640]{2,1,0:T(8,128)(2,1)S(1)}, u32[]{:S(2)}, u32[]{:S(2)}) async-start(bf16[8,32,640]{2,1,0:T(8,128)(2,1)} %bitcast.17), calls=%async_computation | async-start | bytes 655360 | tf_op jit(solution)/shard_map/all_to_all | solution.py:104
  17.0 0.6 copy-start.7
  17.6 2.5 %copy-start.8 = (s32[1,4,2,128]{3,1,2,0:T(4,128)}, s32[1,4,2,128]{3,1,2,0:T(4,128)S(1)}, u32[]{:S(2)}) copy-start(s32[1,4,2,128]{3,1,2,0:T(4,128)S(1)} %copy.202) | copy-start | bytes 12292
  21.9 17.6 %collective-permute-start = (bf16[8,32,640]{2,1,0:T(8,128)(2,1)S(1)}, bf16[8,32,640]{2,1,0:T(8,128)(2,1)S(1)}, u32[]{:S(2)}, u32[]{:S(2)}) collective-permute-start(bf16[8,32,640]{2,1,0:T(8,128)(2,1)S(1)} %all-to-all-done), channel_id=1, source_target_pairs={{0,448},{64,0},{128,64},{192,128},{256,192},{320,256},{384,320},{4... | collective-permute-start | bytes 983048 | tf_op jit(solution)/shard_map/ppermute | solution.py:69
  34.8 10.2 %collective-permute-start.3 = (bf16[8,32,640]{2,1,0:T(8,128)(2,1)S(1)}, bf16[8,32,640]{2,1,0:T(8,128)(2,1)S(1)}, u32[]{:S(2)}, u32[]{:S(2)}) collective-permute-start(bf16[8,32,640]{2,1,0:T(8,128)(2,1)S(1)} %all-to-all-done), channel_id=1, source_target_pairs={{0,64},{64,128},{128,192},{192,256},{256,320},{320,384},{384,448},... | collective-permute-start | bytes 983048 | tf_op jit(solution)/shard_map/ppermute | solution.py:66
  39.7 9.3 %collective-permute-start.1 = (bf16[8,32,640]{2,1,0:T(8,128)(2,1)S(1)}, bf16[8,32,640]{2,1,0:T(8,128)(2,1)S(1)}, u32[]{:S(2)}, u32[]{:S(2)}) collective-permute-start(bf16[8,32,640]{2,1,0:T(8,128)(2,1)S(1)} %collective-permute-done), channel_id=1, source_target_pairs={{0,448},{64,0},{128,64},{192,128},{256,192},{320,256},{384,320},{4... | collective-permute-start | bytes 983048 | tf_op jit(solution)/shard_map/ppermute | solution.py:69
  45.3 9.0 %collective-permute-start.4 = (bf16[8,32,640]{2,1,0:T(8,128)(2,1)S(1)}, bf16[8,32,640]{2,1,0:T(8,128)(2,1)S(1)}, u32[]{:S(2)}, u32[]{:S(2)}) collective-permute-start(bf16[8,32,640]{2,1,0:T(8,128)(2,1)S(1)} %collective-permute-done.3), channel_id=1, source_target_pairs={{0,64},{64,128},{128,192},{192,256},{256,320},{320,384},{384,448},... | collective-permute-start | bytes 983048 | tf_op jit(solution)/shard_map/ppermute | solution.py:66
  54.3 9.0 %collective-permute-start.5 = (bf16[8,32,640]{2,1,0:T(8,128)(2,1)S(1)}, bf16[8,32,640]{2,1,0:T(8,128)(2,1)S(1)}, u32[]{:S(2)}, u32[]{:S(2)}) collective-permute-start(bf16[8,32,640]{2,1,0:T(8,128)(2,1)S(1)} %collective-permute-done.4), channel_id=1, source_target_pairs={{0,64},{64,128},{128,192},{192,256},{256,320},{320,384},{384,448},... | collective-permute-start | bytes 983048 | tf_op jit(solution)/shard_map/ppermute | solution.py:66
  56.4 9.0 %collective-permute-start.2 = (bf16[8,32,640]{2,1,0:T(8,128)(2,1)S(1)}, bf16[8,32,640]{2,1,0:T(8,128)(2,1)S(1)}, u32[]{:S(2)}, u32[]{:S(2)}) collective-permute-start(bf16[8,32,640]{2,1,0:T(8,128)(2,1)S(1)} %collective-permute-done.1), channel_id=1, source_target_pairs={{0,448},{64,0},{128,64},{192,128},{256,192},{320,256},{384,320},{4... | collective-permute-start | bytes 983048 | tf_op jit(solution)/shard_map/ppermute | solution.py:69
  63.5 9.0 %collective-permute-start.6 = (bf16[8,32,640]{2,1,0:T(8,128)(2,1)S(1)}, bf16[8,32,640]{2,1,0:T(8,128)(2,1)S(1)}, u32[]{:S(2)}, u32[]{:S(2)}) collective-permute-start(bf16[8,32,640]{2,1,0:T(8,128)(2,1)S(1)} %collective-permute-done.5), channel_id=1, source_target_pairs={{0,64},{64,128},{128,192},{192,256},{256,320},{320,384},{384,448},... | collective-permute-start | bytes 983048 | tf_op jit(solution)/shard_map/ppermute | solution.py:66
  86.8 43.5 %all-to-all-start.1 = ((bf16[8,323,512]{2,1,0:T(8,128)(2,1)}), bf16[8,323,512]{2,1,0:T(8,128)(2,1)S(1)}, u32[]{:S(2)}, u32[]{:S(2)}) async-start(bf16[8,323,512]{2,1,0:T(8,128)(2,1)} %pad_maximum_fusion), calls=%async_computation.1 | async-start | bytes 5373952 | tf_op jit(solution)/shard_map/all_to_all | solution.py:147
  109.6 6.0 %copy-start.11 = (pred[8]{0:T(512)(128)(4,1)}, pred[8]{0:T(512)(128)(4,1)S(1)}, u32[]{:S(2)}) copy-start(pred[8]{0:T(512)(128)(4,1)S(1)} %iota_compare_fusion.8) | copy-start | bytes 28
  109.6 6.0 %copy-start.10 = (pred[8]{0:T(512)(128)(4,1)}, pred[8]{0:T(512)(128)(4,1)S(1)}, u32[]{:S(2)}) copy-start(pred[8]{0:T(512)(128)(4,1)S(1)} %iota_compare_fusion.9) | copy-start | bytes 28
  110.2 22.9 %copy-start.6 = (pred[256,256]{1,0:T(8,128)(4,1)}, pred[256,256]{1,0:T(8,128)(4,1)S(1)}, u32[]{:S(2)}) copy-start(pred[256,256]{1,0:T(8,128)(4,1)S(1)} %iota_compare_fusion.2) | copy-start | bytes 196612
  111.0 0.6 copy-start.9
  113.2 2.5 %copy-start.1 = (f32[4,256,256]{2,1,0:T(8,128)}, f32[4,256,256]{2,1,0:T(8,128)S(1)}, u32[]{:S(2)}) copy-start(f32[4,256,256]{2,1,0:T(8,128)S(1)} %convolution_multiply_fusion.1) | copy-start | bytes 3145732
  113.2 28.8 %copy-start.4 = (bf16[256,4,1,64]{0,3,2,1:T(8,128)(2,1)S(1)}, bf16[256,4,1,64]{0,3,2,1:T(8,128)(2,1)}, u32[]{:S(2)}) copy-start(bf16[256,4,1,64]{0,3,2,1:T(8,128)(2,1)} %param.13) | copy-start | bytes 393220
  133.2 18.1 %all-to-all-start.2 = ((bf16[64,8,256]{2,1,0:T(8,128)(2,1)}), bf16[64,8,256]{2,1,0:T(8,128)(2,1)}, u32[]{:S(2)}, u32[]{:S(2)}) async-start(bf16[64,8,256]{2,1,0:T(8,128)(2,1)} %bitcast.285), calls=%async_computation.2 | async-start | bytes 524288 | tf_op jit(solution)/shard_map/all_to_all | solution.py:160
  139.0 16.9 %copy-start.3 = (bf16[256,4,1,128]{3,1,2,0:T(4,128)(2,1)S(1)}, bf16[256,4,1,128]{3,1,2,0:T(4,128)(2,1)}, u32[]{:S(2)}) copy-start(bf16[256,4,1,128]{3,1,2,0:T(4,128)(2,1)} %param.15) | copy-start | bytes 786436
  153.9 15.5 %copy-start.2 = (f32[4,256,256]{2,1,0:T(8,128)S(1)}, f32[4,256,256]{2,1,0:T(8,128)}, u32[]{:S(2)}) copy-start(f32[4,256,256]{2,1,0:T(8,128)} %copy-done.1) | copy-start | bytes 3145732
  159.3 16.6 %all-to-all-start.3 = ((bf16[8,4,1,128,64]{3,4,2,1,0:T(8,128)(2,1)}), bf16[8,4,1,128,64]{3,4,2,1,0:T(8,128)(2,1)}, u32[]{:S(2)}, u32[]{:S(2)}) async-start(bf16[8,4,1,128,64]{3,4,2,1,0:T(8,128)(2,1)} %broadcast_in_dim.140), calls=%async_computation.3 | async-start | bytes 1048576 | tf_op jit(solution)/shard_map/all_to_all | solution.py:188
  170.6 8.5 %copy-start.5 = (bf16[256,4,1,128]{3,1,2,0:T(4,128)(2,1)S(1)}, bf16[256,4,1,128]{3,1,2,0:T(4,128)(2,1)}, u32[]{:S(2)}) copy-start(bf16[256,4,1,128]{3,1,2,0:T(4,128)(2,1)} %param.14) | copy-start | bytes 786436
